TPU v7x, 32 devices: a whole 2x2x4 slice. The times are simulated.
32 devices in a mesh: pipe: 2 (over y), expert: 8 (over z, x), dp: 2 (over core).
Axes of the slice: x: 2, y: 2, z: 4, core: 2. Of those that a mesh axis runs over, the one named last changes fastest.
Arguments:
- saved_inputs: bfloat16 [2, 2, 1024, 2560], P('pipe', None, ('expert', 'dp')), may hold values from -30 to 30
- output_grads: bfloat16 [2, 1024, 2560], P(None, ('expert', 'dp')), may hold values from -6 to 6
- entry_grads: bfloat16 [2, 1024, 2560], P('pipe', ('expert', 'dp')), may hold values from -6 to 6
- norm_gain: float32 [2, 2560], P('pipe'), may hold values from 0.4 to 1.6
- expert_ids: int32 [2, 2, 1024, 1], P('pipe', None, ('expert', 'dp')), may hold values from 0 to 1; in each aligned block of 64 rows (0 to 63, 64 to 127, ..., all dimensions but the last counted through in order) at most 48 rows name the same one
- keep_flags: int32 [2, 2, 1024, 1], P('pipe', None, ('expert', 'dp')), may hold values 0 or 1
- combine_weights: bfloat16 [2, 2, 1024, 1], P('pipe', None, ('expert', 'dp')), may hold values from 0.29882812 to 3
- gate_weight: bfloat16 [2, 1536, 2560], P('pipe', 'expert', 'dp'), may hold values from -0.125 to 0.125
- up_weight: bfloat16 [2, 1536, 2560], P('pipe', 'expert', 'dp'), may hold values from -0.125 to 0.125
- down_weight: bfloat16 [2, 1536, 2560], P('pipe', 'expert', 'dp'), may hold values from -0.21875 to 0.21875
Outputs:
- input_grads: bfloat16 [2, 2, 1024, 2560], P('pipe', None, ('expert', 'dp'))
- combine_grads: float32 [2, 2, 1024, 1], P('pipe', None, ('expert', 'dp'))
- gate_grads: bfloat16 [2, 1536, 2560], P('pipe', 'expert', 'dp')
- up_grads: bfloat16 [2, 1536, 2560], P('pipe', 'expert', 'dp')
- down_grads: bfloat16 [2, 1536, 2560], P('pipe', 'expert', 'dp')
Inputs may be any that keep to these rules, and one draw needn't show every extreme that they name: `expert_ids`: within the 64 rows of one device at one section and moment no expert is named more than 48 times; some such blocks reach 48.
All inputs are finite; a program needn't handle non-finite values. No bound on the sum of `keep_flags` on one device may be relied on, other than what follows from the above.
Results may differ from a plain program's by a relative error of at most 0.008.
Values may be sent and summed in bfloat16 or wider, within the bound.
No kernel may reach another device: no remote copies, remote signals or barrier semaphores. Data moves between devices by JAX's collectives and lax.ppermute only.
A program may use at most 64 MiB of HBM per device.

v0:
```python
import jax
import jax.numpy as jnp
from jax import lax
from jax.sharding import PartitionSpec as P

HSPLIT = 4


EPSILON = 1e-06


def shifted(block, axis, distance):
    devices = range(lax.axis_size(axis))
    route = [(i - distance, i) for i in devices if i - distance in devices]
    return lax.ppermute(block, axis, route)


def silu_parts(gate_value):
    sigmoid_value = jax.nn.sigmoid(gate_value)
    return (gate_value * sigmoid_value, sigmoid_value * (1.0 + gate_value * (1.0 - sigmoid_value)))


def contract_last(first_operand, second_operand):
    return lax.dot_general(
        first_operand, second_operand, (((1,), (1,)), ((), ())), preferred_element_type=jnp.float32
    )


def contract_first(first_operand, second_operand):
    return lax.dot_general(
        first_operand, second_operand, (((0,), (0,)), ((), ())), preferred_element_type=jnp.float32
    )


def local(
    saved_inputs,
    output_grads,
    entry_grads,
    norm_gain,
    expert_ids,
    keep_flags,
    combine_weights,
    gate_weight,
    up_weight,
    down_weight,
):
    sections = lax.axis_size("pipe")
    is_last = lax.axis_index("pipe") == sections - 1
    members = lax.axis_size("expert")
    experts_here = members // HSPLIT
    micro_count = saved_inputs.shape[1]
    token_rows = saved_inputs.shape[2]
    feature_count = saved_inputs.shape[3]
    pick_count = expert_ids.shape[3]
    capacity = max(2, 3 * token_rows * pick_count // (2 * experts_here))
    slot_count = experts_here * capacity
    gate_full, up_full, down_full = (
        lax.all_gather(gate_weight[0], "dp", axis=1, tiled=True),
        lax.all_gather(up_weight[0], "dp", axis=1, tiled=True),
        lax.all_gather(down_weight[0], "dp", axis=1, tiled=True),
    )
    hidden_count = gate_full.shape[0]
    paired_weights = jnp.concatenate([gate_full, up_full], axis=0)
    gain_row = norm_gain[0][None, :]
    slot_ids = jnp.arange(slot_count, dtype=jnp.int32)
    expert_range = jnp.arange(experts_here, dtype=jnp.int32)

    def spread(slot_values):
        trailing = slot_values.shape[1:]
        shaped = slot_values.reshape((experts_here, 1, capacity) + trailing)
        tiled = jnp.broadcast_to(shaped, (experts_here, HSPLIT, capacity) + trailing)
        return tiled.reshape((members, capacity) + trailing)

    def prepare(moment):
        inputs = saved_inputs[0, moment].astype(jnp.float32)
        scales = lax.rsqrt(jnp.mean(inputs * inputs, axis=1, keepdims=True) + EPSILON)
        normed = (inputs * scales * gain_row).astype(jnp.bfloat16)
        chosen = expert_ids[0, moment].reshape(-1)
        onehot = (chosen[:, None] == expert_range[None, :]).astype(jnp.int32)
        rank_values = jnp.sum((jnp.cumsum(onehot, axis=0) - 1) * onehot, axis=1)
        places = chosen * capacity + rank_values
        placing = places[:, None] == slot_ids[None, :]
        token_map = jnp.any(placing.reshape(token_rows, pick_count, slot_count), axis=1)
        selector = token_map.T.astype(jnp.bfloat16)
        keeping = keep_flags[0, moment].reshape(-1)
        scaled = (combine_weights[0, moment].reshape(-1) * keeping.astype(jnp.bfloat16)).astype(
            jnp.float32
        )
        weight_slots = jnp.sum(jnp.where(placing, scaled[:, None], 0.0), axis=0).astype(
            jnp.bfloat16
        )
        return (inputs, scales, normed, places, selector, keeping, weight_slots)

    def dispatch_rows(selector, source_rows):
        return spread(
            jnp.dot(selector, source_rows, preferred_element_type=jnp.float32).astype(jnp.bfloat16)
        )

    prepared = [prepare(moment) for moment in range(micro_count)]
    leaving_list = []
    combine_list = []
    kept_list = []
    previous = entry_grads[0]
    for moment in range(micro_count):
        current = prepared[moment]
        if moment == 0:
            arriving = entry_grads[0]
        else:
            arriving = shifted(previous, "pipe", -1)
        incoming = jnp.where(is_last, output_grads[moment], arriving)
        grad_slots = dispatch_rows(current[4], incoming)
        weight_spread = spread(current[6])
        rows_in, grads_in, weights_in = (
            lax.all_to_all(
                dispatch_rows(current[4], current[2]),
                "expert",
                split_axis=0,
                concat_axis=0,
                tiled=True,
            ),
            lax.all_to_all(grad_slots, "expert", split_axis=0, concat_axis=0, tiled=True),
            lax.all_to_all(weight_spread, "expert", split_axis=0, concat_axis=0, tiled=True),
        )
        flat_rows = rows_in.reshape(-1, feature_count)
        flat_grads = grads_in.reshape(-1, feature_count)
        scale_column = weights_in.reshape(-1, 1).astype(jnp.float32)
        gate_value = contract_last(flat_rows, gate_full)
        upward = contract_last(flat_rows, up_full)
        backward = contract_last(flat_grads, down_full)
        active, derivative = silu_parts(gate_value)
        hidden = active * upward
        part_weight = jnp.sum(hidden * backward, axis=1).astype(jnp.bfloat16)
        grad_up = (scale_column * backward * active).astype(jnp.bfloat16)
        grad_gate = (scale_column * backward * upward * derivative).astype(jnp.bfloat16)
        grad_pair = jnp.concatenate([grad_gate, grad_up], axis=1)
        part_rows = jnp.dot(grad_pair, paired_weights, preferred_element_type=jnp.float32).astype(
            jnp.bfloat16
        )
        hidden_scaled = (hidden * scale_column).astype(jnp.bfloat16)
        kept = (grad_pair, hidden_scaled, flat_rows, flat_grads)
        part_rows, part_weight, kept = (
            part_rows.reshape(members, capacity, feature_count),
            part_weight.reshape(members, capacity),
            kept,
        )
        kept_list.append(kept)
        returned_rows, returned_weights = (
            lax.all_to_all(part_rows, "expert", split_axis=0, concat_axis=0, tiled=True),
            lax.all_to_all(part_weight, "expert", split_axis=0, concat_axis=0, tiled=True),
        )
        (
            finish_inputs,
            finish_scales,
            finish_normed,
            finish_places,
            finish_selector,
            finish_keeping,
            finish_weight_slots,
        ) = current
        summed = jnp.sum(
            returned_rows.astype(jnp.float32).reshape(
                experts_here, HSPLIT, capacity, feature_count
            ),
            axis=1,
        ).reshape(slot_count, feature_count)
        weight_sums = jnp.sum(
            returned_weights.astype(jnp.float32).reshape(experts_here, HSPLIT, capacity), axis=1
        ).reshape(slot_count)
        expert_rows = jnp.sum(
            jnp.take(summed, finish_places, axis=0).reshape(token_rows, pick_count, feature_count),
            axis=1,
        )
        combine_grad = (
            jnp.take(weight_sums, finish_places) * finish_keeping.astype(jnp.float32)
        ).reshape(token_rows, pick_count)
        gained = gain_row * expert_rows
        mixed_mean = jnp.mean(finish_inputs * gained, axis=1, keepdims=True)
        leaving = (
            incoming.astype(jnp.float32)
            + finish_scales * gained
            - finish_inputs * (finish_scales * finish_scales * finish_scales) * mixed_mean
        ).astype(jnp.bfloat16)
        previous, combine_grad = (leaving, combine_grad)
        leaving_list.append(previous)
        combine_list.append(combine_grad)
    pair_all = jnp.concatenate([kept[0] for kept in kept_list], axis=0)
    scaled_all = jnp.concatenate([kept[1] for kept in kept_list], axis=0)
    rows_all = jnp.concatenate([kept[2] for kept in kept_list], axis=0)
    grads_all = jnp.concatenate([kept[3] for kept in kept_list], axis=0)
    pair_total = contract_first(pair_all, rows_all).reshape(2, hidden_count, feature_count)
    down_total = contract_first(scaled_all, grads_all)[None]
    pair_reduced, down_reduced = (
        lax.psum_scatter(
            pair_total.astype(jnp.bfloat16), "dp", scatter_dimension=2, tiled=True
        ).astype(jnp.float32),
        lax.psum_scatter(
            down_total.astype(jnp.bfloat16), "dp", scatter_dimension=2, tiled=True
        ).astype(jnp.float32),
    )
    return (
        jnp.stack(leaving_list)[None],
        jnp.stack(combine_list)[None],
        pair_reduced[0:1].astype(jnp.bfloat16),
        pair_reduced[1:2].astype(jnp.bfloat16),
        down_reduced.astype(jnp.bfloat16),
    )


def solution(mesh):
    in_specs = (
        P("pipe", None, ("expert", "dp"), None),
        P(None, ("expert", "dp"), None),
        P("pipe", ("expert", "dp"), None),
        P("pipe", None),
        P("pipe", None, ("expert", "dp"), None),
        P("pipe", None, ("expert", "dp"), None),
        P("pipe", None, ("expert", "dp"), None),
        P("pipe", "expert", "dp"),
        P("pipe", "expert", "dp"),
        P("pipe", "expert", "dp"),
    )
    out_specs = (
        P("pipe", None, ("expert", "dp"), None),
        P("pipe", None, ("expert", "dp"), None),
        P("pipe", "expert", "dp"),
        P("pipe", "expert", "dp"),
        P("pipe", "expert", "dp"),
    )
    return jax.shard_map(local, mesh=mesh, in_specs=in_specs, out_specs=out_specs, check_vma=False)
```

profile of v0, /device:TPU:0, one launch (start us, length us, event | category | flops | bytes accessed | tf_op | source)
XLA Modules:
  0.0 381.8 jit_solution(8575449723714960392)
XLA Ops:
  10.6 7.3 %all-to-all-start = ((bf16[8,1,48]{2,1,0:T(2,128)(2,1)}), bf16[8,1,48]{2,1,0:T(2,128)(2,1)S(1)}, u32[]{:S(2)}, u32[]{:S(2)}) async-start(bf16[8,1,48]{2,1,0:T(2,128)(2,1)} %copy.34), calls=%async_computation | async-start | bytes 8192 | tf_op jit(solution)/shard_map/all_to_all | solution.py:122
  25.7 3.7 all-to-all-start.2
  30.7 43.0 %all-to-all-done.2 = bf16[8,48,2560]{2,1,0:T(8,128)(2,1)S(1)} async-done(((bf16[8,48,2560]{2,1,0:T(8,128)(2,1)}), bf16[8,48,2560]{2,1,0:T(8,128)(2,1)S(1)}, u32[]{:S(2)}, u32[]{:S(2)}) %all-to-all-start.2) | async-done | bytes 1966112 | tf_op jit(solution)/shard_map/all_to_all | solution.py:114
  75.6 4.3 %all-to-all-start.1 = ((bf16[8,48,2560]{2,1,0:T(8,128)(2,1)}), bf16[8,48,2560]{2,1,0:T(8,128)(2,1)}, u32[]{:S(2)}, u32[]{:S(2)}) async-start(bf16[8,48,2560]{2,1,0:T(8,128)(2,1)} %bitcast.8), calls=%async_computation.1 | async-start | bytes 3932160 | tf_op jit(solution)/shard_map/all_to_all | solution.py:121
  87.7 3.4 fusion.90
  92.6 32.3 %all-to-all-done.1 = bf16[8,48,2560]{2,1,0:T(8,128)(2,1)} async-done(((bf16[8,48,2560]{2,1,0:T(8,128)(2,1)}), bf16[8,48,2560]{2,1,0:T(8,128)(2,1)}, u32[]{:S(2)}, u32[]{:S(2)}) %all-to-all-start.1) | async-done | bytes 1966112 | tf_op jit(solution)/shard_map/all_to_all | solution.py:121
  124.9 3.2 multiply_reduce_fusion.1
  128.8 3.6 all-to-all-start.8
  134.9 3.9 %all-to-all-done.8 = bf16[8,1,48]{2,1,0:T(2,128)(2,1)S(1)} async-done(((bf16[8,1,48]{2,1,0:T(2,128)(2,1)}), bf16[8,1,48]{2,1,0:T(2,128)(2,1)S(1)}, u32[]{:S(2)}, u32[]{:S(2)}) %all-to-all-start.8) | async-done | bytes 800 | tf_op jit(solution)/shard_map/all_to_all | solution.py:149
  138.8 3.7 all-to-all-start.3
  144.3 42.7 %all-to-all-done.3 = bf16[8,48,2560]{2,1,0:T(8,128)(2,1)S(1)} async-done(((bf16[8,48,2560]{2,1,0:T(8,128)(2,1)}), bf16[8,48,2560]{2,1,0:T(8,128)(2,1)S(1)}, u32[]{:S(2)}, u32[]{:S(2)}) %all-to-all-start.3) | async-done | bytes 1966112 | tf_op jit(solution)/shard_map/all_to_all | solution.py:148
  188.2 3.6 all-to-all-start.4
  199.7 4.5 %all-to-all-start.6 = ((bf16[8,48,2560]{2,1,0:T(8,128)(2,1)}), bf16[8,48,2560]{2,1,0:T(8,128)(2,1)}, u32[]{:S(2)}, u32[]{:S(2)}) async-start(bf16[8,48,2560]{2,1,0:T(8,128)(2,1)} %bitcast.174), calls=%async_computation.6 | async-start | bytes 3932160 | tf_op jit(solution)/shard_map/all_to_all | solution.py:114
  205.9 8.8 %collective-permute-done = bf16[64,2560]{1,0:T(8,128)(2,1)S(1)} collective-permute-done((bf16[64,2560]{1,0:T(8,128)(2,1)S(1)}, bf16[64,2560]{1,0:T(8,128)(2,1)S(1)}, u32[]{:S(2)}, u32[]{:S(2)}) %collective-permute-start) | collective-permute-done | bytes 327712 | tf_op jit(solution)/shard_map/ppermute | solution.py:15
  215.8 32.8 %all-to-all-done.6 = bf16[8,48,2560]{2,1,0:T(8,128)(2,1)} async-done(((bf16[8,48,2560]{2,1,0:T(8,128)(2,1)}), bf16[8,48,2560]{2,1,0:T(8,128)(2,1)}, u32[]{:S(2)}, u32[]{:S(2)}) %all-to-all-start.6) | async-done | bytes 1966112 | tf_op jit(solution)/shard_map/all_to_all | solution.py:114
  250.2 4.3 %all-to-all-start.5 = ((bf16[8,48,2560]{2,1,0:T(8,128)(2,1)}), bf16[8,48,2560]{2,1,0:T(8,128)(2,1)}, u32[]{:S(2)}, u32[]{:S(2)}) async-start(bf16[8,48,2560]{2,1,0:T(8,128)(2,1)} %bitcast.175), calls=%async_computation.5 | async-start | bytes 3932160 | tf_op jit(solution)/shard_map/all_to_all | solution.py:121
  260.9 38.6 %all-to-all-done.5 = bf16[8,48,2560]{2,1,0:T(8,128)(2,1)} async-done(((bf16[8,48,2560]{2,1,0:T(8,128)(2,1)}), bf16[8,48,2560]{2,1,0:T(8,128)(2,1)}, u32[]{:S(2)}, u32[]{:S(2)}) %all-to-all-start.5) | async-done | bytes 1966112 | tf_op jit(solution)/shard_map/all_to_all | solution.py:121
  299.5 3.6 multiply_reduce_fusion
  303.2 4.6 %convolution_convert_fusion = bf16[384,2560]{1,0:T(8,128)(2,1)} fusion(bf16[384,2560]{1,0:T(8,128)(2,1)} %bitcast.35, bf16[384,2560]{1,0:T(8,128)(2,1)S(1)} %bitcast.182, bf16[384,192]{0,1:T(8,128)(2,1)S(1)} %get-tuple-element.51, bf16[384,192]{0,1:T(8,128)(2,1)S(1)} %get-tuple-element.45, bf16[384,192]{0,1:T(8,128)(2,1)S(1)} %copy-done.22, ...), kind=kOutput, calls=%fused_computation.4 | convolution fusion | flops 1521156096 | bytes 6488064 | tf_op jit(solution)/shard_map/dot_general | solution.py:30
  308.5 3.6 all-to-all-start.9
  312.1 3.5 convolution_convert_fusion.1
  318.6 4.5 %all-to-all-start.7 = ((bf16[8,48,2560]{2,1,0:T(8,128)(2,1)}), bf16[8,48,2560]{2,1,0:T(8,128)(2,1)}, u32[]{:S(2)}, u32[]{:S(2)}) async-start(bf16[8,48,2560]{2,1,0:T(8,128)(2,1)} %bitcast.172), calls=%async_computation.7 | async-start | bytes 3932160 | tf_op jit(solution)/shard_map/all_to_all | solution.py:148
  323.5 4.0 %fusion.10 = bf16[1,192,2560]{2,1,0:T(8,128)(2,1)} fusion(bf16[384,2560]{1,0:T(8,128)(2,1)} %bitcast.30, bf16[384,2560]{1,0:T(8,128)(2,1)} %bitcast.9, bf16[384,192]{0,1:T(8,128)(2,1)S(1)} %copy-done.28, bf16[384,192]{0,1:T(8,128)(2,1)S(1)} %copy-done.27), kind=kOutput, calls=%fused_computation.17 | convolution fusion | flops 763920384 | bytes 5210112 | tf_op jit(solution)/shard_map/dot_general | solution.py:30
  329.0 38.5 %all-to-all-done.7 = bf16[8,48,2560]{2,1,0:T(8,128)(2,1)} async-done(((bf16[8,48,2560]{2,1,0:T(8,128)(2,1)}), bf16[8,48,2560]{2,1,0:T(8,128)(2,1)}, u32[]{:S(2)}, u32[]{:S(2)}) %all-to-all-start.7) | async-done | bytes 1966112 | tf_op jit(solution)/shard_map/all_to_all | solution.py:148
  (136 shorter events, 61.4 us)
Async XLA Ops:
  10.6 13.6 %all-to-all-start = ((bf16[8,1,48]{2,1,0:T(2,128)(2,1)}), bf16[8,1,48]{2,1,0:T(2,128)(2,1)S(1)}, u32[]{:S(2)}, u32[]{:S(2)}) async-start(bf16[8,1,48]{2,1,0:T(2,128)(2,1)} %copy.34), calls=%async_computation | async-start | bytes 8192 | tf_op jit(solution)/shard_map/all_to_all | solution.py:122
  25.7 47.9 %all-to-all-start.2 = ((bf16[8,48,2560]{2,1,0:T(8,128)(2,1)}), bf16[8,48,2560]{2,1,0:T(8,128)(2,1)S(1)}, u32[]{:S(2)}, u32[]{:S(2)}) async-start(bf16[8,48,2560]{2,1,0:T(8,128)(2,1)} %bitcast.13), calls=%async_computation.2 | async-start | bytes 3932160 | tf_op jit(solution)/shard_map/all_to_all | solution.py:114
  75.2 4.7 %copy-start.15 = (bf16[1,192,1280]{2,1,0:T(8,128)(2,1)S(1)}, bf16[1,192,1280]{2,1,0:T(8,128)(2,1)}, u32[]{:S(2)}) copy-start(bf16[1,192,1280]{2,1,0:T(8,128)(2,1)} %param.21) | copy-start | bytes 1474564
  75.2 7.4 %copy-start.16 = (bf16[1,192,1280]{2,1,0:T(8,128)(2,1)S(1)}, bf16[1,192,1280]{2,1,0:T(8,128)(2,1)}, u32[]{:S(2)}) copy-start(bf16[1,192,1280]{2,1,0:T(8,128)(2,1)} %param.22) | copy-start | bytes 1474564
  75.6 49.3 %all-to-all-start.1 = ((bf16[8,48,2560]{2,1,0:T(8,128)(2,1)}), bf16[8,48,2560]{2,1,0:T(8,128)(2,1)}, u32[]{:S(2)}, u32[]{:S(2)}) async-start(bf16[8,48,2560]{2,1,0:T(8,128)(2,1)} %bitcast.8), calls=%async_computation.1 | async-start | bytes 3932160 | tf_op jit(solution)/shard_map/all_to_all | solution.py:121
  79.9 5.2 %copy-start.17 = (bf16[1,192,1280]{2,1,0:T(8,128)(2,1)S(1)}, bf16[1,192,1280]{2,1,0:T(8,128)(2,1)}, u32[]{:S(2)}) copy-start(bf16[1,192,1280]{2,1,0:T(8,128)(2,1)} %param.23) | copy-start | bytes 1474564
  85.1 47.3 %copy-start.1 = (bf16[1,192,2560]{2,1,0:T(8,128)(2,1)}, bf16[1,192,2560]{2,1,0:T(8,128)(2,1)S(1)}, u32[]{:S(2)}) copy-start(bf16[1,192,2560]{2,1,0:T(8,128)(2,1)S(1)} %all-gather.1) | copy-start | bytes 2949124
  87.6 37.3 %copy-start.14 = (bf16[1,192,2560]{2,1,0:T(8,128)(2,1)}, bf16[1,192,2560]{2,1,0:T(8,128)(2,1)S(1)}, u32[]{:S(2)}) copy-start(bf16[1,192,2560]{2,1,0:T(8,128)(2,1)S(1)} %all-gather) | copy-start | bytes 2949124
  128.1 6.8 %copy-start.19 = (bf16[384,192]{0,1:T(8,128)(2,1)}, bf16[384,192]{0,1:T(8,128)(2,1)S(1)}, u32[]{:S(2)}) copy-start(bf16[384,192]{0,1:T(8,128)(2,1)S(1)} %get-tuple-element.47) | copy-start | bytes 442372
  128.1 6.8 %copy-start.21 = (bf16[384,192]{0,1:T(8,128)(2,1)}, bf16[384,192]{0,1:T(8,128)(2,1)S(1)}, u32[]{:S(2)}) copy-start(bf16[384,192]{0,1:T(8,128)(2,1)S(1)} %get-tuple-element.49) | copy-start | bytes 442372
  128.8 10.0 %all-to-all-start.8 = ((bf16[8,1,48]{2,1,0:T(2,128)(2,1)}), bf16[8,1,48]{2,1,0:T(2,128)(2,1)S(1)}, u32[]{:S(2)}, u32[]{:S(2)}) async-start(bf16[8,1,48]{2,1,0:T(2,128)(2,1)} %convert_element_type.335), calls=%async_computation.8 | async-start | bytes 8192 | tf_op jit(solution)/shard_map/all_to_all | solution.py:149
  138.8 5.4 %copy-start.26 = (s32[1,2,64,1]{2,3,1,0:T(1,128)S(1)}, s32[1,2,64,1]{2,3,1,0:T(1,128)}, u32[]{:S(2)}) copy-start(s32[1,2,64,1]{2,3,1,0:T(1,128)} %param.19) | copy-start | bytes 1540
  138.8 48.1 %all-to-all-start.3 = ((bf16[8,48,2560]{2,1,0:T(8,128)(2,1)}), bf16[8,48,2560]{2,1,0:T(8,128)(2,1)S(1)}, u32[]{:S(2)}, u32[]{:S(2)}) async-start(bf16[8,48,2560]{2,1,0:T(8,128)(2,1)} %bitcast.173), calls=%async_computation.3 | async-start | bytes 3932160 | tf_op jit(solution)/shard_map/all_to_all | solution.py:148
  188.2 10.0 %all-to-all-start.4 = ((bf16[8,1,48]{2,1,0:T(2,128)(2,1)}), bf16[8,1,48]{2,1,0:T(2,128)(2,1)S(1)}, u32[]{:S(2)}, u32[]{:S(2)}) async-start(bf16[8,1,48]{2,1,0:T(2,128)(2,1)} %copy.36), calls=%async_computation.4 | async-start | bytes 8192 | tf_op jit(solution)/shard_map/all_to_all | solution.py:122
  199.7 15.7 %copy-start.11 = (bf16[2,64,2560]{2,1,0:T(8,128)(2,1)S(1)}, bf16[2,64,2560]{2,1,0:T(8,128)(2,1)}, u32[]{:S(2)}) copy-start(bf16[2,64,2560]{2,1,0:T(8,128)(2,1)} %param.15) | copy-start | bytes 1966084
  199.7 48.9 %all-to-all-start.6 = ((bf16[8,48,2560]{2,1,0:T(8,128)(2,1)}), bf16[8,48,2560]{2,1,0:T(8,128)(2,1)}, u32[]{:S(2)}, u32[]{:S(2)}) async-start(bf16[8,48,2560]{2,1,0:T(8,128)(2,1)} %bitcast.174), calls=%async_computation.6 | async-start | bytes 3932160 | tf_op jit(solution)/shard_map/all_to_all | solution.py:114
  204.6 10.1 %collective-permute-start = (bf16[64,2560]{1,0:T(8,128)(2,1)S(1)}, bf16[64,2560]{1,0:T(8,128)(2,1)S(1)}, u32[]{:S(2)}, u32[]{:S(2)}) collective-permute-start(bf16[64,2560]{1,0:T(8,128)(2,1)S(1)} %fusion.34), channel_id=1, source_target_pairs={{16,0},{17,1},{18,2},{19,3},{20,4},{21,5},{22,6},{23,7},{24,8},{25... | collective-permute-start | bytes 983048 | tf_op jit(solution)/shard_map/ppermute | solution.py:15
  250.2 49.4 %all-to-all-start.5 = ((bf16[8,48,2560]{2,1,0:T(8,128)(2,1)}), bf16[8,48,2560]{2,1,0:T(8,128)(2,1)}, u32[]{:S(2)}, u32[]{:S(2)}) async-start(bf16[8,48,2560]{2,1,0:T(8,128)(2,1)} %bitcast.175), calls=%async_computation.5 | async-start | bytes 3932160 | tf_op jit(solution)/shard_map/all_to_all | solution.py:121
  254.5 118.3 %reduce-scatter.3.cloned.1.call-start = ((), (), s32[]{:S(2)}) async-start(), calls=%async_computation.12 | async-start | bytes 2949120 | tf_op jit(solution)/shard_map/reduce_scatter | solution.py:193
  308.5 10.1 %all-to-all-start.9 = ((bf16[8,1,48]{2,1,0:T(2,128)(2,1)}), bf16[8,1,48]{2,1,0:T(2,128)(2,1)S(1)}, u32[]{:S(2)}, u32[]{:S(2)}) async-start(bf16[8,1,48]{2,1,0:T(2,128)(2,1)} %convert_element_type.336), calls=%async_computation.9 | async-start | bytes 8192 | tf_op jit(solution)/shard_map/all_to_all | solution.py:149
  318.6 4.9 %copy-start.27 = (bf16[384,192]{0,1:T(8,128)(2,1)S(1)}, bf16[384,192]{0,1:T(8,128)(2,1)}, u32[]{:S(2)}) copy-start(bf16[384,192]{0,1:T(8,128)(2,1)} %get-tuple-element.48) | copy-start | bytes 442372
  318.6 4.9 %copy-start.28 = (bf16[384,192]{0,1:T(8,128)(2,1)S(1)}, bf16[384,192]{0,1:T(8,128)(2,1)}, u32[]{:S(2)}) copy-start(bf16[384,192]{0,1:T(8,128)(2,1)} %get-tuple-element.50) | copy-start | bytes 442372
  318.6 48.9 %all-to-all-start.7 = ((bf16[8,48,2560]{2,1,0:T(8,128)(2,1)}), bf16[8,48,2560]{2,1,0:T(8,128)(2,1)}, u32[]{:S(2)}, u32[]{:S(2)}) async-start(bf16[8,48,2560]{2,1,0:T(8,128)(2,1)} %bitcast.172), calls=%async_computation.7 | async-start | bytes 3932160 | tf_op jit(solution)/shard_map/all_to_all | solution.py:148
  323.0 51.9 %reduce-scatter.5.cloned.1.call-start = ((), (), s32[]{:S(2)}) async-start(), calls=%async_computation.13 | async-start | bytes 1474560 | tf_op jit(solution)/shard_map/reduce_scatter | solution.py:196
  (18 other events, 54.4 us)
Sparse Core Ops, SparseCore 0:
  307.9 8.5 reduce-scatter.2
  327.7 9.7 reduce-scatter.4
where the time goes:
time: 383 us; the launch traced here: 382 us
  waiting for transfers between devices  249 us (65%)
  starting transfers between devices  44.5 us (12%)
  matrix products  35.1 us (9%)
  local copies, waits for them, and re-layouts  18.6 us (5%)
  between operations  14.4 us (4%)
  other arithmetic  12.2 us (3%)
  blocking collectives  7.64 us (2%)
    all_to_all x2, waiting for transfers between devices, local(): lax.all_to_all(part_rows, 'expert', split_axis=0, concat_axis=0, tiled=True)  81.1 us
    all_to_all x2, waiting for transfers between devices, local(): lax.all_to_all(dispatch_rows(current[4], current[2]), 'expert', split_axi...  75.8 us
    all_to_all x2, waiting for transfers between devices, local(): lax.all_to_all(grad_slots, 'expert', split_axis=0, concat_axis=0, tiled=T...  71 us
    dot_general x6, matrix products, contract_last(): lax.dot_general(first_operand, second_operand, (((1,), (1,)), ((), ())),...  17.9 us
    all_to_all x2, starting transfers between devices, local(): lax.all_to_all(weight_spread, 'expert', split_axis=0, concat_axis=0, tile...  10.9 us
    ppermute x1, waiting for transfers between devices, shifted(): return lax.ppermute(block, axis, route)  8.8 us
    all_to_all x2, starting transfers between devices, local(): lax.all_to_all(grad_slots, 'expert', split_axis=0, concat_axis=0, tiled=T...  8.66 us
    dot_general x2, matrix products, contract_first(): lax.dot_general(first_operand, second_operand, (((0,), (0,)), ((), ())),...  8.61 us
  transfers between devices with their start and end apart: 13, of which 11 were waited for; matrix products, arithmetic and copies ran while one was open for 11% of the time, Pallas kernels for 0%

commit v1 on v0

v1 whole, which is shorter than its diff:
```python
import jax
import jax.numpy as jnp
from jax import lax
from jax.sharding import Mesh, PartitionSpec as P

HSPLIT = 4


EPSILON = 1e-06


def shifted(block, axis, distance):
    devices = range(lax.axis_size(axis))
    route = [(i - distance, i) for i in devices if i - distance in devices]
    return lax.ppermute(block, axis, route)


def rotated(block, axis, distance):
    size = lax.axis_size(axis)
    route = [(i, (i + distance) % size) for i in range(size)]
    return lax.ppermute(block, axis, route)


def silu_parts(gate_value):
    sigmoid_value = jax.nn.sigmoid(gate_value)
    return (gate_value * sigmoid_value, sigmoid_value * (1.0 + gate_value * (1.0 - sigmoid_value)))


def contract_last(first_operand, second_operand):
    return lax.dot_general(
        first_operand, second_operand, (((1,), (1,)), ((), ())), preferred_element_type=jnp.float32
    )


def contract_first(first_operand, second_operand):
    return lax.dot_general(
        first_operand, second_operand, (((0,), (0,)), ((), ())), preferred_element_type=jnp.float32
    )


def to_experts(blocks):
    groups = blocks.shape[0]
    moved = [blocks[0]] + [rotated(blocks[s], "eg", s) for s in range(1, groups)]
    return jnp.stack(moved)


def to_owners(blocks):
    groups = blocks.shape[0]
    moved = [blocks[0]] + [rotated(blocks[s], "eg", -s) for s in range(1, groups)]
    return jnp.stack(moved)


def local(
    saved_inputs,
    output_grads,
    entry_grads,
    norm_gain,
    expert_ids,
    keep_flags,
    combine_weights,
    gate_weight,
    up_weight,
    down_weight,
):
    sections = lax.axis_size("pipe")
    is_last = lax.axis_index("pipe") == sections - 1
    groups = lax.axis_size("eg")
    me = lax.axis_index("eg")
    micro_count = saved_inputs.shape[1]
    token_rows = saved_inputs.shape[2]
    feature_count = saved_inputs.shape[3]
    pick_count = expert_ids.shape[3]
    capacity = max(2, 3 * token_rows * pick_count // (2 * groups))
    slot_count = groups * capacity
    gate_full, up_full, down_full = (
        lax.all_gather(gate_weight[0], "dp", axis=1, tiled=True),
        lax.all_gather(up_weight[0], "dp", axis=1, tiled=True),
        lax.all_gather(down_weight[0], "dp", axis=1, tiled=True),
    )
    hidden_count = gate_full.shape[0]
    paired_weights = jnp.concatenate([gate_full, up_full], axis=0)
    gain_row = norm_gain[0][None, :]
    slot_ids = jnp.arange(slot_count, dtype=jnp.int32)
    expert_range = jnp.arange(groups, dtype=jnp.int32)

    def prepare(moment):
        inputs = saved_inputs[0, moment].astype(jnp.float32)
        scales = lax.rsqrt(jnp.mean(inputs * inputs, axis=1, keepdims=True) + EPSILON)
        normed = (inputs * scales * gain_row).astype(jnp.bfloat16)
        chosen = expert_ids[0, moment].reshape(-1)
        onehot = (chosen[:, None] == expert_range[None, :]).astype(jnp.int32)
        rank_values = jnp.sum((jnp.cumsum(onehot, axis=0) - 1) * onehot, axis=1)
        places = ((chosen - me) % groups) * capacity + rank_values
        placing = places[:, None] == slot_ids[None, :]
        token_map = jnp.any(placing.reshape(token_rows, pick_count, slot_count), axis=1)
        selector = token_map.T.astype(jnp.bfloat16)
        keeping = keep_flags[0, moment].reshape(-1)
        scaled = (combine_weights[0, moment].reshape(-1) * keeping.astype(jnp.bfloat16)).astype(
            jnp.float32
        )
        weight_slots = jnp.sum(jnp.where(placing, scaled[:, None], 0.0), axis=0).astype(
            jnp.bfloat16
        )
        return (inputs, scales, normed, places, selector, keeping, weight_slots)

    def dispatch_rows(selector, source_rows):
        picked = jnp.dot(selector, source_rows, preferred_element_type=jnp.float32)
        return picked.astype(jnp.bfloat16).reshape(groups, capacity, feature_count)

    def gather_quad(blocks):
        return lax.all_gather(to_experts(blocks), "ej", axis=0, tiled=True)

    prepared = [prepare(moment) for moment in range(micro_count)]
    rows_gathered = [
        gather_quad(dispatch_rows(current[4], current[2])) for current in prepared
    ]
    weights_gathered = [
        gather_quad(current[6].reshape(groups, capacity)) for current in prepared
    ]
    leaving_list = []
    combine_list = []
    kept_list = []
    previous = entry_grads[0]
    for moment in range(micro_count):
        current = prepared[moment]
        if moment == 0:
            arriving = entry_grads[0]
        else:
            arriving = shifted(previous, "pipe", -1)
        incoming = jnp.where(is_last, output_grads[moment], arriving)
        grads_in = gather_quad(dispatch_rows(current[4], incoming))
        flat_rows = rows_gathered[moment].reshape(-1, feature_count)
        flat_grads = grads_in.reshape(-1, feature_count)
        scale_column = weights_gathered[moment].reshape(-1, 1).astype(jnp.float32)
        gate_value = contract_last(flat_rows, gate_full)
        upward = contract_last(flat_rows, up_full)
        backward = contract_last(flat_grads, down_full)
        active, derivative = silu_parts(gate_value)
        hidden = active * upward
        part_weight = jnp.sum(hidden * backward, axis=1).astype(jnp.bfloat16)
        grad_up = (scale_column * backward * active).astype(jnp.bfloat16)
        grad_gate = (scale_column * backward * upward * derivative).astype(jnp.bfloat16)
        grad_pair = jnp.concatenate([grad_gate, grad_up], axis=1)
        part_rows = jnp.dot(grad_pair, paired_weights, preferred_element_type=jnp.float32).astype(
            jnp.bfloat16
        )
        hidden_scaled = (hidden * scale_column).astype(jnp.bfloat16)
        kept_list.append((grad_pair, hidden_scaled, flat_rows, flat_grads))
        rows_back = to_owners(
            lax.psum_scatter(
                part_rows.reshape(-1, capacity, feature_count), "ej", scatter_dimension=0, tiled=True
            )
        )
        weights_back = to_owners(
            lax.psum_scatter(
                part_weight.astype(jnp.float32).reshape(-1, capacity),
                "ej",
                scatter_dimension=0,
                tiled=True,
            )
        )
        (
            finish_inputs,
            finish_scales,
            finish_normed,
            finish_places,
            finish_selector,
            finish_keeping,
            finish_weight_slots,
        ) = current
        summed = rows_back.astype(jnp.float32).reshape(slot_count, feature_count)
        weight_sums = weights_back.reshape(slot_count)
        expert_rows = jnp.sum(
            jnp.take(summed, finish_places, axis=0).reshape(token_rows, pick_count, feature_count),
            axis=1,
        )
        combine_grad = (
            jnp.take(weight_sums, finish_places) * finish_keeping.astype(jnp.float32)
        ).reshape(token_rows, pick_count)
        gained = gain_row * expert_rows
        mixed_mean = jnp.mean(finish_inputs * gained, axis=1, keepdims=True)
        leaving = (
            incoming.astype(jnp.float32)
            + finish_scales * gained
            - finish_inputs * (finish_scales * finish_scales * finish_scales) * mixed_mean
        ).astype(jnp.bfloat16)
        previous = leaving
        leaving_list.append(leaving)
        combine_list.append(combine_grad)
    pair_all = jnp.concatenate([kept[0] for kept in kept_list], axis=0)
    scaled_all = jnp.concatenate([kept[1] for kept in kept_list], axis=0)
    rows_all = jnp.concatenate([kept[2] for kept in kept_list], axis=0)
    grads_all = jnp.concatenate([kept[3] for kept in kept_list], axis=0)
    pair_total = contract_first(pair_all, rows_all).reshape(2, hidden_count, feature_count)
    down_total = contract_first(scaled_all, grads_all)[None]
    pair_reduced, down_reduced = (
        lax.psum_scatter(
            pair_total.astype(jnp.bfloat16), "dp", scatter_dimension=2, tiled=True
        ).astype(jnp.float32),
        lax.psum_scatter(
            down_total.astype(jnp.bfloat16), "dp", scatter_dimension=2, tiled=True
        ).astype(jnp.float32),
    )
    return (
        jnp.stack(leaving_list)[None],
        jnp.stack(combine_list)[None],
        pair_reduced[0:1].astype(jnp.bfloat16),
        pair_reduced[1:2].astype(jnp.bfloat16),
        down_reduced.astype(jnp.bfloat16),
    )


def solution(mesh):
    sizes = dict(zip(mesh.axis_names, mesh.devices.shape))
    members = sizes["expert"]
    grid = mesh.devices.reshape(sizes["pipe"], members // HSPLIT, HSPLIT, sizes["dp"])
    fine = Mesh(grid, ("pipe", "eg", "ej", "dp"))
    tokens = ("eg", "ej", "dp")
    rows = ("eg", "ej")
    in_specs = (
        P("pipe", None, tokens, None),
        P(None, tokens, None),
        P("pipe", tokens, None),
        P("pipe", None),
        P("pipe", None, tokens, None),
        P("pipe", None, tokens, None),
        P("pipe", None, tokens, None),
        P("pipe", rows, "dp"),
        P("pipe", rows, "dp"),
        P("pipe", rows, "dp"),
    )
    out_specs = (
        P("pipe", None, tokens, None),
        P("pipe", None, tokens, None),
        P("pipe", rows, "dp"),
        P("pipe", rows, "dp"),
        P("pipe", rows, "dp"),
    )
    return jax.shard_map(local, mesh=fine, in_specs=in_specs, out_specs=out_specs, check_vma=False)
```

time: 383 us -> 357 us (0.932)
  starting transfers between devices: 44.5 us -> 15.6 us
  blocking collectives: 7.64 us -> 34.4 us
  waiting for transfers between devices: 249 us -> 236 us
  local copies, waits for them, and re-layouts: 18.6 us -> 12.2 us
    all_to_all x10 -> x0, waiting for transfers between devices: 241 us -> none  [the longest x2 81.1 us: local(): lax.all_to_all(part_rows, 'expert', split_axis=0, concat_axis=0, tiled=True)]
    all_gather x0 -> x4, waiting for transfers between devices: none -> 93.8 us  [gather_quad(): return lax.all_gather(to_experts(blocks), 'ej', axis=0, tiled=True)]
    ppermute x0 -> x10, waiting for transfers between devices: none -> 64.9 us  [rotated(): return lax.ppermute(block, axis, route)]
    reduce_scatter x0 -> x2, waiting for transfers between devices: none -> 54.5 us  [local(): lax.psum_scatter(part_rows.reshape(-1, capacity, feature_count), 'ej', sc...]
    all_to_all x10 -> x0, starting transfers between devices: 43.2 us -> none  [the longest x2 10.9 us: local(): lax.all_to_all(weight_spread, 'expert', split_axis=0, concat_axis=0, tile...]
    all_gather x0 -> x2, blocking collectives: none -> 17.5 us  [gather_quad(): return lax.all_gather(to_experts(blocks), 'ej', axis=0, tiled=True)]
    ppermute x0 -> x10, starting transfers between devices: none -> 14 us  [rotated(): return lax.ppermute(block, axis, route)]
    unnamed x0 -> x1, blocking collectives: none -> 9.3 us
  transfers between devices with their start and end apart: 13 -> 19, of which waited for: 11 -> 16; matrix products, arithmetic and copies ran while one was open for 11% -> 9% of each run, Pallas kernels for 0% -> 0%
where the time goes in v1:
time: 357 us; the launch traced here: 356 us
  waiting for transfers between devices  236 us (66%)
  blocking collectives  34.4 us (10%)
  matrix products  31.7 us (9%)
  starting transfers between devices  15.6 us (4%)
  between operations  15.3 us (4%)
  local copies, waits for them, and re-layouts  12.2 us (3%)
  other arithmetic  11.3 us (3%)
    all_gather x4, waiting for transfers between devices, gather_quad(): return lax.all_gather(to_experts(blocks), 'ej', axis=0, tiled=True)  93.8 us
    ppermute x10, waiting for transfers between devices, rotated(): return lax.ppermute(block, axis, route)  64.9 us
    reduce_scatter x2, waiting for transfers between devices, local(): lax.psum_scatter(part_rows.reshape(-1, capacity, feature_count), 'ej', sc...  54.5 us
    all_gather x2, blocking collectives, gather_quad(): return lax.all_gather(to_experts(blocks), 'ej', axis=0, tiled=True)  17.5 us
    dot_general x6, matrix products, contract_last(): lax.dot_general(first_operand, second_operand, (((1,), (1,)), ((), ())),...  14.8 us
    ppermute x10, starting transfers between devices, rotated(): return lax.ppermute(block, axis, route)  14 us
    unnamed x1, blocking collectives  9.3 us
    dot_general x2, matrix products, contract_first(): lax.dot_general(first_operand, second_operand, (((0,), (0,)), ((), ())),...  9.2 us
  transfers between devices with their start and end apart: 19, of which 16 were waited for; matrix products, arithmetic and copies ran while one was open for 9% of the time, Pallas kernels for 0%

profile of v1, /device:TPU:0, one launch (start us, length us, event | category | flops | bytes accessed | tf_op | source)
XLA Modules:
  0.0 356.2 jit_solution(15069351970934282771)
XLA Ops:
  12.3 4.1 %collective-permute-start.2 = (bf16[48,2560]{1,0:T(8,128)(2,1)S(1)}, bf16[48,2560]{1,0:T(8,128)(2,1)S(1)}, u32[]{:S(2)}, u32[]{:S(2)}) collective-permute-start(bf16[48,2560]{1,0:T(8,128)(2,1)S(1)} %get-tuple-element.56), channel_id=1, source_target_pairs={{0,8},{8,0},{1,9},{9,1},{2,10},{10,2},{3,11},{11,3},{4,12},{12,4},... | collective-permute-start | bytes 737288 | tf_op jit(solution)/shard_map/ppermute | solution.py:21
  16.5 11.2 %collective-permute-done.2 = bf16[48,2560]{1,0:T(8,128)(2,1)S(1)} collective-permute-done((bf16[48,2560]{1,0:T(8,128)(2,1)S(1)}, bf16[48,2560]{1,0:T(8,128)(2,1)S(1)}, u32[]{:S(2)}, u32[]{:S(2)}) %collective-permute-start.2) | collective-permute-done | bytes 245792 | tf_op jit(solution)/shard_map/ppermute | solution.py:21
  29.9 13.4 %collective-permute-done.1 = bf16[48,2560]{1,0:T(8,128)(2,1)S(1)} collective-permute-done((bf16[48,2560]{1,0:T(8,128)(2,1)S(1)}, bf16[48,2560]{1,0:T(8,128)(2,1)S(1)}, u32[]{:S(2)}, u32[]{:S(2)}) %collective-permute-start.1) | collective-permute-done | bytes 245792 | tf_op jit(solution)/shard_map/ppermute | solution.py:21
  52.5 9.2 %all-gather.3 = bf16[4,2,48]{2,1,0:T(2,128)(2,1)S(1)} all-gather(bf16[1,2,48]{2,1,0:T(2,128)(2,1)S(1)} %maximum_bitcast_fusion.2), channel_id=1, replica_groups=mesh['pipe'=2,'eg'=2,'ej'=4,'dp'=2] {'ej'}, dimensions={0}, use_global_device_ids=true | all-gather | bytes 960 | tf_op jit(solution)/shard_map/all_gather | solution.py:111
  61.8 10.2 %all-gather.12.cloned.1.call-done = bf16[8,48,2560]{2,1,0:T(8,128)(2,1)} async-done(((bf16[2,48,2560]{2,1,0:T(8,128)(2,1)}), bf16[8,48,2560]{2,1,0:T(8,128)(2,1)}) %all-gather.12.cloned.1.call-update) | async-done | bytes 1966096 | tf_op jit(solution)/shard_map/all_gather | solution.py:111
  75.3 40.9 %all-gather.10.cloned.1.call-done = bf16[8,48,2560]{2,1,0:T(8,128)(2,1)} async-done(((bf16[2,48,2560]{2,1,0:T(8,128)(2,1)}), bf16[8,48,2560]{2,1,0:T(8,128)(2,1)}) %all-gather.10.cloned.1.call-update) | async-done | bytes 1966096 | tf_op jit(solution)/shard_map/all_gather | solution.py:111
  116.2 3.3 multiply_reduce_fusion.1
  122.1 40.7 %reduce-scatter.5.cloned.1.call-done = bf16[2,48,2560]{2,1,0:T(8,128)(2,1)} async-done(((bf16[8,48,2560]{2,1,0:T(8,128)(2,1)}), bf16[2,48,2560]{2,1,0:T(8,128)(2,1)}) %reduce-scatter.5.cloned.1.call-update) | async-done | bytes 491536 | tf_op jit(solution)/shard_map/reduce_scatter | solution.py:150
  166.3 11.5 %collective-permute-done.3 = bf16[48,2560]{1,0:T(8,128)(2,1)S(1)} collective-permute-done((bf16[48,2560]{1,0:T(8,128)(2,1)S(1)}, bf16[48,2560]{1,0:T(8,128)(2,1)S(1)}, u32[]{:S(2)}, u32[]{:S(2)}) %collective-permute-start.3) | collective-permute-done | bytes 245792 | tf_op jit(solution)/shard_map/ppermute | solution.py:21
  179.9 13.0 %collective-permute-done.7 = bf16[48,2560]{1,0:T(8,128)(2,1)S(1)} collective-permute-done((bf16[48,2560]{1,0:T(8,128)(2,1)S(1)}, bf16[48,2560]{1,0:T(8,128)(2,1)S(1)}, u32[]{:S(2)}, u32[]{:S(2)}) %collective-permute-start.7) | collective-permute-done | bytes 245792 | tf_op jit(solution)/shard_map/ppermute | solution.py:21
  195.5 8.4 %collective-permute-done.4 = bf16[64,2560]{1,0:T(8,128)(2,1)S(1)} collective-permute-done((bf16[64,2560]{1,0:T(8,128)(2,1)S(1)}, bf16[64,2560]{1,0:T(8,128)(2,1)S(1)}, u32[]{:S(2)}, u32[]{:S(2)}) %collective-permute-start.4) | collective-permute-done | bytes 327712 | tf_op jit(solution)/shard_map/ppermute | solution.py:15
  204.5 11.9 %collective-permute-done.6 = bf16[48,2560]{1,0:T(8,128)(2,1)S(1)} collective-permute-done((bf16[48,2560]{1,0:T(8,128)(2,1)S(1)}, bf16[48,2560]{1,0:T(8,128)(2,1)S(1)}, u32[]{:S(2)}, u32[]{:S(2)}) %collective-permute-start.6) | collective-permute-done | bytes 245792 | tf_op jit(solution)/shard_map/ppermute | solution.py:21
  219.0 2.8 collective-permute-done.5
  221.8 8.3 %all-gather.4 = bf16[4,2,48]{2,1,0:T(2,128)(2,1)S(1)} all-gather(bf16[1,2,48]{2,1,0:T(2,128)(2,1)S(1)} %maximum_bitcast_fusion.3), channel_id=1, replica_groups=mesh['pipe'=2,'eg'=2,'ej'=4,'dp'=2] {'ej'}, dimensions={0}, use_global_device_ids=true | all-gather | bytes 960 | tf_op jit(solution)/shard_map/all_gather | solution.py:111
  230.2 3.7 %all-gather.16.cloned.1.call-done = bf16[8,48,2560]{2,1,0:T(8,128)(2,1)} async-done(((bf16[2,48,2560]{2,1,0:T(8,128)(2,1)}), bf16[8,48,2560]{2,1,0:T(8,128)(2,1)}) %all-gather.16.cloned.1.call-update) | async-done | bytes 1966096 | tf_op jit(solution)/shard_map/all_gather | solution.py:111
  233.9 3.2 fusion.94
  238.7 39.0 %all-gather.14.cloned.1.call-done = bf16[8,48,2560]{2,1,0:T(8,128)(2,1)} async-done(((bf16[2,48,2560]{2,1,0:T(8,128)(2,1)}), bf16[8,48,2560]{2,1,0:T(8,128)(2,1)}) %all-gather.14.cloned.1.call-update) | async-done | bytes 1966096 | tf_op jit(solution)/shard_map/all_gather | solution.py:111
  277.7 3.5 multiply_reduce_fusion
  284.7 5.1 %convolution_convert_fusion = bf16[384,2560]{1,0:T(8,128)(2,1)} fusion(bf16[384,2560]{1,0:T(8,128)(2,1)} %bitcast.212, bf16[384,2560]{1,0:T(8,128)(2,1)} %bitcast.207, bf16[384,192]{0,1:T(8,128)(2,1)S(1)} %copy-done.19, bf16[384,192]{0,1:T(8,128)(2,1)S(1)} %copy-done.17, bf16[384,192]{0,1:T(8,128)(2,1)S(1)} %copy-done.15, ...), kind=kOutput, calls=%fused_computation.4 | convolution fusion | flops 1521156096 | bytes 6488064 | tf_op jit(solution)/shard_map/dot_general | solution.py:36
  292.3 9.3 %all-reduce.2 = (f32[8,48]{1,0:T(8,128)S(1)}, f32[8,48]{1,0:T(8,128)S(1)}) all-reduce(f32[8,48]{1,0:T(8,128)S(1)} %reshape.439, f32[8,48]{1,0:T(8,128)S(1)} %reshape.438), channel_id=8, replica_groups=mesh['pipe'=2,'eg'=2,'ej'=4,'dp'=2] {'ej'}, use_global_device_ids=true, to_apply=%region_15.18.clone | all-reduce | flops 768 | bytes 6144
  304.7 4.1 %fusion.10 = bf16[1,192,2560]{2,1,0:T(8,128)(2,1)} fusion(bf16[384,2560]{1,0:T(8,128)(2,1)} %bitcast.210, bf16[384,2560]{1,0:T(8,128)(2,1)} %bitcast.205, bf16[384,192]{0,1:T(8,128)(2,1)S(1)} %copy-done.27, bf16[384,192]{0,1:T(8,128)(2,1)S(1)} %copy-done.26), kind=kOutput, calls=%fused_computation.15 | convolution fusion | flops 763920384 | bytes 5210112 | tf_op jit(solution)/shard_map/dot_general | solution.py:36
  311.2 13.8 %reduce-scatter.7.cloned.1.call-done = bf16[2,48,2560]{2,1,0:T(8,128)(2,1)} async-done(((bf16[8,48,2560]{2,1,0:T(8,128)(2,1)}), bf16[2,48,2560]{2,1,0:T(8,128)(2,1)}) %reduce-scatter.7.cloned.1.call-update) | async-done | bytes 491536 | tf_op jit(solution)/shard_map/reduce_scatter | solution.py:150
  328.5 8.2 %reduce-scatter.9.cloned.1.call-done = bf16[2,192,1280]{2,1,0:T(8,128)(2,1)} async-done(((bf16[2,192,2560]{2,1,0:T(8,128)(2,1)}), bf16[2,192,1280]{2,1,0:T(8,128)(2,1)}) %reduce-scatter.9.cloned.1.call-update) | async-done | bytes 983056 | tf_op jit(solution)/shard_map/reduce_scatter | solution.py:197
  343.6 5.7 %reduce-scatter.11.cloned.1.call-done = bf16[1,192,1280]{2,1,0:T(8,128)(2,1)} async-done(((bf16[1,192,2560]{2,1,0:T(8,128)(2,1)}), bf16[1,192,1280]{2,1,0:T(8,128)(2,1)}) %reduce-scatter.11.cloned.1.call-update) | async-done | bytes 491536 | tf_op jit(solution)/shard_map/reduce_scatter | solution.py:200
  (163 shorter events, 56.4 us)
Async XLA Ops:
  7.2 21.4 %copy-start.6 = (bf16[2,64,2560]{2,1,0:T(8,128)(2,1)S(1)}, bf16[2,64,2560]{2,1,0:T(8,128)(2,1)}, u32[]{:S(2)}) copy-start(bf16[2,64,2560]{2,1,0:T(8,128)(2,1)} %param.15) | copy-start | bytes 1966084
  7.2 21.4 %copy-start.13 = (bf16[1,64,2560]{2,1,0:T(8,128)(2,1)S(1)}, bf16[1,64,2560]{2,1,0:T(8,128)(2,1)}, u32[]{:S(2)}) copy-start(bf16[1,64,2560]{2,1,0:T(8,128)(2,1)} %param.16) | copy-start | bytes 983044
  7.2 64.8 %all-gather.12.cloned.1.call-start = ((), (), s32[]{:S(2)}) async-start(), calls=%async_computation.5 | async-start | bytes 2457600 | tf_op jit(solution)/shard_map/all_gather | solution.py:111
  12.3 15.3 %collective-permute-start.2 = (bf16[48,2560]{1,0:T(8,128)(2,1)S(1)}, bf16[48,2560]{1,0:T(8,128)(2,1)S(1)}, u32[]{:S(2)}, u32[]{:S(2)}) collective-permute-start(bf16[48,2560]{1,0:T(8,128)(2,1)S(1)} %get-tuple-element.56), channel_id=1, source_target_pairs={{0,8},{8,0},{1,9},{9,1},{2,10},{10,2},{3,11},{11,3},{4,12},{12,4},... | collective-permute-start | bytes 737288 | tf_op jit(solution)/shard_map/ppermute | solution.py:21
  28.5 87.6 %all-gather.10.cloned.1.call-start = ((), (), s32[]{:S(2)}) async-start(), calls=%async_computation.4 | async-start | bytes 2457600 | tf_op jit(solution)/shard_map/all_gather | solution.py:111
  29.9 13.5 %collective-permute-start.1 = (bf16[48,2560]{1,0:T(8,128)(2,1)S(1)}, bf16[48,2560]{1,0:T(8,128)(2,1)S(1)}, u32[]{:S(2)}, u32[]{:S(2)}) collective-permute-start(bf16[48,2560]{1,0:T(8,128)(2,1)S(1)} %get-tuple-element.58), channel_id=1, source_target_pairs={{0,8},{8,0},{1,9},{9,1},{2,10},{10,2},{3,11},{11,3},{4,12},{12,4},... | collective-permute-start | bytes 737288 | tf_op jit(solution)/shard_map/ppermute | solution.py:21
  44.2 118.5 %reduce-scatter.5.cloned.1.call-start = ((), (), s32[]{:S(2)}) async-start(), calls=%async_computation.6 | async-start | bytes 2457600 | tf_op jit(solution)/shard_map/reduce_scatter | solution.py:150
  44.8 7.7 %collective-permute-start = (bf16[48]{0:T(256)(128)(2,1)S(1)}, bf16[48]{0:T(256)(128)(2,1)S(1)}, u32[]{:S(2)}, u32[]{:S(2)}) collective-permute-start(bf16[48]{0:T(256)(128)(2,1)S(1)} %get-tuple-element.75), channel_id=1, source_target_pairs={{0,8},{8,0},{1,9},{9,1},{2,10},{10,2},{3,11},{11,3},{4,12},{12,4},... | collective-permute-start | bytes 296 | tf_op jit(solution)/shard_map/ppermute | solution.py:21
  49.9 69.6 %copy-start.1 = (bf16[1,192,2560]{2,1,0:T(8,128)(2,1)}, bf16[1,192,2560]{2,1,0:T(8,128)(2,1)S(1)}, u32[]{:S(2)}) copy-start(bf16[1,192,2560]{2,1,0:T(8,128)(2,1)S(1)} %all-gather.1) | copy-start | bytes 2949124
  122.0 111.9 %all-gather.16.cloned.1.call-start = ((), (), s32[]{:S(2)}) async-start(), calls=%async_computation.8 | async-start | bytes 2457600 | tf_op jit(solution)/shard_map/all_gather | solution.py:111
  163.8 14.0 %collective-permute-start.3 = (bf16[48,2560]{1,0:T(8,128)(2,1)S(1)}, bf16[48,2560]{1,0:T(8,128)(2,1)S(1)}, u32[]{:S(2)}, u32[]{:S(2)}) collective-permute-start(bf16[48,2560]{1,0:T(8,128)(2,1)S(1)} %get-tuple-element.54), channel_id=1, source_target_pairs={{0,8},{8,0},{1,9},{9,1},{2,10},{10,2},{3,11},{11,3},{4,12},{12,4},... | collective-permute-start | bytes 737288 | tf_op jit(solution)/shard_map/ppermute | solution.py:21
  179.8 24.1 %copy-start.7 = (bf16[2,64,2560]{2,1,0:T(8,128)(2,1)S(1)}, bf16[2,64,2560]{2,1,0:T(8,128)(2,1)}, u32[]{:S(2)}) copy-start(bf16[2,64,2560]{2,1,0:T(8,128)(2,1)} %param.15) | copy-start | bytes 1966084
  179.8 13.1 %collective-permute-start.7 = (bf16[48,2560]{1,0:T(8,128)(2,1)S(1)}, bf16[48,2560]{1,0:T(8,128)(2,1)S(1)}, u32[]{:S(2)}, u32[]{:S(2)}) collective-permute-start(bf16[48,2560]{1,0:T(8,128)(2,1)S(1)} %get-tuple-element.50), channel_id=1, source_target_pairs={{0,8},{8,0},{1,9},{9,1},{2,10},{10,2},{3,11},{11,3},{4,12},{12,4},... | collective-permute-start | bytes 737288 | tf_op jit(solution)/shard_map/ppermute | solution.py:21
  193.7 83.9 %all-gather.14.cloned.1.call-start = ((), (), s32[]{:S(2)}) async-start(), calls=%async_computation.7 | async-start | bytes 2457600 | tf_op jit(solution)/shard_map/all_gather | solution.py:111
  194.2 9.7 %collective-permute-start.4 = (bf16[64,2560]{1,0:T(8,128)(2,1)S(1)}, bf16[64,2560]{1,0:T(8,128)(2,1)S(1)}, u32[]{:S(2)}, u32[]{:S(2)}) collective-permute-start(bf16[64,2560]{1,0:T(8,128)(2,1)S(1)} %fusion.34), channel_id=1, source_target_pairs={{16,0},{17,1},{18,2},{19,3},{20,4},{21,5},{22,6},{23,7},{24,8},{25... | collective-permute-start | bytes 983048 | tf_op jit(solution)/shard_map/ppermute | solution.py:15
  203.9 30.0 %copy-start.9 = (bf16[64,2560]{1,0:T(8,128)(2,1)}, bf16[64,2560]{1,0:T(8,128)(2,1)S(1)}, u32[]{:S(2)}) copy-start(bf16[64,2560]{1,0:T(8,128)(2,1)S(1)} %collective-permute-done.4) | copy-start | bytes 983044
  204.4 12.0 %collective-permute-start.6 = (bf16[48,2560]{1,0:T(8,128)(2,1)S(1)}, bf16[48,2560]{1,0:T(8,128)(2,1)S(1)}, u32[]{:S(2)}, u32[]{:S(2)}) collective-permute-start(bf16[48,2560]{1,0:T(8,128)(2,1)S(1)} %get-tuple-element.52), channel_id=1, source_target_pairs={{0,8},{8,0},{1,9},{9,1},{2,10},{10,2},{3,11},{11,3},{4,12},{12,4},... | collective-permute-start | bytes 737288 | tf_op jit(solution)/shard_map/ppermute | solution.py:21
  217.2 107.8 %reduce-scatter.7.cloned.1.call-start = ((), (), s32[]{:S(2)}) async-start(), calls=%async_computation.9 | async-start | bytes 2457600 | tf_op jit(solution)/shard_map/reduce_scatter | solution.py:150
  217.3 4.4 %collective-permute-start.5 = (bf16[48]{0:T(256)(128)(2,1)S(1)}, bf16[48]{0:T(256)(128)(2,1)S(1)}, u32[]{:S(2)}, u32[]{:S(2)}) collective-permute-start(bf16[48]{0:T(256)(128)(2,1)S(1)} %get-tuple-element.71), channel_id=1, source_target_pairs={{0,8},{8,0},{1,9},{9,1},{2,10},{10,2},{3,11},{11,3},{4,12},{12,4},... | collective-permute-start | bytes 296 | tf_op jit(solution)/shard_map/ppermute | solution.py:21
  283.7 53.0 %reduce-scatter.9.cloned.1.call-start = ((), (), s32[]{:S(2)}) async-start(), calls=%async_computation.10 | async-start | bytes 2949120 | tf_op jit(solution)/shard_map/reduce_scatter | solution.py:197
  289.9 59.4 %reduce-scatter.11.cloned.1.call-start = ((), (), s32[]{:S(2)}) async-start(), calls=%async_computation.11 | async-start | bytes 1474560 | tf_op jit(solution)/shard_map/reduce_scatter | solution.py:200
  301.6 7.2 %collective-permute-start.10 = (f32[48]{0:T(128)S(1)}, f32[48]{0:T(128)S(1)}, u32[]{:S(2)}, u32[]{:S(2)}) collective-permute-start(f32[48]{0:T(128)S(1)} %get-tuple-element.65), channel_id=1, source_target_pairs={{0,8},{8,0},{1,9},{9,1},{2,10},{10,2},{3,11},{11,3},{4,12},{12,4},... | collective-permute-start | bytes 584 | tf_op jit(solution)/shard_map/ppermute | solution.py:21
  304.1 4.8 %collective-permute-start.9 = (f32[48]{0:T(128)S(1)}, f32[48]{0:T(128)S(1)}, u32[]{:S(2)}, u32[]{:S(2)}) collective-permute-start(f32[48]{0:T(128)S(1)} %get-tuple-element.63), channel_id=1, source_target_pairs={{0,8},{8,0},{1,9},{9,1},{2,10},{10,2},{3,11},{11,3},{4,12},{12,4},... | collective-permute-start | bytes 584 | tf_op jit(solution)/shard_map/ppermute | solution.py:21
  326.1 14.0 %collective-permute-start.8 = (bf16[48,2560]{1,0:T(8,128)(2,1)S(1)}, bf16[48,2560]{1,0:T(8,128)(2,1)S(1)}, u32[]{:S(2)}, u32[]{:S(2)}) collective-permute-start(bf16[48,2560]{1,0:T(8,128)(2,1)S(1)} %get-tuple-element.48), channel_id=1, source_target_pairs={{0,8},{8,0},{1,9},{9,1},{2,10},{10,2},{3,11},{11,3},{4,12},{12,4},... | collective-permute-start | bytes 737288 | tf_op jit(solution)/shard_map/ppermute | solution.py:21
  (23 other events, 156.0 us)
Sparse Core Ops, SparseCore 0:
  28.6 43.2 all-gather.11
  74.1 42.0 all-gather.9
  122.1 40.5 reduce-scatter.4
  193.9 39.9 all-gather.15
  235.9 41.7 all-gather.13
  283.9 41.0 reduce-scatter.6
  327.2 9.4 reduce-scatter.8
  339.6 9.6 reduce-scatter.10

commit v2 on v1

--- a/solution.py
+++ b/solution.py
@@ -21,6 +21,12 @@
     return lax.ppermute(block, axis, route)
 
 
+def flipped(block, axis, mask):
+    size = lax.axis_size(axis)
+    route = [(i, i ^ mask) for i in range(size)]
+    return lax.ppermute(block, axis, route)
+
+
 def silu_parts(gate_value):
     sigmoid_value = jax.nn.sigmoid(gate_value)
     return (gate_value * sigmoid_value, sigmoid_value * (1.0 + gate_value * (1.0 - sigmoid_value)))
@@ -46,8 +52,31 @@
 
 def to_owners(blocks):
     groups = blocks.shape[0]
+    moved = [blocks[0]] + [
+        rotated(blocks[s].astype(jnp.bfloat16), "eg", -s).astype(jnp.float32)
+        for s in range(1, groups)
+    ]
+    return jnp.stack(moved)
+
+
+def weights_to_owners(blocks):
+    groups = blocks.shape[0]
     moved = [blocks[0]] + [rotated(blocks[s], "eg", -s) for s in range(1, groups)]
     return jnp.stack(moved)
+
+
+def gather_quad(blocks):
+    staged = to_experts(blocks)
+    quad = lax.axis_size("ej")
+    return jnp.stack([staged] + [flipped(staged, "ej", t) for t in range(1, quad)])
+
+
+def reduce_quad(parts):
+    quad = parts.shape[0]
+    total = parts[0].astype(jnp.float32)
+    for t in range(1, quad):
+        total = total + flipped(parts[t], "ej", t).astype(jnp.float32)
+    return total
 
 
 def local(
@@ -106,9 +135,6 @@
     def dispatch_rows(selector, source_rows):
         picked = jnp.dot(selector, source_rows, preferred_element_type=jnp.float32)
         return picked.astype(jnp.bfloat16).reshape(groups, capacity, feature_count)
-
-    def gather_quad(blocks):
-        return lax.all_gather(to_experts(blocks), "ej", axis=0, tiled=True)
 
     prepared = [prepare(moment) for moment in range(micro_count)]
     rows_gathered = [
@@ -147,17 +173,10 @@
         hidden_scaled = (hidden * scale_column).astype(jnp.bfloat16)
         kept_list.append((grad_pair, hidden_scaled, flat_rows, flat_grads))
         rows_back = to_owners(
-            lax.psum_scatter(
-                part_rows.reshape(-1, capacity, feature_count), "ej", scatter_dimension=0, tiled=True
-            )
-        )
-        weights_back = to_owners(
-            lax.psum_scatter(
-                part_weight.astype(jnp.float32).reshape(-1, capacity),
-                "ej",
-                scatter_dimension=0,
-                tiled=True,
-            )
+            reduce_quad(part_rows.reshape(-1, groups, capacity, feature_count))
+        )
+        weights_back = weights_to_owners(
+            reduce_quad(part_weight.reshape(-1, groups, capacity))
         )
         (
             finish_inputs,
@@ -168,7 +187,7 @@
             finish_keeping,
             finish_weight_slots,
         ) = current
-        summed = rows_back.astype(jnp.float32).reshape(slot_count, feature_count)
+        summed = rows_back.reshape(slot_count, feature_count)
         weight_sums = weights_back.reshape(slot_count)
         expert_rows = jnp.sum(
             jnp.take(summed, finish_places, axis=0).reshape(token_rows, pick_count, feature_count),

time: 357 us -> 273 us (0.76)
  waiting for transfers between devices: 236 us -> 141 us
  starting transfers between devices: 15.6 us -> 49.7 us
  blocking collectives: 34.4 us -> 7.63 us
  matrix products: 31.7 us -> 16.2 us
  other arithmetic: 11.3 us -> 22.3 us
  local copies, waits for them, and re-layouts: 12.2 us -> 16.9 us
    all_gather x4 -> x0, waiting for transfers between devices: 93.8 us -> none  [gather_quad(): return lax.all_gather(to_experts(blocks), 'ej', axis=0, tiled=True)]
    ppermute x0 -> x30, waiting for transfers between devices: none -> 85.5 us  [flipped(): return lax.ppermute(block, axis, route)]
    reduce_scatter x2 -> x0, waiting for transfers between devices: 54.5 us -> none  [local(): lax.psum_scatter(part_rows.reshape(-1, capacity, feature_count), 'ej', sc...]
    ppermute x0 -> x30, starting transfers between devices: none -> 34.9 us  [flipped(): return lax.ppermute(block, axis, route)]
    all_gather x2 -> x0, blocking collectives: 17.5 us -> none  [gather_quad(): return lax.all_gather(to_experts(blocks), 'ej', axis=0, tiled=True)]
    ppermute x10, waiting for transfers between devices: 64.9 us -> 48.7 us  [rotated(): return lax.ppermute(block, axis, route)]
    unnamed x1 -> x0, blocking collectives: 9.3 us -> none
    dot_general x6, matrix products: 14.8 us -> 6.29 us  [contract_last(): lax.dot_general(first_operand, second_operand, (((1,), (1,)), ((), ())),...]
  transfers between devices with their start and end apart: 19 -> 43, of which waited for: 16 -> 19; matrix products, arithmetic and copies ran while one was open for 9% -> 14% of each run, Pallas kernels for 0% -> 0%
where the time goes in v2:
time: 273 us; the launch traced here: 269 us
  waiting for transfers between devices  141 us (52%)
  starting transfers between devices  49.7 us (18%)
  other arithmetic  22.3 us (8%)
  local copies, waits for them, and re-layouts  16.9 us (6%)
  matrix products  16.2 us (6%)
  between operations  14.7 us (5%)
  blocking collectives  7.63 us (3%)
    ppermute x30, waiting for transfers between devices, flipped(): return lax.ppermute(block, axis, route)  85.5 us
    ppermute x10, waiting for transfers between devices, rotated(): return lax.ppermute(block, axis, route)  48.7 us
    ppermute x30, starting transfers between devices, flipped(): return lax.ppermute(block, axis, route)  34.9 us
    ppermute x10, starting transfers between devices, rotated(): return lax.ppermute(block, axis, route)  13.3 us
    ppermute x1, waiting for transfers between devices, shifted(): return lax.ppermute(block, axis, route)  6.93 us
    another operation x10, other arithmetic, gather_quad(): jnp.stack([staged] + [flipped(staged, 'ej', t) for t in range(1, quad)])  6.58 us
    dot_general x6, matrix products, contract_last(): lax.dot_general(first_operand, second_operand, (((1,), (1,)), ((), ())),...  6.29 us
  transfers between devices with their start and end apart: 43, of which 19 were waited for; matrix products, arithmetic and copies ran while one was open for 14% of the time, Pallas kernels for 0%

profile of v2, /device:TPU:0, one launch (start us, length us, event | category | flops | bytes accessed | tf_op | source)
XLA Modules:
  0.0 268.6 jit_solution(9418292772603265590)
XLA Ops:
  10.8 4.0 %collective-permute-start = (bf16[48]{0:T(256)(128)(2,1)S(1)}, bf16[48]{0:T(256)(128)(2,1)S(1)}, u32[]{:S(2)}, u32[]{:S(2)}) collective-permute-start(bf16[48]{0:T(256)(128)(2,1)S(1)} %get-tuple-element.91), channel_id=1, source_target_pairs={{0,8},{8,0},{1,9},{9,1},{2,10},{10,2},{3,11},{11,3},{4,12},{12,4},... | collective-permute-start | bytes 296 | tf_op jit(solution)/shard_map/ppermute | solution.py:21
  17.9 2.9 %collective-permute-start.4 = (bf16[48,2560]{1,0:T(8,128)(2,1)}, bf16[48,2560]{1,0:T(8,128)(2,1)}, u32[]{:S(2)}, u32[]{:S(2)}) collective-permute-start(bf16[48,2560]{1,0:T(8,128)(2,1)} %get-tuple-element.65), channel_id=1, source_target_pairs={{0,8},{8,0},{1,9},{9,1},{2,10},{10,2},{3,11},{11,3},{4,12},{12,4},... | collective-permute-start | bytes 737288 | tf_op jit(solution)/shard_map/ppermute | solution.py:21
  21.6 2.5 all-gather.2
  24.1 2.5 all-gather.1
  26.7 2.6 all-gather
  32.8 9.5 %collective-permute-done.8 = bf16[48,2560]{1,0:T(8,128)(2,1)S(1)} collective-permute-done((bf16[48,2560]{1,0:T(8,128)(2,1)S(1)}, bf16[48,2560]{1,0:T(8,128)(2,1)S(1)}, u32[]{:S(2)}, u32[]{:S(2)}) %collective-permute-start.8) | collective-permute-done | bytes 245792 | tf_op jit(solution)/shard_map/ppermute | solution.py:21
  51.9 7.3 %collective-permute-done.10 = bf16[2,48,2560]{2,1,0:T(8,128)(2,1)} collective-permute-done((bf16[2,48,2560]{2,1,0:T(8,128)(2,1)}, bf16[2,48,2560]{2,1,0:T(8,128)(2,1)}, u32[]{:S(2)}, u32[]{:S(2)}) %collective-permute-start.10) | collective-permute-done | bytes 491552 | tf_op jit(solution)/shard_map/ppermute | solution.py:27
  60.5 10.6 %collective-permute-done.9 = bf16[2,48,2560]{2,1,0:T(8,128)(2,1)} collective-permute-done((bf16[2,48,2560]{2,1,0:T(8,128)(2,1)}, bf16[2,48,2560]{2,1,0:T(8,128)(2,1)}, u32[]{:S(2)}, u32[]{:S(2)}) %collective-permute-start.9) | collective-permute-done | bytes 491552 | tf_op jit(solution)/shard_map/ppermute | solution.py:27
  74.8 5.4 %collective-permute-done.6 = bf16[2,48,2560]{2,1,0:T(8,128)(2,1)S(1)} collective-permute-done((bf16[2,48,2560]{2,1,0:T(8,128)(2,1)S(1)}, bf16[2,48,2560]{2,1,0:T(8,128)(2,1)S(1)}, u32[]{:S(2)}, u32[]{:S(2)}) %collective-permute-start.6) | collective-permute-done | bytes 491552 | tf_op jit(solution)/shard_map/ppermute | solution.py:27
  80.2 9.3 %collective-permute-done.7 = bf16[2,48,2560]{2,1,0:T(8,128)(2,1)S(1)} collective-permute-done((bf16[2,48,2560]{2,1,0:T(8,128)(2,1)S(1)}, bf16[2,48,2560]{2,1,0:T(8,128)(2,1)S(1)}, u32[]{:S(2)}, u32[]{:S(2)}) %collective-permute-start.7) | collective-permute-done | bytes 491552 | tf_op jit(solution)/shard_map/ppermute | solution.py:27
  101.4 16.9 %collective-permute-done.35 = bf16[2,48]{1,0:T(2,128)(2,1)S(1)} collective-permute-done((bf16[2,48]{1,0:T(2,128)(2,1)S(1)}, bf16[2,48]{1,0:T(2,128)(2,1)S(1)}, u32[]{:S(2)}, u32[]{:S(2)}) %collective-permute-start.35) | collective-permute-done | bytes 224 | tf_op jit(solution)/shard_map/ppermute | solution.py:27
  123.7 3.7 %collective-permute-start.36 = (f32[48]{0:T(128)S(1)}, f32[48]{0:T(128)S(1)}, u32[]{:S(2)}, u32[]{:S(2)}) collective-permute-start(f32[48]{0:T(128)S(1)} %get-tuple-element.79), channel_id=1, source_target_pairs={{0,8},{8,0},{1,9},{9,1},{2,10},{10,2},{3,11},{11,3},{4,12},{12,4},... | collective-permute-start | bytes 584 | tf_op jit(solution)/shard_map/ppermute | solution.py:21
  131.2 8.5 %collective-permute-done.15 = bf16[48,2560]{1,0:T(8,128)(2,1)S(1)} collective-permute-done((bf16[48,2560]{1,0:T(8,128)(2,1)}, bf16[48,2560]{1,0:T(8,128)(2,1)S(1)}, u32[]{:S(2)}, u32[]{:S(2)}) %collective-permute-start.15) | collective-permute-done | bytes 245792 | tf_op jit(solution)/shard_map/ppermute | solution.py:21
  144.9 6.9 %collective-permute-done.16 = bf16[64,2560]{1,0:T(8,128)(2,1)S(1)} collective-permute-done((bf16[64,2560]{1,0:T(8,128)(2,1)S(1)}, bf16[64,2560]{1,0:T(8,128)(2,1)S(1)}, u32[]{:S(2)}, u32[]{:S(2)}) %collective-permute-start.16) | collective-permute-done | bytes 327712 | tf_op jit(solution)/shard_map/ppermute | solution.py:15
  153.0 7.2 %collective-permute-done.25 = bf16[48,2560]{1,0:T(8,128)(2,1)S(1)} collective-permute-done((bf16[48,2560]{1,0:T(8,128)(2,1)S(1)}, bf16[48,2560]{1,0:T(8,128)(2,1)S(1)}, u32[]{:S(2)}, u32[]{:S(2)}) %collective-permute-start.25) | collective-permute-done | bytes 245792 | tf_op jit(solution)/shard_map/ppermute | solution.py:21
  168.1 6.7 %collective-permute-done.27 = bf16[2,48,2560]{2,1,0:T(8,128)(2,1)} collective-permute-done((bf16[2,48,2560]{2,1,0:T(8,128)(2,1)S(1)}, bf16[2,48,2560]{2,1,0:T(8,128)(2,1)}, u32[]{:S(2)}, u32[]{:S(2)}) %collective-permute-start.27) | collective-permute-done | bytes 491552 | tf_op jit(solution)/shard_map/ppermute | solution.py:27
  175.8 3.1 %collective-permute-done.26 = bf16[2,48,2560]{2,1,0:T(8,128)(2,1)} collective-permute-done((bf16[2,48,2560]{2,1,0:T(8,128)(2,1)S(1)}, bf16[2,48,2560]{2,1,0:T(8,128)(2,1)}, u32[]{:S(2)}, u32[]{:S(2)}) %collective-permute-start.26) | collective-permute-done | bytes 491552 | tf_op jit(solution)/shard_map/ppermute | solution.py:27
  178.9 7.8 %collective-permute-done.28 = bf16[2,48,2560]{2,1,0:T(8,128)(2,1)} collective-permute-done((bf16[2,48,2560]{2,1,0:T(8,128)(2,1)S(1)}, bf16[2,48,2560]{2,1,0:T(8,128)(2,1)}, u32[]{:S(2)}, u32[]{:S(2)}) %collective-permute-start.28) | collective-permute-done | bytes 491552 | tf_op jit(solution)/shard_map/ppermute | solution.py:27
  190.3 5.5 %collective-permute-done.23 = bf16[2,48,2560]{2,1,0:T(8,128)(2,1)S(1)} collective-permute-done((bf16[2,48,2560]{2,1,0:T(8,128)(2,1)S(1)}, bf16[2,48,2560]{2,1,0:T(8,128)(2,1)S(1)}, u32[]{:S(2)}, u32[]{:S(2)}) %collective-permute-start.23) | collective-permute-done | bytes 491552 | tf_op jit(solution)/shard_map/ppermute | solution.py:27
  195.8 9.9 %collective-permute-done.24 = bf16[2,48,2560]{2,1,0:T(8,128)(2,1)S(1)} collective-permute-done((bf16[2,48,2560]{2,1,0:T(8,128)(2,1)S(1)}, bf16[2,48,2560]{2,1,0:T(8,128)(2,1)S(1)}, u32[]{:S(2)}, u32[]{:S(2)}) %collective-permute-start.24) | collective-permute-done | bytes 491552 | tf_op jit(solution)/shard_map/ppermute | solution.py:27
  208.5 3.0 %convolution_convert_fusion = bf16[384,2560]{1,0:T(8,128)(2,1)} fusion(bf16[384,2560]{1,0:T(8,128)(2,1)S(1)} %bitcast.236, bf16[384,2560]{1,0:T(8,128)(2,1)S(1)} %bitcast.230, bf16[384,192]{0,1:T(8,128)(2,1)S(1)} %get-tuple-element.49, bf16[384,192]{0,1:T(8,128)(2,1)S(1)} %get-tuple-element.43, bf16[384,192]{0,1:T(8,128)(2,1)S(1)} %copy-done.24, ...), kind=kOutput, calls=%fused_computation.4 | convolution fusion | flops 1521156096 | bytes 6488064 | tf_op jit(solution)/shard_map/dot_general | solution.py:42
  214.8 3.4 %collective-permute-start.37 = (bf16[2,48]{1,0:T(2,128)(2,1)S(1)}, bf16[2,48]{1,0:T(2,128)(2,1)S(1)}, u32[]{:S(2)}, u32[]{:S(2)}) collective-permute-start(bf16[2,48]{1,0:T(2,128)(2,1)S(1)} %slice.267), channel_id=1, source_target_pairs={{0,2},{2,0},{4,6},{6,4},{1,3},{3,1},{5,7},{7,5},{8,10},{10,8},{12,... | collective-permute-start | bytes 584 | tf_op jit(solution)/shard_map/ppermute | solution.py:27
  227.0 13.4 %collective-permute-done.40 = f32[48]{0:T(128)S(1)} collective-permute-done((f32[48]{0:T(128)S(1)}, f32[48]{0:T(128)S(1)}, u32[]{:S(2)}, u32[]{:S(2)}) %collective-permute-start.40) | collective-permute-done | bytes 224 | tf_op jit(solution)/shard_map/ppermute | solution.py:21
  246.6 10.1 %collective-permute-done.32 = bf16[48,2560]{1,0:T(8,128)(2,1)S(1)} collective-permute-done((bf16[48,2560]{1,0:T(8,128)(2,1)S(1)}, bf16[48,2560]{1,0:T(8,128)(2,1)S(1)}, u32[]{:S(2)}, u32[]{:S(2)}) %collective-permute-start.32) | collective-permute-done | bytes 245792 | tf_op jit(solution)/shard_map/ppermute | solution.py:21
  (256 shorter events, 91.2 us)
Async XLA Ops:
  7.2 252.4 %reduce-scatter.3.cloned.1.call-start = ((), (), s32[]{:S(2)}) async-start(), calls=%async_computation.2 | async-start | bytes 2949120 | tf_op jit(solution)/shard_map/reduce_scatter | solution.py:216
  15.0 29.8 %collective-permute-start.17 = (bf16[48]{0:T(256)(128)(2,1)S(1)}, bf16[48]{0:T(256)(128)(2,1)S(1)}, u32[]{:S(2)}, u32[]{:S(2)}) collective-permute-start(bf16[48]{0:T(256)(128)(2,1)S(1)} %get-tuple-element.87), channel_id=1, source_target_pairs={{0,8},{8,0},{1,9},{9,1},{2,10},{10,2},{3,11},{11,3},{4,12},{12,4},... | collective-permute-start | bytes 296 | tf_op jit(solution)/shard_map/ppermute | solution.py:21
  17.9 31.0 %collective-permute-start.4 = (bf16[48,2560]{1,0:T(8,128)(2,1)}, bf16[48,2560]{1,0:T(8,128)(2,1)}, u32[]{:S(2)}, u32[]{:S(2)}) collective-permute-start(bf16[48,2560]{1,0:T(8,128)(2,1)} %get-tuple-element.65), channel_id=1, source_target_pairs={{0,8},{8,0},{1,9},{9,1},{2,10},{10,2},{3,11},{11,3},{4,12},{12,4},... | collective-permute-start | bytes 737288 | tf_op jit(solution)/shard_map/ppermute | solution.py:21
  21.5 20.7 %collective-permute-start.8 = (bf16[48,2560]{1,0:T(8,128)(2,1)S(1)}, bf16[48,2560]{1,0:T(8,128)(2,1)S(1)}, u32[]{:S(2)}, u32[]{:S(2)}) collective-permute-start(bf16[48,2560]{1,0:T(8,128)(2,1)S(1)} %get-tuple-element.61), channel_id=1, source_target_pairs={{0,8},{8,0},{1,9},{9,1},{2,10},{10,2},{3,11},{11,3},{4,12},{12,4},... | collective-permute-start | bytes 737288 | tf_op jit(solution)/shard_map/ppermute | solution.py:21
  46.1 25.0 %collective-permute-start.9 = (bf16[2,48,2560]{2,1,0:T(8,128)(2,1)}, bf16[2,48,2560]{2,1,0:T(8,128)(2,1)}, u32[]{:S(2)}, u32[]{:S(2)}) collective-permute-start(bf16[2,48,2560]{2,1,0:T(8,128)(2,1)} %get-tuple-element.59), channel_id=1, source_target_pairs={{0,2},{2,0},{4,6},{6,4},{1,3},{3,1},{5,7},{7,5},{8,10},{10,8},{12,... | collective-permute-start | bytes 1474568 | tf_op jit(solution)/shard_map/ppermute | solution.py:27
  46.6 24.5 %collective-permute-start.11 = (bf16[2,48,2560]{2,1,0:T(8,128)(2,1)}, bf16[2,48,2560]{2,1,0:T(8,128)(2,1)}, u32[]{:S(2)}, u32[]{:S(2)}) collective-permute-start(bf16[2,48,2560]{2,1,0:T(8,128)(2,1)} %get-tuple-element.59), channel_id=1, source_target_pairs={{0,6},{2,4},{4,2},{6,0},{1,7},{3,5},{5,3},{7,1},{8,14},{10,12},{12... | collective-permute-start | bytes 1474568 | tf_op jit(solution)/shard_map/ppermute | solution.py:27
  50.0 30.2 %collective-permute-start.6 = (bf16[2,48,2560]{2,1,0:T(8,128)(2,1)S(1)}, bf16[2,48,2560]{2,1,0:T(8,128)(2,1)S(1)}, u32[]{:S(2)}, u32[]{:S(2)}) collective-permute-start(bf16[2,48,2560]{2,1,0:T(8,128)(2,1)S(1)} %get-tuple-element.63), channel_id=1, source_target_pairs={{0,4},{2,6},{4,0},{6,2},{1,5},{3,7},{5,1},{7,3},{8,12},{10,14},{12... | collective-permute-start | bytes 1474568 | tf_op jit(solution)/shard_map/ppermute | solution.py:27
  51.4 28.9 %collective-permute-start.5 = (bf16[2,48,2560]{2,1,0:T(8,128)(2,1)S(1)}, bf16[2,48,2560]{2,1,0:T(8,128)(2,1)S(1)}, u32[]{:S(2)}, u32[]{:S(2)}) collective-permute-start(bf16[2,48,2560]{2,1,0:T(8,128)(2,1)S(1)} %get-tuple-element.63), channel_id=1, source_target_pairs={{0,2},{2,0},{4,6},{6,4},{1,3},{3,1},{5,7},{7,5},{8,10},{10,8},{12,... | collective-permute-start | bytes 1474568 | tf_op jit(solution)/shard_map/ppermute | solution.py:27
  59.2 30.3 %collective-permute-start.7 = (bf16[2,48,2560]{2,1,0:T(8,128)(2,1)S(1)}, bf16[2,48,2560]{2,1,0:T(8,128)(2,1)S(1)}, u32[]{:S(2)}, u32[]{:S(2)}) collective-permute-start(bf16[2,48,2560]{2,1,0:T(8,128)(2,1)S(1)} %get-tuple-element.63), channel_id=1, source_target_pairs={{0,6},{2,4},{4,2},{6,0},{1,7},{3,5},{5,3},{7,1},{8,14},{10,12},{12... | collective-permute-start | bytes 1474568 | tf_op jit(solution)/shard_map/ppermute | solution.py:27
  94.7 28.6 %collective-permute-start.14 = (bf16[2,48,2560]{2,1,0:T(8,128)(2,1)}, bf16[2,48,2560]{2,1,0:T(8,128)(2,1)S(1)}, u32[]{:S(2)}, u32[]{:S(2)}) collective-permute-start(bf16[2,48,2560]{2,1,0:T(8,128)(2,1)} %bitcast.33), channel_id=1, source_target_pairs={{0,6},{2,4},{4,2},{6,0},{1,7},{3,5},{5,3},{7,1},{8,14},{10,12},{12... | collective-permute-start | bytes 1474568 | tf_op jit(solution)/shard_map/ppermute | solution.py:27
  96.3 27.4 %collective-permute-start.12 = (bf16[2,48,2560]{2,1,0:T(8,128)(2,1)}, bf16[2,48,2560]{2,1,0:T(8,128)(2,1)}, u32[]{:S(2)}, u32[]{:S(2)}) collective-permute-start(bf16[2,48,2560]{2,1,0:T(8,128)(2,1)} %bitcast.31), channel_id=1, source_target_pairs={{0,2},{2,0},{4,6},{6,4},{1,3},{3,1},{5,7},{7,5},{8,10},{10,8},{12,... | collective-permute-start | bytes 1474568 | tf_op jit(solution)/shard_map/ppermute | solution.py:27
  97.8 29.6 %collective-permute-start.13 = (bf16[2,48,2560]{2,1,0:T(8,128)(2,1)S(1)}, bf16[2,48,2560]{2,1,0:T(8,128)(2,1)}, u32[]{:S(2)}, u32[]{:S(2)}) collective-permute-start(bf16[2,48,2560]{2,1,0:T(8,128)(2,1)S(1)} %bitcast.239), channel_id=1, source_target_pairs={{0,4},{2,6},{4,0},{6,2},{1,5},{3,7},{5,1},{7,3},{8,12},{10,14},{12... | collective-permute-start | bytes 1474568 | tf_op jit(solution)/shard_map/ppermute | solution.py:27
  98.4 19.9 %collective-permute-start.35 = (bf16[2,48]{1,0:T(2,128)(2,1)S(1)}, bf16[2,48]{1,0:T(2,128)(2,1)S(1)}, u32[]{:S(2)}, u32[]{:S(2)}) collective-permute-start(bf16[2,48]{1,0:T(2,128)(2,1)S(1)} %slice.262), channel_id=1, source_target_pairs={{0,6},{2,4},{4,2},{6,0},{1,7},{3,5},{5,3},{7,1},{8,14},{10,12},{12... | collective-permute-start | bytes 584 | tf_op jit(solution)/shard_map/ppermute | solution.py:27
  100.1 19.7 %collective-permute-start.34 = (bf16[2,48]{1,0:T(2,128)(2,1)S(1)}, bf16[2,48]{1,0:T(2,128)(2,1)S(1)}, u32[]{:S(2)}, u32[]{:S(2)}) collective-permute-start(bf16[2,48]{1,0:T(2,128)(2,1)S(1)} %slice.260), channel_id=1, source_target_pairs={{0,4},{2,6},{4,0},{6,2},{1,5},{3,7},{5,1},{7,3},{8,12},{10,14},{12... | collective-permute-start | bytes 584 | tf_op jit(solution)/shard_map/ppermute | solution.py:27
  119.8 40.5 %collective-permute-start.19 = (bf16[2,48]{1,0:T(2,128)(2,1)}, bf16[2,48]{1,0:T(2,128)(2,1)S(1)}, u32[]{:S(2)}, u32[]{:S(2)}) collective-permute-start(bf16[2,48]{1,0:T(2,128)(2,1)} %pad_maximum_fusion.16), channel_id=1, source_target_pairs={{0,4},{2,6},{4,0},{6,2},{1,5},{3,7},{5,1},{7,3},{8,12},{10,14},{12... | collective-permute-start | bytes 584 | tf_op jit(solution)/shard_map/ppermute | solution.py:27
  121.8 40.3 %collective-permute-start.18 = (bf16[2,48]{1,0:T(2,128)(2,1)}, bf16[2,48]{1,0:T(2,128)(2,1)}, u32[]{:S(2)}, u32[]{:S(2)}) collective-permute-start(bf16[2,48]{1,0:T(2,128)(2,1)} %pad_maximum_fusion.16), channel_id=1, source_target_pairs={{0,2},{2,0},{4,6},{6,4},{1,3},{3,1},{5,7},{7,5},{8,10},{10,8},{12,... | collective-permute-start | bytes 584 | tf_op jit(solution)/shard_map/ppermute | solution.py:27
  123.3 40.5 %collective-permute-start.20 = (bf16[2,48]{1,0:T(2,128)(2,1)}, bf16[2,48]{1,0:T(2,128)(2,1)}, u32[]{:S(2)}, u32[]{:S(2)}) collective-permute-start(bf16[2,48]{1,0:T(2,128)(2,1)} %pad_maximum_fusion.16), channel_id=1, source_target_pairs={{0,6},{2,4},{4,2},{6,0},{1,7},{3,5},{5,3},{7,1},{8,14},{10,12},{12... | collective-permute-start | bytes 584 | tf_op jit(solution)/shard_map/ppermute | solution.py:27
  162.1 24.6 %collective-permute-start.28 = (bf16[2,48,2560]{2,1,0:T(8,128)(2,1)S(1)}, bf16[2,48,2560]{2,1,0:T(8,128)(2,1)}, u32[]{:S(2)}, u32[]{:S(2)}) collective-permute-start(bf16[2,48,2560]{2,1,0:T(8,128)(2,1)S(1)} %get-tuple-element.51), channel_id=1, source_target_pairs={{0,6},{2,4},{4,2},{6,0},{1,7},{3,5},{5,3},{7,1},{8,14},{10,12},{12... | collective-permute-start | bytes 1474568 | tf_op jit(solution)/shard_map/ppermute | solution.py:27
  166.2 29.6 %collective-permute-start.23 = (bf16[2,48,2560]{2,1,0:T(8,128)(2,1)S(1)}, bf16[2,48,2560]{2,1,0:T(8,128)(2,1)S(1)}, u32[]{:S(2)}, u32[]{:S(2)}) collective-permute-start(bf16[2,48,2560]{2,1,0:T(8,128)(2,1)S(1)} %get-tuple-element.55), channel_id=1, source_target_pairs={{0,4},{2,6},{4,0},{6,2},{1,5},{3,7},{5,1},{7,3},{8,12},{10,14},{12... | collective-permute-start | bytes 1474568 | tf_op jit(solution)/shard_map/ppermute | solution.py:27
  166.5 29.3 %collective-permute-start.22 = (bf16[2,48,2560]{2,1,0:T(8,128)(2,1)S(1)}, bf16[2,48,2560]{2,1,0:T(8,128)(2,1)S(1)}, u32[]{:S(2)}, u32[]{:S(2)}) collective-permute-start(bf16[2,48,2560]{2,1,0:T(8,128)(2,1)S(1)} %get-tuple-element.55), channel_id=1, source_target_pairs={{0,2},{2,0},{4,6},{6,4},{1,3},{3,1},{5,7},{7,5},{8,10},{10,8},{12,... | collective-permute-start | bytes 1474568 | tf_op jit(solution)/shard_map/ppermute | solution.py:27
  174.8 30.9 %collective-permute-start.24 = (bf16[2,48,2560]{2,1,0:T(8,128)(2,1)S(1)}, bf16[2,48,2560]{2,1,0:T(8,128)(2,1)S(1)}, u32[]{:S(2)}, u32[]{:S(2)}) collective-permute-start(bf16[2,48,2560]{2,1,0:T(8,128)(2,1)S(1)} %get-tuple-element.55), channel_id=1, source_target_pairs={{0,6},{2,4},{4,2},{6,0},{1,7},{3,5},{5,3},{7,1},{8,14},{10,12},{12... | collective-permute-start | bytes 1474568 | tf_op jit(solution)/shard_map/ppermute | solution.py:27
  211.6 50.2 %reduce-scatter.5.cloned.1.call-start = ((), (), s32[]{:S(2)}) async-start(), calls=%async_computation.3 | async-start | bytes 1474560 | tf_op jit(solution)/shard_map/reduce_scatter | solution.py:219
  221.4 19.9 %collective-permute-start.31 = (bf16[2,48,2560]{2,1,0:T(8,128)(2,1)}, bf16[2,48,2560]{2,1,0:T(8,128)(2,1)S(1)}, u32[]{:S(2)}, u32[]{:S(2)}) collective-permute-start(bf16[2,48,2560]{2,1,0:T(8,128)(2,1)} %bitcast.69), channel_id=1, source_target_pairs={{0,6},{2,4},{4,2},{6,0},{1,7},{3,5},{5,3},{7,1},{8,14},{10,12},{12... | collective-permute-start | bytes 1474568 | tf_op jit(solution)/shard_map/ppermute | solution.py:27
  221.4 20.9 %collective-permute-start.29 = (bf16[2,48,2560]{2,1,0:T(8,128)(2,1)S(1)}, bf16[2,48,2560]{2,1,0:T(8,128)(2,1)S(1)}, u32[]{:S(2)}, u32[]{:S(2)}) collective-permute-start(bf16[2,48,2560]{2,1,0:T(8,128)(2,1)S(1)} %bitcast.241), channel_id=1, source_target_pairs={{0,2},{2,0},{4,6},{6,4},{1,3},{3,1},{5,7},{7,5},{8,10},{10,8},{12,... | collective-permute-start | bytes 1474568 | tf_op jit(solution)/shard_map/ppermute | solution.py:27
  (64 other events, 675.9 us)
Sparse Core Ops, SparseCore 0:
  211.7 10.4 reduce-scatter.2
  227.1 10.7 reduce-scatter.4

commit v3 on v2

--- a/solution.py
+++ b/solution.py
@@ -47,21 +47,6 @@
 def to_experts(blocks):
     groups = blocks.shape[0]
     moved = [blocks[0]] + [rotated(blocks[s], "eg", s) for s in range(1, groups)]
-    return jnp.stack(moved)
-
-
-def to_owners(blocks):
-    groups = blocks.shape[0]
-    moved = [blocks[0]] + [
-        rotated(blocks[s].astype(jnp.bfloat16), "eg", -s).astype(jnp.float32)
-        for s in range(1, groups)
-    ]
-    return jnp.stack(moved)
-
-
-def weights_to_owners(blocks):
-    groups = blocks.shape[0]
-    moved = [blocks[0]] + [rotated(blocks[s], "eg", -s) for s in range(1, groups)]
     return jnp.stack(moved)
 
 
@@ -136,12 +121,48 @@
         picked = jnp.dot(selector, source_rows, preferred_element_type=jnp.float32)
         return picked.astype(jnp.bfloat16).reshape(groups, capacity, feature_count)
 
+    def weight_row(weight_slots):
+        shaped = weight_slots.reshape(groups, 1, capacity)
+        return jnp.pad(shaped, ((0, 0), (0, 0), (0, feature_count - capacity)))
+
+    def send_back(part_rows, part_weight):
+        quad_rows = part_rows.reshape(-1, groups, capacity, feature_count)
+        quad_weight = jnp.pad(
+            part_weight.reshape(-1, groups, 1, capacity),
+            ((0, 0), (0, 0), (0, 0), (0, feature_count - capacity)),
+        )
+        total = reduce_quad(jnp.concatenate([quad_rows, quad_weight], axis=2))
+        back_rows = [total[0, :capacity]]
+        back_weight = [total[0, capacity, :capacity]]
+        for s in range(1, groups):
+            high = total[s, capacity:].astype(jnp.bfloat16)
+            low = (total[s, capacity:] - high.astype(jnp.float32)).astype(jnp.bfloat16)
+            block = jnp.concatenate([total[s, :capacity].astype(jnp.bfloat16), high, low], axis=0)
+            got = rotated(block, "eg", -s).astype(jnp.float32)
+            back_rows.append(got[:capacity])
+            back_weight.append(got[capacity, :capacity] + got[capacity + 1, :capacity])
+        return (
+            jnp.stack(back_rows).reshape(slot_count, feature_count),
+            jnp.stack(back_weight).reshape(slot_count),
+        )
+
     prepared = [prepare(moment) for moment in range(micro_count)]
+    first_incoming = jnp.where(is_last, output_grads[0], entry_grads[0])
+    payload = jnp.concatenate(
+        [dispatch_rows(current[4], current[2]) for current in prepared]
+        + [dispatch_rows(prepared[0][4], first_incoming)]
+        + [weight_row(current[6]) for current in prepared],
+        axis=1,
+    )
+    gathered = gather_quad(payload)
     rows_gathered = [
-        gather_quad(dispatch_rows(current[4], current[2])) for current in prepared
+        gathered[:, :, moment * capacity : (moment + 1) * capacity].reshape(-1, feature_count)
+        for moment in range(micro_count)
     ]
+    first_grads = gathered[:, :, micro_count * capacity : (micro_count + 1) * capacity]
     weights_gathered = [
-        gather_quad(current[6].reshape(groups, capacity)) for current in prepared
+        gathered[:, :, (micro_count + 1) * capacity + moment, :capacity].reshape(-1, 1)
+        for moment in range(micro_count)
     ]
     leaving_list = []
     combine_list = []
@@ -150,14 +171,15 @@
     for moment in range(micro_count):
         current = prepared[moment]
         if moment == 0:
-            arriving = entry_grads[0]
+            incoming = first_incoming
+            grads_in = first_grads
         else:
             arriving = shifted(previous, "pipe", -1)
-        incoming = jnp.where(is_last, output_grads[moment], arriving)
-        grads_in = gather_quad(dispatch_rows(current[4], incoming))
-        flat_rows = rows_gathered[moment].reshape(-1, feature_count)
+            incoming = jnp.where(is_last, output_grads[moment], arriving)
+            grads_in = gather_quad(dispatch_rows(current[4], incoming))
+        flat_rows = rows_gathered[moment]
         flat_grads = grads_in.reshape(-1, feature_count)
-        scale_column = weights_gathered[moment].reshape(-1, 1).astype(jnp.float32)
+        scale_column = weights_gathered[moment].astype(jnp.float32)
         gate_value = contract_last(flat_rows, gate_full)
         upward = contract_last(flat_rows, up_full)
         backward = contract_last(flat_grads, down_full)
@@ -172,12 +194,7 @@
         )
         hidden_scaled = (hidden * scale_column).astype(jnp.bfloat16)
         kept_list.append((grad_pair, hidden_scaled, flat_rows, flat_grads))
-        rows_back = to_owners(
-            reduce_quad(part_rows.reshape(-1, groups, capacity, feature_count))
-        )
-        weights_back = weights_to_owners(
-            reduce_quad(part_weight.reshape(-1, groups, capacity))
-        )
+        summed, weight_sums = send_back(part_rows, part_weight)
         (
             finish_inputs,
             finish_scales,
@@ -187,8 +204,6 @@
             finish_keeping,
             finish_weight_slots,
         ) = current
-        summed = rows_back.reshape(slot_count, feature_count)
-        weight_sums = weights_back.reshape(slot_count)
         expert_rows = jnp.sum(
             jnp.take(summed, finish_places, axis=0).reshape(token_rows, pick_count, feature_count),
             axis=1,

time: 273 us -> 312 us (1.14); the launches traced: 269 us -> 311 us
  waiting for transfers between devices: 141 us -> 191 us
  starting transfers between devices: 49.7 us -> 24.2 us
  local copies, waits for them, and re-layouts: 16.9 us -> 27.8 us
  matrix products: 16.2 us -> 20.7 us
    ppermute x30 -> x12, waiting for transfers between devices: 85.5 us -> 115 us  [flipped(): return lax.ppermute(block, axis, route)]
    ppermute x30 -> x12, starting transfers between devices: 34.9 us -> 14.1 us  [flipped(): return lax.ppermute(block, axis, route)]
    ppermute x10 -> x4, waiting for transfers between devices: 48.7 us -> 65.8 us  [rotated(): return lax.ppermute(block, axis, route)]
    ppermute x10 -> x4, starting transfers between devices: 13.3 us -> 8.24 us  [rotated(): return lax.ppermute(block, axis, route)]
    another operation x10 -> x4, other arithmetic: 6.58 us -> 6.68 us  [gather_quad(): jnp.stack([staged] + [flipped(staged, 'ej', t) for t in range(1, quad)])]
  transfers between devices with their start and end apart: 43 -> 19, of which waited for: 19 -> 15; matrix products, arithmetic and copies ran while one was open for 14% -> 6% of each run, Pallas kernels for 0% -> 0%
where the time goes in v3:
time: 312 us; the launch traced here: 311 us
  waiting for transfers between devices  191 us (61%)
  local copies, waits for them, and re-layouts  27.8 us (9%)
  other arithmetic  25.4 us (8%)
  starting transfers between devices  24.2 us (8%)
  matrix products  20.7 us (7%)
  between operations  14.8 us (5%)
  blocking collectives  7.76 us (2%)
    ppermute x12, waiting for transfers between devices, flipped(): return lax.ppermute(block, axis, route)  115 us
    ppermute x4, waiting for transfers between devices, rotated(): return lax.ppermute(block, axis, route)  65.8 us
    ppermute x12, starting transfers between devices, flipped(): return lax.ppermute(block, axis, route)  14.1 us
    ppermute x1, waiting for transfers between devices, shifted(): return lax.ppermute(block, axis, route)  10 us
    dot_general x6, matrix products, contract_last(): lax.dot_general(first_operand, second_operand, (((1,), (1,)), ((), ())),...  8.29 us
    ppermute x4, starting transfers between devices, rotated(): return lax.ppermute(block, axis, route)  8.24 us
    another operation x4, other arithmetic, gather_quad(): jnp.stack([staged] + [flipped(staged, 'ej', t) for t in range(1, quad)])  6.68 us
  transfers between devices with their start and end apart: 19, of which 15 were waited for; matrix products, arithmetic and copies ran while one was open for 6% of the time, Pallas kernels for 0%

profile of v3, /device:TPU:0, one launch (start us, length us, event | category | flops | bytes accessed | tf_op | source)
XLA Modules:
  0.0 311.4 jit_solution(8196474957923304864)
XLA Ops:
  17.1 3.1 concatenate.36
  20.3 4.1 %collective-permute-start = (bf16[146,2560]{1,0:T(8,128)(2,1)S(1)}, bf16[146,2560]{1,0:T(8,128)(2,1)S(1)}, u32[]{:S(2)}, u32[]{:S(2)}) collective-permute-start(bf16[146,2560]{1,0:T(8,128)(2,1)S(1)} %get-tuple-element.55), channel_id=1, source_target_pairs={{0,8},{8,0},{1,9},{9,1},{2,10},{10,2},{3,11},{11,3},{4,12},{12,4},... | collective-permute-start | bytes 2242568 | tf_op jit(solution)/shard_map/ppermute | solution.py:21
  24.4 34.0 %collective-permute-done = bf16[146,2560]{1,0:T(8,128)(2,1)S(1)} collective-permute-done((bf16[146,2560]{1,0:T(8,128)(2,1)S(1)}, bf16[146,2560]{1,0:T(8,128)(2,1)S(1)}, u32[]{:S(2)}, u32[]{:S(2)}) %collective-permute-start) | collective-permute-done | bytes 747552 | tf_op jit(solution)/shard_map/ppermute | solution.py:21
  66.0 2.6 all-gather.1
  68.6 2.6 all-gather
  71.2 25.3 %collective-permute-done.3 = bf16[2,146,2560]{2,0,1:T(2,128)(2,1)S(1)} collective-permute-done((bf16[2,146,2560]{2,0,1:T(2,128)(2,1)S(1)}, bf16[2,146,2560]{2,0,1:T(2,128)(2,1)S(1)}, u32[]{:S(2)}, u32[]{:S(2)}) %collective-permute-start.3) | collective-permute-done | bytes 1495072 | tf_op jit(solution)/shard_map/ppermute | solution.py:27
  96.7 29.9 %collective-permute-done.2 = bf16[2,146,2560]{2,0,1:T(2,128)(2,1)S(1)} collective-permute-done((bf16[2,146,2560]{2,0,1:T(2,128)(2,1)S(1)}, bf16[2,146,2560]{2,0,1:T(2,128)(2,1)S(1)}, u32[]{:S(2)}, u32[]{:S(2)}) %collective-permute-start.2) | collective-permute-done | bytes 1495072 | tf_op jit(solution)/shard_map/ppermute | solution.py:27
  128.5 3.8 %pad_maximum_fusion = bf16[4,2,146,2560]{3,2,1,0:T(8,128)(2,1)} fusion(bf16[1,2,146,2560]{3,2,1,0:T(8,128)(2,1)S(1)} %bitcast.226, bf16[1,2,146,2560]{3,2,1,0:T(8,128)(2,1)S(1)} %bitcast.229, bf16[1,2,146,2560]{3,2,1,0:T(8,128)(2,1)S(1)} %bitcast.232, bf16[1,2,146,2560]{3,2,1,0:T(8,128)(2,1)S(1)} %get-tuple-element.52), kind=kLoop, calls=%fused_computation.4 | loop fusion | flops 8970240 | bytes 11960320 | tf_op jit(solution)/shard_map/stack | solution.py:56
  141.3 2.6 convolution_convert_fusion.2
  149.0 10.9 %collective-permute-done.5 = bf16[2,49,2560]{2,0,1:T(2,128)(2,1)S(1)} collective-permute-done((bf16[2,49,2560]{2,0,1:T(2,128)(2,1)S(1)}, bf16[2,49,2560]{2,0,1:T(2,128)(2,1)S(1)}, u32[]{:S(2)}, u32[]{:S(2)}) %collective-permute-start.5) | collective-permute-done | bytes 501792 | tf_op jit(solution)/shard_map/ppermute | solution.py:27
  159.9 10.1 %collective-permute-done.6 = bf16[2,49,2560]{2,0,1:T(2,128)(2,1)S(1)} collective-permute-done((bf16[2,49,2560]{2,0,1:T(2,128)(2,1)S(1)}, bf16[2,49,2560]{2,0,1:T(2,128)(2,1)S(1)}, u32[]{:S(2)}, u32[]{:S(2)}) %collective-permute-start.6) | collective-permute-done | bytes 501792 | tf_op jit(solution)/shard_map/ppermute | solution.py:27
  171.7 3.4 %collective-permute-start.7 = (bf16[50,2560]{1,0:T(8,128)(2,1)S(1)}, bf16[50,2560]{1,0:T(8,128)(2,1)S(1)}, u32[]{:S(2)}, u32[]{:S(2)}) collective-permute-start(bf16[50,2560]{1,0:T(8,128)(2,1)S(1)} %pad_maximum_fusion.10), channel_id=1, source_target_pairs={{0,8},{8,0},{1,9},{9,1},{2,10},{10,2},{3,11},{11,3},{4,12},{12,4},... | collective-permute-start | bytes 768008 | tf_op jit(solution)/shard_map/ppermute | solution.py:21
  176.5 10.6 %collective-permute-done.7 = bf16[50,2560]{1,0:T(8,128)(2,1)S(1)} collective-permute-done((bf16[50,2560]{1,0:T(8,128)(2,1)S(1)}, bf16[50,2560]{1,0:T(8,128)(2,1)S(1)}, u32[]{:S(2)}, u32[]{:S(2)}) %collective-permute-start.7) | collective-permute-done | bytes 256032 | tf_op jit(solution)/shard_map/ppermute | solution.py:21
  198.3 10.0 %collective-permute-done.8 = bf16[64,2560]{1,0:T(8,128)(2,1)S(1)} collective-permute-done((bf16[64,2560]{1,0:T(8,128)(2,1)S(1)}, bf16[64,2560]{1,0:T(8,128)(2,1)S(1)}, u32[]{:S(2)}, u32[]{:S(2)}) %collective-permute-start.8) | collective-permute-done | bytes 327712 | tf_op jit(solution)/shard_map/ppermute | solution.py:15
  208.9 11.2 %collective-permute-done.9 = bf16[48,2560]{1,0:T(8,128)(2,1)S(1)} collective-permute-done((bf16[48,2560]{1,0:T(8,128)(2,1)S(1)}, bf16[48,2560]{1,0:T(8,128)(2,1)S(1)}, u32[]{:S(2)}, u32[]{:S(2)}) %collective-permute-start.9) | collective-permute-done | bytes 245792 | tf_op jit(solution)/shard_map/ppermute | solution.py:21
  221.1 3.5 %collective-permute-start.12 = (bf16[2,48,2560]{2,1,0:T(8,128)(2,1)}, bf16[2,48,2560]{2,1,0:T(8,128)(2,1)}, u32[]{:S(2)}, u32[]{:S(2)}) collective-permute-start(bf16[2,48,2560]{2,1,0:T(8,128)(2,1)} %get-tuple-element.67), channel_id=1, source_target_pairs={{0,6},{2,4},{4,2},{6,0},{1,7},{3,5},{5,3},{7,1},{8,14},{10,12},{12... | collective-permute-start | bytes 1474568 | tf_op jit(solution)/shard_map/ppermute | solution.py:27
  226.2 2.7 fusion.112
  228.8 6.7 %collective-permute-done.11 = bf16[2,48,2560]{2,1,0:T(8,128)(2,1)} collective-permute-done((bf16[2,48,2560]{2,1,0:T(8,128)(2,1)}, bf16[2,48,2560]{2,1,0:T(8,128)(2,1)}, u32[]{:S(2)}, u32[]{:S(2)}) %collective-permute-start.11) | collective-permute-done | bytes 491552 | tf_op jit(solution)/shard_map/ppermute | solution.py:27
  235.5 9.6 %collective-permute-done.10 = bf16[2,48,2560]{2,1,0:T(8,128)(2,1)} collective-permute-done((bf16[2,48,2560]{2,1,0:T(8,128)(2,1)}, bf16[2,48,2560]{2,1,0:T(8,128)(2,1)}, u32[]{:S(2)}, u32[]{:S(2)}) %collective-permute-start.10) | collective-permute-done | bytes 491552 | tf_op jit(solution)/shard_map/ppermute | solution.py:27
  250.9 3.0 convolution_convert_fusion
  253.9 2.5 convolution_convert_fusion.1
  264.3 9.7 %collective-permute-done.14 = bf16[2,49,2560]{2,0,1:T(2,128)(2,1)S(1)} collective-permute-done((bf16[2,49,2560]{2,0,1:T(2,128)(2,1)S(1)}, bf16[2,49,2560]{2,0,1:T(2,128)(2,1)S(1)}, u32[]{:S(2)}, u32[]{:S(2)}) %collective-permute-start.14) | collective-permute-done | bytes 501792 | tf_op jit(solution)/shard_map/ppermute | solution.py:27
  274.1 9.9 %collective-permute-done.15 = bf16[2,49,2560]{2,0,1:T(2,128)(2,1)S(1)} collective-permute-done((bf16[2,49,2560]{2,0,1:T(2,128)(2,1)S(1)}, bf16[2,49,2560]{2,0,1:T(2,128)(2,1)S(1)}, u32[]{:S(2)}, u32[]{:S(2)}) %collective-permute-start.15) | collective-permute-done | bytes 501792 | tf_op jit(solution)/shard_map/ppermute | solution.py:27
  288.3 10.0 %collective-permute-done.16 = bf16[50,2560]{1,0:T(8,128)(2,1)S(1)} collective-permute-done((bf16[50,2560]{1,0:T(8,128)(2,1)S(1)}, bf16[50,2560]{1,0:T(8,128)(2,1)S(1)}, u32[]{:S(2)}, u32[]{:S(2)}) %collective-permute-start.16) | collective-permute-done | bytes 256032 | tf_op jit(solution)/shard_map/ppermute | solution.py:21
  (213 shorter events, 74.7 us)
Async XLA Ops:
  7.2 295.2 %reduce-scatter.3.cloned.1.call-start = ((), (), s32[]{:S(2)}) async-start(), calls=%async_computation.2 | async-start | bytes 2949120 | tf_op jit(solution)/shard_map/reduce_scatter | solution.py:231
  20.3 38.1 %collective-permute-start = (bf16[146,2560]{1,0:T(8,128)(2,1)S(1)}, bf16[146,2560]{1,0:T(8,128)(2,1)S(1)}, u32[]{:S(2)}, u32[]{:S(2)}) collective-permute-start(bf16[146,2560]{1,0:T(8,128)(2,1)S(1)} %get-tuple-element.55), channel_id=1, source_target_pairs={{0,8},{8,0},{1,9},{9,1},{2,10},{10,2},{3,11},{11,3},{4,12},{12,4},... | collective-permute-start | bytes 2242568 | tf_op jit(solution)/shard_map/ppermute | solution.py:21
  59.9 36.7 %collective-permute-start.3 = (bf16[2,146,2560]{2,0,1:T(2,128)(2,1)S(1)}, bf16[2,146,2560]{2,0,1:T(2,128)(2,1)S(1)}, u32[]{:S(2)}, u32[]{:S(2)}) collective-permute-start(bf16[2,146,2560]{2,0,1:T(2,128)(2,1)S(1)} %copy.76), channel_id=1, source_target_pairs={{0,6},{2,4},{4,2},{6,0},{1,7},{3,5},{5,3},{7,1},{8,14},{10,12},{12... | collective-permute-start | bytes 4485128 | tf_op jit(solution)/shard_map/ppermute | solution.py:27
  61.6 65.0 %collective-permute-start.2 = (bf16[2,146,2560]{2,0,1:T(2,128)(2,1)S(1)}, bf16[2,146,2560]{2,0,1:T(2,128)(2,1)S(1)}, u32[]{:S(2)}, u32[]{:S(2)}) collective-permute-start(bf16[2,146,2560]{2,0,1:T(2,128)(2,1)S(1)} %copy.76), channel_id=1, source_target_pairs={{0,4},{2,6},{4,0},{6,2},{1,5},{3,7},{5,1},{7,3},{8,12},{10,14},{12... | collective-permute-start | bytes 4485128 | tf_op jit(solution)/shard_map/ppermute | solution.py:27
  63.0 63.8 %collective-permute-start.1 = (bf16[2,146,2560]{2,0,1:T(2,128)(2,1)S(1)}, bf16[2,146,2560]{2,0,1:T(2,128)(2,1)S(1)}, u32[]{:S(2)}, u32[]{:S(2)}) collective-permute-start(bf16[2,146,2560]{2,0,1:T(2,128)(2,1)S(1)} %copy.76), channel_id=1, source_target_pairs={{0,2},{2,0},{4,6},{6,4},{1,3},{3,1},{5,7},{7,5},{8,10},{10,8},{12,... | collective-permute-start | bytes 4485128 | tf_op jit(solution)/shard_map/ppermute | solution.py:27
  66.0 75.4 %copy-start.8 = (bf16[1,192,2560]{2,1,0:T(8,128)(2,1)}, bf16[1,192,2560]{2,1,0:T(8,128)(2,1)S(1)}, u32[]{:S(2)}) copy-start(bf16[1,192,2560]{2,1,0:T(8,128)(2,1)S(1)} %all-gather.2) | copy-start | bytes 2949124
  96.7 30.3 %copy-start = (bf16[2,146,2560]{2,1,0:T(8,128)(2,1)}, bf16[2,146,2560]{2,1,0:T(8,128)(2,1)S(1)}, u32[]{:S(2)}) copy-start(bf16[2,146,2560]{2,1,0:T(8,128)(2,1)S(1)} %copy.110) | copy-start | bytes 4485124
  145.4 29.7 %copy-start.42 = (s32[64]{0:T(128)S(1)}, s32[64]{0:T(128)}, u32[]{:S(2)}) copy-start(s32[64]{0:T(128)} %get-tuple-element.72) | copy-start | bytes 772
  145.4 14.4 %collective-permute-start.5 = (bf16[2,49,2560]{2,0,1:T(2,128)(2,1)S(1)}, bf16[2,49,2560]{2,0,1:T(2,128)(2,1)S(1)}, u32[]{:S(2)}, u32[]{:S(2)}) collective-permute-start(bf16[2,49,2560]{2,0,1:T(2,128)(2,1)S(1)} %copy.85), channel_id=1, source_target_pairs={{0,4},{2,6},{4,0},{6,2},{1,5},{3,7},{5,1},{7,3},{8,12},{10,14},{12... | collective-permute-start | bytes 1505288 | tf_op jit(solution)/shard_map/ppermute | solution.py:27
  147.2 22.8 %collective-permute-start.6 = (bf16[2,49,2560]{2,0,1:T(2,128)(2,1)S(1)}, bf16[2,49,2560]{2,0,1:T(2,128)(2,1)S(1)}, u32[]{:S(2)}, u32[]{:S(2)}) collective-permute-start(bf16[2,49,2560]{2,0,1:T(2,128)(2,1)S(1)} %copy.87), channel_id=1, source_target_pairs={{0,6},{2,4},{4,2},{6,0},{1,7},{3,5},{5,3},{7,1},{8,14},{10,12},{12... | collective-permute-start | bytes 1505288 | tf_op jit(solution)/shard_map/ppermute | solution.py:27
  147.8 23.6 %collective-permute-start.4 = (bf16[2,49,2560]{2,0,1:T(2,128)(2,1)S(1)}, bf16[2,49,2560]{2,0,1:T(2,128)(2,1)S(1)}, u32[]{:S(2)}, u32[]{:S(2)}) collective-permute-start(bf16[2,49,2560]{2,0,1:T(2,128)(2,1)S(1)} %copy.83), channel_id=1, source_target_pairs={{0,2},{2,0},{4,6},{6,4},{1,3},{3,1},{5,7},{7,5},{8,10},{10,8},{12,... | collective-permute-start | bytes 1505288 | tf_op jit(solution)/shard_map/ppermute | solution.py:27
  171.7 15.4 %collective-permute-start.7 = (bf16[50,2560]{1,0:T(8,128)(2,1)S(1)}, bf16[50,2560]{1,0:T(8,128)(2,1)S(1)}, u32[]{:S(2)}, u32[]{:S(2)}) collective-permute-start(bf16[50,2560]{1,0:T(8,128)(2,1)S(1)} %pad_maximum_fusion.10), channel_id=1, source_target_pairs={{0,8},{8,0},{1,9},{9,1},{2,10},{10,2},{3,11},{11,3},{4,12},{12,4},... | collective-permute-start | bytes 768008 | tf_op jit(solution)/shard_map/ppermute | solution.py:21
  195.3 29.2 %copy-start.5 = (bf16[2,146,2560]{2,1,0:T(8,128)(2,1)S(1)}, bf16[2,146,2560]{2,1,0:T(8,128)(2,1)}, u32[]{:S(2)}) copy-start(bf16[2,146,2560]{2,1,0:T(8,128)(2,1)} %copy-done.4) | copy-start | bytes 4485124
  196.5 28.0 %copy-start.1 = (bf16[2,146,2560]{2,1,0:T(8,128)(2,1)S(1)}, bf16[2,146,2560]{2,1,0:T(8,128)(2,1)}, u32[]{:S(2)}) copy-start(bf16[2,146,2560]{2,1,0:T(8,128)(2,1)} %copy-done) | copy-start | bytes 4485124
  196.5 11.8 %collective-permute-start.8 = (bf16[64,2560]{1,0:T(8,128)(2,1)S(1)}, bf16[64,2560]{1,0:T(8,128)(2,1)S(1)}, u32[]{:S(2)}, u32[]{:S(2)}) collective-permute-start(bf16[64,2560]{1,0:T(8,128)(2,1)S(1)} %fusion.42), channel_id=1, source_target_pairs={{16,0},{17,1},{18,2},{19,3},{20,4},{21,5},{22,6},{23,7},{24,8},{25... | collective-permute-start | bytes 983048 | tf_op jit(solution)/shard_map/ppermute | solution.py:15
  208.8 11.3 %collective-permute-start.9 = (bf16[48,2560]{1,0:T(8,128)(2,1)S(1)}, bf16[48,2560]{1,0:T(8,128)(2,1)S(1)}, u32[]{:S(2)}, u32[]{:S(2)}) collective-permute-start(bf16[48,2560]{1,0:T(8,128)(2,1)S(1)} %get-tuple-element.69), channel_id=1, source_target_pairs={{0,8},{8,0},{1,9},{9,1},{2,10},{10,2},{3,11},{11,3},{4,12},{12,4},... | collective-permute-start | bytes 737288 | tf_op jit(solution)/shard_map/ppermute | solution.py:21
  221.1 14.4 %collective-permute-start.11 = (bf16[2,48,2560]{2,1,0:T(8,128)(2,1)}, bf16[2,48,2560]{2,1,0:T(8,128)(2,1)}, u32[]{:S(2)}, u32[]{:S(2)}) collective-permute-start(bf16[2,48,2560]{2,1,0:T(8,128)(2,1)} %get-tuple-element.67), channel_id=1, source_target_pairs={{0,4},{2,6},{4,0},{6,2},{1,5},{3,7},{5,1},{7,3},{8,12},{10,14},{12... | collective-permute-start | bytes 1474568 | tf_op jit(solution)/shard_map/ppermute | solution.py:27
  221.1 24.0 %collective-permute-start.10 = (bf16[2,48,2560]{2,1,0:T(8,128)(2,1)}, bf16[2,48,2560]{2,1,0:T(8,128)(2,1)}, u32[]{:S(2)}, u32[]{:S(2)}) collective-permute-start(bf16[2,48,2560]{2,1,0:T(8,128)(2,1)} %get-tuple-element.67), channel_id=1, source_target_pairs={{0,2},{2,0},{4,6},{6,4},{1,3},{3,1},{5,7},{7,5},{8,10},{10,8},{12,... | collective-permute-start | bytes 1474568 | tf_op jit(solution)/shard_map/ppermute | solution.py:27
  221.1 24.0 %collective-permute-start.12 = (bf16[2,48,2560]{2,1,0:T(8,128)(2,1)}, bf16[2,48,2560]{2,1,0:T(8,128)(2,1)}, u32[]{:S(2)}, u32[]{:S(2)}) collective-permute-start(bf16[2,48,2560]{2,1,0:T(8,128)(2,1)} %get-tuple-element.67), channel_id=1, source_target_pairs={{0,6},{2,4},{4,2},{6,0},{1,7},{3,5},{5,3},{7,1},{8,14},{10,12},{12... | collective-permute-start | bytes 1474568 | tf_op jit(solution)/shard_map/ppermute | solution.py:27
  256.4 48.2 %reduce-scatter.5.cloned.1.call-start = ((), (), s32[]{:S(2)}) async-start(), calls=%async_computation.3 | async-start | bytes 1474560 | tf_op jit(solution)/shard_map/reduce_scatter | solution.py:234
  259.6 14.4 %collective-permute-start.14 = (bf16[2,49,2560]{2,0,1:T(2,128)(2,1)S(1)}, bf16[2,49,2560]{2,0,1:T(2,128)(2,1)S(1)}, u32[]{:S(2)}, u32[]{:S(2)}) collective-permute-start(bf16[2,49,2560]{2,0,1:T(2,128)(2,1)S(1)} %copy.92), channel_id=1, source_target_pairs={{0,4},{2,6},{4,0},{6,2},{1,5},{3,7},{5,1},{7,3},{8,12},{10,14},{12... | collective-permute-start | bytes 1505288 | tf_op jit(solution)/shard_map/ppermute | solution.py:27
  261.4 22.5 %collective-permute-start.15 = (bf16[2,49,2560]{2,0,1:T(2,128)(2,1)S(1)}, bf16[2,49,2560]{2,0,1:T(2,128)(2,1)S(1)}, u32[]{:S(2)}, u32[]{:S(2)}) collective-permute-start(bf16[2,49,2560]{2,0,1:T(2,128)(2,1)S(1)} %copy.94), channel_id=1, source_target_pairs={{0,6},{2,4},{4,2},{6,0},{1,7},{3,5},{5,3},{7,1},{8,14},{10,12},{12... | collective-permute-start | bytes 1505288 | tf_op jit(solution)/shard_map/ppermute | solution.py:27
  262.6 22.7 %collective-permute-start.13 = (bf16[2,49,2560]{2,0,1:T(2,128)(2,1)S(1)}, bf16[2,49,2560]{2,0,1:T(2,128)(2,1)S(1)}, u32[]{:S(2)}, u32[]{:S(2)}) collective-permute-start(bf16[2,49,2560]{2,0,1:T(2,128)(2,1)S(1)} %copy.90), channel_id=1, source_target_pairs={{0,2},{2,0},{4,6},{6,4},{1,3},{3,1},{5,7},{7,5},{8,10},{10,8},{12,... | collective-permute-start | bytes 1505288 | tf_op jit(solution)/shard_map/ppermute | solution.py:27
  285.6 12.7 %collective-permute-start.16 = (bf16[50,2560]{1,0:T(8,128)(2,1)S(1)}, bf16[50,2560]{1,0:T(8,128)(2,1)S(1)}, u32[]{:S(2)}, u32[]{:S(2)}) collective-permute-start(bf16[50,2560]{1,0:T(8,128)(2,1)S(1)} %pad_maximum_fusion.11), channel_id=1, source_target_pairs={{0,8},{8,0},{1,9},{9,1},{2,10},{10,2},{3,11},{11,3},{4,12},{12,4},... | collective-permute-start | bytes 768008 | tf_op jit(solution)/shard_map/ppermute | solution.py:21
  (40 other events, 260.8 us)
Sparse Core Ops, SparseCore 0:
  256.5 8.1 reduce-scatter.2
  288.3 7.4 reduce-scatter.4

commit v4 on v1

--- a/solution.py
+++ b/solution.py
@@ -21,6 +21,12 @@
     return lax.ppermute(block, axis, route)
 
 
+def flipped(block, axis, mask):
+    size = lax.axis_size(axis)
+    route = [(i, i ^ mask) for i in range(size)]
+    return lax.ppermute(block, axis, route)
+
+
 def silu_parts(gate_value):
     sigmoid_value = jax.nn.sigmoid(gate_value)
     return (gate_value * sigmoid_value, sigmoid_value * (1.0 + gate_value * (1.0 - sigmoid_value)))
@@ -36,18 +42,6 @@
     return lax.dot_general(
         first_operand, second_operand, (((0,), (0,)), ((), ())), preferred_element_type=jnp.float32
     )
-
-
-def to_experts(blocks):
-    groups = blocks.shape[0]
-    moved = [blocks[0]] + [rotated(blocks[s], "eg", s) for s in range(1, groups)]
-    return jnp.stack(moved)
-
-
-def to_owners(blocks):
-    groups = blocks.shape[0]
-    moved = [blocks[0]] + [rotated(blocks[s], "eg", -s) for s in range(1, groups)]
-    return jnp.stack(moved)
 
 
 def local(
@@ -107,31 +101,22 @@
         picked = jnp.dot(selector, source_rows, preferred_element_type=jnp.float32)
         return picked.astype(jnp.bfloat16).reshape(groups, capacity, feature_count)
 
-    def gather_quad(blocks):
-        return lax.all_gather(to_experts(blocks), "ej", axis=0, tiled=True)
-
-    prepared = [prepare(moment) for moment in range(micro_count)]
-    rows_gathered = [
-        gather_quad(dispatch_rows(current[4], current[2])) for current in prepared
-    ]
-    weights_gathered = [
-        gather_quad(current[6].reshape(groups, capacity)) for current in prepared
-    ]
-    leaving_list = []
-    combine_list = []
-    kept_list = []
-    previous = entry_grads[0]
-    for moment in range(micro_count):
-        current = prepared[moment]
-        if moment == 0:
-            arriving = entry_grads[0]
-        else:
-            arriving = shifted(previous, "pipe", -1)
-        incoming = jnp.where(is_last, output_grads[moment], arriving)
-        grads_in = gather_quad(dispatch_rows(current[4], incoming))
-        flat_rows = rows_gathered[moment].reshape(-1, feature_count)
-        flat_grads = grads_in.reshape(-1, feature_count)
-        scale_column = weights_gathered[moment].reshape(-1, 1).astype(jnp.float32)
+    quad = lax.axis_size("ej")
+
+    def weight_row(weight_slots):
+        shaped = weight_slots.reshape(groups, 1, capacity)
+        return jnp.pad(shaped, ((0, 0), (0, 0), (0, feature_count - capacity)))
+
+    def across(block, s):
+        return block if s == 0 else rotated(block, "eg", s)
+
+    def around(block):
+        return jnp.stack([block] + [flipped(block, "ej", t) for t in range(1, quad)])
+
+    def run_block(rows_block, grads_block, weight_block):
+        flat_rows = rows_block.reshape(-1, feature_count)
+        flat_grads = grads_block.reshape(-1, feature_count)
+        scale_column = weight_block.reshape(-1, 1).astype(jnp.float32)
         gate_value = contract_last(flat_rows, gate_full)
         upward = contract_last(flat_rows, up_full)
         backward = contract_last(flat_grads, down_full)
@@ -145,20 +130,66 @@
             jnp.bfloat16
         )
         hidden_scaled = (hidden * scale_column).astype(jnp.bfloat16)
-        kept_list.append((grad_pair, hidden_scaled, flat_rows, flat_grads))
-        rows_back = to_owners(
-            lax.psum_scatter(
-                part_rows.reshape(-1, capacity, feature_count), "ej", scatter_dimension=0, tiled=True
+        return (grad_pair, hidden_scaled, flat_rows, flat_grads), part_rows, part_weight
+
+    def send_back(part_rows, part_weight, s):
+        quad_rows = part_rows.reshape(quad, capacity, feature_count)
+        quad_weight = jnp.pad(
+            part_weight.reshape(quad, 1, capacity), ((0, 0), (0, 0), (0, feature_count - capacity))
+        )
+        stacked = jnp.concatenate([quad_rows, quad_weight], axis=1)
+        total = stacked[0].astype(jnp.float32)
+        for t in range(1, quad):
+            total = total + flipped(stacked[t], "ej", t).astype(jnp.float32)
+        if s == 0:
+            return total[:capacity], total[capacity, :capacity]
+        high = total[capacity:].astype(jnp.bfloat16)
+        low = (total[capacity:] - high.astype(jnp.float32)).astype(jnp.bfloat16)
+        block = jnp.concatenate([total[:capacity].astype(jnp.bfloat16), high, low], axis=0)
+        got = rotated(block, "eg", -s).astype(jnp.float32)
+        return got[:capacity], got[capacity, :capacity] + got[capacity + 1, :capacity]
+
+    prepared = [prepare(moment) for moment in range(micro_count)]
+    first_incoming = jnp.where(is_last, output_grads[0], entry_grads[0])
+    staged_rows = []
+    for moment, current in enumerate(prepared):
+        normed_slots = dispatch_rows(current[4], current[2])
+        weight_rows = weight_row(current[6])
+        pieces = [normed_slots]
+        if moment == 0:
+            pieces.append(dispatch_rows(current[4], first_incoming))
+        pieces.append(weight_rows)
+        payload = jnp.concatenate(pieces, axis=1)
+        staged_rows.append([around(across(payload[s], s)) for s in range(groups)])
+    leaving_list = []
+    combine_list = []
+    kept_list = []
+    previous = entry_grads[0]
+    for moment in range(micro_count):
+        current = prepared[moment]
+        if moment == 0:
+            incoming = first_incoming
+            grads_blocks = [staged[:, capacity : 2 * capacity] for staged in staged_rows[0]]
+            weight_at = 2 * capacity
+        else:
+            arriving = shifted(previous, "pipe", -1)
+            incoming = jnp.where(is_last, output_grads[moment], arriving)
+            grads_slots = dispatch_rows(current[4], incoming)
+            grads_blocks = [around(across(grads_slots[s], s)) for s in range(groups)]
+            weight_at = capacity
+        rows_parts = []
+        weight_parts = []
+        for s in range(groups):
+            staged = staged_rows[moment][s]
+            kept, part_rows, part_weight = run_block(
+                staged[:, :capacity], grads_blocks[s], staged[:, weight_at, :capacity]
             )
-        )
-        weights_back = to_owners(
-            lax.psum_scatter(
-                part_weight.astype(jnp.float32).reshape(-1, capacity),
-                "ej",
-                scatter_dimension=0,
-                tiled=True,
-            )
-        )
+            kept_list.append(kept)
+            back_rows, back_weight = send_back(part_rows, part_weight, s)
+            rows_parts.append(back_rows)
+            weight_parts.append(back_weight)
+        summed = jnp.stack(rows_parts).reshape(slot_count, feature_count)
+        weight_sums = jnp.stack(weight_parts).reshape(slot_count)
         (
             finish_inputs,
             finish_scales,
@@ -168,8 +199,6 @@
             finish_keeping,
             finish_weight_slots,
         ) = current
-        summed = rows_back.astype(jnp.float32).reshape(slot_count, feature_count)
-        weight_sums = weights_back.reshape(slot_count)
         expert_rows = jnp.sum(
             jnp.take(summed, finish_places, axis=0).reshape(token_rows, pick_count, feature_count),
             axis=1,

time: 357 us -> 276 us (0.77)
  waiting for transfers between devices: 236 us -> 124 us
  starting transfers between devices: 15.6 us -> 48.4 us
  blocking collectives: 34.4 us -> 7.84 us
  other arithmetic: 11.3 us -> 32 us
  local copies, waits for them, and re-layouts: 12.2 us -> 16.9 us
    ppermute x0 -> x30, waiting for transfers between devices: none -> 100 us  [flipped(): return lax.ppermute(block, axis, route)]
    all_gather x4 -> x0, waiting for transfers between devices: 93.8 us -> none  [gather_quad(): return lax.all_gather(to_experts(blocks), 'ej', axis=0, tiled=True)]
    reduce_scatter x2 -> x0, waiting for transfers between devices: 54.5 us -> none  [local(): lax.psum_scatter(part_rows.reshape(-1, capacity, feature_count), 'ej', sc...]
    ppermute x10 -> x5, waiting for transfers between devices: 64.9 us -> 24.1 us  [rotated(): return lax.ppermute(block, axis, route)]
    ppermute x0 -> x30, starting transfers between devices: none -> 35.8 us  [flipped(): return lax.ppermute(block, axis, route)]
    all_gather x2 -> x0, blocking collectives: 17.5 us -> none  [gather_quad(): return lax.all_gather(to_experts(blocks), 'ej', axis=0, tiled=True)]
    unnamed x1 -> x0, blocking collectives: 9.3 us -> none
    another operation x8 -> x10, other arithmetic: 3.4 us -> 11.9 us  [the longest x6 10.7 us: around(): jnp.stack([block] + [flipped(block, 'ej', t) for t in range(1, quad)])]
  transfers between devices with their start and end apart: 19 -> 38, of which waited for: 16 -> 21; matrix products, arithmetic and copies ran while one was open for 9% -> 20% of each run, Pallas kernels for 0% -> 0%
where the time goes in v4:
time: 276 us; the launch traced here: 275 us
  waiting for transfers between devices  124 us (45%)
  starting transfers between devices  48.4 us (18%)
  other arithmetic  32 us (12%)
  matrix products  30.9 us (11%)
  local copies, waits for them, and re-layouts  16.9 us (6%)
  between operations  15 us (5%)
  blocking collectives  7.84 us (3%)
    ppermute x30, waiting for transfers between devices, flipped(): return lax.ppermute(block, axis, route)  100 us
    ppermute x30, starting transfers between devices, flipped(): return lax.ppermute(block, axis, route)  35.8 us
    ppermute x5, waiting for transfers between devices, rotated(): return lax.ppermute(block, axis, route)  24.1 us
    dot_general x12, matrix products, contract_last(): lax.dot_general(first_operand, second_operand, (((1,), (1,)), ((), ())),...  15.2 us
    ppermute x5, starting transfers between devices, rotated(): return lax.ppermute(block, axis, route)  11 us
    another operation x6, other arithmetic, around(): jnp.stack([block] + [flipped(block, 'ej', t) for t in range(1, quad)])  10.7 us
    dot_general x4, matrix products, run_block(): jnp.dot(grad_pair, paired_weights, preferred_element_type=jnp.float32)  8.01 us
  transfers between devices with their start and end apart: 38, of which 21 were waited for; matrix products, arithmetic and copies ran while one was open for 20% of the time, Pallas kernels for 0%

profile of v4, /device:TPU:0, one launch (start us, length us, event | category | flops | bytes accessed | tf_op | source)
XLA Modules:
  0.0 275.1 jit_solution(6885203662616906766)
XLA Ops:
  15.7 4.0 %collective-permute-start.2 = (bf16[97,2560]{1,0:T(8,128)(2,1)}, bf16[97,2560]{1,0:T(8,128)(2,1)S(1)}, u32[]{:S(2)}, u32[]{:S(2)}) collective-permute-start(bf16[97,2560]{1,0:T(8,128)(2,1)} %get-tuple-element.49), channel_id=1, source_target_pairs={{0,6},{2,4},{4,2},{6,0},{1,7},{3,5},{5,3},{7,1},{8,14},{10,12},{12... | collective-permute-start | bytes 1489928 | tf_op jit(solution)/shard_map/ppermute | solution.py:27
  20.3 3.0 %collective-permute-start.6 = (bf16[97,2560]{1,0:T(8,128)(2,1)}, bf16[97,2560]{1,0:T(8,128)(2,1)}, u32[]{:S(2)}, u32[]{:S(2)}) collective-permute-start(bf16[97,2560]{1,0:T(8,128)(2,1)} %get-tuple-element.50), channel_id=1, source_target_pairs={{0,8},{8,0},{1,9},{9,1},{2,10},{10,2},{3,11},{11,3},{4,12},{12,4},... | collective-permute-start | bytes 1489928 | tf_op jit(solution)/shard_map/ppermute | solution.py:21
  23.3 2.6 all-gather.2
  28.5 2.7 all-gather
  31.2 13.1 %collective-permute-done.2 = bf16[97,2560]{1,0:T(8,128)(2,1)S(1)} collective-permute-done((bf16[97,2560]{1,0:T(8,128)(2,1)}, bf16[97,2560]{1,0:T(8,128)(2,1)S(1)}, u32[]{:S(2)}, u32[]{:S(2)}) %collective-permute-start.2) | collective-permute-done | bytes 496672 | tf_op jit(solution)/shard_map/ppermute | solution.py:27
  44.3 10.9 %collective-permute-done.1 = bf16[97,2560]{1,0:T(8,128)(2,1)} collective-permute-done((bf16[97,2560]{1,0:T(8,128)(2,1)}, bf16[97,2560]{1,0:T(8,128)(2,1)}, u32[]{:S(2)}, u32[]{:S(2)}) %collective-permute-start.1) | collective-permute-done | bytes 496672 | tf_op jit(solution)/shard_map/ppermute | solution.py:27
  55.8 2.6 pad_maximum_fusion.11
  70.3 10.3 %collective-permute-done.9 = bf16[97,2560]{1,0:T(8,128)(2,1)S(1)} collective-permute-done((bf16[97,2560]{1,0:T(8,128)(2,1)}, bf16[97,2560]{1,0:T(8,128)(2,1)S(1)}, u32[]{:S(2)}, u32[]{:S(2)}) %collective-permute-start.9) | collective-permute-done | bytes 496672 | tf_op jit(solution)/shard_map/ppermute | solution.py:27
  80.6 10.3 %collective-permute-done.8 = bf16[97,2560]{1,0:T(8,128)(2,1)S(1)} collective-permute-done((bf16[97,2560]{1,0:T(8,128)(2,1)}, bf16[97,2560]{1,0:T(8,128)(2,1)S(1)}, u32[]{:S(2)}, u32[]{:S(2)}) %collective-permute-start.8) | collective-permute-done | bytes 496672 | tf_op jit(solution)/shard_map/ppermute | solution.py:27
  106.0 10.0 %collective-permute-done.10 = bf16[49,2560]{1,0:T(8,128)(2,1)S(1)} collective-permute-done((bf16[49,2560]{1,0:T(8,128)(2,1)S(1)}, bf16[49,2560]{1,0:T(8,128)(2,1)S(1)}, u32[]{:S(2)}, u32[]{:S(2)}) %collective-permute-start.10) | collective-permute-done | bytes 250912 | tf_op jit(solution)/shard_map/ppermute | solution.py:27
  119.2 12.7 %collective-permute-done.13 = bf16[50,2560]{1,0:T(8,128)(2,1)S(1)} collective-permute-done((bf16[50,2560]{1,0:T(8,128)(2,1)S(1)}, bf16[50,2560]{1,0:T(8,128)(2,1)S(1)}, u32[]{:S(2)}, u32[]{:S(2)}) %collective-permute-start.13) | collective-permute-done | bytes 256032 | tf_op jit(solution)/shard_map/ppermute | solution.py:21
  147.7 9.4 %collective-permute-done.17 = bf16[49,2560]{1,0:T(8,128)(2,1)S(1)} collective-permute-done((bf16[49,2560]{1,0:T(8,128)(2,1)S(1)}, bf16[49,2560]{1,0:T(8,128)(2,1)S(1)}, u32[]{:S(2)}, u32[]{:S(2)}) %collective-permute-start.17) | collective-permute-done | bytes 250912 | tf_op jit(solution)/shard_map/ppermute | solution.py:27
  157.1 3.2 %collective-permute-done.16 = bf16[49,2560]{1,0:T(8,128)(2,1)S(1)} collective-permute-done((bf16[49,2560]{1,0:T(8,128)(2,1)S(1)}, bf16[49,2560]{1,0:T(8,128)(2,1)S(1)}, u32[]{:S(2)}, u32[]{:S(2)}) %collective-permute-start.16) | collective-permute-done | bytes 250912 | tf_op jit(solution)/shard_map/ppermute | solution.py:27
  174.8 4.4 %collective-permute-done.26 = bf16[49,2560]{1,0:T(8,128)(2,1)S(1)} collective-permute-done((bf16[49,2560]{1,0:T(8,128)(2,1)}, bf16[49,2560]{1,0:T(8,128)(2,1)S(1)}, u32[]{:S(2)}, u32[]{:S(2)}) %collective-permute-start.26) | collective-permute-done | bytes 250912 | tf_op jit(solution)/shard_map/ppermute | solution.py:27
  186.4 3.2 %collective-permute-done.19 = bf16[48,2560]{1,0:T(8,128)(2,1)} collective-permute-done((bf16[48,2560]{1,0:T(8,128)(2,1)}, bf16[48,2560]{1,0:T(8,128)(2,1)}, u32[]{:S(2)}, u32[]{:S(2)}) %collective-permute-start.19) | collective-permute-done | bytes 245792 | tf_op jit(solution)/shard_map/ppermute | solution.py:27
  189.6 3.1 %collective-permute-done.20 = bf16[48,2560]{1,0:T(8,128)(2,1)} collective-permute-done((bf16[48,2560]{1,0:T(8,128)(2,1)}, bf16[48,2560]{1,0:T(8,128)(2,1)}, u32[]{:S(2)}, u32[]{:S(2)}) %collective-permute-start.20) | collective-permute-done | bytes 245792 | tf_op jit(solution)/shard_map/ppermute | solution.py:27
  200.0 4.1 %collective-permute-done.31 = bf16[48,2560]{1,0:T(8,128)(2,1)S(1)} collective-permute-done((bf16[48,2560]{1,0:T(8,128)(2,1)}, bf16[48,2560]{1,0:T(8,128)(2,1)S(1)}, u32[]{:S(2)}, u32[]{:S(2)}) %collective-permute-start.31) | collective-permute-done | bytes 245792 | tf_op jit(solution)/shard_map/ppermute | solution.py:27
  209.8 3.1 %convolution_convert_fusion = bf16[384,2560]{1,0:T(8,128)(2,1)} fusion(bf16[192,2560]{1,0:T(8,128)(2,1)S(1)} %bitcast.277, bf16[192,2560]{1,0:T(8,128)(2,1)S(1)} %bitcast.270, bf16[192,2560]{1,0:T(8,128)(2,1)S(1)} %bitcast.287, bf16[192,2560]{1,0:T(8,128)(2,1)S(1)} %bitcast.284, bf16[192,192]{1,0:T(8,128)(2,1)S(1)} %get-tuple-element.74, ...), kind=kOutput, calls=%fused_computation.4 | convolution fusion | flops 1531379712 | bytes 6488064 | tf_op jit(solution)/shard_map/dot_general | solution.py:42
  218.9 2.5 collective-permute-start.23
  225.7 2.5 collective-permute-start.34
  230.3 7.9 %collective-permute-done.21 = bf16[49,2560]{1,0:T(8,128)(2,1)S(1)} collective-permute-done((bf16[49,2560]{1,0:T(8,128)(2,1)S(1)}, bf16[49,2560]{1,0:T(8,128)(2,1)S(1)}, u32[]{:S(2)}, u32[]{:S(2)}) %collective-permute-start.21) | collective-permute-done | bytes 250912 | tf_op jit(solution)/shard_map/ppermute | solution.py:27
  240.8 3.3 %collective-permute-done.32 = bf16[49,2560]{1,0:T(8,128)(2,1)} collective-permute-done((bf16[49,2560]{1,0:T(8,128)(2,1)}, bf16[49,2560]{1,0:T(8,128)(2,1)}, u32[]{:S(2)}, u32[]{:S(2)}) %collective-permute-start.32) | collective-permute-done | bytes 250912 | tf_op jit(solution)/shard_map/ppermute | solution.py:27
  246.8 2.8 %collective-permute-start.35 = (bf16[50,2560]{1,0:T(8,128)(2,1)S(1)}, bf16[50,2560]{1,0:T(8,128)(2,1)S(1)}, u32[]{:S(2)}, u32[]{:S(2)}) collective-permute-start(bf16[50,2560]{1,0:T(8,128)(2,1)S(1)} %pad_maximum_fusion.20), channel_id=1, source_target_pairs={{0,8},{8,0},{1,9},{9,1},{2,10},{10,2},{3,11},{11,3},{4,12},{12,4},... | collective-permute-start | bytes 768008 | tf_op jit(solution)/shard_map/ppermute | solution.py:21
  249.6 11.4 %collective-permute-done.35 = bf16[50,2560]{1,0:T(8,128)(2,1)S(1)} collective-permute-done((bf16[50,2560]{1,0:T(8,128)(2,1)S(1)}, bf16[50,2560]{1,0:T(8,128)(2,1)S(1)}, u32[]{:S(2)}, u32[]{:S(2)}) %collective-permute-start.35) | collective-permute-done | bytes 256032 | tf_op jit(solution)/shard_map/ppermute | solution.py:21
  (297 shorter events, 117.0 us)
Async XLA Ops:
  7.2 258.9 %reduce-scatter.3.cloned.1.call-start = ((), (), s32[]{:S(2)}) async-start(), calls=%async_computation.2 | async-start | bytes 2949120 | tf_op jit(solution)/shard_map/reduce_scatter | solution.py:226
  15.7 28.5 %collective-permute-start.2 = (bf16[97,2560]{1,0:T(8,128)(2,1)}, bf16[97,2560]{1,0:T(8,128)(2,1)S(1)}, u32[]{:S(2)}, u32[]{:S(2)}) collective-permute-start(bf16[97,2560]{1,0:T(8,128)(2,1)} %get-tuple-element.49), channel_id=1, source_target_pairs={{0,6},{2,4},{4,2},{6,0},{1,7},{3,5},{5,3},{7,1},{8,14},{10,12},{12... | collective-permute-start | bytes 1489928 | tf_op jit(solution)/shard_map/ppermute | solution.py:27
  19.7 35.5 %collective-permute-start.1 = (bf16[97,2560]{1,0:T(8,128)(2,1)}, bf16[97,2560]{1,0:T(8,128)(2,1)}, u32[]{:S(2)}, u32[]{:S(2)}) collective-permute-start(bf16[97,2560]{1,0:T(8,128)(2,1)} %get-tuple-element.49), channel_id=1, source_target_pairs={{0,4},{2,6},{4,0},{6,2},{1,5},{3,7},{5,1},{7,3},{8,12},{10,14},{12... | collective-permute-start | bytes 1489928 | tf_op jit(solution)/shard_map/ppermute | solution.py:27
  20.1 35.0 %collective-permute-start = (bf16[97,2560]{1,0:T(8,128)(2,1)}, bf16[97,2560]{1,0:T(8,128)(2,1)}, u32[]{:S(2)}, u32[]{:S(2)}) collective-permute-start(bf16[97,2560]{1,0:T(8,128)(2,1)} %get-tuple-element.49), channel_id=1, source_target_pairs={{0,2},{2,0},{4,6},{6,4},{1,3},{3,1},{5,7},{7,5},{8,10},{10,8},{12,... | collective-permute-start | bytes 1489928 | tf_op jit(solution)/shard_map/ppermute | solution.py:27
  20.3 44.1 %collective-permute-start.6 = (bf16[97,2560]{1,0:T(8,128)(2,1)}, bf16[97,2560]{1,0:T(8,128)(2,1)}, u32[]{:S(2)}, u32[]{:S(2)}) collective-permute-start(bf16[97,2560]{1,0:T(8,128)(2,1)} %get-tuple-element.50), channel_id=1, source_target_pairs={{0,8},{8,0},{1,9},{9,1},{2,10},{10,2},{3,11},{11,3},{4,12},{12,4},... | collective-permute-start | bytes 1489928 | tf_op jit(solution)/shard_map/ppermute | solution.py:21
  64.4 26.5 %collective-permute-start.8 = (bf16[97,2560]{1,0:T(8,128)(2,1)}, bf16[97,2560]{1,0:T(8,128)(2,1)S(1)}, u32[]{:S(2)}, u32[]{:S(2)}) collective-permute-start(bf16[97,2560]{1,0:T(8,128)(2,1)} %collective-permute-done.6), channel_id=1, source_target_pairs={{0,4},{2,6},{4,0},{6,2},{1,5},{3,7},{5,1},{7,3},{8,12},{10,14},{12... | collective-permute-start | bytes 1489928 | tf_op jit(solution)/shard_map/ppermute | solution.py:27
  66.3 25.8 %collective-permute-start.7 = (bf16[97,2560]{1,0:T(8,128)(2,1)}, bf16[97,2560]{1,0:T(8,128)(2,1)S(1)}, u32[]{:S(2)}, u32[]{:S(2)}) collective-permute-start(bf16[97,2560]{1,0:T(8,128)(2,1)} %collective-permute-done.6), channel_id=1, source_target_pairs={{0,2},{2,0},{4,6},{6,4},{1,3},{3,1},{5,7},{7,5},{8,10},{10,8},{12,... | collective-permute-start | bytes 1489928 | tf_op jit(solution)/shard_map/ppermute | solution.py:27
  68.8 33.5 %collective-permute-start.3 = (bf16[49,2560]{1,0:T(8,128)(2,1)}, bf16[49,2560]{1,0:T(8,128)(2,1)S(1)}, u32[]{:S(2)}, u32[]{:S(2)}) collective-permute-start(bf16[49,2560]{1,0:T(8,128)(2,1)} %get-tuple-element.42), channel_id=1, source_target_pairs={{0,2},{2,0},{4,6},{6,4},{1,3},{3,1},{5,7},{7,5},{8,10},{10,8},{12,... | collective-permute-start | bytes 752648 | tf_op jit(solution)/shard_map/ppermute | solution.py:27
  69.2 35.6 %collective-permute-start.5 = (bf16[49,2560]{1,0:T(8,128)(2,1)}, bf16[49,2560]{1,0:T(8,128)(2,1)}, u32[]{:S(2)}, u32[]{:S(2)}) collective-permute-start(bf16[49,2560]{1,0:T(8,128)(2,1)} %get-tuple-element.43), channel_id=1, source_target_pairs={{0,6},{2,4},{4,2},{6,0},{1,7},{3,5},{5,3},{7,1},{8,14},{10,12},{12... | collective-permute-start | bytes 752648 | tf_op jit(solution)/shard_map/ppermute | solution.py:27
  80.6 24.2 %collective-permute-start.4 = (bf16[49,2560]{1,0:T(8,128)(2,1)}, bf16[49,2560]{1,0:T(8,128)(2,1)}, u32[]{:S(2)}, u32[]{:S(2)}) collective-permute-start(bf16[49,2560]{1,0:T(8,128)(2,1)} %get-tuple-element.44), channel_id=1, source_target_pairs={{0,4},{2,6},{4,0},{6,2},{1,5},{3,7},{5,1},{7,3},{8,12},{10,14},{12... | collective-permute-start | bytes 752648 | tf_op jit(solution)/shard_map/ppermute | solution.py:27
  140.3 16.9 %collective-permute-start.17 = (bf16[49,2560]{1,0:T(8,128)(2,1)S(1)}, bf16[49,2560]{1,0:T(8,128)(2,1)S(1)}, u32[]{:S(2)}, u32[]{:S(2)}) collective-permute-start(bf16[49,2560]{1,0:T(8,128)(2,1)S(1)} %get-tuple-element.62), channel_id=1, source_target_pairs={{0,6},{2,4},{4,2},{6,0},{1,7},{3,5},{5,3},{7,1},{8,14},{10,12},{12... | collective-permute-start | bytes 752648 | tf_op jit(solution)/shard_map/ppermute | solution.py:27
  141.0 19.3 %collective-permute-start.16 = (bf16[49,2560]{1,0:T(8,128)(2,1)S(1)}, bf16[49,2560]{1,0:T(8,128)(2,1)S(1)}, u32[]{:S(2)}, u32[]{:S(2)}) collective-permute-start(bf16[49,2560]{1,0:T(8,128)(2,1)S(1)} %get-tuple-element.62), channel_id=1, source_target_pairs={{0,4},{2,6},{4,0},{6,2},{1,5},{3,7},{5,1},{7,3},{8,12},{10,14},{12... | collective-permute-start | bytes 752648 | tf_op jit(solution)/shard_map/ppermute | solution.py:27
  142.3 18.0 %collective-permute-start.15 = (bf16[49,2560]{1,0:T(8,128)(2,1)S(1)}, bf16[49,2560]{1,0:T(8,128)(2,1)S(1)}, u32[]{:S(2)}, u32[]{:S(2)}) collective-permute-start(bf16[49,2560]{1,0:T(8,128)(2,1)S(1)} %get-tuple-element.62), channel_id=1, source_target_pairs={{0,2},{2,0},{4,6},{6,4},{1,3},{3,1},{5,7},{7,5},{8,10},{10,8},{12,... | collective-permute-start | bytes 752648 | tf_op jit(solution)/shard_map/ppermute | solution.py:27
  144.9 23.0 %collective-permute-start.14 = (bf16[64,2560]{1,0:T(8,128)(2,1)}, bf16[64,2560]{1,0:T(8,128)(2,1)}, u32[]{:S(2)}, u32[]{:S(2)}) collective-permute-start(bf16[64,2560]{1,0:T(8,128)(2,1)} %fusion.57), channel_id=1, source_target_pairs={{16,0},{17,1},{18,2},{19,3},{20,4},{21,5},{22,6},{23,7},{24,8},{25... | collective-permute-start | bytes 983048 | tf_op jit(solution)/shard_map/ppermute | solution.py:15
  165.1 16.3 %collective-permute-start.25 = (bf16[49,2560]{1,0:T(8,128)(2,1)}, bf16[49,2560]{1,0:T(8,128)(2,1)S(1)}, u32[]{:S(2)}, u32[]{:S(2)}) collective-permute-start(bf16[49,2560]{1,0:T(8,128)(2,1)} %collective-permute-done.24), channel_id=1, source_target_pairs={{0,2},{2,0},{4,6},{6,4},{1,3},{3,1},{5,7},{7,5},{8,10},{10,8},{12,... | collective-permute-start | bytes 752648 | tf_op jit(solution)/shard_map/ppermute | solution.py:27
  170.1 19.5 %collective-permute-start.19 = (bf16[48,2560]{1,0:T(8,128)(2,1)}, bf16[48,2560]{1,0:T(8,128)(2,1)}, u32[]{:S(2)}, u32[]{:S(2)}) collective-permute-start(bf16[48,2560]{1,0:T(8,128)(2,1)} %get-tuple-element.66), channel_id=1, source_target_pairs={{0,4},{2,6},{4,0},{6,2},{1,5},{3,7},{5,1},{7,3},{8,12},{10,14},{12... | collective-permute-start | bytes 737288 | tf_op jit(solution)/shard_map/ppermute | solution.py:27
  170.9 18.7 %collective-permute-start.18 = (bf16[48,2560]{1,0:T(8,128)(2,1)}, bf16[48,2560]{1,0:T(8,128)(2,1)}, u32[]{:S(2)}, u32[]{:S(2)}) collective-permute-start(bf16[48,2560]{1,0:T(8,128)(2,1)} %get-tuple-element.66), channel_id=1, source_target_pairs={{0,2},{2,0},{4,6},{6,4},{1,3},{3,1},{5,7},{7,5},{8,10},{10,8},{12,... | collective-permute-start | bytes 737288 | tf_op jit(solution)/shard_map/ppermute | solution.py:27
  173.0 19.6 %collective-permute-start.20 = (bf16[48,2560]{1,0:T(8,128)(2,1)}, bf16[48,2560]{1,0:T(8,128)(2,1)}, u32[]{:S(2)}, u32[]{:S(2)}) collective-permute-start(bf16[48,2560]{1,0:T(8,128)(2,1)} %get-tuple-element.66), channel_id=1, source_target_pairs={{0,6},{2,4},{4,2},{6,0},{1,7},{3,5},{5,3},{7,1},{8,14},{10,12},{12... | collective-permute-start | bytes 737288 | tf_op jit(solution)/shard_map/ppermute | solution.py:27
  213.0 55.3 %reduce-scatter.5.cloned.1.call-start = ((), (), s32[]{:S(2)}) async-start(), calls=%async_computation.3 | async-start | bytes 1474560 | tf_op jit(solution)/shard_map/reduce_scatter | solution.py:229
  218.2 20.1 %collective-permute-start.21 = (bf16[49,2560]{1,0:T(8,128)(2,1)S(1)}, bf16[49,2560]{1,0:T(8,128)(2,1)S(1)}, u32[]{:S(2)}, u32[]{:S(2)}) collective-permute-start(bf16[49,2560]{1,0:T(8,128)(2,1)S(1)} %get-tuple-element.36), channel_id=1, source_target_pairs={{0,2},{2,0},{4,6},{6,4},{1,3},{3,1},{5,7},{7,5},{8,10},{10,8},{12,... | collective-permute-start | bytes 752648 | tf_op jit(solution)/shard_map/ppermute | solution.py:27
  218.9 20.8 %collective-permute-start.23 = (bf16[49,2560]{1,0:T(8,128)(2,1)S(1)}, bf16[49,2560]{1,0:T(8,128)(2,1)S(1)}, u32[]{:S(2)}, u32[]{:S(2)}) collective-permute-start(bf16[49,2560]{1,0:T(8,128)(2,1)S(1)} %get-tuple-element.37), channel_id=1, source_target_pairs={{0,6},{2,4},{4,2},{6,0},{1,7},{3,5},{5,3},{7,1},{8,14},{10,12},{12... | collective-permute-start | bytes 752648 | tf_op jit(solution)/shard_map/ppermute | solution.py:27
  221.4 18.2 %collective-permute-start.22 = (bf16[49,2560]{1,0:T(8,128)(2,1)S(1)}, bf16[49,2560]{1,0:T(8,128)(2,1)}, u32[]{:S(2)}, u32[]{:S(2)}) collective-permute-start(bf16[49,2560]{1,0:T(8,128)(2,1)S(1)} %get-tuple-element.38), channel_id=1, source_target_pairs={{0,4},{2,6},{4,0},{6,2},{1,5},{3,7},{5,1},{7,3},{8,12},{10,14},{12... | collective-permute-start | bytes 752648 | tf_op jit(solution)/shard_map/ppermute | solution.py:27
  225.1 19.0 %collective-permute-start.32 = (bf16[49,2560]{1,0:T(8,128)(2,1)}, bf16[49,2560]{1,0:T(8,128)(2,1)}, u32[]{:S(2)}, u32[]{:S(2)}) collective-permute-start(bf16[49,2560]{1,0:T(8,128)(2,1)} %get-tuple-element.39), channel_id=1, source_target_pairs={{0,2},{2,0},{4,6},{6,4},{1,3},{3,1},{5,7},{7,5},{8,10},{10,8},{12,... | collective-permute-start | bytes 752648 | tf_op jit(solution)/shard_map/ppermute | solution.py:27
  225.7 18.4 %collective-permute-start.34 = (bf16[49,2560]{1,0:T(8,128)(2,1)}, bf16[49,2560]{1,0:T(8,128)(2,1)}, u32[]{:S(2)}, u32[]{:S(2)}) collective-permute-start(bf16[49,2560]{1,0:T(8,128)(2,1)} %get-tuple-element.40), channel_id=1, source_target_pairs={{0,6},{2,4},{4,2},{6,0},{1,7},{3,5},{5,3},{7,1},{8,14},{10,12},{12... | collective-permute-start | bytes 752648 | tf_op jit(solution)/shard_map/ppermute | solution.py:27
  (76 other events, 563.5 us)
Sparse Core Ops, SparseCore 0:
  213.1 9.5 reduce-scatter.2
  230.4 7.4 reduce-scatter.4

commit v5 on v4

--- a/solution.py
+++ b/solution.py
@@ -111,7 +111,8 @@
         return block if s == 0 else rotated(block, "eg", s)
 
     def around(block):
-        return jnp.stack([block] + [flipped(block, "ej", t) for t in range(1, quad)])
+        copies = jnp.broadcast_to(block[None], (quad,) + block.shape)
+        return lax.all_to_all(copies, "ej", split_axis=0, concat_axis=0, tiled=True)
 
     def run_block(rows_block, grads_block, weight_block):
         flat_rows = rows_block.reshape(-1, feature_count)
@@ -138,9 +139,8 @@
             part_weight.reshape(quad, 1, capacity), ((0, 0), (0, 0), (0, feature_count - capacity))
         )
         stacked = jnp.concatenate([quad_rows, quad_weight], axis=1)
-        total = stacked[0].astype(jnp.float32)
-        for t in range(1, quad):
-            total = total + flipped(stacked[t], "ej", t).astype(jnp.float32)
+        returned = lax.all_to_all(stacked, "ej", split_axis=0, concat_axis=0, tiled=True)
+        total = jnp.sum(returned.astype(jnp.float32), axis=0)
         if s == 0:
             return total[:capacity], total[capacity, :capacity]
         high = total[capacity:].astype(jnp.bfloat16)

time: 276 us -> 319 us (1.16)
  waiting for transfers between devices: 124 us -> 157 us
  local copies, waits for them, and re-layouts: 16.9 us -> 30.8 us
  other arithmetic: 32 us -> 25.9 us
    ppermute x30 -> x0, waiting for transfers between devices: 100 us -> none  [flipped(): return lax.ppermute(block, axis, route)]
    ppermute x5, waiting for transfers between devices: 24.1 us -> 91.9 us  [rotated(): return lax.ppermute(block, axis, route)]
    all_to_all x0 -> x10, waiting for transfers between devices: none -> 55.6 us  [the longest x4 36.2 us: send_back(): lax.all_to_all(stacked, 'ej', split_axis=0, concat_axis=0, tiled=True)]
    all_to_all x0 -> x10, starting transfers between devices: none -> 42.9 us  [the longest x6 27.3 us: around(): return lax.all_to_all(copies, 'ej', split_axis=0, concat_axis=0, tiled=True)]
    ppermute x30 -> x0, starting transfers between devices: 35.8 us -> none  [flipped(): return lax.ppermute(block, axis, route)]
    another operation x6 -> x0, other arithmetic: 10.7 us -> none  [around(): jnp.stack([block] + [flipped(block, 'ej', t) for t in range(1, quad)])]
    ppermute x1, waiting for transfers between devices: 0.01 us -> 9.43 us  [shifted(): return lax.ppermute(block, axis, route)]
    broadcast_in_dim x0 -> x8, local copies, waits for them, and re-layouts: none -> 9.15 us  [around(): copies = jnp.broadcast_to(block[None], (quad,) + block.shape)]
  transfers between devices with their start and end apart: 38 -> 18, of which waited for: 21 -> 16; matrix products, arithmetic and copies ran while one was open for 20% -> 16% of each run, Pallas kernels for 0% -> 0%
where the time goes in v5:
time: 319 us; the launch traced here: 317 us
  waiting for transfers between devices  157 us (49%)
  starting transfers between devices  48.4 us (15%)
  matrix products  32.1 us (10%)
  local copies, waits for them, and re-layouts  30.8 us (10%)
  other arithmetic  25.9 us (8%)
  between operations  15 us (5%)
  blocking collectives  7.62 us (2%)
    ppermute x5, waiting for transfers between devices, rotated(): return lax.ppermute(block, axis, route)  91.9 us
    all_to_all x4, waiting for transfers between devices, send_back(): lax.all_to_all(stacked, 'ej', split_axis=0, concat_axis=0, tiled=True)  36.2 us
    all_to_all x6, starting transfers between devices, around(): return lax.all_to_all(copies, 'ej', split_axis=0, concat_axis=0, tiled=True)  27.3 us
    all_to_all x6, waiting for transfers between devices, around(): return lax.all_to_all(copies, 'ej', split_axis=0, concat_axis=0, tiled=True)  19.4 us
    all_to_all x4, starting transfers between devices, send_back(): lax.all_to_all(stacked, 'ej', split_axis=0, concat_axis=0, tiled=True)  15.6 us
    dot_general x12, matrix products, contract_last(): lax.dot_general(first_operand, second_operand, (((1,), (1,)), ((), ())),...  13.9 us
    ppermute x1, waiting for transfers between devices, shifted(): return lax.ppermute(block, axis, route)  9.43 us
    broadcast_in_dim x8, local copies, waits for them, and re-layouts, around(): copies = jnp.broadcast_to(block[None], (quad,) + block.shape)  9.15 us
  transfers between devices with their start and end apart: 18, of which 16 were waited for; matrix products, arithmetic and copies ran while one was open for 16% of the time, Pallas kernels for 0%

profile of v5, /device:TPU:0, one launch (start us, length us, event | category | flops | bytes accessed | tf_op | source)
XLA Modules:
  0.0 316.8 jit_solution(1658007400679318068)
XLA Ops:
  16.9 5.2 %all-to-all-start = ((bf16[4,97,2560]{2,1,0:T(8,128)(2,1)}), bf16[4,97,2560]{2,1,0:T(8,128)(2,1)S(1)}, u32[]{:S(2)}, u32[]{:S(2)}) async-start(bf16[4,97,2560]{2,1,0:T(8,128)(2,1)} %broadcast_in_dim.92), calls=%async_computation | async-start | bytes 4259840 | tf_op jit(solution)/shard_map/all_to_all | solution.py:115
  24.7 31.8 %collective-permute-done = bf16[97,2560]{1,0:T(8,128)(2,1)S(1)} collective-permute-done((bf16[97,2560]{1,0:T(8,128)(2,1)S(1)}, bf16[97,2560]{1,0:T(8,128)(2,1)S(1)}, u32[]{:S(2)}, u32[]{:S(2)}) %collective-permute-start) | collective-permute-done | bytes 496672 | tf_op jit(solution)/shard_map/ppermute | solution.py:21
  60.8 4.9 %all-to-all-start.2 = ((bf16[4,97,2560]{2,1,0:T(8,128)(2,1)}), bf16[4,97,2560]{2,1,0:T(8,128)(2,1)}, u32[]{:S(2)}, u32[]{:S(2)}) async-start(bf16[4,97,2560]{2,1,0:T(8,128)(2,1)} %broadcast_in_dim.93), calls=%async_computation.2 | async-start | bytes 4259840 | tf_op jit(solution)/shard_map/all_to_all | solution.py:115
  81.2 9.6 %all-to-all-done.2 = bf16[4,97,2560]{2,1,0:T(8,128)(2,1)} async-done(((bf16[4,97,2560]{2,1,0:T(8,128)(2,1)}), bf16[4,97,2560]{2,1,0:T(8,128)(2,1)}, u32[]{:S(2)}, u32[]{:S(2)}) %all-to-all-start.2) | async-done | bytes 1986592 | tf_op jit(solution)/shard_map/all_to_all | solution.py:115
  90.8 3.5 %all-to-all-start.1 = ((bf16[4,49,2560]{2,1,0:T(8,128)(2,1)}), bf16[4,49,2560]{2,1,0:T(8,128)(2,1)S(1)}, u32[]{:S(2)}, u32[]{:S(2)}) async-start(bf16[4,49,2560]{2,1,0:T(8,128)(2,1)} %fusion.26), calls=%async_computation.1 | async-start | bytes 2293760 | tf_op jit(solution)/shard_map/all_to_all | solution.py:142
  94.3 3.0 fusion.163
  105.0 3.5 %all-to-all-done.1 = bf16[4,49,2560]{2,1,0:T(8,128)(2,1)S(1)} async-done(((bf16[4,49,2560]{2,1,0:T(8,128)(2,1)}), bf16[4,49,2560]{2,1,0:T(8,128)(2,1)S(1)}, u32[]{:S(2)}, u32[]{:S(2)}) %all-to-all-start.1) | async-done | bytes 1003552 | tf_op jit(solution)/shard_map/all_to_all | solution.py:142
  108.4 4.3 %all-to-all-start.3 = ((bf16[4,49,2560]{2,1,0:T(8,128)(2,1)}), bf16[4,49,2560]{2,1,0:T(8,128)(2,1)}, u32[]{:S(2)}, u32[]{:S(2)}) async-start(bf16[4,49,2560]{2,1,0:T(8,128)(2,1)} %fusion.27), calls=%async_computation.3 | async-start | bytes 2293760 | tf_op jit(solution)/shard_map/all_to_all | solution.py:142
  113.8 13.0 %all-to-all-done.3 = bf16[4,49,2560]{2,1,0:T(8,128)(2,1)} async-done(((bf16[4,49,2560]{2,1,0:T(8,128)(2,1)}), bf16[4,49,2560]{2,1,0:T(8,128)(2,1)}, u32[]{:S(2)}, u32[]{:S(2)}) %all-to-all-start.3) | async-done | bytes 1003552 | tf_op jit(solution)/shard_map/all_to_all | solution.py:142
  129.6 13.0 %collective-permute-done.1 = bf16[50,2560]{1,0:T(8,128)(2,1)S(1)} collective-permute-done((bf16[50,2560]{1,0:T(8,128)(2,1)S(1)}, bf16[50,2560]{1,0:T(8,128)(2,1)S(1)}, u32[]{:S(2)}, u32[]{:S(2)}) %collective-permute-start.1) | collective-permute-done | bytes 256032 | tf_op jit(solution)/shard_map/ppermute | solution.py:21
  152.9 4.3 %all-to-all-start.4 = ((bf16[4,49,2560]{2,1,0:T(8,128)(2,1)}), bf16[4,49,2560]{2,1,0:T(8,128)(2,1)}, u32[]{:S(2)}, u32[]{:S(2)}) async-start(bf16[4,49,2560]{2,1,0:T(8,128)(2,1)} %broadcast_in_dim.96), calls=%async_computation.4 | async-start | bytes 2293760 | tf_op jit(solution)/shard_map/all_to_all | solution.py:115
  157.3 17.1 %collective-permute-done.3 = bf16[49,2560]{1,0:T(8,128)(2,1)} collective-permute-done((bf16[49,2560]{1,0:T(8,128)(2,1)}, bf16[49,2560]{1,0:T(8,128)(2,1)}, u32[]{:S(2)}, u32[]{:S(2)}) %collective-permute-start.3) | collective-permute-done | bytes 250912 | tf_op jit(solution)/shard_map/ppermute | solution.py:21
  178.6 4.4 %all-to-all-start.7 = ((bf16[4,49,2560]{2,1,0:T(8,128)(2,1)}), bf16[4,49,2560]{2,1,0:T(8,128)(2,1)}, u32[]{:S(2)}, u32[]{:S(2)}) async-start(bf16[4,49,2560]{2,1,0:T(8,128)(2,1)} %broadcast_in_dim.98), calls=%async_computation.7 | async-start | bytes 2293760 | tf_op jit(solution)/shard_map/all_to_all | solution.py:115
  185.7 9.4 %collective-permute-done.2 = bf16[64,2560]{1,0:T(8,128)(2,1)S(1)} collective-permute-done((bf16[64,2560]{1,0:T(8,128)(2,1)S(1)}, bf16[64,2560]{1,0:T(8,128)(2,1)S(1)}, u32[]{:S(2)}, u32[]{:S(2)}) %collective-permute-start.2) | collective-permute-done | bytes 327712 | tf_op jit(solution)/shard_map/ppermute | solution.py:15
  200.0 4.3 %all-to-all-start.5 = ((bf16[4,48,2560]{2,1,0:T(8,128)(2,1)}), bf16[4,48,2560]{2,1,0:T(8,128)(2,1)}, u32[]{:S(2)}, u32[]{:S(2)}) async-start(bf16[4,48,2560]{2,1,0:T(8,128)(2,1)} %broadcast_in_dim.97), calls=%async_computation.5 | async-start | bytes 1966080 | tf_op jit(solution)/shard_map/all_to_all | solution.py:115
  204.4 15.4 %collective-permute-done.4 = bf16[48,2560]{1,0:T(8,128)(2,1)S(1)} collective-permute-done((bf16[48,2560]{1,0:T(8,128)(2,1)}, bf16[48,2560]{1,0:T(8,128)(2,1)S(1)}, u32[]{:S(2)}, u32[]{:S(2)}) %collective-permute-start.4) | collective-permute-done | bytes 245792 | tf_op jit(solution)/shard_map/ppermute | solution.py:21
  223.2 4.2 %all-to-all-start.8 = ((bf16[4,48,2560]{2,1,0:T(8,128)(2,1)}), bf16[4,48,2560]{2,1,0:T(8,128)(2,1)}, u32[]{:S(2)}, u32[]{:S(2)}) async-start(bf16[4,48,2560]{2,1,0:T(8,128)(2,1)} %broadcast_in_dim.99), calls=%async_computation.8 | async-start | bytes 1966080 | tf_op jit(solution)/shard_map/all_to_all | solution.py:115
  243.8 3.1 convolution_convert_fusion
  251.0 4.3 %all-to-all-start.6 = ((bf16[4,49,2560]{2,1,0:T(8,128)(2,1)}), bf16[4,49,2560]{2,1,0:T(8,128)(2,1)}, u32[]{:S(2)}, u32[]{:S(2)}) async-start(bf16[4,49,2560]{2,1,0:T(8,128)(2,1)} %fusion.28), calls=%async_computation.6 | async-start | bytes 2293760 | tf_op jit(solution)/shard_map/all_to_all | solution.py:142
  258.4 11.7 %all-to-all-done.6 = bf16[4,49,2560]{2,1,0:T(8,128)(2,1)} async-done(((bf16[4,49,2560]{2,1,0:T(8,128)(2,1)}), bf16[4,49,2560]{2,1,0:T(8,128)(2,1)}, u32[]{:S(2)}, u32[]{:S(2)}) %all-to-all-start.6) | async-done | bytes 1003552 | tf_op jit(solution)/shard_map/all_to_all | solution.py:142
  270.1 3.5 %all-to-all-start.9 = ((bf16[4,49,2560]{2,1,0:T(8,128)(2,1)}), bf16[4,49,2560]{2,1,0:T(8,128)(2,1)S(1)}, u32[]{:S(2)}, u32[]{:S(2)}) async-start(bf16[4,49,2560]{2,1,0:T(8,128)(2,1)} %fusion.29), calls=%async_computation.9 | async-start | bytes 2293760 | tf_op jit(solution)/shard_map/all_to_all | solution.py:142
  274.2 4.1 %fusion.18 = bf16[1,192,2560]{2,1,0:T(8,128)(2,1)} fusion(bf16[192,2560]{1,0:T(8,128)(2,1)} %bitcast.39, bf16[192,2560]{1,0:T(8,128)(2,1)} %bitcast.34, bf16[192,2560]{1,0:T(8,128)(2,1)} %bitcast.209, bf16[192,2560]{1,0:T(8,128)(2,1)} %bitcast.208, bf16[192,192]{1,0:T(8,128)(2,1)} %get-tuple-element.58, bf16[192,192]{1,0:T(8,128)(2,1)S(1)} %copy-done.45, ...), kind=kOutput, calls=%fused_computation.25 | convolution fusion | flops 772374528 | bytes 5210112 | tf_op jit(solution)/shard_map/dot_general | solution.py:42
  279.7 8.0 %all-to-all-done.9 = bf16[4,49,2560]{2,1,0:T(8,128)(2,1)S(1)} async-done(((bf16[4,49,2560]{2,1,0:T(8,128)(2,1)}), bf16[4,49,2560]{2,1,0:T(8,128)(2,1)S(1)}, u32[]{:S(2)}, u32[]{:S(2)}) %all-to-all-start.9) | async-done | bytes 1003552 | tf_op jit(solution)/shard_map/all_to_all | solution.py:142
  288.2 14.5 %collective-permute-done.5 = bf16[50,2560]{1,0:T(8,128)(2,1)S(1)} collective-permute-done((bf16[50,2560]{1,0:T(8,128)(2,1)S(1)}, bf16[50,2560]{1,0:T(8,128)(2,1)S(1)}, u32[]{:S(2)}, u32[]{:S(2)}) %collective-permute-start.5) | collective-permute-done | bytes 256032 | tf_op jit(solution)/shard_map/ppermute | solution.py:21
  (241 shorter events, 101.6 us)
Async XLA Ops:
  16.9 41.8 %all-to-all-start = ((bf16[4,97,2560]{2,1,0:T(8,128)(2,1)}), bf16[4,97,2560]{2,1,0:T(8,128)(2,1)S(1)}, u32[]{:S(2)}, u32[]{:S(2)}) async-start(bf16[4,97,2560]{2,1,0:T(8,128)(2,1)} %broadcast_in_dim.92), calls=%async_computation | async-start | bytes 4259840 | tf_op jit(solution)/shard_map/all_to_all | solution.py:115
  22.1 34.4 %collective-permute-start = (bf16[97,2560]{1,0:T(8,128)(2,1)S(1)}, bf16[97,2560]{1,0:T(8,128)(2,1)S(1)}, u32[]{:S(2)}, u32[]{:S(2)}) collective-permute-start(bf16[97,2560]{1,0:T(8,128)(2,1)S(1)} %get-tuple-element.37), channel_id=1, source_target_pairs={{0,8},{8,0},{1,9},{9,1},{2,10},{10,2},{3,11},{11,3},{4,12},{12,4},... | collective-permute-start | bytes 1489928 | tf_op jit(solution)/shard_map/ppermute | solution.py:21
  60.8 30.0 %all-to-all-start.2 = ((bf16[4,97,2560]{2,1,0:T(8,128)(2,1)}), bf16[4,97,2560]{2,1,0:T(8,128)(2,1)}, u32[]{:S(2)}, u32[]{:S(2)}) async-start(bf16[4,97,2560]{2,1,0:T(8,128)(2,1)} %broadcast_in_dim.93), calls=%async_computation.2 | async-start | bytes 4259840 | tf_op jit(solution)/shard_map/all_to_all | solution.py:115
  90.8 17.7 %all-to-all-start.1 = ((bf16[4,49,2560]{2,1,0:T(8,128)(2,1)}), bf16[4,49,2560]{2,1,0:T(8,128)(2,1)S(1)}, u32[]{:S(2)}, u32[]{:S(2)}) async-start(bf16[4,49,2560]{2,1,0:T(8,128)(2,1)} %fusion.26), calls=%async_computation.1 | async-start | bytes 2293760 | tf_op jit(solution)/shard_map/all_to_all | solution.py:142
  108.4 18.4 %all-to-all-start.3 = ((bf16[4,49,2560]{2,1,0:T(8,128)(2,1)}), bf16[4,49,2560]{2,1,0:T(8,128)(2,1)}, u32[]{:S(2)}, u32[]{:S(2)}) async-start(bf16[4,49,2560]{2,1,0:T(8,128)(2,1)} %fusion.27), calls=%async_computation.3 | async-start | bytes 2293760 | tf_op jit(solution)/shard_map/all_to_all | solution.py:142
  128.4 14.2 %collective-permute-start.1 = (bf16[50,2560]{1,0:T(8,128)(2,1)S(1)}, bf16[50,2560]{1,0:T(8,128)(2,1)S(1)}, u32[]{:S(2)}, u32[]{:S(2)}) collective-permute-start(bf16[50,2560]{1,0:T(8,128)(2,1)S(1)} %pad_maximum_fusion.3), channel_id=1, source_target_pairs={{0,8},{8,0},{1,9},{9,1},{2,10},{10,2},{3,11},{11,3},{4,12},{12,4},... | collective-permute-start | bytes 768008 | tf_op jit(solution)/shard_map/ppermute | solution.py:21
  152.9 23.7 %all-to-all-start.4 = ((bf16[4,49,2560]{2,1,0:T(8,128)(2,1)}), bf16[4,49,2560]{2,1,0:T(8,128)(2,1)}, u32[]{:S(2)}, u32[]{:S(2)}) async-start(bf16[4,49,2560]{2,1,0:T(8,128)(2,1)} %broadcast_in_dim.96), calls=%async_computation.4 | async-start | bytes 2293760 | tf_op jit(solution)/shard_map/all_to_all | solution.py:115
  157.2 25.9 %copy-start.1 = (bf16[1,2,64,2560]{3,2,1,0:T(8,128)(2,1)S(1)}, bf16[1,2,64,2560]{3,2,1,0:T(8,128)(2,1)}, u32[]{:S(2)}) copy-start(bf16[1,2,64,2560]{3,2,1,0:T(8,128)(2,1)} %param.14) | copy-start | bytes 1966084
  157.2 25.9 %copy-start.2 = (f32[64,2560]{1,0:T(8,128)S(1)}, f32[64,2560]{1,0:T(8,128)}, u32[]{:S(2)}) copy-start(f32[64,2560]{1,0:T(8,128)} %gather_fusion) | copy-start | bytes 1966084
  157.2 17.2 %collective-permute-start.3 = (bf16[49,2560]{1,0:T(8,128)(2,1)}, bf16[49,2560]{1,0:T(8,128)(2,1)}, u32[]{:S(2)}, u32[]{:S(2)}) collective-permute-start(bf16[49,2560]{1,0:T(8,128)(2,1)} %get-tuple-element.49), channel_id=1, source_target_pairs={{0,8},{8,0},{1,9},{9,1},{2,10},{10,2},{3,11},{11,3},{4,12},{12,4},... | collective-permute-start | bytes 752648 | tf_op jit(solution)/shard_map/ppermute | solution.py:21
  157.3 27.1 %copy-start.30 = (f32[64]{0:T(128)}, f32[64]{0:T(128)S(1)}, u32[]{:S(2)}) copy-start(f32[64]{0:T(128)S(1)} %broadcast_multiply_fusion.1) | copy-start | bytes 772
  178.6 20.4 %all-to-all-start.7 = ((bf16[4,49,2560]{2,1,0:T(8,128)(2,1)}), bf16[4,49,2560]{2,1,0:T(8,128)(2,1)}, u32[]{:S(2)}, u32[]{:S(2)}) async-start(bf16[4,49,2560]{2,1,0:T(8,128)(2,1)} %broadcast_in_dim.98), calls=%async_computation.7 | async-start | bytes 2293760 | tf_op jit(solution)/shard_map/all_to_all | solution.py:115
  184.4 10.7 %collective-permute-start.2 = (bf16[64,2560]{1,0:T(8,128)(2,1)S(1)}, bf16[64,2560]{1,0:T(8,128)(2,1)S(1)}, u32[]{:S(2)}, u32[]{:S(2)}) collective-permute-start(bf16[64,2560]{1,0:T(8,128)(2,1)S(1)} %fusion.57), channel_id=1, source_target_pairs={{16,0},{17,1},{18,2},{19,3},{20,4},{21,5},{22,6},{23,7},{24,8},{25... | collective-permute-start | bytes 983048 | tf_op jit(solution)/shard_map/ppermute | solution.py:15
  200.0 22.1 %all-to-all-start.5 = ((bf16[4,48,2560]{2,1,0:T(8,128)(2,1)}), bf16[4,48,2560]{2,1,0:T(8,128)(2,1)}, u32[]{:S(2)}, u32[]{:S(2)}) async-start(bf16[4,48,2560]{2,1,0:T(8,128)(2,1)} %broadcast_in_dim.97), calls=%async_computation.5 | async-start | bytes 1966080 | tf_op jit(solution)/shard_map/all_to_all | solution.py:115
  204.3 15.5 %collective-permute-start.4 = (bf16[48,2560]{1,0:T(8,128)(2,1)}, bf16[48,2560]{1,0:T(8,128)(2,1)S(1)}, u32[]{:S(2)}, u32[]{:S(2)}) collective-permute-start(bf16[48,2560]{1,0:T(8,128)(2,1)} %get-tuple-element.51), channel_id=1, source_target_pairs={{0,8},{8,0},{1,9},{9,1},{2,10},{10,2},{3,11},{11,3},{4,12},{12,4},... | collective-permute-start | bytes 737288 | tf_op jit(solution)/shard_map/ppermute | solution.py:21
  223.2 16.9 %all-to-all-start.8 = ((bf16[4,48,2560]{2,1,0:T(8,128)(2,1)}), bf16[4,48,2560]{2,1,0:T(8,128)(2,1)}, u32[]{:S(2)}, u32[]{:S(2)}) async-start(bf16[4,48,2560]{2,1,0:T(8,128)(2,1)} %broadcast_in_dim.99), calls=%async_computation.8 | async-start | bytes 1966080 | tf_op jit(solution)/shard_map/all_to_all | solution.py:115
  227.4 80.4 %reduce-scatter.3.cloned.1.call-start = ((), (), s32[]{:S(2)}) async-start(), calls=%async_computation.12 | async-start | bytes 2949120 | tf_op jit(solution)/shard_map/reduce_scatter | solution.py:226
  251.0 19.2 %all-to-all-start.6 = ((bf16[4,49,2560]{2,1,0:T(8,128)(2,1)}), bf16[4,49,2560]{2,1,0:T(8,128)(2,1)}, u32[]{:S(2)}, u32[]{:S(2)}) async-start(bf16[4,49,2560]{2,1,0:T(8,128)(2,1)} %fusion.28), calls=%async_computation.6 | async-start | bytes 2293760 | tf_op jit(solution)/shard_map/all_to_all | solution.py:142
  257.3 16.4 %copy-start.34 = (s32[64]{0:T(128)S(1)}, s32[64]{0:T(128)}, u32[]{:S(2)}) copy-start(s32[64]{0:T(128)} %get-tuple-element.28) | copy-start | bytes 772
  257.3 16.4 %copy-start.5 = (bf16[1,64,2560]{2,1,0:T(8,128)(2,1)S(1)}, bf16[1,64,2560]{2,1,0:T(8,128)(2,1)}, u32[]{:S(2)}) copy-start(bf16[1,64,2560]{2,1,0:T(8,128)(2,1)} %copy-done.4) | copy-start | bytes 983044
  257.3 16.4 %copy-start.31 = (f32[64]{0:T(128)S(1)}, f32[64]{0:T(128)}, u32[]{:S(2)}) copy-start(f32[64]{0:T(128)} %copy-done.30) | copy-start | bytes 772
  270.1 17.6 %all-to-all-start.9 = ((bf16[4,49,2560]{2,1,0:T(8,128)(2,1)}), bf16[4,49,2560]{2,1,0:T(8,128)(2,1)S(1)}, u32[]{:S(2)}, u32[]{:S(2)}) async-start(bf16[4,49,2560]{2,1,0:T(8,128)(2,1)} %fusion.29), calls=%async_computation.9 | async-start | bytes 2293760 | tf_op jit(solution)/shard_map/all_to_all | solution.py:142
  273.7 36.3 %reduce-scatter.5.cloned.1.call-start = ((), (), s32[]{:S(2)}) async-start(), calls=%async_computation.13 | async-start | bytes 1474560 | tf_op jit(solution)/shard_map/reduce_scatter | solution.py:229
  288.1 14.7 %collective-permute-start.5 = (bf16[50,2560]{1,0:T(8,128)(2,1)S(1)}, bf16[50,2560]{1,0:T(8,128)(2,1)S(1)}, u32[]{:S(2)}, u32[]{:S(2)}) collective-permute-start(bf16[50,2560]{1,0:T(8,128)(2,1)S(1)} %pad_maximum_fusion.4), channel_id=1, source_target_pairs={{0,8},{8,0},{1,9},{9,1},{2,10},{10,2},{3,11},{11,3},{4,12},{12,4},... | collective-permute-start | bytes 768008 | tf_op jit(solution)/shard_map/ppermute | solution.py:21
  (48 other events, 202.2 us)
Sparse Core Ops, SparseCore 0:
  247.1 7.5 reduce-scatter.2
  278.4 7.9 reduce-scatter.4

commit v6 on v2

--- a/solution.py
+++ b/solution.py
@@ -65,18 +65,45 @@
     return jnp.stack(moved)
 
 
+def relayed(block):
+    width = block.shape[-1]
+    return lax.axis_size("ej") == 4 and width >= 256 and width % 256 == 0
+
+
 def gather_quad(blocks):
     staged = to_experts(blocks)
     quad = lax.axis_size("ej")
-    return jnp.stack([staged] + [flipped(staged, "ej", t) for t in range(1, quad)])
+    if not relayed(staged):
+        return jnp.stack([staged] + [flipped(staged, "ej", t) for t in range(1, quad)])
+    half = staged.shape[-1] // 2
+    first = flipped(staged, "ej", 1)
+    second = flipped(staged, "ej", 2)
+    diagonal = jnp.concatenate(
+        [flipped(first[..., :half], "ej", 2), flipped(second[..., half:], "ej", 1)], axis=-1
+    )
+    return jnp.stack([staged, first, second, diagonal])
 
 
 def reduce_quad(parts):
     quad = parts.shape[0]
     total = parts[0].astype(jnp.float32)
-    for t in range(1, quad):
-        total = total + flipped(parts[t], "ej", t).astype(jnp.float32)
-    return total
+    if not relayed(parts):
+        for t in range(1, quad):
+            total = total + flipped(parts[t], "ej", t).astype(jnp.float32)
+        return total
+    half = parts.shape[-1] // 2
+    from_first = flipped(parts[3][..., :half], "ej", 1).astype(jnp.float32)
+    from_second = flipped(parts[3][..., half:], "ej", 2).astype(jnp.float32)
+    toward_second = jnp.concatenate(
+        [(parts[2][..., :half].astype(jnp.float32) + from_first).astype(parts.dtype), parts[2][..., half:]],
+        axis=-1,
+    )
+    toward_first = jnp.concatenate(
+        [parts[1][..., :half], (parts[1][..., half:].astype(jnp.float32) + from_second).astype(parts.dtype)],
+        axis=-1,
+    )
+    total = total + flipped(toward_second, "ej", 2).astype(jnp.float32)
+    return total + flipped(toward_first, "ej", 1).astype(jnp.float32)
 
 
 def local(
@@ -101,10 +128,22 @@
     pick_count = expert_ids.shape[3]
     capacity = max(2, 3 * token_rows * pick_count // (2 * groups))
     slot_count = groups * capacity
+    low_half = lax.axis_index("dp") == 0
+
+    def whole_rows(stored):
+        if lax.axis_size("dp") != 2:
+            return lax.all_gather(stored, "dp", axis=1, tiled=True)
+        partner = flipped(stored, "dp", 1)
+        return jnp.where(
+            low_half,
+            jnp.concatenate([stored, partner], axis=1),
+            jnp.concatenate([partner, stored], axis=1),
+        )
+
     gate_full, up_full, down_full = (
-        lax.all_gather(gate_weight[0], "dp", axis=1, tiled=True),
-        lax.all_gather(up_weight[0], "dp", axis=1, tiled=True),
-        lax.all_gather(down_weight[0], "dp", axis=1, tiled=True),
+        whole_rows(gate_weight[0]),
+        whole_rows(up_weight[0]),
+        whole_rows(down_weight[0]),
     )
     hidden_count = gate_full.shape[0]
     paired_weights = jnp.concatenate([gate_full, up_full], axis=0)

time: 273 us -> 239 us (0.88); the launches traced: 269 us -> 239 us
  waiting for transfers between devices: 141 us -> 106 us
  starting transfers between devices: 49.7 us -> 64.1 us
  blocking collectives: 7.63 us -> 0 us
    ppermute x30 -> x39, waiting for transfers between devices: 85.5 us -> 66.6 us  [flipped(): return lax.ppermute(block, axis, route)]
    ppermute x10, waiting for transfers between devices: 48.7 us -> 39.6 us  [rotated(): return lax.ppermute(block, axis, route)]
    ppermute x30 -> x39, starting transfers between devices: 34.9 us -> 43.7 us  [flipped(): return lax.ppermute(block, axis, route)]
    all_gather x3 -> x0, blocking collectives: 7.63 us -> none  [the longest x1 2.63 us: local(): lax.all_gather(down_weight[0], 'dp', axis=1, tiled=True)]
    ppermute x1, waiting for transfers between devices: 6.93 us -> 0.01 us  [shifted(): return lax.ppermute(block, axis, route)]
    another operation x10 -> x2, other arithmetic: 6.58 us -> 0.02 us  [gather_quad(): jnp.stack([staged] + [flipped(staged, 'ej', t) for t in range(1, quad)])]
    ppermute x10, starting transfers between devices: 13.3 us -> 18.8 us  [rotated(): return lax.ppermute(block, axis, route)]
    another operation x0 -> x12, other arithmetic: none -> 5.08 us  [gather_quad(): return jnp.stack([staged, first, second, diagonal])]
  transfers between devices with their start and end apart: 43 -> 52, of which waited for: 19 -> 26; matrix products, arithmetic and copies ran while one was open for 14% -> 17% of each run, Pallas kernels for 0% -> 0%
where the time goes in v6:
time: 239 us
  waiting for transfers between devices  106 us (44%)
  starting transfers between devices  64.1 us (27%)
  other arithmetic  23.2 us (10%)
  matrix products  16.1 us (7%)
  between operations  15 us (6%)
  local copies, waits for them, and re-layouts  14.2 us (6%)
    ppermute x39, waiting for transfers between devices, flipped(): return lax.ppermute(block, axis, route)  66.6 us
    ppermute x39, starting transfers between devices, flipped(): return lax.ppermute(block, axis, route)  43.7 us
    ppermute x10, waiting for transfers between devices, rotated(): return lax.ppermute(block, axis, route)  39.6 us
    ppermute x10, starting transfers between devices, rotated(): return lax.ppermute(block, axis, route)  18.8 us
    dot_general x6, matrix products, contract_last(): lax.dot_general(first_operand, second_operand, (((1,), (1,)), ((), ())),...  6.3 us
    another operation x12, other arithmetic, gather_quad(): return jnp.stack([staged, first, second, diagonal])  5.08 us
    dot_general x2, matrix products, contract_first(): lax.dot_general(first_operand, second_operand, (((0,), (0,)), ((), ())),...  4.91 us
  transfers between devices with their start and end apart: 52, of which 26 were waited for; matrix products, arithmetic and copies ran while one was open for 17% of the time, Pallas kernels for 0%

profile of v6, /device:TPU:0, one launch (start us, length us, event | category | flops | bytes accessed | tf_op | source)
XLA Modules:
  0.0 238.8 jit_solution(14268718052787654372)
XLA Ops:
  10.3 4.0 %collective-permute-start = (bf16[48]{0:T(256)(128)(2,1)S(1)}, bf16[48]{0:T(256)(128)(2,1)S(1)}, u32[]{:S(2)}, u32[]{:S(2)}) collective-permute-start(bf16[48]{0:T(256)(128)(2,1)S(1)} %get-tuple-element.95), channel_id=1, source_target_pairs={{0,8},{8,0},{1,9},{9,1},{2,10},{10,2},{3,11},{11,3},{4,12},{12,4},... | collective-permute-start | bytes 296 | tf_op jit(solution)/shard_map/ppermute | solution.py:21
  18.0 2.9 %collective-permute-start.10 = (bf16[48,2560]{1,0:T(8,128)(2,1)}, bf16[48,2560]{1,0:T(8,128)(2,1)}, u32[]{:S(2)}, u32[]{:S(2)}) collective-permute-start(bf16[48,2560]{1,0:T(8,128)(2,1)} %get-tuple-element.65), channel_id=1, source_target_pairs={{0,8},{8,0},{1,9},{9,1},{2,10},{10,2},{3,11},{11,3},{4,12},{12,4},... | collective-permute-start | bytes 737288 | tf_op jit(solution)/shard_map/ppermute | solution.py:21
  24.1 3.4 %collective-permute-done.2 = bf16[2,48]{1,0:T(2,128)(2,1)S(1)} collective-permute-done((bf16[2,48]{1,0:T(2,128)(2,1)S(1)}, bf16[2,48]{1,0:T(2,128)(2,1)S(1)}, u32[]{:S(2)}, u32[]{:S(2)}) %collective-permute-start.2) | collective-permute-done | bytes 224 | tf_op jit(solution)/shard_map/ppermute | solution.py:27
  27.5 3.3 %collective-permute-start.3 = (bf16[2,48]{1,0:T(2,128)(2,1)S(1)}, bf16[2,48]{1,0:T(2,128)(2,1)S(1)}, u32[]{:S(2)}, u32[]{:S(2)}) collective-permute-start(bf16[2,48]{1,0:T(2,128)(2,1)S(1)} %pad_maximum_fusion.19), channel_id=1, source_target_pairs={{0,6},{2,4},{4,2},{6,0},{1,7},{3,5},{5,3},{7,1},{8,14},{10,12},{12... | collective-permute-start | bytes 584 | tf_op jit(solution)/shard_map/ppermute | solution.py:27
  32.4 8.6 %collective-permute-done.10 = bf16[48,2560]{1,0:T(8,128)(2,1)} collective-permute-done((bf16[48,2560]{1,0:T(8,128)(2,1)}, bf16[48,2560]{1,0:T(8,128)(2,1)}, u32[]{:S(2)}, u32[]{:S(2)}) %collective-permute-start.10) | collective-permute-done | bytes 245792 | tf_op jit(solution)/shard_map/ppermute | solution.py:21
  46.6 9.7 %collective-permute-done.11 = bf16[2,48,2560]{2,1,0:T(8,128)(2,1)S(1)} collective-permute-done((bf16[2,48,2560]{2,1,0:T(8,128)(2,1)S(1)}, bf16[2,48,2560]{2,1,0:T(8,128)(2,1)S(1)}, u32[]{:S(2)}, u32[]{:S(2)}) %collective-permute-start.11) | collective-permute-done | bytes 491552 | tf_op jit(solution)/shard_map/ppermute | solution.py:27
  59.9 6.9 %collective-permute-done.5 = bf16[2,48,2560]{2,1,0:T(8,128)(2,1)S(1)} collective-permute-done((bf16[2,48,2560]{2,1,0:T(8,128)(2,1)S(1)}, bf16[2,48,2560]{2,1,0:T(8,128)(2,1)S(1)}, u32[]{:S(2)}, u32[]{:S(2)}) %collective-permute-start.5) | collective-permute-done | bytes 491552 | tf_op jit(solution)/shard_map/ppermute | solution.py:27
  69.0 4.6 %collective-permute-done.13 = bf16[2,48,1280]{2,1,0:T(8,128)(2,1)S(1)} collective-permute-done((bf16[2,48,1280]{2,1,0:T(8,128)(2,1)S(1)}, bf16[2,48,1280]{2,1,0:T(8,128)(2,1)S(1)}, u32[]{:S(2)}, u32[]{:S(2)}) %collective-permute-start.13) | collective-permute-done | bytes 245792 | tf_op jit(solution)/shard_map/ppermute | solution.py:27
  81.1 2.6 %collective-permute-start.23 = (bf16[48]{0:T(256)(128)(2,1)S(1)}, bf16[48]{0:T(256)(128)(2,1)S(1)}, u32[]{:S(2)}, u32[]{:S(2)}) collective-permute-start(bf16[48]{0:T(256)(128)(2,1)S(1)} %get-tuple-element.91), channel_id=1, source_target_pairs={{0,8},{8,0},{1,9},{9,1},{2,10},{10,2},{3,11},{11,3},{4,12},{12,4},... | collective-permute-start | bytes 296 | tf_op jit(solution)/shard_map/ppermute | solution.py:21
  89.1 6.0 %collective-permute-done.17 = bf16[2,48,1280]{2,1,0:T(8,128)(2,1)S(1)} collective-permute-done((bf16[2,48,1280]{2,1,0:T(8,128)(2,1)S(1)}, bf16[2,48,1280]{2,1,0:T(8,128)(2,1)S(1)}, u32[]{:S(2)}, u32[]{:S(2)}) %collective-permute-start.17) | collective-permute-done | bytes 245792 | tf_op jit(solution)/shard_map/ppermute | solution.py:27
  96.0 3.3 %collective-permute-start.18 = (bf16[2,48,2560]{2,1,0:T(8,128)(2,1)}, bf16[2,48,2560]{2,1,0:T(8,128)(2,1)S(1)}, u32[]{:S(2)}, u32[]{:S(2)}) collective-permute-start(bf16[2,48,2560]{2,1,0:T(8,128)(2,1)} %pad_maximum_fusion.11), channel_id=1, source_target_pairs={{0,4},{2,6},{4,0},{6,2},{1,5},{3,7},{5,1},{7,3},{8,12},{10,14},{12... | collective-permute-start | bytes 1474568 | tf_op jit(solution)/shard_map/ppermute | solution.py:27
  103.2 3.1 %collective-permute-done.44 = bf16[2,48]{1,0:T(2,128)(2,1)S(1)} collective-permute-done((bf16[2,48]{1,0:T(2,128)(2,1)S(1)}, bf16[2,48]{1,0:T(2,128)(2,1)S(1)}, u32[]{:S(2)}, u32[]{:S(2)}) %collective-permute-start.44) | collective-permute-done | bytes 224 | tf_op jit(solution)/shard_map/ppermute | solution.py:27
  110.7 3.0 %collective-permute-start.21 = (bf16[48,2560]{1,0:T(8,128)(2,1)S(1)}, bf16[48,2560]{1,0:T(8,128)(2,1)S(1)}, u32[]{:S(2)}, u32[]{:S(2)}) collective-permute-start(bf16[48,2560]{1,0:T(8,128)(2,1)S(1)} %fusion.67), channel_id=1, source_target_pairs={{0,8},{8,0},{1,9},{9,1},{2,10},{10,2},{3,11},{11,3},{4,12},{12,4},... | collective-permute-start | bytes 737288 | tf_op jit(solution)/shard_map/ppermute | solution.py:21
  115.1 9.8 %collective-permute-done.21 = bf16[48,2560]{1,0:T(8,128)(2,1)S(1)} collective-permute-done((bf16[48,2560]{1,0:T(8,128)(2,1)S(1)}, bf16[48,2560]{1,0:T(8,128)(2,1)S(1)}, u32[]{:S(2)}, u32[]{:S(2)}) %collective-permute-start.21) | collective-permute-done | bytes 245792 | tf_op jit(solution)/shard_map/ppermute | solution.py:21
  129.2 9.4 %collective-permute-done.32 = bf16[48,2560]{1,0:T(8,128)(2,1)S(1)} collective-permute-done((bf16[48,2560]{1,0:T(8,128)(2,1)S(1)}, bf16[48,2560]{1,0:T(8,128)(2,1)S(1)}, u32[]{:S(2)}, u32[]{:S(2)}) %collective-permute-start.32) | collective-permute-done | bytes 245792 | tf_op jit(solution)/shard_map/ppermute | solution.py:21
  139.4 4.5 %collective-permute-start.33 = (bf16[2,48,2560]{2,1,0:T(8,128)(2,1)}, bf16[2,48,2560]{2,1,0:T(8,128)(2,1)S(1)}, u32[]{:S(2)}, u32[]{:S(2)}) collective-permute-start(bf16[2,48,2560]{2,1,0:T(8,128)(2,1)} %get-tuple-element.53), channel_id=1, source_target_pairs={{0,2},{2,0},{4,6},{6,4},{1,3},{3,1},{5,7},{7,5},{8,10},{10,8},{12,... | collective-permute-start | bytes 1474568 | tf_op jit(solution)/shard_map/ppermute | solution.py:27
  148.8 7.4 %collective-permute-done.24 = bf16[2,48]{1,0:T(2,128)(2,1)S(1)} collective-permute-done((bf16[2,48]{1,0:T(2,128)(2,1)}, bf16[2,48]{1,0:T(2,128)(2,1)S(1)}, u32[]{:S(2)}, u32[]{:S(2)}) %collective-permute-start.24) | collective-permute-done | bytes 224 | tf_op jit(solution)/shard_map/ppermute | solution.py:27
  156.2 4.2 %collective-permute-done.26 = bf16[2,48]{1,0:T(2,128)(2,1)S(1)} collective-permute-done((bf16[2,48]{1,0:T(2,128)(2,1)}, bf16[2,48]{1,0:T(2,128)(2,1)S(1)}, u32[]{:S(2)}, u32[]{:S(2)}) %collective-permute-start.26) | collective-permute-done | bytes 224 | tf_op jit(solution)/shard_map/ppermute | solution.py:27
  172.5 3.1 %collective-permute-done.28 = bf16[2,48,2560]{2,1,0:T(8,128)(2,1)S(1)} collective-permute-done((bf16[2,48,2560]{2,1,0:T(8,128)(2,1)S(1)}, bf16[2,48,2560]{2,1,0:T(8,128)(2,1)S(1)}, u32[]{:S(2)}, u32[]{:S(2)}) %collective-permute-start.28) | collective-permute-done | bytes 491552 | tf_op jit(solution)/shard_map/ppermute | solution.py:27
  178.7 5.6 %collective-permute-done.30 = bf16[2,48,1280]{2,1,0:T(8,128)(2,1)S(1)} collective-permute-done((bf16[2,48,1280]{2,1,0:T(8,128)(2,1)S(1)}, bf16[2,48,1280]{2,1,0:T(8,128)(2,1)S(1)}, u32[]{:S(2)}, u32[]{:S(2)}) %collective-permute-start.30) | collective-permute-done | bytes 245792 | tf_op jit(solution)/shard_map/ppermute | solution.py:27
  187.1 3.0 %convolution_convert_fusion = bf16[384,2560]{1,0:T(8,128)(2,1)} fusion(bf16[384,2560]{1,0:T(8,128)(2,1)S(1)} %bitcast.226, bf16[384,2560]{1,0:T(8,128)(2,1)S(1)} %bitcast.220, bf16[384,192]{0,1:T(8,128)(2,1)S(1)} %get-tuple-element.49, bf16[384,192]{0,1:T(8,128)(2,1)S(1)} %get-tuple-element.43, bf16[384,192]{0,1:T(8,128)(2,1)S(1)} %copy-done.22, ...), kind=kOutput, calls=%fused_computation.4 | convolution fusion | flops 1521156096 | bytes 6488064 | tf_op jit(solution)/shard_map/dot_general | solution.py:42
  211.3 3.7 %collective-permute-done.49 = f32[48]{0:T(128)S(1)} collective-permute-done((f32[48]{0:T(128)S(1)}, f32[48]{0:T(128)S(1)}, u32[]{:S(2)}, u32[]{:S(2)}) %collective-permute-start.49) | collective-permute-done | bytes 224 | tf_op jit(solution)/shard_map/ppermute | solution.py:21
  216.4 3.0 %collective-permute-start.41 = (bf16[48,2560]{1,0:T(8,128)(2,1)S(1)}, bf16[48,2560]{1,0:T(8,128)(2,1)S(1)}, u32[]{:S(2)}, u32[]{:S(2)}) collective-permute-start(bf16[48,2560]{1,0:T(8,128)(2,1)S(1)} %fusion.68), channel_id=1, source_target_pairs={{0,8},{8,0},{1,9},{9,1},{2,10},{10,2},{3,11},{11,3},{4,12},{12,4},... | collective-permute-start | bytes 737288 | tf_op jit(solution)/shard_map/ppermute | solution.py:21
  220.0 6.2 %collective-permute-done.41 = bf16[48,2560]{1,0:T(8,128)(2,1)S(1)} collective-permute-done((bf16[48,2560]{1,0:T(8,128)(2,1)S(1)}, bf16[48,2560]{1,0:T(8,128)(2,1)S(1)}, u32[]{:S(2)}, u32[]{:S(2)}) %collective-permute-start.41) | collective-permute-done | bytes 245792 | tf_op jit(solution)/shard_map/ppermute | solution.py:21
  (301 shorter events, 102.5 us)
Async XLA Ops:
  7.2 222.6 %reduce-scatter.3.cloned.1.call-start = ((), (), s32[]{:S(2)}) async-start(), calls=%async_computation.2 | async-start | bytes 2949120 | tf_op jit(solution)/shard_map/reduce_scatter | solution.py:255
  16.6 27.0 %collective-permute-start.4 = (bf16[48,2560]{1,0:T(8,128)(2,1)}, bf16[48,2560]{1,0:T(8,128)(2,1)S(1)}, u32[]{:S(2)}, u32[]{:S(2)}) collective-permute-start(bf16[48,2560]{1,0:T(8,128)(2,1)} %get-tuple-element.69), channel_id=1, source_target_pairs={{0,8},{8,0},{1,9},{9,1},{2,10},{10,2},{3,11},{11,3},{4,12},{12,4},... | collective-permute-start | bytes 737288 | tf_op jit(solution)/shard_map/ppermute | solution.py:21
  18.0 23.0 %collective-permute-start.10 = (bf16[48,2560]{1,0:T(8,128)(2,1)}, bf16[48,2560]{1,0:T(8,128)(2,1)}, u32[]{:S(2)}, u32[]{:S(2)}) collective-permute-start(bf16[48,2560]{1,0:T(8,128)(2,1)} %get-tuple-element.65), channel_id=1, source_target_pairs={{0,8},{8,0},{1,9},{9,1},{2,10},{10,2},{3,11},{11,3},{4,12},{12,4},... | collective-permute-start | bytes 737288 | tf_op jit(solution)/shard_map/ppermute | solution.py:21
  20.9 23.4 %collective-permute-start.16 = (bf16[192,1280]{1,0:T(8,128)(2,1)S(1)}, bf16[192,1280]{1,0:T(8,128)(2,1)S(1)}, u32[]{:S(2)}, u32[]{:S(2)}) collective-permute-start(bf16[192,1280]{1,0:T(8,128)(2,1)S(1)} %bitcast.244), channel_id=1, source_target_pairs={{0,1},{1,0},{2,3},{3,2},{4,5},{5,4},{6,7},{7,6},{8,9},{9,8},{10,11... | collective-permute-start | bytes 1474568 | tf_op jit(solution)/shard_map/ppermute | solution.py:27
  30.8 27.0 %collective-permute-start.15 = (bf16[192,1280]{1,0:T(8,128)(2,1)S(1)}, bf16[192,1280]{1,0:T(8,128)(2,1)}, u32[]{:S(2)}, u32[]{:S(2)}) collective-permute-start(bf16[192,1280]{1,0:T(8,128)(2,1)S(1)} %bitcast.246), channel_id=1, source_target_pairs={{0,1},{1,0},{2,3},{3,2},{4,5},{5,4},{6,7},{7,6},{8,9},{9,8},{10,11... | collective-permute-start | bytes 1474568 | tf_op jit(solution)/shard_map/ppermute | solution.py:27
  42.1 14.2 %collective-permute-start.11 = (bf16[2,48,2560]{2,1,0:T(8,128)(2,1)S(1)}, bf16[2,48,2560]{2,1,0:T(8,128)(2,1)S(1)}, u32[]{:S(2)}, u32[]{:S(2)}) collective-permute-start(bf16[2,48,2560]{2,1,0:T(8,128)(2,1)S(1)} %get-tuple-element.63), channel_id=1, source_target_pairs={{0,2},{2,0},{4,6},{6,4},{1,3},{3,1},{5,7},{7,5},{8,10},{10,8},{12,... | collective-permute-start | bytes 1474568 | tf_op jit(solution)/shard_map/ppermute | solution.py:27
  43.7 14.2 %collective-permute-start.12 = (bf16[2,48,2560]{2,1,0:T(8,128)(2,1)S(1)}, bf16[2,48,2560]{2,1,0:T(8,128)(2,1)S(1)}, u32[]{:S(2)}, u32[]{:S(2)}) collective-permute-start(bf16[2,48,2560]{2,1,0:T(8,128)(2,1)S(1)} %get-tuple-element.63), channel_id=1, source_target_pairs={{0,4},{2,6},{4,0},{6,2},{1,5},{3,7},{5,1},{7,3},{8,12},{10,14},{12... | collective-permute-start | bytes 1474568 | tf_op jit(solution)/shard_map/ppermute | solution.py:27
  43.7 23.1 %collective-permute-start.5 = (bf16[2,48,2560]{2,1,0:T(8,128)(2,1)S(1)}, bf16[2,48,2560]{2,1,0:T(8,128)(2,1)S(1)}, u32[]{:S(2)}, u32[]{:S(2)}) collective-permute-start(bf16[2,48,2560]{2,1,0:T(8,128)(2,1)S(1)} %get-tuple-element.67), channel_id=1, source_target_pairs={{0,2},{2,0},{4,6},{6,4},{1,3},{3,1},{5,7},{7,5},{8,10},{10,8},{12,... | collective-permute-start | bytes 1474568 | tf_op jit(solution)/shard_map/ppermute | solution.py:27
  44.3 24.0 %collective-permute-start.6 = (bf16[2,48,2560]{2,1,0:T(8,128)(2,1)S(1)}, bf16[2,48,2560]{2,1,0:T(8,128)(2,1)S(1)}, u32[]{:S(2)}, u32[]{:S(2)}) collective-permute-start(bf16[2,48,2560]{2,1,0:T(8,128)(2,1)S(1)} %get-tuple-element.67), channel_id=1, source_target_pairs={{0,4},{2,6},{4,0},{6,2},{1,5},{3,7},{5,1},{7,3},{8,12},{10,14},{12... | collective-permute-start | bytes 1474568 | tf_op jit(solution)/shard_map/ppermute | solution.py:27
  56.3 21.3 %collective-permute-start.9 = (bf16[192,1280]{1,0:T(8,128)(2,1)S(1)}, bf16[192,1280]{1,0:T(8,128)(2,1)S(1)}, u32[]{:S(2)}, u32[]{:S(2)}) collective-permute-start(bf16[192,1280]{1,0:T(8,128)(2,1)S(1)} %bitcast.260), channel_id=1, source_target_pairs={{0,1},{1,0},{2,3},{3,2},{4,5},{5,4},{6,7},{7,6},{8,9},{9,8},{10,11... | collective-permute-start | bytes 1474568 | tf_op jit(solution)/shard_map/ppermute | solution.py:27
  57.8 15.8 %collective-permute-start.13 = (bf16[2,48,1280]{2,1,0:T(8,128)(2,1)S(1)}, bf16[2,48,1280]{2,1,0:T(8,128)(2,1)S(1)}, u32[]{:S(2)}, u32[]{:S(2)}) collective-permute-start(bf16[2,48,1280]{2,1,0:T(8,128)(2,1)S(1)} %slice.376), channel_id=1, source_target_pairs={{0,4},{2,6},{4,0},{6,2},{1,5},{3,7},{5,1},{7,3},{8,12},{10,14},{12... | collective-permute-start | bytes 737288 | tf_op jit(solution)/shard_map/ppermute | solution.py:27
  57.8 15.8 %collective-permute-start.14 = (bf16[2,48,1280]{2,1,0:T(8,128)(2,1)S(1)}, bf16[2,48,1280]{2,1,0:T(8,128)(2,1)S(1)}, u32[]{:S(2)}, u32[]{:S(2)}) collective-permute-start(bf16[2,48,1280]{2,1,0:T(8,128)(2,1)S(1)} %slice.377), channel_id=1, source_target_pairs={{0,2},{2,0},{4,6},{6,4},{1,3},{3,1},{5,7},{7,5},{8,10},{10,8},{12,... | collective-permute-start | bytes 737288 | tf_op jit(solution)/shard_map/ppermute | solution.py:27
  87.8 20.6 %collective-permute-start.20 = (bf16[2,48,2560]{2,1,0:T(8,128)(2,1)}, bf16[2,48,2560]{2,1,0:T(8,128)(2,1)S(1)}, u32[]{:S(2)}, u32[]{:S(2)}) collective-permute-start(bf16[2,48,2560]{2,1,0:T(8,128)(2,1)} %pad_maximum_fusion.12), channel_id=1, source_target_pairs={{0,2},{2,0},{4,6},{6,4},{1,3},{3,1},{5,7},{7,5},{8,10},{10,8},{12,... | collective-permute-start | bytes 1474568 | tf_op jit(solution)/shard_map/ppermute | solution.py:27
  96.0 12.4 %collective-permute-start.18 = (bf16[2,48,2560]{2,1,0:T(8,128)(2,1)}, bf16[2,48,2560]{2,1,0:T(8,128)(2,1)S(1)}, u32[]{:S(2)}, u32[]{:S(2)}) collective-permute-start(bf16[2,48,2560]{2,1,0:T(8,128)(2,1)} %pad_maximum_fusion.11), channel_id=1, source_target_pairs={{0,4},{2,6},{4,0},{6,2},{1,5},{3,7},{5,1},{7,3},{8,12},{10,14},{12... | collective-permute-start | bytes 1474568 | tf_op jit(solution)/shard_map/ppermute | solution.py:27
  106.2 41.2 %collective-permute-start.25 = (bf16[2,48]{1,0:T(2,128)(2,1)}, bf16[2,48]{1,0:T(2,128)(2,1)}, u32[]{:S(2)}, u32[]{:S(2)}) collective-permute-start(bf16[2,48]{1,0:T(2,128)(2,1)} %pad_maximum_fusion.20), channel_id=1, source_target_pairs={{0,4},{2,6},{4,0},{6,2},{1,5},{3,7},{5,1},{7,3},{8,12},{10,14},{12... | collective-permute-start | bytes 584 | tf_op jit(solution)/shard_map/ppermute | solution.py:27
  110.7 14.2 %collective-permute-start.21 = (bf16[48,2560]{1,0:T(8,128)(2,1)S(1)}, bf16[48,2560]{1,0:T(8,128)(2,1)S(1)}, u32[]{:S(2)}, u32[]{:S(2)}) collective-permute-start(bf16[48,2560]{1,0:T(8,128)(2,1)S(1)} %fusion.67), channel_id=1, source_target_pairs={{0,8},{8,0},{1,9},{9,1},{2,10},{10,2},{3,11},{11,3},{4,12},{12,4},... | collective-permute-start | bytes 737288 | tf_op jit(solution)/shard_map/ppermute | solution.py:21
  127.2 11.4 %collective-permute-start.32 = (bf16[48,2560]{1,0:T(8,128)(2,1)S(1)}, bf16[48,2560]{1,0:T(8,128)(2,1)S(1)}, u32[]{:S(2)}, u32[]{:S(2)}) collective-permute-start(bf16[48,2560]{1,0:T(8,128)(2,1)S(1)} %get-tuple-element.55), channel_id=1, source_target_pairs={{0,8},{8,0},{1,9},{9,1},{2,10},{10,2},{3,11},{11,3},{4,12},{12,4},... | collective-permute-start | bytes 737288 | tf_op jit(solution)/shard_map/ppermute | solution.py:21
  127.7 16.3 %collective-permute-start.22 = (bf16[64,2560]{1,0:T(8,128)(2,1)S(1)}, bf16[64,2560]{1,0:T(8,128)(2,1)S(1)}, u32[]{:S(2)}, u32[]{:S(2)}) collective-permute-start(bf16[64,2560]{1,0:T(8,128)(2,1)S(1)} %fusion.32), channel_id=1, source_target_pairs={{16,0},{17,1},{18,2},{19,3},{20,4},{21,5},{22,6},{23,7},{24,8},{25... | collective-permute-start | bytes 983048 | tf_op jit(solution)/shard_map/ppermute | solution.py:15
  139.4 22.2 %collective-permute-start.33 = (bf16[2,48,2560]{2,1,0:T(8,128)(2,1)}, bf16[2,48,2560]{2,1,0:T(8,128)(2,1)S(1)}, u32[]{:S(2)}, u32[]{:S(2)}) collective-permute-start(bf16[2,48,2560]{2,1,0:T(8,128)(2,1)} %get-tuple-element.53), channel_id=1, source_target_pairs={{0,2},{2,0},{4,6},{6,4},{1,3},{3,1},{5,7},{7,5},{8,10},{10,8},{12,... | collective-permute-start | bytes 1474568 | tf_op jit(solution)/shard_map/ppermute | solution.py:27
  144.0 19.2 %collective-permute-start.34 = (bf16[2,48,2560]{2,1,0:T(8,128)(2,1)}, bf16[2,48,2560]{2,1,0:T(8,128)(2,1)}, u32[]{:S(2)}, u32[]{:S(2)}) collective-permute-start(bf16[2,48,2560]{2,1,0:T(8,128)(2,1)} %get-tuple-element.53), channel_id=1, source_target_pairs={{0,4},{2,6},{4,0},{6,2},{1,5},{3,7},{5,1},{7,3},{8,12},{10,14},{12... | collective-permute-start | bytes 1474568 | tf_op jit(solution)/shard_map/ppermute | solution.py:27
  145.2 19.6 %collective-permute-start.27 = (bf16[48,2560]{1,0:T(8,128)(2,1)}, bf16[48,2560]{1,0:T(8,128)(2,1)}, u32[]{:S(2)}, u32[]{:S(2)}) collective-permute-start(bf16[48,2560]{1,0:T(8,128)(2,1)} %get-tuple-element.59), channel_id=1, source_target_pairs={{0,8},{8,0},{1,9},{9,1},{2,10},{10,2},{3,11},{11,3},{4,12},{12,4},... | collective-permute-start | bytes 737288 | tf_op jit(solution)/shard_map/ppermute | solution.py:21
  147.4 13.0 %collective-permute-start.26 = (bf16[2,48]{1,0:T(2,128)(2,1)}, bf16[2,48]{1,0:T(2,128)(2,1)S(1)}, u32[]{:S(2)}, u32[]{:S(2)}) collective-permute-start(bf16[2,48]{1,0:T(2,128)(2,1)} %pad_maximum_fusion.20), channel_id=1, source_target_pairs={{0,6},{2,4},{4,2},{6,0},{1,7},{3,5},{5,3},{7,1},{8,14},{10,12},{12... | collective-permute-start | bytes 584 | tf_op jit(solution)/shard_map/ppermute | solution.py:27
  190.1 41.9 %reduce-scatter.5.cloned.1.call-start = ((), (), s32[]{:S(2)}) async-start(), calls=%async_computation.3 | async-start | bytes 1474560 | tf_op jit(solution)/shard_map/reduce_scatter | solution.py:258
  204.2 11.6 %collective-permute-start.40 = (bf16[2,48,2560]{2,1,0:T(8,128)(2,1)S(1)}, bf16[2,48,2560]{2,1,0:T(8,128)(2,1)S(1)}, u32[]{:S(2)}, u32[]{:S(2)}) collective-permute-start(bf16[2,48,2560]{2,1,0:T(8,128)(2,1)S(1)} %pad_maximum_fusion.16), channel_id=1, source_target_pairs={{0,2},{2,0},{4,6},{6,4},{1,3},{3,1},{5,7},{7,5},{8,10},{10,8},{12,... | collective-permute-start | bytes 1474568 | tf_op jit(solution)/shard_map/ppermute | solution.py:27
  (74 other events, 644.7 us)
Sparse Core Ops, SparseCore 0:
  190.2 8.5 reduce-scatter.2
  211.4 7.9 reduce-scatter.4

commit v7 on v6

--- a/solution.py
+++ b/solution.py
@@ -47,21 +47,6 @@
 def to_experts(blocks):
     groups = blocks.shape[0]
     moved = [blocks[0]] + [rotated(blocks[s], "eg", s) for s in range(1, groups)]
-    return jnp.stack(moved)
-
-
-def to_owners(blocks):
-    groups = blocks.shape[0]
-    moved = [blocks[0]] + [
-        rotated(blocks[s].astype(jnp.bfloat16), "eg", -s).astype(jnp.float32)
-        for s in range(1, groups)
-    ]
-    return jnp.stack(moved)
-
-
-def weights_to_owners(blocks):
-    groups = blocks.shape[0]
-    moved = [blocks[0]] + [rotated(blocks[s], "eg", -s) for s in range(1, groups)]
     return jnp.stack(moved)
 
 
@@ -130,21 +115,17 @@
     slot_count = groups * capacity
     low_half = lax.axis_index("dp") == 0
 
-    def whole_rows(stored):
-        if lax.axis_size("dp") != 2:
-            return lax.all_gather(stored, "dp", axis=1, tiled=True)
+    stored = jnp.stack([gate_weight[0], up_weight[0], down_weight[0]])
+    if lax.axis_size("dp") == 2:
         partner = flipped(stored, "dp", 1)
-        return jnp.where(
+        whole = jnp.where(
             low_half,
-            jnp.concatenate([stored, partner], axis=1),
-            jnp.concatenate([partner, stored], axis=1),
-        )
-
-    gate_full, up_full, down_full = (
-        whole_rows(gate_weight[0]),
-        whole_rows(up_weight[0]),
-        whole_rows(down_weight[0]),
-    )
+            jnp.concatenate([stored, partner], axis=2),
+            jnp.concatenate([partner, stored], axis=2),
+        )
+    else:
+        whole = lax.all_gather(stored, "dp", axis=2, tiled=True)
+    gate_full, up_full, down_full = whole[0], whole[1], whole[2]
     hidden_count = gate_full.shape[0]
     paired_weights = jnp.concatenate([gate_full, up_full], axis=0)
     gain_row = norm_gain[0][None, :]
@@ -175,12 +156,46 @@
         picked = jnp.dot(selector, source_rows, preferred_element_type=jnp.float32)
         return picked.astype(jnp.bfloat16).reshape(groups, capacity, feature_count)
 
+    def padded_row(values):
+        shaped = values[..., None, :]
+        width = [(0, 0)] * (shaped.ndim - 1) + [(0, feature_count - capacity)]
+        return jnp.pad(shaped, width)
+
+    def send_back(part_rows, part_weight):
+        stacked = jnp.concatenate(
+            [
+                part_rows.reshape(-1, groups, capacity, feature_count),
+                padded_row(part_weight.reshape(-1, groups, capacity)),
+            ],
+            axis=2,
+        )
+        total = reduce_quad(stacked)
+        back_rows = [total[0, :capacity]]
+        back_weight = [total[0, capacity, :capacity]]
+        for s in range(1, groups):
+            high = total[s, capacity:].astype(jnp.bfloat16)
+            low = (total[s, capacity:] - high.astype(jnp.float32)).astype(jnp.bfloat16)
+            block = jnp.concatenate([total[s, :capacity].astype(jnp.bfloat16), high, low], axis=0)
+            got = rotated(block, "eg", -s).astype(jnp.float32)
+            back_rows.append(got[:capacity])
+            back_weight.append(got[capacity, :capacity] + got[capacity + 1, :capacity])
+        return (
+            jnp.stack(back_rows).reshape(slot_count, feature_count),
+            jnp.stack(back_weight).reshape(slot_count),
+        )
+
     prepared = [prepare(moment) for moment in range(micro_count)]
-    rows_gathered = [
-        gather_quad(dispatch_rows(current[4], current[2])) for current in prepared
-    ]
-    weights_gathered = [
-        gather_quad(current[6].reshape(groups, capacity)) for current in prepared
+    packed_gathered = [
+        gather_quad(
+            jnp.concatenate(
+                [
+                    dispatch_rows(current[4], current[2]),
+                    padded_row(current[6].reshape(groups, capacity)),
+                ],
+                axis=1,
+            )
+        )
+        for current in prepared
     ]
     leaving_list = []
     combine_list = []
@@ -194,9 +209,10 @@
             arriving = shifted(previous, "pipe", -1)
         incoming = jnp.where(is_last, output_grads[moment], arriving)
         grads_in = gather_quad(dispatch_rows(current[4], incoming))
-        flat_rows = rows_gathered[moment].reshape(-1, feature_count)
+        packed = packed_gathered[moment]
+        flat_rows = packed[:, :, :capacity].reshape(-1, feature_count)
         flat_grads = grads_in.reshape(-1, feature_count)
-        scale_column = weights_gathered[moment].reshape(-1, 1).astype(jnp.float32)
+        scale_column = packed[:, :, capacity, :capacity].reshape(-1, 1).astype(jnp.float32)
         gate_value = contract_last(flat_rows, gate_full)
         upward = contract_last(flat_rows, up_full)
         backward = contract_last(flat_grads, down_full)
@@ -211,12 +227,7 @@
         )
         hidden_scaled = (hidden * scale_column).astype(jnp.bfloat16)
         kept_list.append((grad_pair, hidden_scaled, flat_rows, flat_grads))
-        rows_back = to_owners(
-            reduce_quad(part_rows.reshape(-1, groups, capacity, feature_count))
-        )
-        weights_back = weights_to_owners(
-            reduce_quad(part_weight.reshape(-1, groups, capacity))
-        )
+        summed, weight_sums = send_back(part_rows, part_weight)
         (
             finish_inputs,
             finish_scales,
@@ -226,8 +237,6 @@
             finish_keeping,
             finish_weight_slots,
         ) = current
-        summed = rows_back.reshape(slot_count, feature_count)
-        weight_sums = weights_back.reshape(slot_count)
         expert_rows = jnp.sum(
             jnp.take(summed, finish_places, axis=0).reshape(token_rows, pick_count, feature_count),
             axis=1,

time: 239 us -> 245 us (1.025)
  starting transfers between devices: 64.1 us -> 36.4 us
  waiting for transfers between devices: 106 us -> 127 us
  local copies, waits for them, and re-layouts: 14.2 us -> 26.2 us
    ppermute x39 -> x25, starting transfers between devices: 43.7 us -> 23 us  [flipped(): return lax.ppermute(block, axis, route)]
    ppermute x39 -> x25, waiting for transfers between devices: 66.6 us -> 77.7 us  [flipped(): return lax.ppermute(block, axis, route)]
    ppermute x10 -> x6, waiting for transfers between devices: 39.6 us -> 49.7 us  [rotated(): return lax.ppermute(block, axis, route)]
    ppermute x10 -> x6, starting transfers between devices: 18.8 us -> 11.8 us  [rotated(): return lax.ppermute(block, axis, route)]
    unnamed x92 -> x94, local copies, waits for them, and re-layouts: 2.6 us -> 8.74 us
    another operation x0 -> x7, local copies, waits for them, and re-layouts: none -> 3.24 us  [the longest x2 1.56 us: to_experts(): return jnp.stack(moved)]
  transfers between devices with their start and end apart: 52 -> 34, of which waited for: 26 -> 26; matrix products, arithmetic and copies ran while one was open for 17% -> 14% of each run, Pallas kernels for 0% -> 0%
where the time goes in v7:
time: 245 us
  waiting for transfers between devices  127 us (52%)
  starting transfers between devices  36.4 us (15%)
  local copies, waits for them, and re-layouts  26.2 us (11%)
  other arithmetic  23.2 us (9%)
  matrix products  16.3 us (7%)
  between operations  15.1 us (6%)
    ppermute x25, waiting for transfers between devices, flipped(): return lax.ppermute(block, axis, route)  77.7 us
    ppermute x6, waiting for transfers between devices, rotated(): return lax.ppermute(block, axis, route)  49.7 us
    ppermute x25, starting transfers between devices, flipped(): return lax.ppermute(block, axis, route)  23 us
    ppermute x6, starting transfers between devices, rotated(): return lax.ppermute(block, axis, route)  11.8 us
    unnamed x94, local copies, waits for them, and re-layouts  8.74 us
    another operation x12, other arithmetic, gather_quad(): return jnp.stack([staged, first, second, diagonal])  7.07 us
    dot_general x6, matrix products, contract_last(): lax.dot_general(first_operand, second_operand, (((1,), (1,)), ((), ())),...  6.45 us
    dot_general x2, matrix products, contract_first(): lax.dot_general(first_operand, second_operand, (((0,), (0,)), ((), ())),...  4.95 us
  transfers between devices with their start and end apart: 34, of which 26 were waited for; matrix products, arithmetic and copies ran while one was open for 14% of the time, Pallas kernels for 0%

profile of v7, /device:TPU:0, one launch (start us, length us, event | category | flops | bytes accessed | tf_op | source)
XLA Modules:
  0.0 244.7 jit_solution(8680453070101103877)
XLA Ops:
  11.7 4.1 %collective-permute-start.5 = (bf16[48,2560]{1,0:T(8,128)(2,1)S(1)}, bf16[48,2560]{1,0:T(8,128)(2,1)S(1)}, u32[]{:S(2)}, u32[]{:S(2)}) collective-permute-start(bf16[48,2560]{1,0:T(8,128)(2,1)S(1)} %get-tuple-element.79), channel_id=1, source_target_pairs={{0,8},{8,0},{1,9},{9,1},{2,10},{10,2},{3,11},{11,3},{4,12},{12,4},... | collective-permute-start | bytes 737288 | tf_op jit(solution)/shard_map/ppermute | solution.py:21
  16.8 17.1 %collective-permute-done.5 = bf16[48,2560]{1,0:T(8,128)(2,1)S(1)} collective-permute-done((bf16[48,2560]{1,0:T(8,128)(2,1)S(1)}, bf16[48,2560]{1,0:T(8,128)(2,1)S(1)}, u32[]{:S(2)}, u32[]{:S(2)}) %collective-permute-start.5) | collective-permute-done | bytes 245792 | tf_op jit(solution)/shard_map/ppermute | solution.py:21
  36.0 3.4 %collective-permute-done = bf16[49,2560]{1,0:T(8,128)(2,1)S(1)} collective-permute-done((bf16[49,2560]{1,0:T(8,128)(2,1)S(1)}, bf16[49,2560]{1,0:T(8,128)(2,1)S(1)}, u32[]{:S(2)}, u32[]{:S(2)}) %collective-permute-start) | collective-permute-done | bytes 250912 | tf_op jit(solution)/shard_map/ppermute | solution.py:21
  43.7 3.8 %collective-permute-done.6 = bf16[2,48,2560]{2,1,0:T(8,128)(2,1)S(1)} collective-permute-done((bf16[2,48,2560]{2,1,0:T(8,128)(2,1)S(1)}, bf16[2,48,2560]{2,1,0:T(8,128)(2,1)S(1)}, u32[]{:S(2)}, u32[]{:S(2)}) %collective-permute-start.6) | collective-permute-done | bytes 491552 | tf_op jit(solution)/shard_map/ppermute | solution.py:27
  54.6 6.2 %collective-permute-done.2 = bf16[2,49,2560]{2,0,1:T(2,128)(2,1)S(1)} collective-permute-done((bf16[2,49,2560]{2,0,1:T(2,128)(2,1)}, bf16[2,49,2560]{2,0,1:T(2,128)(2,1)S(1)}, u32[]{:S(2)}, u32[]{:S(2)}) %collective-permute-start.2) | collective-permute-done | bytes 501792 | tf_op jit(solution)/shard_map/ppermute | solution.py:27
  63.0 3.2 %collective-permute-done.8 = bf16[2,48,1280]{2,1,0:T(8,128)(2,1)} collective-permute-done((bf16[2,48,1280]{2,1,0:T(8,128)(2,1)}, bf16[2,48,1280]{2,1,0:T(8,128)(2,1)}, u32[]{:S(2)}, u32[]{:S(2)}) %collective-permute-start.8) | collective-permute-done | bytes 245792 | tf_op jit(solution)/shard_map/ppermute | solution.py:27
  72.3 3.7 %maximum_select_fusion = bf16[3,192,2560]{2,1,0:T(8,128)(2,1)S(1)} fusion(bf16[3,192,1280]{2,1,0:T(8,128)(2,1)} %collective-permute-done.10, bf16[3,192,1280]{2,1,0:T(8,128)(2,1)} %constant_dynamic-update-slice_fusion, pred[]{:T(512)S(6)} %eq.120), kind=kLoop, calls=%fused_computation.23 | loop fusion | flops 13271040 | bytes 5898241 | tf_op jit(solution)/shard_map/jit(_where)/select_n | solution.py:121
  84.9 6.9 %collective-permute-done.11 = bf16[2,49,1280]{2,1,0:T(8,128)(2,1)S(1)} collective-permute-done((bf16[2,49,1280]{2,1,0:T(8,128)(2,1)S(1)}, bf16[2,49,1280]{2,1,0:T(8,128)(2,1)S(1)}, u32[]{:S(2)}, u32[]{:S(2)}) %collective-permute-start.11) | collective-permute-done | bytes 250912 | tf_op jit(solution)/shard_map/ppermute | solution.py:27
  94.7 11.5 %collective-permute-done.14 = bf16[2,49,2560]{2,0,1:T(2,128)(2,1)S(1)} collective-permute-done((bf16[2,49,2560]{2,0,1:T(2,128)(2,1)S(1)}, bf16[2,49,2560]{2,0,1:T(2,128)(2,1)S(1)}, u32[]{:S(2)}, u32[]{:S(2)}) %collective-permute-start.14) | collective-permute-done | bytes 501792 | tf_op jit(solution)/shard_map/ppermute | solution.py:27
  107.2 2.4 collective-permute-start.15
  110.5 10.5 %collective-permute-done.15 = bf16[50,2560]{1,0:T(8,128)(2,1)S(1)} collective-permute-done((bf16[50,2560]{1,0:T(8,128)(2,1)S(1)}, bf16[50,2560]{1,0:T(8,128)(2,1)S(1)}, u32[]{:S(2)}, u32[]{:S(2)}) %collective-permute-start.15) | collective-permute-done | bytes 256032 | tf_op jit(solution)/shard_map/ppermute | solution.py:21
  127.5 12.9 %collective-permute-done.17 = bf16[49,2560]{1,0:T(8,128)(2,1)S(1)} collective-permute-done((bf16[49,2560]{1,0:T(8,128)(2,1)S(1)}, bf16[49,2560]{1,0:T(8,128)(2,1)S(1)}, u32[]{:S(2)}, u32[]{:S(2)}) %collective-permute-start.17) | collective-permute-done | bytes 250912 | tf_op jit(solution)/shard_map/ppermute | solution.py:21
  144.6 13.2 %collective-permute-done.19 = bf16[2,49,2560]{2,0,1:T(2,128)(2,1)S(1)} collective-permute-done((bf16[2,49,2560]{2,0,1:T(2,128)(2,1)S(1)}, bf16[2,49,2560]{2,0,1:T(2,128)(2,1)S(1)}, u32[]{:S(2)}, u32[]{:S(2)}) %collective-permute-start.19) | collective-permute-done | bytes 501792 | tf_op jit(solution)/shard_map/ppermute | solution.py:27
  158.0 2.4 collective-permute-start.21
  163.9 4.3 %collective-permute-done.21 = bf16[2,49,1280]{2,1,0:T(8,128)(2,1)S(1)} collective-permute-done((bf16[2,49,1280]{2,1,0:T(8,128)(2,1)S(1)}, bf16[2,49,1280]{2,1,0:T(8,128)(2,1)S(1)}, u32[]{:S(2)}, u32[]{:S(2)}) %collective-permute-start.21) | collective-permute-done | bytes 250912 | tf_op jit(solution)/shard_map/ppermute | solution.py:27
  172.9 3.5 %collective-permute-done.23 = bf16[2,48,2560]{2,1,0:T(8,128)(2,1)} collective-permute-done((bf16[2,48,2560]{2,1,0:T(8,128)(2,1)}, bf16[2,48,2560]{2,1,0:T(8,128)(2,1)}, u32[]{:S(2)}, u32[]{:S(2)}) %collective-permute-start.23) | collective-permute-done | bytes 491552 | tf_op jit(solution)/shard_map/ppermute | solution.py:27
  181.1 2.6 %collective-permute-done.25 = bf16[2,48,1280]{2,1,0:T(8,128)(2,1)S(1)} collective-permute-done((bf16[2,48,1280]{2,1,0:T(8,128)(2,1)S(1)}, bf16[2,48,1280]{2,1,0:T(8,128)(2,1)S(1)}, u32[]{:S(2)}, u32[]{:S(2)}) %collective-permute-start.25) | collective-permute-done | bytes 245792 | tf_op jit(solution)/shard_map/ppermute | solution.py:27
  195.5 3.0 %convolution_convert_fusion = bf16[384,2560]{1,0:T(8,128)(2,1)} fusion(bf16[384,2560]{1,0:T(8,128)(2,1)S(1)} %bitcast.265, bf16[384,2560]{1,0:T(8,128)(2,1)S(1)} %bitcast.259, bf16[384,192]{0,1:T(8,128)(2,1)S(1)} %copy-done.38, bf16[384,192]{0,1:T(8,128)(2,1)S(1)} %copy-done.37, bf16[384,192]{0,1:T(8,128)(2,1)S(1)} %copy-done.35, ...), kind=kOutput, calls=%fused_computation.7 | convolution fusion | flops 1521156096 | bytes 6488064 | tf_op jit(solution)/shard_map/dot_general | solution.py:42
  202.1 3.7 %collective-permute-done.29 = bf16[2,49,1280]{2,1,0:T(8,128)(2,1)S(1)} collective-permute-done((bf16[2,49,1280]{2,1,0:T(8,128)(2,1)S(1)}, bf16[2,49,1280]{2,1,0:T(8,128)(2,1)S(1)}, u32[]{:S(2)}, u32[]{:S(2)}) %collective-permute-start.29) | collective-permute-done | bytes 250912 | tf_op jit(solution)/shard_map/ppermute | solution.py:27
  207.5 2.5 %collective-permute-start.28 = (bf16[2,49,2560]{2,0,1:T(2,128)(2,1)S(1)}, bf16[2,49,2560]{2,0,1:T(2,128)(2,1)S(1)}, u32[]{:S(2)}, u32[]{:S(2)}) collective-permute-start(bf16[2,49,2560]{2,0,1:T(2,128)(2,1)S(1)} %copy.93), channel_id=1, source_target_pairs={{0,4},{2,6},{4,0},{6,2},{1,5},{3,7},{5,1},{7,3},{8,12},{10,14},{12... | collective-permute-start | bytes 1505288 | tf_op jit(solution)/shard_map/ppermute | solution.py:27
  211.1 4.2 %collective-permute-done.30 = bf16[2,49,2560]{2,0,1:T(2,128)(2,1)S(1)} collective-permute-done((bf16[2,49,2560]{2,0,1:T(2,128)(2,1)S(1)}, bf16[2,49,2560]{2,0,1:T(2,128)(2,1)S(1)}, u32[]{:S(2)}, u32[]{:S(2)}) %collective-permute-start.30) | collective-permute-done | bytes 501792 | tf_op jit(solution)/shard_map/ppermute | solution.py:27
  215.4 2.8 %collective-permute-done.28 = bf16[2,49,2560]{2,0,1:T(2,128)(2,1)S(1)} collective-permute-done((bf16[2,49,2560]{2,0,1:T(2,128)(2,1)S(1)}, bf16[2,49,2560]{2,0,1:T(2,128)(2,1)S(1)}, u32[]{:S(2)}, u32[]{:S(2)}) %collective-permute-start.28) | collective-permute-done | bytes 501792 | tf_op jit(solution)/shard_map/ppermute | solution.py:27
  219.5 3.5 %collective-permute-start.31 = (bf16[50,2560]{1,0:T(8,128)(2,1)S(1)}, bf16[50,2560]{1,0:T(8,128)(2,1)S(1)}, u32[]{:S(2)}, u32[]{:S(2)}) collective-permute-start(bf16[50,2560]{1,0:T(8,128)(2,1)S(1)} %pad_maximum_fusion.22), channel_id=1, source_target_pairs={{0,8},{8,0},{1,9},{9,1},{2,10},{10,2},{3,11},{11,3},{4,12},{12,4},... | collective-permute-start | bytes 768008 | tf_op jit(solution)/shard_map/ppermute | solution.py:21
  225.0 5.6 %collective-permute-done.31 = bf16[50,2560]{1,0:T(8,128)(2,1)S(1)} collective-permute-done((bf16[50,2560]{1,0:T(8,128)(2,1)S(1)}, bf16[50,2560]{1,0:T(8,128)(2,1)S(1)}, u32[]{:S(2)}, u32[]{:S(2)}) %collective-permute-start.31) | collective-permute-done | bytes 256032 | tf_op jit(solution)/shard_map/ppermute | solution.py:21
  (278 shorter events, 92.4 us)
Async XLA Ops:
  7.2 228.5 %reduce-scatter.3.cloned.1.call-start = ((), (), s32[]{:S(2)}) async-start(), calls=%async_computation.2 | async-start | bytes 2949120 | tf_op jit(solution)/shard_map/reduce_scatter | solution.py:264
  11.7 22.3 %collective-permute-start.5 = (bf16[48,2560]{1,0:T(8,128)(2,1)S(1)}, bf16[48,2560]{1,0:T(8,128)(2,1)S(1)}, u32[]{:S(2)}, u32[]{:S(2)}) collective-permute-start(bf16[48,2560]{1,0:T(8,128)(2,1)S(1)} %get-tuple-element.79), channel_id=1, source_target_pairs={{0,8},{8,0},{1,9},{9,1},{2,10},{10,2},{3,11},{11,3},{4,12},{12,4},... | collective-permute-start | bytes 737288 | tf_op jit(solution)/shard_map/ppermute | solution.py:21
  16.7 22.6 %collective-permute-start = (bf16[49,2560]{1,0:T(8,128)(2,1)S(1)}, bf16[49,2560]{1,0:T(8,128)(2,1)S(1)}, u32[]{:S(2)}, u32[]{:S(2)}) collective-permute-start(bf16[49,2560]{1,0:T(8,128)(2,1)S(1)} %get-tuple-element.71), channel_id=1, source_target_pairs={{0,8},{8,0},{1,9},{9,1},{2,10},{10,2},{3,11},{11,3},{4,12},{12,4},... | collective-permute-start | bytes 752648 | tf_op jit(solution)/shard_map/ppermute | solution.py:21
  34.0 13.4 %collective-permute-start.6 = (bf16[2,48,2560]{2,1,0:T(8,128)(2,1)S(1)}, bf16[2,48,2560]{2,1,0:T(8,128)(2,1)S(1)}, u32[]{:S(2)}, u32[]{:S(2)}) collective-permute-start(bf16[2,48,2560]{2,1,0:T(8,128)(2,1)S(1)} %get-tuple-element.77), channel_id=1, source_target_pairs={{0,2},{2,0},{4,6},{6,4},{1,3},{3,1},{5,7},{7,5},{8,10},{10,8},{12,... | collective-permute-start | bytes 1474568 | tf_op jit(solution)/shard_map/ppermute | solution.py:27
  35.9 14.1 %collective-permute-start.7 = (bf16[2,48,2560]{2,1,0:T(8,128)(2,1)S(1)}, bf16[2,48,2560]{2,1,0:T(8,128)(2,1)S(1)}, u32[]{:S(2)}, u32[]{:S(2)}) collective-permute-start(bf16[2,48,2560]{2,1,0:T(8,128)(2,1)S(1)} %get-tuple-element.77), channel_id=1, source_target_pairs={{0,4},{2,6},{4,0},{6,2},{1,5},{3,7},{5,1},{7,3},{8,12},{10,14},{12... | collective-permute-start | bytes 1474568 | tf_op jit(solution)/shard_map/ppermute | solution.py:27
  40.7 20.1 %collective-permute-start.2 = (bf16[2,49,2560]{2,0,1:T(2,128)(2,1)}, bf16[2,49,2560]{2,0,1:T(2,128)(2,1)S(1)}, u32[]{:S(2)}, u32[]{:S(2)}) collective-permute-start(bf16[2,49,2560]{2,0,1:T(2,128)(2,1)} %copy.73), channel_id=1, source_target_pairs={{0,4},{2,6},{4,0},{6,2},{1,5},{3,7},{5,1},{7,3},{8,12},{10,14},{12... | collective-permute-start | bytes 1505288 | tf_op jit(solution)/shard_map/ppermute | solution.py:27
  41.3 21.2 %collective-permute-start.1 = (bf16[2,49,2560]{2,0,1:T(2,128)(2,1)}, bf16[2,49,2560]{2,0,1:T(2,128)(2,1)S(1)}, u32[]{:S(2)}, u32[]{:S(2)}) collective-permute-start(bf16[2,49,2560]{2,0,1:T(2,128)(2,1)} %copy.73), channel_id=1, source_target_pairs={{0,2},{2,0},{4,6},{6,4},{1,3},{3,1},{5,7},{7,5},{8,10},{10,8},{12,... | collective-permute-start | bytes 1505288 | tf_op jit(solution)/shard_map/ppermute | solution.py:27
  48.2 17.9 %collective-permute-start.8 = (bf16[2,48,1280]{2,1,0:T(8,128)(2,1)}, bf16[2,48,1280]{2,1,0:T(8,128)(2,1)}, u32[]{:S(2)}, u32[]{:S(2)}) collective-permute-start(bf16[2,48,1280]{2,1,0:T(8,128)(2,1)} %slice.312), channel_id=1, source_target_pairs={{0,4},{2,6},{4,0},{6,2},{1,5},{3,7},{5,1},{7,3},{8,12},{10,14},{12... | collective-permute-start | bytes 737288 | tf_op jit(solution)/shard_map/ppermute | solution.py:27
  51.5 14.6 %collective-permute-start.9 = (bf16[2,48,1280]{2,1,0:T(8,128)(2,1)}, bf16[2,48,1280]{2,1,0:T(8,128)(2,1)}, u32[]{:S(2)}, u32[]{:S(2)}) collective-permute-start(bf16[2,48,1280]{2,1,0:T(8,128)(2,1)} %slice.313), channel_id=1, source_target_pairs={{0,2},{2,0},{4,6},{6,4},{1,3},{3,1},{5,7},{7,5},{8,10},{10,8},{12,... | collective-permute-start | bytes 737288 | tf_op jit(solution)/shard_map/ppermute | solution.py:27
  54.6 17.7 %collective-permute-start.10 = (bf16[3,192,1280]{2,1,0:T(8,128)(2,1)}, bf16[3,192,1280]{2,1,0:T(8,128)(2,1)}, u32[]{:S(2)}, u32[]{:S(2)}) collective-permute-start(bf16[3,192,1280]{2,1,0:T(8,128)(2,1)} %constant_dynamic-update-slice_fusion), channel_id=1, source_target_pairs={{0,1},{1,0},{2,3},{3,2},{4,5},{5,4},{6,7},{7,6},{8,9},{9,8},{10,11... | collective-permute-start | bytes 4423688 | tf_op jit(solution)/shard_map/ppermute | solution.py:27
  93.9 12.3 %collective-permute-start.14 = (bf16[2,49,2560]{2,0,1:T(2,128)(2,1)S(1)}, bf16[2,49,2560]{2,0,1:T(2,128)(2,1)S(1)}, u32[]{:S(2)}, u32[]{:S(2)}) collective-permute-start(bf16[2,49,2560]{2,0,1:T(2,128)(2,1)S(1)} %copy.82), channel_id=1, source_target_pairs={{0,2},{2,0},{4,6},{6,4},{1,3},{3,1},{5,7},{7,5},{8,10},{10,8},{12,... | collective-permute-start | bytes 1505288 | tf_op jit(solution)/shard_map/ppermute | solution.py:27
  94.7 12.2 %collective-permute-start.12 = (bf16[2,49,2560]{2,0,1:T(2,128)(2,1)S(1)}, bf16[2,49,2560]{2,0,1:T(2,128)(2,1)S(1)}, u32[]{:S(2)}, u32[]{:S(2)}) collective-permute-start(bf16[2,49,2560]{2,0,1:T(2,128)(2,1)S(1)} %copy.80), channel_id=1, source_target_pairs={{0,4},{2,6},{4,0},{6,2},{1,5},{3,7},{5,1},{7,3},{8,12},{10,14},{12... | collective-permute-start | bytes 1505288 | tf_op jit(solution)/shard_map/ppermute | solution.py:27
  107.2 13.8 %collective-permute-start.15 = (bf16[50,2560]{1,0:T(8,128)(2,1)S(1)}, bf16[50,2560]{1,0:T(8,128)(2,1)S(1)}, u32[]{:S(2)}, u32[]{:S(2)}) collective-permute-start(bf16[50,2560]{1,0:T(8,128)(2,1)S(1)} %pad_maximum_fusion.21), channel_id=1, source_target_pairs={{0,8},{8,0},{1,9},{9,1},{2,10},{10,2},{3,11},{11,3},{4,12},{12,4},... | collective-permute-start | bytes 768008 | tf_op jit(solution)/shard_map/ppermute | solution.py:21
  125.5 14.9 %collective-permute-start.17 = (bf16[49,2560]{1,0:T(8,128)(2,1)S(1)}, bf16[49,2560]{1,0:T(8,128)(2,1)S(1)}, u32[]{:S(2)}, u32[]{:S(2)}) collective-permute-start(bf16[49,2560]{1,0:T(8,128)(2,1)S(1)} %get-tuple-element.65), channel_id=1, source_target_pairs={{0,8},{8,0},{1,9},{9,1},{2,10},{10,2},{3,11},{11,3},{4,12},{12,4},... | collective-permute-start | bytes 752648 | tf_op jit(solution)/shard_map/ppermute | solution.py:21
  126.0 16.4 %collective-permute-start.16 = (bf16[64,2560]{1,0:T(8,128)(2,1)S(1)}, bf16[64,2560]{1,0:T(8,128)(2,1)S(1)}, u32[]{:S(2)}, u32[]{:S(2)}) collective-permute-start(bf16[64,2560]{1,0:T(8,128)(2,1)S(1)} %fusion.40), channel_id=1, source_target_pairs={{16,0},{17,1},{18,2},{19,3},{20,4},{21,5},{22,6},{23,7},{24,8},{25... | collective-permute-start | bytes 983048 | tf_op jit(solution)/shard_map/ppermute | solution.py:15
  140.9 16.9 %collective-permute-start.19 = (bf16[2,49,2560]{2,0,1:T(2,128)(2,1)S(1)}, bf16[2,49,2560]{2,0,1:T(2,128)(2,1)S(1)}, u32[]{:S(2)}, u32[]{:S(2)}) collective-permute-start(bf16[2,49,2560]{2,0,1:T(2,128)(2,1)S(1)} %copy.86), channel_id=1, source_target_pairs={{0,4},{2,6},{4,0},{6,2},{1,5},{3,7},{5,1},{7,3},{8,12},{10,14},{12... | collective-permute-start | bytes 1505288 | tf_op jit(solution)/shard_map/ppermute | solution.py:27
  141.0 19.4 %collective-permute-start.18 = (bf16[2,49,2560]{2,0,1:T(2,128)(2,1)S(1)}, bf16[2,49,2560]{2,0,1:T(2,128)(2,1)S(1)}, u32[]{:S(2)}, u32[]{:S(2)}) collective-permute-start(bf16[2,49,2560]{2,0,1:T(2,128)(2,1)S(1)} %copy.86), channel_id=1, source_target_pairs={{0,2},{2,0},{4,6},{6,4},{1,3},{3,1},{5,7},{7,5},{8,10},{10,8},{12,... | collective-permute-start | bytes 1505288 | tf_op jit(solution)/shard_map/ppermute | solution.py:27
  142.8 17.9 %collective-permute-start.22 = (bf16[48,2560]{1,0:T(8,128)(2,1)S(1)}, bf16[48,2560]{1,0:T(8,128)(2,1)S(1)}, u32[]{:S(2)}, u32[]{:S(2)}) collective-permute-start(bf16[48,2560]{1,0:T(8,128)(2,1)S(1)} %get-tuple-element.75), channel_id=1, source_target_pairs={{0,8},{8,0},{1,9},{9,1},{2,10},{10,2},{3,11},{11,3},{4,12},{12,4},... | collective-permute-start | bytes 737288 | tf_op jit(solution)/shard_map/ppermute | solution.py:21
  158.0 10.2 %collective-permute-start.21 = (bf16[2,49,1280]{2,1,0:T(8,128)(2,1)S(1)}, bf16[2,49,1280]{2,1,0:T(8,128)(2,1)S(1)}, u32[]{:S(2)}, u32[]{:S(2)}) collective-permute-start(bf16[2,49,1280]{2,1,0:T(8,128)(2,1)S(1)} %copy.112), channel_id=1, source_target_pairs={{0,2},{2,0},{4,6},{6,4},{1,3},{3,1},{5,7},{7,5},{8,10},{10,8},{12,... | collective-permute-start | bytes 752648 | tf_op jit(solution)/shard_map/ppermute | solution.py:27
  161.7 14.7 %collective-permute-start.23 = (bf16[2,48,2560]{2,1,0:T(8,128)(2,1)}, bf16[2,48,2560]{2,1,0:T(8,128)(2,1)}, u32[]{:S(2)}, u32[]{:S(2)}) collective-permute-start(bf16[2,48,2560]{2,1,0:T(8,128)(2,1)} %get-tuple-element.73), channel_id=1, source_target_pairs={{0,2},{2,0},{4,6},{6,4},{1,3},{3,1},{5,7},{7,5},{8,10},{10,8},{12,... | collective-permute-start | bytes 1474568 | tf_op jit(solution)/shard_map/ppermute | solution.py:27
  161.7 16.6 %collective-permute-start.24 = (bf16[2,48,2560]{2,1,0:T(8,128)(2,1)}, bf16[2,48,2560]{2,1,0:T(8,128)(2,1)}, u32[]{:S(2)}, u32[]{:S(2)}) collective-permute-start(bf16[2,48,2560]{2,1,0:T(8,128)(2,1)} %get-tuple-element.73), channel_id=1, source_target_pairs={{0,4},{2,6},{4,0},{6,2},{1,5},{3,7},{5,1},{7,3},{8,12},{10,14},{12... | collective-permute-start | bytes 1474568 | tf_op jit(solution)/shard_map/ppermute | solution.py:27
  198.5 39.3 %reduce-scatter.5.cloned.1.call-start = ((), (), s32[]{:S(2)}) async-start(), calls=%async_computation.3 | async-start | bytes 1474560 | tf_op jit(solution)/shard_map/reduce_scatter | solution.py:267
  207.5 10.7 %collective-permute-start.28 = (bf16[2,49,2560]{2,0,1:T(2,128)(2,1)S(1)}, bf16[2,49,2560]{2,0,1:T(2,128)(2,1)S(1)}, u32[]{:S(2)}, u32[]{:S(2)}) collective-permute-start(bf16[2,49,2560]{2,0,1:T(2,128)(2,1)S(1)} %copy.93), channel_id=1, source_target_pairs={{0,4},{2,6},{4,0},{6,2},{1,5},{3,7},{5,1},{7,3},{8,12},{10,14},{12... | collective-permute-start | bytes 1505288 | tf_op jit(solution)/shard_map/ppermute | solution.py:27
  219.5 11.1 %collective-permute-start.31 = (bf16[50,2560]{1,0:T(8,128)(2,1)S(1)}, bf16[50,2560]{1,0:T(8,128)(2,1)S(1)}, u32[]{:S(2)}, u32[]{:S(2)}) collective-permute-start(bf16[50,2560]{1,0:T(8,128)(2,1)S(1)} %pad_maximum_fusion.22), channel_id=1, source_target_pairs={{0,8},{8,0},{1,9},{9,1},{2,10},{10,2},{3,11},{11,3},{4,12},{12,4},... | collective-permute-start | bytes 768008 | tf_op jit(solution)/shard_map/ppermute | solution.py:21
  (54 other events, 394.1 us)
Sparse Core Ops, SparseCore 0:
  198.6 9.6 reduce-scatter.2
  225.1 5.9 reduce-scatter.4

commit v8 on v5

--- a/solution.py
+++ b/solution.py
@@ -42,6 +42,46 @@
     return lax.dot_general(
         first_operand, second_operand, (((0,), (0,)), ((), ())), preferred_element_type=jnp.float32
     )
+
+
+def relayed(block):
+    width = block.shape[-1]
+    return lax.axis_size("ej") == 4 and width >= 256 and width % 256 == 0
+
+
+def gather_quad(staged):
+    quad = lax.axis_size("ej")
+    if not relayed(staged):
+        return jnp.stack([staged] + [flipped(staged, "ej", t) for t in range(1, quad)])
+    half = staged.shape[-1] // 2
+    first = flipped(staged, "ej", 1)
+    second = flipped(staged, "ej", 2)
+    diagonal = jnp.concatenate(
+        [flipped(first[..., :half], "ej", 2), flipped(second[..., half:], "ej", 1)], axis=-1
+    )
+    return jnp.stack([staged, first, second, diagonal])
+
+
+def reduce_quad(parts):
+    quad = parts.shape[0]
+    total = parts[0].astype(jnp.float32)
+    if not relayed(parts):
+        for t in range(1, quad):
+            total = total + flipped(parts[t], "ej", t).astype(jnp.float32)
+        return total
+    half = parts.shape[-1] // 2
+    from_first = flipped(parts[3][..., :half], "ej", 1).astype(jnp.float32)
+    from_second = flipped(parts[3][..., half:], "ej", 2).astype(jnp.float32)
+    toward_second = jnp.concatenate(
+        [(parts[2][..., :half].astype(jnp.float32) + from_first).astype(parts.dtype), parts[2][..., half:]],
+        axis=-1,
+    )
+    toward_first = jnp.concatenate(
+        [parts[1][..., :half], (parts[1][..., half:].astype(jnp.float32) + from_second).astype(parts.dtype)],
+        axis=-1,
+    )
+    total = total + flipped(toward_second, "ej", 2).astype(jnp.float32)
+    return total + flipped(toward_first, "ej", 1).astype(jnp.float32)
 
 
 def local(
@@ -66,10 +106,22 @@
     pick_count = expert_ids.shape[3]
     capacity = max(2, 3 * token_rows * pick_count // (2 * groups))
     slot_count = groups * capacity
+    low_half = lax.axis_index("dp") == 0
+
+    def whole_rows(stored):
+        if lax.axis_size("dp") != 2:
+            return lax.all_gather(stored, "dp", axis=1, tiled=True)
+        partner = flipped(stored, "dp", 1)
+        return jnp.where(
+            low_half,
+            jnp.concatenate([stored, partner], axis=1),
+            jnp.concatenate([partner, stored], axis=1),
+        )
+
     gate_full, up_full, down_full = (
-        lax.all_gather(gate_weight[0], "dp", axis=1, tiled=True),
-        lax.all_gather(up_weight[0], "dp", axis=1, tiled=True),
-        lax.all_gather(down_weight[0], "dp", axis=1, tiled=True),
+        whole_rows(gate_weight[0]),
+        whole_rows(up_weight[0]),
+        whole_rows(down_weight[0]),
     )
     hidden_count = gate_full.shape[0]
     paired_weights = jnp.concatenate([gate_full, up_full], axis=0)
@@ -111,8 +163,7 @@
         return block if s == 0 else rotated(block, "eg", s)
 
     def around(block):
-        copies = jnp.broadcast_to(block[None], (quad,) + block.shape)
-        return lax.all_to_all(copies, "ej", split_axis=0, concat_axis=0, tiled=True)
+        return gather_quad(block)
 
     def run_block(rows_block, grads_block, weight_block):
         flat_rows = rows_block.reshape(-1, feature_count)
@@ -138,9 +189,7 @@
         quad_weight = jnp.pad(
             part_weight.reshape(quad, 1, capacity), ((0, 0), (0, 0), (0, feature_count - capacity))
         )
-        stacked = jnp.concatenate([quad_rows, quad_weight], axis=1)
-        returned = lax.all_to_all(stacked, "ej", split_axis=0, concat_axis=0, tiled=True)
-        total = jnp.sum(returned.astype(jnp.float32), axis=0)
+        total = reduce_quad(jnp.concatenate([quad_rows, quad_weight], axis=1))
         if s == 0:
             return total[:capacity], total[capacity, :capacity]
         high = total[capacity:].astype(jnp.bfloat16)

time: 319 us -> 269 us (0.84)
  waiting for transfers between devices: 157 us -> 116 us
  blocking collectives: 7.62 us -> 0 us
  other arithmetic: 25.9 us -> 33.3 us
  local copies, waits for them, and re-layouts: 30.8 us -> 24.8 us
    ppermute x0 -> x43, waiting for transfers between devices: none -> 92.9 us  [flipped(): return lax.ppermute(block, axis, route)]
    ppermute x5, waiting for transfers between devices: 91.9 us -> 23 us  [rotated(): return lax.ppermute(block, axis, route)]
    all_to_all x10 -> x0, waiting for transfers between devices: 55.6 us -> none  [the longest x4 36.2 us: send_back(): lax.all_to_all(stacked, 'ej', split_axis=0, concat_axis=0, tiled=True)]
    all_to_all x10 -> x0, starting transfers between devices: 42.9 us -> none  [the longest x6 27.3 us: around(): return lax.all_to_all(copies, 'ej', split_axis=0, concat_axis=0, tiled=True)]
    ppermute x0 -> x43, starting transfers between devices: none -> 38.2 us  [flipped(): return lax.ppermute(block, axis, route)]
    another operation x0 -> x12, other arithmetic: none -> 9.59 us  [gather_quad(): return jnp.stack([staged, first, second, diagonal])]
    ppermute x1, waiting for transfers between devices: 9.43 us -> 0.01 us  [shifted(): return lax.ppermute(block, axis, route)]
    broadcast_in_dim x8 -> x0, local copies, waits for them, and re-layouts: 9.15 us -> none  [around(): copies = jnp.broadcast_to(block[None], (quad,) + block.shape)]
  transfers between devices with their start and end apart: 18 -> 51, of which waited for: 16 -> 24; matrix products, arithmetic and copies ran while one was open for 16% -> 29% of each run, Pallas kernels for 0% -> 0%
where the time goes in v8:
time: 269 us; the launch traced here: 268 us
  waiting for transfers between devices  116 us (43%)
  starting transfers between devices  48.4 us (18%)
  other arithmetic  33.3 us (12%)
  matrix products  30.4 us (11%)
  local copies, waits for them, and re-layouts  24.8 us (9%)
  between operations  15.4 us (6%)
    ppermute x43, waiting for transfers between devices, flipped(): return lax.ppermute(block, axis, route)  92.9 us
    ppermute x43, starting transfers between devices, flipped(): return lax.ppermute(block, axis, route)  38.2 us
    ppermute x5, waiting for transfers between devices, rotated(): return lax.ppermute(block, axis, route)  23 us
    dot_general x12, matrix products, contract_last(): lax.dot_general(first_operand, second_operand, (((1,), (1,)), ((), ())),...  17 us
    another operation x12, other arithmetic, gather_quad(): return jnp.stack([staged, first, second, diagonal])  9.59 us
    ppermute x5, starting transfers between devices, rotated(): return lax.ppermute(block, axis, route)  8.5 us
    dot_general x4, matrix products, run_block(): jnp.dot(grad_pair, paired_weights, preferred_element_type=jnp.float32)  6.66 us
    unnamed x134, local copies, waits for them, and re-layouts  6.03 us
  transfers between devices with their start and end apart: 51, of which 24 were waited for; matrix products, arithmetic and copies ran while one was open for 29% of the time, Pallas kernels for 0%

profile of v8, /device:TPU:0, one launch (start us, length us, event | category | flops | bytes accessed | tf_op | source)
XLA Modules:
  0.0 268.4 jit_solution(11327129684924475774)
XLA Ops:
  15.6 2.6 collective-permute-start.1
  20.2 2.6 collective-permute-start.11
  22.8 2.7 %maximum_select_fusion.2 = bf16[192,2560]{1,0:T(8,128)(2,1)} fusion(bf16[192,1280]{1,0:T(8,128)(2,1)} %collective-permute-done.6, bf16[192,1280]{1,0:T(8,128)(2,1)} %bitcast.293, pred[]{:T(512)S(6)} %eq.120), kind=kLoop, calls=%fused_computation.61 | loop fusion | flops 4423680 | bytes 1966081 | tf_op jit(solution)/shard_map/jit(_where)/select_n | solution.py:115
  25.5 14.7 %collective-permute-done.1 = bf16[97,2560]{1,0:T(8,128)(2,1)S(1)} collective-permute-done((bf16[97,2560]{1,0:T(8,128)(2,1)S(1)}, bf16[97,2560]{1,0:T(8,128)(2,1)S(1)}, u32[]{:S(2)}, u32[]{:S(2)}) %collective-permute-start.1) | collective-permute-done | bytes 496672 | tf_op jit(solution)/shard_map/ppermute | solution.py:27
  40.3 2.7 collective-permute-start.3
  45.5 3.8 %collective-permute-done.3 = bf16[97,1280]{1,0:T(8,128)(2,1)S(1)} collective-permute-done((bf16[97,1280]{1,0:T(8,128)(2,1)S(1)}, bf16[97,1280]{1,0:T(8,128)(2,1)S(1)}, u32[]{:S(2)}, u32[]{:S(2)}) %collective-permute-start.3) | collective-permute-done | bytes 248352 | tf_op jit(solution)/shard_map/ppermute | solution.py:27
  49.4 3.2 %collective-permute-done.2 = bf16[97,1280]{1,0:T(8,128)(2,1)S(1)} collective-permute-done((bf16[97,1280]{1,0:T(8,128)(2,1)S(1)}, bf16[97,1280]{1,0:T(8,128)(2,1)S(1)}, u32[]{:S(2)}, u32[]{:S(2)}) %collective-permute-start.2) | collective-permute-done | bytes 248352 | tf_op jit(solution)/shard_map/ppermute | solution.py:27
  65.2 2.3 collective-permute-done.9
  67.6 10.3 %collective-permute-done.13 = bf16[97,2560]{1,0:T(8,128)(2,1)S(1)} collective-permute-done((bf16[97,2560]{1,0:T(8,128)(2,1)}, bf16[97,2560]{1,0:T(8,128)(2,1)S(1)}, u32[]{:S(2)}, u32[]{:S(2)}) %collective-permute-start.13) | collective-permute-done | bytes 496672 | tf_op jit(solution)/shard_map/ppermute | solution.py:27
  78.4 2.9 %collective-permute-done.7 = bf16[49,1280]{1,0:T(8,128)(2,1)S(1)} collective-permute-done((bf16[49,1280]{1,0:T(8,128)(2,1)S(1)}, bf16[49,1280]{1,0:T(8,128)(2,1)S(1)}, u32[]{:S(2)}, u32[]{:S(2)}) %collective-permute-start.7) | collective-permute-done | bytes 125472 | tf_op jit(solution)/shard_map/ppermute | solution.py:27
  81.4 10.2 %collective-permute-done.15 = bf16[97,1280]{1,0:T(8,128)(2,1)S(1)} collective-permute-done((bf16[97,1280]{1,0:T(8,128)(2,1)S(1)}, bf16[97,1280]{1,0:T(8,128)(2,1)S(1)}, u32[]{:S(2)}, u32[]{:S(2)}) %collective-permute-start.15) | collective-permute-done | bytes 248352 | tf_op jit(solution)/shard_map/ppermute | solution.py:27
  104.3 4.2 %collective-permute-done.18 = bf16[49,1280]{1,0:T(8,128)(2,1)S(1)} collective-permute-done((bf16[49,1280]{1,0:T(8,128)(2,1)S(1)}, bf16[49,1280]{1,0:T(8,128)(2,1)S(1)}, u32[]{:S(2)}, u32[]{:S(2)}) %collective-permute-start.18) | collective-permute-done | bytes 125472 | tf_op jit(solution)/shard_map/ppermute | solution.py:27
  111.1 3.5 %collective-permute-done.8 = bf16[49,2560]{1,0:T(8,128)(2,1)S(1)} collective-permute-done((bf16[49,2560]{1,0:T(8,128)(2,1)S(1)}, bf16[49,2560]{1,0:T(8,128)(2,1)S(1)}, u32[]{:S(2)}, u32[]{:S(2)}) %collective-permute-start.8) | collective-permute-done | bytes 250912 | tf_op jit(solution)/shard_map/ppermute | solution.py:27
  115.8 2.5 collective-permute-done.17
  120.3 11.7 %collective-permute-done.20 = bf16[50,2560]{1,0:T(8,128)(2,1)S(1)} collective-permute-done((bf16[50,2560]{1,0:T(8,128)(2,1)S(1)}, bf16[50,2560]{1,0:T(8,128)(2,1)S(1)}, u32[]{:S(2)}, u32[]{:S(2)}) %collective-permute-start.20) | collective-permute-done | bytes 256032 | tf_op jit(solution)/shard_map/ppermute | solution.py:21
  140.6 2.4 collective-permute-start.34
  143.0 10.1 %collective-permute-done.23 = bf16[49,2560]{1,0:T(8,128)(2,1)S(1)} collective-permute-done((bf16[49,2560]{1,0:T(8,128)(2,1)S(1)}, bf16[49,2560]{1,0:T(8,128)(2,1)S(1)}, u32[]{:S(2)}, u32[]{:S(2)}) %collective-permute-start.23) | collective-permute-done | bytes 250912 | tf_op jit(solution)/shard_map/ppermute | solution.py:27
  162.5 9.1 %collective-permute-done.36 = bf16[49,2560]{1,0:T(8,128)(2,1)S(1)} collective-permute-done((bf16[49,2560]{1,0:T(8,128)(2,1)S(1)}, bf16[49,2560]{1,0:T(8,128)(2,1)S(1)}, u32[]{:S(2)}, u32[]{:S(2)}) %collective-permute-start.36) | collective-permute-done | bytes 250912 | tf_op jit(solution)/shard_map/ppermute | solution.py:27
  205.2 2.3 fusion.140
  209.6 3.1 %convolution_convert_fusion = bf16[384,2560]{1,0:T(8,128)(2,1)} fusion(bf16[192,2560]{1,0:T(8,128)(2,1)S(1)} %bitcast.251, bf16[192,2560]{1,0:T(8,128)(2,1)S(1)} %bitcast.248, bf16[192,2560]{1,0:T(8,128)(2,1)S(1)} %bitcast.257, bf16[192,2560]{1,0:T(8,128)(2,1)S(1)} %bitcast.254, bf16[192,192]{1,0:T(8,128)(2,1)S(1)} %get-tuple-element.74, ...), kind=kOutput, calls=%fused_computation.4 | convolution fusion | flops 1531379712 | bytes 6488064 | tf_op jit(solution)/shard_map/dot_general | solution.py:42
  217.7 2.6 collective-permute-done.30
  238.0 2.9 %collective-permute-done.47 = bf16[49,2560]{1,0:T(8,128)(2,1)S(1)} collective-permute-done((bf16[49,2560]{1,0:T(8,128)(2,1)S(1)}, bf16[49,2560]{1,0:T(8,128)(2,1)S(1)}, u32[]{:S(2)}, u32[]{:S(2)}) %collective-permute-start.47) | collective-permute-done | bytes 250912 | tf_op jit(solution)/shard_map/ppermute | solution.py:27
  240.8 3.6 %collective-permute-done.45 = bf16[49,2560]{1,0:T(8,128)(2,1)S(1)} collective-permute-done((bf16[49,2560]{1,0:T(8,128)(2,1)S(1)}, bf16[49,2560]{1,0:T(8,128)(2,1)S(1)}, u32[]{:S(2)}, u32[]{:S(2)}) %collective-permute-start.45) | collective-permute-done | bytes 250912 | tf_op jit(solution)/shard_map/ppermute | solution.py:27
  245.2 9.1 %collective-permute-done.48 = bf16[50,2560]{1,0:T(8,128)(2,1)S(1)} collective-permute-done((bf16[50,2560]{1,0:T(8,128)(2,1)S(1)}, bf16[50,2560]{1,0:T(8,128)(2,1)S(1)}, u32[]{:S(2)}, u32[]{:S(2)}) %collective-permute-start.48) | collective-permute-done | bytes 256032 | tf_op jit(solution)/shard_map/ppermute | solution.py:21
  (378 shorter events, 127.8 us)
Async XLA Ops:
  7.2 252.1 %reduce-scatter.3.cloned.1.call-start = ((), (), s32[]{:S(2)}) async-start(), calls=%async_computation.2 | async-start | bytes 2949120 | tf_op jit(solution)/shard_map/reduce_scatter | solution.py:275
  15.6 24.6 %collective-permute-start.1 = (bf16[97,2560]{1,0:T(8,128)(2,1)S(1)}, bf16[97,2560]{1,0:T(8,128)(2,1)S(1)}, u32[]{:S(2)}, u32[]{:S(2)}) collective-permute-start(bf16[97,2560]{1,0:T(8,128)(2,1)S(1)} %get-tuple-element.49), channel_id=1, source_target_pairs={{0,4},{2,6},{4,0},{6,2},{1,5},{3,7},{5,1},{7,3},{8,12},{10,14},{12... | collective-permute-start | bytes 1489928 | tf_op jit(solution)/shard_map/ppermute | solution.py:27
  18.2 24.7 %collective-permute-start = (bf16[97,2560]{1,0:T(8,128)(2,1)S(1)}, bf16[97,2560]{1,0:T(8,128)(2,1)S(1)}, u32[]{:S(2)}, u32[]{:S(2)}) collective-permute-start(bf16[97,2560]{1,0:T(8,128)(2,1)S(1)} %get-tuple-element.49), channel_id=1, source_target_pairs={{0,2},{2,0},{4,6},{6,4},{1,3},{3,1},{5,7},{7,5},{8,10},{10,8},{12,... | collective-permute-start | bytes 1489928 | tf_op jit(solution)/shard_map/ppermute | solution.py:27
  19.7 24.0 %collective-permute-start.5 = (bf16[192,1280]{1,0:T(8,128)(2,1)}, bf16[192,1280]{1,0:T(8,128)(2,1)}, u32[]{:S(2)}, u32[]{:S(2)}) collective-permute-start(bf16[192,1280]{1,0:T(8,128)(2,1)} %bitcast.16), channel_id=1, source_target_pairs={{0,1},{1,0},{2,3},{3,2},{4,5},{5,4},{6,7},{7,6},{8,9},{9,8},{10,11... | collective-permute-start | bytes 1474568 | tf_op jit(solution)/shard_map/ppermute | solution.py:27
  19.7 35.5 %collective-permute-start.4 = (bf16[192,1280]{1,0:T(8,128)(2,1)}, bf16[192,1280]{1,0:T(8,128)(2,1)}, u32[]{:S(2)}, u32[]{:S(2)}) collective-permute-start(bf16[192,1280]{1,0:T(8,128)(2,1)} %bitcast.14), channel_id=1, source_target_pairs={{0,1},{1,0},{2,3},{3,2},{4,5},{5,4},{6,7},{7,6},{8,9},{9,8},{10,11... | collective-permute-start | bytes 1474568 | tf_op jit(solution)/shard_map/ppermute | solution.py:27
  20.2 40.7 %collective-permute-start.11 = (bf16[97,2560]{1,0:T(8,128)(2,1)}, bf16[97,2560]{1,0:T(8,128)(2,1)}, u32[]{:S(2)}, u32[]{:S(2)}) collective-permute-start(bf16[97,2560]{1,0:T(8,128)(2,1)} %get-tuple-element.50), channel_id=1, source_target_pairs={{0,8},{8,0},{1,9},{9,1},{2,10},{10,2},{3,11},{11,3},{4,12},{12,4},... | collective-permute-start | bytes 1489928 | tf_op jit(solution)/shard_map/ppermute | solution.py:21
  61.0 17.0 %collective-permute-start.13 = (bf16[97,2560]{1,0:T(8,128)(2,1)}, bf16[97,2560]{1,0:T(8,128)(2,1)S(1)}, u32[]{:S(2)}, u32[]{:S(2)}) collective-permute-start(bf16[97,2560]{1,0:T(8,128)(2,1)} %collective-permute-done.11), channel_id=1, source_target_pairs={{0,4},{2,6},{4,0},{6,2},{1,5},{3,7},{5,1},{7,3},{8,12},{10,14},{12... | collective-permute-start | bytes 1489928 | tf_op jit(solution)/shard_map/ppermute | solution.py:27
  63.0 15.2 %collective-permute-start.12 = (bf16[97,2560]{1,0:T(8,128)(2,1)}, bf16[97,2560]{1,0:T(8,128)(2,1)S(1)}, u32[]{:S(2)}, u32[]{:S(2)}) collective-permute-start(bf16[97,2560]{1,0:T(8,128)(2,1)} %collective-permute-done.11), channel_id=1, source_target_pairs={{0,2},{2,0},{4,6},{6,4},{1,3},{3,1},{5,7},{7,5},{8,10},{10,8},{12,... | collective-permute-start | bytes 1489928 | tf_op jit(solution)/shard_map/ppermute | solution.py:27
  63.1 18.3 %collective-permute-start.7 = (bf16[49,1280]{1,0:T(8,128)(2,1)S(1)}, bf16[49,1280]{1,0:T(8,128)(2,1)S(1)}, u32[]{:S(2)}, u32[]{:S(2)}) collective-permute-start(bf16[49,1280]{1,0:T(8,128)(2,1)S(1)} %get-tuple-element.79), channel_id=1, source_target_pairs={{0,2},{2,0},{4,6},{6,4},{1,3},{3,1},{5,7},{7,5},{8,10},{10,8},{12,... | collective-permute-start | bytes 376328 | tf_op jit(solution)/shard_map/ppermute | solution.py:27
  67.5 43.6 %collective-permute-start.10 = (bf16[49,2560]{1,0:T(8,128)(2,1)S(1)}, bf16[49,2560]{1,0:T(8,128)(2,1)}, u32[]{:S(2)}, u32[]{:S(2)}) collective-permute-start(bf16[49,2560]{1,0:T(8,128)(2,1)S(1)} %pad_maximum_fusion.20), channel_id=1, source_target_pairs={{0,2},{2,0},{4,6},{6,4},{1,3},{3,1},{5,7},{7,5},{8,10},{10,8},{12,... | collective-permute-start | bytes 752648 | tf_op jit(solution)/shard_map/ppermute | solution.py:27
  137.4 20.0 %collective-permute-start.21 = (bf16[64,2560]{1,0:T(8,128)(2,1)S(1)}, bf16[64,2560]{1,0:T(8,128)(2,1)S(1)}, u32[]{:S(2)}, u32[]{:S(2)}) collective-permute-start(bf16[64,2560]{1,0:T(8,128)(2,1)S(1)} %fusion.49), channel_id=1, source_target_pairs={{16,0},{17,1},{18,2},{19,3},{20,4},{21,5},{22,6},{23,7},{24,8},{25... | collective-permute-start | bytes 983048 | tf_op jit(solution)/shard_map/ppermute | solution.py:15
  139.6 13.9 %collective-permute-start.22 = (bf16[49,2560]{1,0:T(8,128)(2,1)S(1)}, bf16[49,2560]{1,0:T(8,128)(2,1)S(1)}, u32[]{:S(2)}, u32[]{:S(2)}) collective-permute-start(bf16[49,2560]{1,0:T(8,128)(2,1)S(1)} %get-tuple-element.62), channel_id=1, source_target_pairs={{0,2},{2,0},{4,6},{6,4},{1,3},{3,1},{5,7},{7,5},{8,10},{10,8},{12,... | collective-permute-start | bytes 752648 | tf_op jit(solution)/shard_map/ppermute | solution.py:27
  140.6 15.2 %collective-permute-start.34 = (bf16[49,2560]{1,0:T(8,128)(2,1)S(1)}, bf16[49,2560]{1,0:T(8,128)(2,1)S(1)}, u32[]{:S(2)}, u32[]{:S(2)}) collective-permute-start(bf16[49,2560]{1,0:T(8,128)(2,1)S(1)} %get-tuple-element.63), channel_id=1, source_target_pairs={{0,8},{8,0},{1,9},{9,1},{2,10},{10,2},{3,11},{11,3},{4,12},{12,4},... | collective-permute-start | bytes 752648 | tf_op jit(solution)/shard_map/ppermute | solution.py:21
  155.8 15.8 %collective-permute-start.36 = (bf16[49,2560]{1,0:T(8,128)(2,1)S(1)}, bf16[49,2560]{1,0:T(8,128)(2,1)S(1)}, u32[]{:S(2)}, u32[]{:S(2)}) collective-permute-start(bf16[49,2560]{1,0:T(8,128)(2,1)S(1)} %collective-permute-done.34), channel_id=1, source_target_pairs={{0,4},{2,6},{4,0},{6,2},{1,5},{3,7},{5,1},{7,3},{8,12},{10,14},{12... | collective-permute-start | bytes 752648 | tf_op jit(solution)/shard_map/ppermute | solution.py:27
  155.8 18.3 %collective-permute-start.35 = (bf16[49,2560]{1,0:T(8,128)(2,1)S(1)}, bf16[49,2560]{1,0:T(8,128)(2,1)S(1)}, u32[]{:S(2)}, u32[]{:S(2)}) collective-permute-start(bf16[49,2560]{1,0:T(8,128)(2,1)S(1)} %collective-permute-done.34), channel_id=1, source_target_pairs={{0,2},{2,0},{4,6},{6,4},{1,3},{3,1},{5,7},{7,5},{8,10},{10,8},{12,... | collective-permute-start | bytes 752648 | tf_op jit(solution)/shard_map/ppermute | solution.py:27
  158.6 17.5 %collective-permute-start.26 = (bf16[48,2560]{1,0:T(8,128)(2,1)}, bf16[48,2560]{1,0:T(8,128)(2,1)}, u32[]{:S(2)}, u32[]{:S(2)}) collective-permute-start(bf16[48,2560]{1,0:T(8,128)(2,1)} %get-tuple-element.66), channel_id=1, source_target_pairs={{0,2},{2,0},{4,6},{6,4},{1,3},{3,1},{5,7},{7,5},{8,10},{10,8},{12,... | collective-permute-start | bytes 737288 | tf_op jit(solution)/shard_map/ppermute | solution.py:27
  159.9 19.8 %collective-permute-start.27 = (bf16[48,2560]{1,0:T(8,128)(2,1)}, bf16[48,2560]{1,0:T(8,128)(2,1)}, u32[]{:S(2)}, u32[]{:S(2)}) collective-permute-start(bf16[48,2560]{1,0:T(8,128)(2,1)} %get-tuple-element.66), channel_id=1, source_target_pairs={{0,4},{2,6},{4,0},{6,2},{1,5},{3,7},{5,1},{7,3},{8,12},{10,14},{12... | collective-permute-start | bytes 737288 | tf_op jit(solution)/shard_map/ppermute | solution.py:27
  161.1 20.3 %collective-permute-start.39 = (bf16[48,2560]{1,0:T(8,128)(2,1)}, bf16[48,2560]{1,0:T(8,128)(2,1)}, u32[]{:S(2)}, u32[]{:S(2)}) collective-permute-start(bf16[48,2560]{1,0:T(8,128)(2,1)} %get-tuple-element.65), channel_id=1, source_target_pairs={{0,8},{8,0},{1,9},{9,1},{2,10},{10,2},{3,11},{11,3},{4,12},{12,4},... | collective-permute-start | bytes 737288 | tf_op jit(solution)/shard_map/ppermute | solution.py:21
  181.4 15.3 %collective-permute-start.41 = (bf16[48,2560]{1,0:T(8,128)(2,1)}, bf16[48,2560]{1,0:T(8,128)(2,1)}, u32[]{:S(2)}, u32[]{:S(2)}) collective-permute-start(bf16[48,2560]{1,0:T(8,128)(2,1)} %collective-permute-done.39), channel_id=1, source_target_pairs={{0,4},{2,6},{4,0},{6,2},{1,5},{3,7},{5,1},{7,3},{8,12},{10,14},{12... | collective-permute-start | bytes 737288 | tf_op jit(solution)/shard_map/ppermute | solution.py:27
  181.5 16.5 %collective-permute-start.40 = (bf16[48,2560]{1,0:T(8,128)(2,1)}, bf16[48,2560]{1,0:T(8,128)(2,1)}, u32[]{:S(2)}, u32[]{:S(2)}) collective-permute-start(bf16[48,2560]{1,0:T(8,128)(2,1)} %collective-permute-done.39), channel_id=1, source_target_pairs={{0,2},{2,0},{4,6},{6,4},{1,3},{3,1},{5,7},{7,5},{8,10},{10,8},{12,... | collective-permute-start | bytes 737288 | tf_op jit(solution)/shard_map/ppermute | solution.py:27
  201.6 14.8 %collective-permute-start.32 = (bf16[49,1280]{1,0:T(8,128)(2,1)}, bf16[49,1280]{1,0:T(8,128)(2,1)}, u32[]{:S(2)}, u32[]{:S(2)}) collective-permute-start(bf16[49,1280]{1,0:T(8,128)(2,1)} %get-tuple-element.76), channel_id=1, source_target_pairs={{0,4},{2,6},{4,0},{6,2},{1,5},{3,7},{5,1},{7,3},{8,12},{10,14},{12... | collective-permute-start | bytes 376328 | tf_op jit(solution)/shard_map/ppermute | solution.py:27
  212.8 48.8 %reduce-scatter.5.cloned.1.call-start = ((), (), s32[]{:S(2)}) async-start(), calls=%async_computation.3 | async-start | bytes 1474560 | tf_op jit(solution)/shard_map/reduce_scatter | solution.py:278
  217.4 19.3 %collective-permute-start.33 = (bf16[49,2560]{1,0:T(8,128)(2,1)S(1)}, bf16[49,2560]{1,0:T(8,128)(2,1)}, u32[]{:S(2)}, u32[]{:S(2)}) collective-permute-start(bf16[49,2560]{1,0:T(8,128)(2,1)S(1)} %pad_maximum_fusion.25), channel_id=1, source_target_pairs={{0,2},{2,0},{4,6},{6,4},{1,3},{3,1},{5,7},{7,5},{8,10},{10,8},{12,... | collective-permute-start | bytes 752648 | tf_op jit(solution)/shard_map/ppermute | solution.py:27
  221.1 15.6 %collective-permute-start.31 = (bf16[49,2560]{1,0:T(8,128)(2,1)}, bf16[49,2560]{1,0:T(8,128)(2,1)}, u32[]{:S(2)}, u32[]{:S(2)}) collective-permute-start(bf16[49,2560]{1,0:T(8,128)(2,1)} %pad_maximum_fusion.24), channel_id=1, source_target_pairs={{0,4},{2,6},{4,0},{6,2},{1,5},{3,7},{5,1},{7,3},{8,12},{10,14},{12... | collective-permute-start | bytes 752648 | tf_op jit(solution)/shard_map/ppermute | solution.py:27
  (94 other events, 583.8 us)
Sparse Core Ops, SparseCore 0:
  212.9 10.7 reduce-scatter.2
  231.0 8.1 reduce-scatter.4

commit v9 on v6

--- a/solution.py
+++ b/solution.py
@@ -128,17 +128,9 @@
     pick_count = expert_ids.shape[3]
     capacity = max(2, 3 * token_rows * pick_count // (2 * groups))
     slot_count = groups * capacity
-    low_half = lax.axis_index("dp") == 0
 
     def whole_rows(stored):
-        if lax.axis_size("dp") != 2:
-            return lax.all_gather(stored, "dp", axis=1, tiled=True)
-        partner = flipped(stored, "dp", 1)
-        return jnp.where(
-            low_half,
-            jnp.concatenate([stored, partner], axis=1),
-            jnp.concatenate([partner, stored], axis=1),
-        )
+        return lax.all_gather(stored, "dp", axis=1, tiled=True)
 
     gate_full, up_full, down_full = (
         whole_rows(gate_weight[0]),

time: 239 us -> 250 us (1.046)
  starting transfers between devices: 64.1 us -> 54.6 us
  blocking collectives: 0 us -> 7.62 us
  waiting for transfers between devices: 106 us -> 113 us
  local copies, waits for them, and re-layouts: 14.2 us -> 17.3 us
    ppermute x10, waiting for transfers between devices: 39.6 us -> 55.5 us  [rotated(): return lax.ppermute(block, axis, route)]
    ppermute x39 -> x36, waiting for transfers between devices: 66.6 us -> 57.9 us  [flipped(): return lax.ppermute(block, axis, route)]
    ppermute x39 -> x36, starting transfers between devices: 43.7 us -> 36 us  [flipped(): return lax.ppermute(block, axis, route)]
    all_gather x0 -> x3, blocking collectives: none -> 7.62 us  [whole_rows(): return lax.all_gather(stored, 'dp', axis=1, tiled=True)]
    another operation x12, other arithmetic: 5.08 us -> 8.6 us  [gather_quad(): return jnp.stack([staged, first, second, diagonal])]
  transfers between devices with their start and end apart: 52 -> 49, of which waited for: 26 -> 22; matrix products, arithmetic and copies ran while one was open for 17% -> 17% of each run, Pallas kernels for 0% -> 0%
where the time goes in v9:
time: 250 us; the launch traced here: 249 us
  waiting for transfers between devices  113 us (45%)
  starting transfers between devices  54.6 us (22%)
  other arithmetic  25 us (10%)
  local copies, waits for them, and re-layouts  17.3 us (7%)
  matrix products  16.1 us (6%)
  between operations  15 us (6%)
  blocking collectives  7.62 us (3%)
    ppermute x36, waiting for transfers between devices, flipped(): return lax.ppermute(block, axis, route)  57.9 us
    ppermute x10, waiting for transfers between devices, rotated(): return lax.ppermute(block, axis, route)  55.5 us
    ppermute x36, starting transfers between devices, flipped(): return lax.ppermute(block, axis, route)  36 us
    ppermute x10, starting transfers between devices, rotated(): return lax.ppermute(block, axis, route)  17 us
    another operation x12, other arithmetic, gather_quad(): return jnp.stack([staged, first, second, diagonal])  8.6 us
    all_gather x3, blocking collectives, whole_rows(): return lax.all_gather(stored, 'dp', axis=1, tiled=True)  7.62 us
    dot_general x6, matrix products, contract_last(): lax.dot_general(first_operand, second_operand, (((1,), (1,)), ((), ())),...  6.27 us
  transfers between devices with their start and end apart: 49, of which 22 were waited for; matrix products, arithmetic and copies ran while one was open for 17% of the time, Pallas kernels for 0%

profile of v9, /device:TPU:0, one launch (start us, length us, event | category | flops | bytes accessed | tf_op | source)
XLA Modules:
  0.0 249.0 jit_solution(13140338831935796091)
XLA Ops:
  10.3 4.0 %collective-permute-start = (bf16[48]{0:T(256)(128)(2,1)S(1)}, bf16[48]{0:T(256)(128)(2,1)S(1)}, u32[]{:S(2)}, u32[]{:S(2)}) collective-permute-start(bf16[48]{0:T(256)(128)(2,1)S(1)} %get-tuple-element.95), channel_id=1, source_target_pairs={{0,8},{8,0},{1,9},{9,1},{2,10},{10,2},{3,11},{11,3},{4,12},{12,4},... | collective-permute-start | bytes 296 | tf_op jit(solution)/shard_map/ppermute | solution.py:21
  17.4 3.0 %collective-permute-start.9 = (bf16[48,2560]{1,0:T(8,128)(2,1)S(1)}, bf16[48,2560]{1,0:T(8,128)(2,1)S(1)}, u32[]{:S(2)}, u32[]{:S(2)}) collective-permute-start(bf16[48,2560]{1,0:T(8,128)(2,1)S(1)} %get-tuple-element.65), channel_id=1, source_target_pairs={{0,8},{8,0},{1,9},{9,1},{2,10},{10,2},{3,11},{11,3},{4,12},{12,4},... | collective-permute-start | bytes 737288 | tf_op jit(solution)/shard_map/ppermute | solution.py:21
  20.3 2.5 %all-gather.2 = bf16[1,192,2560]{2,1,0:T(8,128)(2,1)S(1)} all-gather(bf16[1,192,1280]{2,1,0:T(8,128)(2,1)S(1)} %copy-done.24), channel_id=4, replica_groups=mesh['pipe'=2,'eg'=2,'ej'=4,'dp'=2] {'dp'}, dimensions={2}, use_global_device_ids=true | all-gather | bytes 1474560 | tf_op jit(solution)/shard_map/all_gather | solution.py:133
  22.8 18.1 %collective-permute-done.9 = bf16[48,2560]{1,0:T(8,128)(2,1)S(1)} collective-permute-done((bf16[48,2560]{1,0:T(8,128)(2,1)S(1)}, bf16[48,2560]{1,0:T(8,128)(2,1)S(1)}, u32[]{:S(2)}, u32[]{:S(2)}) %collective-permute-start.9) | collective-permute-done | bytes 245792 | tf_op jit(solution)/shard_map/ppermute | solution.py:21
  42.6 2.5 %all-gather.1 = bf16[1,192,2560]{2,1,0:T(8,128)(2,1)S(1)} all-gather(bf16[1,192,1280]{2,1,0:T(8,128)(2,1)S(1)} %copy-done.25), channel_id=3, replica_groups=mesh['pipe'=2,'eg'=2,'ej'=4,'dp'=2] {'dp'}, dimensions={2}, use_global_device_ids=true | all-gather | bytes 1474560 | tf_op jit(solution)/shard_map/all_gather | solution.py:133
  50.0 5.3 %collective-permute-done.10 = bf16[2,48,2560]{2,1,0:T(8,128)(2,1)S(1)} collective-permute-done((bf16[2,48,2560]{2,1,0:T(8,128)(2,1)S(1)}, bf16[2,48,2560]{2,1,0:T(8,128)(2,1)S(1)}, u32[]{:S(2)}, u32[]{:S(2)}) %collective-permute-start.10) | collective-permute-done | bytes 491552 | tf_op jit(solution)/shard_map/ppermute | solution.py:27
  58.3 9.1 %collective-permute-done.2 = bf16[2,48]{1,0:T(2,128)(2,1)S(1)} collective-permute-done((bf16[2,48]{1,0:T(2,128)(2,1)S(1)}, bf16[2,48]{1,0:T(2,128)(2,1)S(1)}, u32[]{:S(2)}, u32[]{:S(2)}) %collective-permute-start.2) | collective-permute-done | bytes 224 | tf_op jit(solution)/shard_map/ppermute | solution.py:27
  67.9 2.6 %all-gather = bf16[1,192,2560]{2,1,0:T(8,128)(2,1)} all-gather(bf16[1,192,1280]{2,1,0:T(8,128)(2,1)S(1)} %copy-done.26), channel_id=2, replica_groups=mesh['pipe'=2,'eg'=2,'ej'=4,'dp'=2] {'dp'}, dimensions={2}, use_global_device_ids=true | all-gather | bytes 1474560 | tf_op jit(solution)/shard_map/all_gather | solution.py:133
  71.5 3.5 %collective-permute-done.3 = bf16[2,48]{1,0:T(2,128)(2,1)S(1)} collective-permute-done((bf16[2,48]{1,0:T(2,128)(2,1)S(1)}, bf16[2,48]{1,0:T(2,128)(2,1)S(1)}, u32[]{:S(2)}, u32[]{:S(2)}) %collective-permute-start.3) | collective-permute-done | bytes 224 | tf_op jit(solution)/shard_map/ppermute | solution.py:27
  90.6 4.4 %collective-permute-done.20 = bf16[48]{0:T(256)(128)(2,1)S(1)} collective-permute-done((bf16[48]{0:T(256)(128)(2,1)S(1)}, bf16[48]{0:T(256)(128)(2,1)S(1)}, u32[]{:S(2)}, u32[]{:S(2)}) %collective-permute-start.20) | collective-permute-done | bytes 128 | tf_op jit(solution)/shard_map/ppermute | solution.py:21
  98.6 6.0 %collective-permute-done.14 = bf16[2,48,1280]{2,1,0:T(8,128)(2,1)S(1)} collective-permute-done((bf16[2,48,1280]{2,1,0:T(8,128)(2,1)S(1)}, bf16[2,48,1280]{2,1,0:T(8,128)(2,1)S(1)}, u32[]{:S(2)}, u32[]{:S(2)}) %collective-permute-start.14) | collective-permute-done | bytes 245792 | tf_op jit(solution)/shard_map/ppermute | solution.py:27
  110.7 4.7 %collective-permute-done.41 = bf16[2,48]{1,0:T(2,128)(2,1)S(1)} collective-permute-done((bf16[2,48]{1,0:T(2,128)(2,1)S(1)}, bf16[2,48]{1,0:T(2,128)(2,1)S(1)}, u32[]{:S(2)}, u32[]{:S(2)}) %collective-permute-start.41) | collective-permute-done | bytes 224 | tf_op jit(solution)/shard_map/ppermute | solution.py:27
  115.4 2.3 collective-permute-start.22
  124.6 11.0 %collective-permute-done.18 = bf16[48,2560]{1,0:T(8,128)(2,1)S(1)} collective-permute-done((bf16[48,2560]{1,0:T(8,128)(2,1)S(1)}, bf16[48,2560]{1,0:T(8,128)(2,1)S(1)}, u32[]{:S(2)}, u32[]{:S(2)}) %collective-permute-start.18) | collective-permute-done | bytes 245792 | tf_op jit(solution)/shard_map/ppermute | solution.py:21
  139.7 12.7 %collective-permute-done.29 = bf16[48,2560]{1,0:T(8,128)(2,1)S(1)} collective-permute-done((bf16[48,2560]{1,0:T(8,128)(2,1)S(1)}, bf16[48,2560]{1,0:T(8,128)(2,1)S(1)}, u32[]{:S(2)}, u32[]{:S(2)}) %collective-permute-start.29) | collective-permute-done | bytes 245792 | tf_op jit(solution)/shard_map/ppermute | solution.py:21
  154.9 2.3 collective-permute-start.24
  158.8 8.8 %collective-permute-done.21 = bf16[2,48]{1,0:T(2,128)(2,1)S(1)} collective-permute-done((bf16[2,48]{1,0:T(2,128)(2,1)}, bf16[2,48]{1,0:T(2,128)(2,1)S(1)}, u32[]{:S(2)}, u32[]{:S(2)}) %collective-permute-start.21) | collective-permute-done | bytes 224 | tf_op jit(solution)/shard_map/ppermute | solution.py:27
  167.6 3.4 %collective-permute-done.23 = bf16[2,48]{1,0:T(2,128)(2,1)S(1)} collective-permute-done((bf16[2,48]{1,0:T(2,128)(2,1)}, bf16[2,48]{1,0:T(2,128)(2,1)S(1)}, u32[]{:S(2)}, u32[]{:S(2)}) %collective-permute-start.23) | collective-permute-done | bytes 224 | tf_op jit(solution)/shard_map/ppermute | solution.py:27
  182.4 3.1 %collective-permute-done.25 = bf16[2,48,2560]{2,1,0:T(8,128)(2,1)S(1)} collective-permute-done((bf16[2,48,2560]{2,1,0:T(8,128)(2,1)S(1)}, bf16[2,48,2560]{2,1,0:T(8,128)(2,1)S(1)}, u32[]{:S(2)}, u32[]{:S(2)}) %collective-permute-start.25) | collective-permute-done | bytes 491552 | tf_op jit(solution)/shard_map/ppermute | solution.py:27
  188.4 5.5 %collective-permute-done.27 = bf16[2,48,1280]{2,1,0:T(8,128)(2,1)S(1)} collective-permute-done((bf16[2,48,1280]{2,1,0:T(8,128)(2,1)S(1)}, bf16[2,48,1280]{2,1,0:T(8,128)(2,1)S(1)}, u32[]{:S(2)}, u32[]{:S(2)}) %collective-permute-start.27) | collective-permute-done | bytes 245792 | tf_op jit(solution)/shard_map/ppermute | solution.py:27
  196.7 3.0 %convolution_convert_fusion = bf16[384,2560]{1,0:T(8,128)(2,1)} fusion(bf16[384,2560]{1,0:T(8,128)(2,1)S(1)} %bitcast.242, bf16[384,2560]{1,0:T(8,128)(2,1)S(1)} %bitcast.236, bf16[384,192]{0,1:T(8,128)(2,1)S(1)} %get-tuple-element.49, bf16[384,192]{0,1:T(8,128)(2,1)S(1)} %get-tuple-element.43, bf16[384,192]{0,1:T(8,128)(2,1)S(1)} %copy-done.30, ...), kind=kOutput, calls=%fused_computation.4 | convolution fusion | flops 1521156096 | bytes 6488064 | tf_op jit(solution)/shard_map/dot_general | solution.py:42
  222.0 2.6 %collective-permute-done.46 = f32[48]{0:T(128)S(1)} collective-permute-done((f32[48]{0:T(128)S(1)}, f32[48]{0:T(128)S(1)}, u32[]{:S(2)}, u32[]{:S(2)}) %collective-permute-start.46) | collective-permute-done | bytes 224 | tf_op jit(solution)/shard_map/ppermute | solution.py:21
  226.6 2.4 collective-permute-start.38
  229.6 6.8 %collective-permute-done.38 = bf16[48,2560]{1,0:T(8,128)(2,1)S(1)} collective-permute-done((bf16[48,2560]{1,0:T(8,128)(2,1)S(1)}, bf16[48,2560]{1,0:T(8,128)(2,1)S(1)}, u32[]{:S(2)}, u32[]{:S(2)}) %collective-permute-start.38) | collective-permute-done | bytes 245792 | tf_op jit(solution)/shard_map/ppermute | solution.py:21
  (304 shorter events, 104.4 us)
Async XLA Ops:
  7.2 232.8 %reduce-scatter.3.cloned.1.call-start = ((), (), s32[]{:S(2)}) async-start(), calls=%async_computation.2 | async-start | bytes 2949120 | tf_op jit(solution)/shard_map/reduce_scatter | solution.py:247
  10.3 39.5 %collective-permute-start = (bf16[48]{0:T(256)(128)(2,1)S(1)}, bf16[48]{0:T(256)(128)(2,1)S(1)}, u32[]{:S(2)}, u32[]{:S(2)}) collective-permute-start(bf16[48]{0:T(256)(128)(2,1)S(1)} %get-tuple-element.95), channel_id=1, source_target_pairs={{0,8},{8,0},{1,9},{9,1},{2,10},{10,2},{3,11},{11,3},{4,12},{12,4},... | collective-permute-start | bytes 296 | tf_op jit(solution)/shard_map/ppermute | solution.py:21
  16.6 28.5 %collective-permute-start.4 = (bf16[48,2560]{1,0:T(8,128)(2,1)}, bf16[48,2560]{1,0:T(8,128)(2,1)}, u32[]{:S(2)}, u32[]{:S(2)}) collective-permute-start(bf16[48,2560]{1,0:T(8,128)(2,1)} %get-tuple-element.69), channel_id=1, source_target_pairs={{0,8},{8,0},{1,9},{9,1},{2,10},{10,2},{3,11},{11,3},{4,12},{12,4},... | collective-permute-start | bytes 737288 | tf_op jit(solution)/shard_map/ppermute | solution.py:21
  17.4 23.6 %collective-permute-start.9 = (bf16[48,2560]{1,0:T(8,128)(2,1)S(1)}, bf16[48,2560]{1,0:T(8,128)(2,1)S(1)}, u32[]{:S(2)}, u32[]{:S(2)}) collective-permute-start(bf16[48,2560]{1,0:T(8,128)(2,1)S(1)} %get-tuple-element.65), channel_id=1, source_target_pairs={{0,8},{8,0},{1,9},{9,1},{2,10},{10,2},{3,11},{11,3},{4,12},{12,4},... | collective-permute-start | bytes 737288 | tf_op jit(solution)/shard_map/ppermute | solution.py:21
  41.0 14.2 %collective-permute-start.10 = (bf16[2,48,2560]{2,1,0:T(8,128)(2,1)S(1)}, bf16[2,48,2560]{2,1,0:T(8,128)(2,1)S(1)}, u32[]{:S(2)}, u32[]{:S(2)}) collective-permute-start(bf16[2,48,2560]{2,1,0:T(8,128)(2,1)S(1)} %get-tuple-element.63), channel_id=1, source_target_pairs={{0,2},{2,0},{4,6},{6,4},{1,3},{3,1},{5,7},{7,5},{8,10},{10,8},{12,... | collective-permute-start | bytes 1474568 | tf_op jit(solution)/shard_map/ppermute | solution.py:27
  42.6 14.2 %collective-permute-start.11 = (bf16[2,48,2560]{2,1,0:T(8,128)(2,1)S(1)}, bf16[2,48,2560]{2,1,0:T(8,128)(2,1)S(1)}, u32[]{:S(2)}, u32[]{:S(2)}) collective-permute-start(bf16[2,48,2560]{2,1,0:T(8,128)(2,1)S(1)} %get-tuple-element.63), channel_id=1, source_target_pairs={{0,4},{2,6},{4,0},{6,2},{1,5},{3,7},{5,1},{7,3},{8,12},{10,14},{12... | collective-permute-start | bytes 1474568 | tf_op jit(solution)/shard_map/ppermute | solution.py:27
  47.3 27.8 %collective-permute-start.5 = (bf16[2,48,2560]{2,1,0:T(8,128)(2,1)}, bf16[2,48,2560]{2,1,0:T(8,128)(2,1)}, u32[]{:S(2)}, u32[]{:S(2)}) collective-permute-start(bf16[2,48,2560]{2,1,0:T(8,128)(2,1)} %get-tuple-element.67), channel_id=1, source_target_pairs={{0,2},{2,0},{4,6},{6,4},{1,3},{3,1},{5,7},{7,5},{8,10},{10,8},{12,... | collective-permute-start | bytes 1474568 | tf_op jit(solution)/shard_map/ppermute | solution.py:27
  47.8 28.4 %collective-permute-start.6 = (bf16[2,48,2560]{2,1,0:T(8,128)(2,1)}, bf16[2,48,2560]{2,1,0:T(8,128)(2,1)}, u32[]{:S(2)}, u32[]{:S(2)}) collective-permute-start(bf16[2,48,2560]{2,1,0:T(8,128)(2,1)} %get-tuple-element.67), channel_id=1, source_target_pairs={{0,4},{2,6},{4,0},{6,2},{1,5},{3,7},{5,1},{7,3},{8,12},{10,14},{12... | collective-permute-start | bytes 1474568 | tf_op jit(solution)/shard_map/ppermute | solution.py:27
  49.9 17.5 %collective-permute-start.2 = (bf16[2,48]{1,0:T(2,128)(2,1)S(1)}, bf16[2,48]{1,0:T(2,128)(2,1)S(1)}, u32[]{:S(2)}, u32[]{:S(2)}) collective-permute-start(bf16[2,48]{1,0:T(2,128)(2,1)S(1)} %pad_maximum_fusion.19), channel_id=1, source_target_pairs={{0,4},{2,6},{4,0},{6,2},{1,5},{3,7},{5,1},{7,3},{8,12},{10,14},{12... | collective-permute-start | bytes 584 | tf_op jit(solution)/shard_map/ppermute | solution.py:27
  55.3 15.3 %collective-permute-start.1 = (bf16[2,48]{1,0:T(2,128)(2,1)S(1)}, bf16[2,48]{1,0:T(2,128)(2,1)S(1)}, u32[]{:S(2)}, u32[]{:S(2)}) collective-permute-start(bf16[2,48]{1,0:T(2,128)(2,1)S(1)} %pad_maximum_fusion.19), channel_id=1, source_target_pairs={{0,2},{2,0},{4,6},{6,4},{1,3},{3,1},{5,7},{7,5},{8,10},{10,8},{12,... | collective-permute-start | bytes 584 | tf_op jit(solution)/shard_map/ppermute | solution.py:27
  56.8 22.0 %collective-permute-start.12 = (bf16[2,48,1280]{2,1,0:T(8,128)(2,1)S(1)}, bf16[2,48,1280]{2,1,0:T(8,128)(2,1)}, u32[]{:S(2)}, u32[]{:S(2)}) collective-permute-start(bf16[2,48,1280]{2,1,0:T(8,128)(2,1)S(1)} %slice.376), channel_id=1, source_target_pairs={{0,4},{2,6},{4,0},{6,2},{1,5},{3,7},{5,1},{7,3},{8,12},{10,14},{12... | collective-permute-start | bytes 737288 | tf_op jit(solution)/shard_map/ppermute | solution.py:27
  67.4 11.4 %collective-permute-start.13 = (bf16[2,48,1280]{2,1,0:T(8,128)(2,1)}, bf16[2,48,1280]{2,1,0:T(8,128)(2,1)}, u32[]{:S(2)}, u32[]{:S(2)}) collective-permute-start(bf16[2,48,1280]{2,1,0:T(8,128)(2,1)} %slice.377), channel_id=1, source_target_pairs={{0,2},{2,0},{4,6},{6,4},{1,3},{3,1},{5,7},{7,5},{8,10},{10,8},{12,... | collective-permute-start | bytes 737288 | tf_op jit(solution)/shard_map/ppermute | solution.py:27
  98.0 21.5 %collective-permute-start.17 = (bf16[2,48,2560]{2,1,0:T(8,128)(2,1)}, bf16[2,48,2560]{2,1,0:T(8,128)(2,1)S(1)}, u32[]{:S(2)}, u32[]{:S(2)}) collective-permute-start(bf16[2,48,2560]{2,1,0:T(8,128)(2,1)} %pad_maximum_fusion.12), channel_id=1, source_target_pairs={{0,2},{2,0},{4,6},{6,4},{1,3},{3,1},{5,7},{7,5},{8,10},{10,8},{12,... | collective-permute-start | bytes 1474568 | tf_op jit(solution)/shard_map/ppermute | solution.py:27
  105.4 14.0 %collective-permute-start.15 = (bf16[2,48,2560]{2,1,0:T(8,128)(2,1)}, bf16[2,48,2560]{2,1,0:T(8,128)(2,1)S(1)}, u32[]{:S(2)}, u32[]{:S(2)}) collective-permute-start(bf16[2,48,2560]{2,1,0:T(8,128)(2,1)} %pad_maximum_fusion.11), channel_id=1, source_target_pairs={{0,4},{2,6},{4,0},{6,2},{1,5},{3,7},{5,1},{7,3},{8,12},{10,14},{12... | collective-permute-start | bytes 1474568 | tf_op jit(solution)/shard_map/ppermute | solution.py:27
  115.4 43.2 %collective-permute-start.22 = (bf16[2,48]{1,0:T(2,128)(2,1)}, bf16[2,48]{1,0:T(2,128)(2,1)}, u32[]{:S(2)}, u32[]{:S(2)}) collective-permute-start(bf16[2,48]{1,0:T(2,128)(2,1)} %pad_maximum_fusion.20), channel_id=1, source_target_pairs={{0,4},{2,6},{4,0},{6,2},{1,5},{3,7},{5,1},{7,3},{8,12},{10,14},{12... | collective-permute-start | bytes 584 | tf_op jit(solution)/shard_map/ppermute | solution.py:27
  121.9 13.7 %collective-permute-start.18 = (bf16[48,2560]{1,0:T(8,128)(2,1)S(1)}, bf16[48,2560]{1,0:T(8,128)(2,1)S(1)}, u32[]{:S(2)}, u32[]{:S(2)}) collective-permute-start(bf16[48,2560]{1,0:T(8,128)(2,1)S(1)} %fusion.71), channel_id=1, source_target_pairs={{0,8},{8,0},{1,9},{9,1},{2,10},{10,2},{3,11},{11,3},{4,12},{12,4},... | collective-permute-start | bytes 737288 | tf_op jit(solution)/shard_map/ppermute | solution.py:21
  137.7 14.6 %collective-permute-start.29 = (bf16[48,2560]{1,0:T(8,128)(2,1)S(1)}, bf16[48,2560]{1,0:T(8,128)(2,1)S(1)}, u32[]{:S(2)}, u32[]{:S(2)}) collective-permute-start(bf16[48,2560]{1,0:T(8,128)(2,1)S(1)} %get-tuple-element.55), channel_id=1, source_target_pairs={{0,8},{8,0},{1,9},{9,1},{2,10},{10,2},{3,11},{11,3},{4,12},{12,4},... | collective-permute-start | bytes 737288 | tf_op jit(solution)/shard_map/ppermute | solution.py:21
  138.2 15.5 %collective-permute-start.19 = (bf16[64,2560]{1,0:T(8,128)(2,1)S(1)}, bf16[64,2560]{1,0:T(8,128)(2,1)S(1)}, u32[]{:S(2)}, u32[]{:S(2)}) collective-permute-start(bf16[64,2560]{1,0:T(8,128)(2,1)S(1)} %fusion.36), channel_id=1, source_target_pairs={{16,0},{17,1},{18,2},{19,3},{20,4},{21,5},{22,6},{23,7},{24,8},{25... | collective-permute-start | bytes 983048 | tf_op jit(solution)/shard_map/ppermute | solution.py:15
  153.2 19.1 %collective-permute-start.30 = (bf16[2,48,2560]{2,1,0:T(8,128)(2,1)}, bf16[2,48,2560]{2,1,0:T(8,128)(2,1)S(1)}, u32[]{:S(2)}, u32[]{:S(2)}) collective-permute-start(bf16[2,48,2560]{2,1,0:T(8,128)(2,1)} %get-tuple-element.53), channel_id=1, source_target_pairs={{0,2},{2,0},{4,6},{6,4},{1,3},{3,1},{5,7},{7,5},{8,10},{10,8},{12,... | collective-permute-start | bytes 1474568 | tf_op jit(solution)/shard_map/ppermute | solution.py:27
  153.8 19.2 %collective-permute-start.31 = (bf16[2,48,2560]{2,1,0:T(8,128)(2,1)}, bf16[2,48,2560]{2,1,0:T(8,128)(2,1)}, u32[]{:S(2)}, u32[]{:S(2)}) collective-permute-start(bf16[2,48,2560]{2,1,0:T(8,128)(2,1)} %get-tuple-element.53), channel_id=1, source_target_pairs={{0,4},{2,6},{4,0},{6,2},{1,5},{3,7},{5,1},{7,3},{8,12},{10,14},{12... | collective-permute-start | bytes 1474568 | tf_op jit(solution)/shard_map/ppermute | solution.py:27
  154.9 19.8 %collective-permute-start.24 = (bf16[48,2560]{1,0:T(8,128)(2,1)}, bf16[48,2560]{1,0:T(8,128)(2,1)}, u32[]{:S(2)}, u32[]{:S(2)}) collective-permute-start(bf16[48,2560]{1,0:T(8,128)(2,1)} %get-tuple-element.59), channel_id=1, source_target_pairs={{0,8},{8,0},{1,9},{9,1},{2,10},{10,2},{3,11},{11,3},{4,12},{12,4},... | collective-permute-start | bytes 737288 | tf_op jit(solution)/shard_map/ppermute | solution.py:21
  158.6 12.4 %collective-permute-start.23 = (bf16[2,48]{1,0:T(2,128)(2,1)}, bf16[2,48]{1,0:T(2,128)(2,1)S(1)}, u32[]{:S(2)}, u32[]{:S(2)}) collective-permute-start(bf16[2,48]{1,0:T(2,128)(2,1)} %pad_maximum_fusion.20), channel_id=1, source_target_pairs={{0,6},{2,4},{4,2},{6,0},{1,7},{3,5},{5,3},{7,1},{8,14},{10,12},{12... | collective-permute-start | bytes 584 | tf_op jit(solution)/shard_map/ppermute | solution.py:27
  199.7 42.4 %reduce-scatter.5.cloned.1.call-start = ((), (), s32[]{:S(2)}) async-start(), calls=%async_computation.3 | async-start | bytes 1474560 | tf_op jit(solution)/shard_map/reduce_scatter | solution.py:250
  213.8 11.6 %collective-permute-start.37 = (bf16[2,48,2560]{2,1,0:T(8,128)(2,1)S(1)}, bf16[2,48,2560]{2,1,0:T(8,128)(2,1)S(1)}, u32[]{:S(2)}, u32[]{:S(2)}) collective-permute-start(bf16[2,48,2560]{2,1,0:T(8,128)(2,1)S(1)} %pad_maximum_fusion.16), channel_id=1, source_target_pairs={{0,2},{2,0},{4,6},{6,4},{1,3},{3,1},{5,7},{7,5},{8,10},{10,8},{12,... | collective-permute-start | bytes 1474568 | tf_op jit(solution)/shard_map/ppermute | solution.py:27
  (75 other events, 664.8 us)
Sparse Core Ops, SparseCore 0:
  199.8 8.5 reduce-scatter.2
  222.1 7.0 reduce-scatter.4

commit v10 on v6

--- a/solution.py
+++ b/solution.py
@@ -176,12 +176,16 @@
         return picked.astype(jnp.bfloat16).reshape(groups, capacity, feature_count)
 
     prepared = [prepare(moment) for moment in range(micro_count)]
-    rows_gathered = [
-        gather_quad(dispatch_rows(current[4], current[2])) for current in prepared
-    ]
-    weights_gathered = [
-        gather_quad(current[6].reshape(groups, capacity)) for current in prepared
-    ]
+    first_incoming = jnp.where(is_last, output_grads[0], entry_grads[0])
+    first_grads = gather_quad(dispatch_rows(prepared[0][4], first_incoming))
+    rows_gathered = [gather_quad(dispatch_rows(prepared[0][4], prepared[0][2]))]
+    weights_gathered = [gather_quad(prepared[0][6].reshape(groups, capacity))]
+    for current in prepared[1:]:
+        later_rows, later_weights, _ = lax.optimization_barrier(
+            (dispatch_rows(current[4], current[2]), current[6], first_grads)
+        )
+        rows_gathered.append(gather_quad(later_rows))
+        weights_gathered.append(gather_quad(later_weights.reshape(groups, capacity)))
     leaving_list = []
     combine_list = []
     kept_list = []
@@ -189,11 +193,12 @@
     for moment in range(micro_count):
         current = prepared[moment]
         if moment == 0:
-            arriving = entry_grads[0]
+            incoming = first_incoming
+            grads_in = first_grads
         else:
             arriving = shifted(previous, "pipe", -1)
-        incoming = jnp.where(is_last, output_grads[moment], arriving)
-        grads_in = gather_quad(dispatch_rows(current[4], incoming))
+            incoming = jnp.where(is_last, output_grads[moment], arriving)
+            grads_in = gather_quad(dispatch_rows(current[4], incoming))
         flat_rows = rows_gathered[moment].reshape(-1, feature_count)
         flat_grads = grads_in.reshape(-1, feature_count)
         scale_column = weights_gathered[moment].reshape(-1, 1).astype(jnp.float32)

time: 239 us -> 238 us (level)
  starting transfers between devices: 64.1 us -> 55 us
  waiting for transfers between devices: 106 us -> 115 us
    ppermute x39, waiting for transfers between devices: 66.6 us -> 76.3 us  [flipped(): return lax.ppermute(block, axis, route)]
    ppermute x39, starting transfers between devices: 43.7 us -> 36.3 us  [flipped(): return lax.ppermute(block, axis, route)]
  transfers between devices with their start and end apart: 52 -> 52, of which waited for: 26 -> 26; matrix products, arithmetic and copies ran while one was open for 17% -> 16% of each run, Pallas kernels for 0% -> 0%
where the time goes in v10:
time: 238 us; the launch traced here: 237 us
  waiting for transfers between devices  115 us (48%)
  starting transfers between devices  55 us (23%)
  other arithmetic  22 us (9%)
  matrix products  16.1 us (7%)
  between operations  14.9 us (6%)
  local copies, waits for them, and re-layouts  14.2 us (6%)
    ppermute x39, waiting for transfers between devices, flipped(): return lax.ppermute(block, axis, route)  76.3 us
    ppermute x10, waiting for transfers between devices, rotated(): return lax.ppermute(block, axis, route)  38.7 us
    ppermute x39, starting transfers between devices, flipped(): return lax.ppermute(block, axis, route)  36.3 us
    ppermute x10, starting transfers between devices, rotated(): return lax.ppermute(block, axis, route)  17.2 us
    dot_general x6, matrix products, contract_last(): lax.dot_general(first_operand, second_operand, (((1,), (1,)), ((), ())),...  6.31 us
    another operation x12, other arithmetic, gather_quad(): return jnp.stack([staged, first, second, diagonal])  5.08 us
    dot_general x2, matrix products, contract_first(): lax.dot_general(first_operand, second_operand, (((0,), (0,)), ((), ())),...  4.91 us
  transfers between devices with their start and end apart: 52, of which 26 were waited for; matrix products, arithmetic and copies ran while one was open for 16% of the time, Pallas kernels for 0%

profile of v10, /device:TPU:0, one launch (start us, length us, event | category | flops | bytes accessed | tf_op | source)
XLA Modules:
  0.0 237.4 jit_solution(3832372614929248251)
XLA Ops:
  10.1 4.0 %collective-permute-start = (bf16[48]{0:T(256)(128)(2,1)S(1)}, bf16[48]{0:T(256)(128)(2,1)S(1)}, u32[]{:S(2)}, u32[]{:S(2)}) collective-permute-start(bf16[48]{0:T(256)(128)(2,1)S(1)} %get-tuple-element.99), channel_id=1, source_target_pairs={{0,8},{8,0},{1,9},{9,1},{2,10},{10,2},{3,11},{11,3},{4,12},{12,4},... | collective-permute-start | bytes 296 | tf_op jit(solution)/shard_map/ppermute | solution.py:21
  17.8 2.9 %collective-permute-start.10 = (bf16[48,2560]{1,0:T(8,128)(2,1)}, bf16[48,2560]{1,0:T(8,128)(2,1)}, u32[]{:S(2)}, u32[]{:S(2)}) collective-permute-start(bf16[48,2560]{1,0:T(8,128)(2,1)} %get-tuple-element.69), channel_id=1, source_target_pairs={{0,8},{8,0},{1,9},{9,1},{2,10},{10,2},{3,11},{11,3},{4,12},{12,4},... | collective-permute-start | bytes 737288 | tf_op jit(solution)/shard_map/ppermute | solution.py:21
  23.9 3.4 %collective-permute-done.2 = bf16[2,48]{1,0:T(2,128)(2,1)S(1)} collective-permute-done((bf16[2,48]{1,0:T(2,128)(2,1)S(1)}, bf16[2,48]{1,0:T(2,128)(2,1)S(1)}, u32[]{:S(2)}, u32[]{:S(2)}) %collective-permute-start.2) | collective-permute-done | bytes 224 | tf_op jit(solution)/shard_map/ppermute | solution.py:27
  27.3 3.3 %collective-permute-start.3 = (bf16[2,48]{1,0:T(2,128)(2,1)S(1)}, bf16[2,48]{1,0:T(2,128)(2,1)S(1)}, u32[]{:S(2)}, u32[]{:S(2)}) collective-permute-start(bf16[2,48]{1,0:T(2,128)(2,1)S(1)} %pad_maximum_fusion.19), channel_id=1, source_target_pairs={{0,6},{2,4},{4,2},{6,0},{1,7},{3,5},{5,3},{7,1},{8,14},{10,12},{12... | collective-permute-start | bytes 584 | tf_op jit(solution)/shard_map/ppermute | solution.py:27
  32.2 8.6 %collective-permute-done.10 = bf16[48,2560]{1,0:T(8,128)(2,1)} collective-permute-done((bf16[48,2560]{1,0:T(8,128)(2,1)}, bf16[48,2560]{1,0:T(8,128)(2,1)}, u32[]{:S(2)}, u32[]{:S(2)}) %collective-permute-start.10) | collective-permute-done | bytes 245792 | tf_op jit(solution)/shard_map/ppermute | solution.py:21
  46.4 9.7 %collective-permute-done.11 = bf16[2,48,2560]{2,1,0:T(8,128)(2,1)S(1)} collective-permute-done((bf16[2,48,2560]{2,1,0:T(8,128)(2,1)S(1)}, bf16[2,48,2560]{2,1,0:T(8,128)(2,1)S(1)}, u32[]{:S(2)}, u32[]{:S(2)}) %collective-permute-start.11) | collective-permute-done | bytes 491552 | tf_op jit(solution)/shard_map/ppermute | solution.py:27
  59.7 7.0 %collective-permute-done.5 = bf16[2,48,2560]{2,1,0:T(8,128)(2,1)S(1)} collective-permute-done((bf16[2,48,2560]{2,1,0:T(8,128)(2,1)S(1)}, bf16[2,48,2560]{2,1,0:T(8,128)(2,1)S(1)}, u32[]{:S(2)}, u32[]{:S(2)}) %collective-permute-start.5) | collective-permute-done | bytes 491552 | tf_op jit(solution)/shard_map/ppermute | solution.py:27
  68.8 4.6 %collective-permute-done.13 = bf16[2,48,1280]{2,1,0:T(8,128)(2,1)S(1)} collective-permute-done((bf16[2,48,1280]{2,1,0:T(8,128)(2,1)S(1)}, bf16[2,48,1280]{2,1,0:T(8,128)(2,1)S(1)}, u32[]{:S(2)}, u32[]{:S(2)}) %collective-permute-start.13) | collective-permute-done | bytes 245792 | tf_op jit(solution)/shard_map/ppermute | solution.py:27
  81.5 5.2 %collective-permute-done.19 = bf16[2,48,1280]{2,1,0:T(8,128)(2,1)S(1)} collective-permute-done((bf16[2,48,1280]{2,1,0:T(8,128)(2,1)S(1)}, bf16[2,48,1280]{2,1,0:T(8,128)(2,1)S(1)}, u32[]{:S(2)}, u32[]{:S(2)}) %collective-permute-start.19) | collective-permute-done | bytes 245792 | tf_op jit(solution)/shard_map/ppermute | solution.py:27
  89.0 2.2 collective-permute-start.18
  95.1 4.5 %collective-permute-done.44 = bf16[2,48]{1,0:T(2,128)(2,1)S(1)} collective-permute-done((bf16[2,48]{1,0:T(2,128)(2,1)S(1)}, bf16[2,48]{1,0:T(2,128)(2,1)S(1)}, u32[]{:S(2)}, u32[]{:S(2)}) %collective-permute-start.44) | collective-permute-done | bytes 224 | tf_op jit(solution)/shard_map/ppermute | solution.py:27
  99.6 3.6 %collective-permute-start.45 = (f32[48]{0:T(128)S(1)}, f32[48]{0:T(128)S(1)}, u32[]{:S(2)}, u32[]{:S(2)}) collective-permute-start(f32[48]{0:T(128)S(1)} %get-tuple-element.87), channel_id=1, source_target_pairs={{0,8},{8,0},{1,9},{9,1},{2,10},{10,2},{3,11},{11,3},{4,12},{12,4},... | collective-permute-start | bytes 584 | tf_op jit(solution)/shard_map/ppermute | solution.py:21
  107.1 9.0 %collective-permute-done.21 = bf16[48,2560]{1,0:T(8,128)(2,1)S(1)} collective-permute-done((bf16[48,2560]{1,0:T(8,128)(2,1)S(1)}, bf16[48,2560]{1,0:T(8,128)(2,1)S(1)}, u32[]{:S(2)}, u32[]{:S(2)}) %collective-permute-start.21) | collective-permute-done | bytes 245792 | tf_op jit(solution)/shard_map/ppermute | solution.py:21
  118.5 3.0 %collective-permute-start.32 = (bf16[48,2560]{1,0:T(8,128)(2,1)S(1)}, bf16[48,2560]{1,0:T(8,128)(2,1)S(1)}, u32[]{:S(2)}, u32[]{:S(2)}) collective-permute-start(bf16[48,2560]{1,0:T(8,128)(2,1)S(1)} %get-tuple-element.59), channel_id=1, source_target_pairs={{0,8},{8,0},{1,9},{9,1},{2,10},{10,2},{3,11},{11,3},{4,12},{12,4},... | collective-permute-start | bytes 737288 | tf_op jit(solution)/shard_map/ppermute | solution.py:21
  123.4 7.3 %collective-permute-done.32 = bf16[48,2560]{1,0:T(8,128)(2,1)S(1)} collective-permute-done((bf16[48,2560]{1,0:T(8,128)(2,1)S(1)}, bf16[48,2560]{1,0:T(8,128)(2,1)S(1)}, u32[]{:S(2)}, u32[]{:S(2)}) %collective-permute-start.32) | collective-permute-done | bytes 245792 | tf_op jit(solution)/shard_map/ppermute | solution.py:21
  137.4 7.4 %collective-permute-done.24 = bf16[2,48]{1,0:T(2,128)(2,1)S(1)} collective-permute-done((bf16[2,48]{1,0:T(2,128)(2,1)S(1)}, bf16[2,48]{1,0:T(2,128)(2,1)S(1)}, u32[]{:S(2)}, u32[]{:S(2)}) %collective-permute-start.24) | collective-permute-done | bytes 224 | tf_op jit(solution)/shard_map/ppermute | solution.py:27
  144.8 6.4 %collective-permute-done.26 = bf16[2,48]{1,0:T(2,128)(2,1)S(1)} collective-permute-done((bf16[2,48]{1,0:T(2,128)(2,1)S(1)}, bf16[2,48]{1,0:T(2,128)(2,1)S(1)}, u32[]{:S(2)}, u32[]{:S(2)}) %collective-permute-start.26) | collective-permute-done | bytes 224 | tf_op jit(solution)/shard_map/ppermute | solution.py:27
  159.0 3.2 %collective-permute-done.36 = bf16[2,48,1280]{2,1,0:T(8,128)(2,1)S(1)} collective-permute-done((bf16[2,48,1280]{2,1,0:T(8,128)(2,1)S(1)}, bf16[2,48,1280]{2,1,0:T(8,128)(2,1)S(1)}, u32[]{:S(2)}, u32[]{:S(2)}) %collective-permute-start.36) | collective-permute-done | bytes 245792 | tf_op jit(solution)/shard_map/ppermute | solution.py:27
  164.3 6.1 %collective-permute-done.28 = bf16[2,48,2560]{2,1,0:T(8,128)(2,1)S(1)} collective-permute-done((bf16[2,48,2560]{2,1,0:T(8,128)(2,1)S(1)}, bf16[2,48,2560]{2,1,0:T(8,128)(2,1)S(1)}, u32[]{:S(2)}, u32[]{:S(2)}) %collective-permute-start.28) | collective-permute-done | bytes 491552 | tf_op jit(solution)/shard_map/ppermute | solution.py:27
  173.6 3.1 %collective-permute-done.30 = bf16[2,48,1280]{2,1,0:T(8,128)(2,1)S(1)} collective-permute-done((bf16[2,48,1280]{2,1,0:T(8,128)(2,1)S(1)}, bf16[2,48,1280]{2,1,0:T(8,128)(2,1)S(1)}, u32[]{:S(2)}, u32[]{:S(2)}) %collective-permute-start.30) | collective-permute-done | bytes 245792 | tf_op jit(solution)/shard_map/ppermute | solution.py:27
  180.6 3.0 %convolution_convert_fusion = bf16[384,2560]{1,0:T(8,128)(2,1)} fusion(bf16[384,2560]{1,0:T(8,128)(2,1)S(1)} %bitcast.228, bf16[384,2560]{1,0:T(8,128)(2,1)S(1)} %bitcast.222, bf16[384,192]{0,1:T(8,128)(2,1)S(1)} %get-tuple-element.53, bf16[384,192]{0,1:T(8,128)(2,1)S(1)} %get-tuple-element.47, bf16[384,192]{0,1:T(8,128)(2,1)S(1)} %copy-done.22, ...), kind=kOutput, calls=%fused_computation.4 | convolution fusion | flops 1521156096 | bytes 6488064 | tf_op jit(solution)/shard_map/dot_general | solution.py:42
  197.4 5.0 %collective-permute-done.37 = bf16[2,48,1280]{2,1,0:T(8,128)(2,1)S(1)} collective-permute-done((bf16[2,48,1280]{2,1,0:T(8,128)(2,1)S(1)}, bf16[2,48,1280]{2,1,0:T(8,128)(2,1)S(1)}, u32[]{:S(2)}, u32[]{:S(2)}) %collective-permute-start.37) | collective-permute-done | bytes 245792 | tf_op jit(solution)/shard_map/ppermute | solution.py:27
  206.0 7.0 %collective-permute-done.49 = f32[48]{0:T(128)S(1)} collective-permute-done((f32[48]{0:T(128)S(1)}, f32[48]{0:T(128)S(1)}, u32[]{:S(2)}, u32[]{:S(2)}) %collective-permute-start.49) | collective-permute-done | bytes 224 | tf_op jit(solution)/shard_map/ppermute | solution.py:21
  218.0 6.8 %collective-permute-done.41 = bf16[48,2560]{1,0:T(8,128)(2,1)S(1)} collective-permute-done((bf16[48,2560]{1,0:T(8,128)(2,1)S(1)}, bf16[48,2560]{1,0:T(8,128)(2,1)S(1)}, u32[]{:S(2)}, u32[]{:S(2)}) %collective-permute-start.41) | collective-permute-done | bytes 245792 | tf_op jit(solution)/shard_map/ppermute | solution.py:21
  (293 shorter events, 96.2 us)
Async XLA Ops:
  7.2 221.1 %reduce-scatter.3.cloned.1.call-start = ((), (), s32[]{:S(2)}) async-start(), calls=%async_computation.2 | async-start | bytes 2949120 | tf_op jit(solution)/shard_map/reduce_scatter | solution.py:260
  16.4 27.0 %collective-permute-start.4 = (bf16[48,2560]{1,0:T(8,128)(2,1)}, bf16[48,2560]{1,0:T(8,128)(2,1)S(1)}, u32[]{:S(2)}, u32[]{:S(2)}) collective-permute-start(bf16[48,2560]{1,0:T(8,128)(2,1)} %get-tuple-element.73), channel_id=1, source_target_pairs={{0,8},{8,0},{1,9},{9,1},{2,10},{10,2},{3,11},{11,3},{4,12},{12,4},... | collective-permute-start | bytes 737288 | tf_op jit(solution)/shard_map/ppermute | solution.py:21
  17.8 23.0 %collective-permute-start.10 = (bf16[48,2560]{1,0:T(8,128)(2,1)}, bf16[48,2560]{1,0:T(8,128)(2,1)}, u32[]{:S(2)}, u32[]{:S(2)}) collective-permute-start(bf16[48,2560]{1,0:T(8,128)(2,1)} %get-tuple-element.69), channel_id=1, source_target_pairs={{0,8},{8,0},{1,9},{9,1},{2,10},{10,2},{3,11},{11,3},{4,12},{12,4},... | collective-permute-start | bytes 737288 | tf_op jit(solution)/shard_map/ppermute | solution.py:21
  20.7 23.4 %collective-permute-start.16 = (bf16[192,1280]{1,0:T(8,128)(2,1)S(1)}, bf16[192,1280]{1,0:T(8,128)(2,1)S(1)}, u32[]{:S(2)}, u32[]{:S(2)}) collective-permute-start(bf16[192,1280]{1,0:T(8,128)(2,1)S(1)} %bitcast.246), channel_id=1, source_target_pairs={{0,1},{1,0},{2,3},{3,2},{4,5},{5,4},{6,7},{7,6},{8,9},{9,8},{10,11... | collective-permute-start | bytes 1474568 | tf_op jit(solution)/shard_map/ppermute | solution.py:27
  30.6 27.0 %collective-permute-start.15 = (bf16[192,1280]{1,0:T(8,128)(2,1)S(1)}, bf16[192,1280]{1,0:T(8,128)(2,1)}, u32[]{:S(2)}, u32[]{:S(2)}) collective-permute-start(bf16[192,1280]{1,0:T(8,128)(2,1)S(1)} %bitcast.248), channel_id=1, source_target_pairs={{0,1},{1,0},{2,3},{3,2},{4,5},{5,4},{6,7},{7,6},{8,9},{9,8},{10,11... | collective-permute-start | bytes 1474568 | tf_op jit(solution)/shard_map/ppermute | solution.py:27
  41.9 14.2 %collective-permute-start.11 = (bf16[2,48,2560]{2,1,0:T(8,128)(2,1)S(1)}, bf16[2,48,2560]{2,1,0:T(8,128)(2,1)S(1)}, u32[]{:S(2)}, u32[]{:S(2)}) collective-permute-start(bf16[2,48,2560]{2,1,0:T(8,128)(2,1)S(1)} %get-tuple-element.67), channel_id=1, source_target_pairs={{0,2},{2,0},{4,6},{6,4},{1,3},{3,1},{5,7},{7,5},{8,10},{10,8},{12,... | collective-permute-start | bytes 1474568 | tf_op jit(solution)/shard_map/ppermute | solution.py:27
  43.4 14.2 %collective-permute-start.12 = (bf16[2,48,2560]{2,1,0:T(8,128)(2,1)S(1)}, bf16[2,48,2560]{2,1,0:T(8,128)(2,1)S(1)}, u32[]{:S(2)}, u32[]{:S(2)}) collective-permute-start(bf16[2,48,2560]{2,1,0:T(8,128)(2,1)S(1)} %get-tuple-element.67), channel_id=1, source_target_pairs={{0,4},{2,6},{4,0},{6,2},{1,5},{3,7},{5,1},{7,3},{8,12},{10,14},{12... | collective-permute-start | bytes 1474568 | tf_op jit(solution)/shard_map/ppermute | solution.py:27
  43.5 23.1 %collective-permute-start.5 = (bf16[2,48,2560]{2,1,0:T(8,128)(2,1)S(1)}, bf16[2,48,2560]{2,1,0:T(8,128)(2,1)S(1)}, u32[]{:S(2)}, u32[]{:S(2)}) collective-permute-start(bf16[2,48,2560]{2,1,0:T(8,128)(2,1)S(1)} %get-tuple-element.71), channel_id=1, source_target_pairs={{0,2},{2,0},{4,6},{6,4},{1,3},{3,1},{5,7},{7,5},{8,10},{10,8},{12,... | collective-permute-start | bytes 1474568 | tf_op jit(solution)/shard_map/ppermute | solution.py:27
  44.1 24.0 %collective-permute-start.6 = (bf16[2,48,2560]{2,1,0:T(8,128)(2,1)S(1)}, bf16[2,48,2560]{2,1,0:T(8,128)(2,1)S(1)}, u32[]{:S(2)}, u32[]{:S(2)}) collective-permute-start(bf16[2,48,2560]{2,1,0:T(8,128)(2,1)S(1)} %get-tuple-element.71), channel_id=1, source_target_pairs={{0,4},{2,6},{4,0},{6,2},{1,5},{3,7},{5,1},{7,3},{8,12},{10,14},{12... | collective-permute-start | bytes 1474568 | tf_op jit(solution)/shard_map/ppermute | solution.py:27
  56.1 21.3 %collective-permute-start.9 = (bf16[192,1280]{1,0:T(8,128)(2,1)S(1)}, bf16[192,1280]{1,0:T(8,128)(2,1)S(1)}, u32[]{:S(2)}, u32[]{:S(2)}) collective-permute-start(bf16[192,1280]{1,0:T(8,128)(2,1)S(1)} %bitcast.263), channel_id=1, source_target_pairs={{0,1},{1,0},{2,3},{3,2},{4,5},{5,4},{6,7},{7,6},{8,9},{9,8},{10,11... | collective-permute-start | bytes 1474568 | tf_op jit(solution)/shard_map/ppermute | solution.py:27
  57.6 15.8 %collective-permute-start.13 = (bf16[2,48,1280]{2,1,0:T(8,128)(2,1)S(1)}, bf16[2,48,1280]{2,1,0:T(8,128)(2,1)S(1)}, u32[]{:S(2)}, u32[]{:S(2)}) collective-permute-start(bf16[2,48,1280]{2,1,0:T(8,128)(2,1)S(1)} %slice.371), channel_id=1, source_target_pairs={{0,4},{2,6},{4,0},{6,2},{1,5},{3,7},{5,1},{7,3},{8,12},{10,14},{12... | collective-permute-start | bytes 737288 | tf_op jit(solution)/shard_map/ppermute | solution.py:27
  57.6 15.8 %collective-permute-start.14 = (bf16[2,48,1280]{2,1,0:T(8,128)(2,1)S(1)}, bf16[2,48,1280]{2,1,0:T(8,128)(2,1)S(1)}, u32[]{:S(2)}, u32[]{:S(2)}) collective-permute-start(bf16[2,48,1280]{2,1,0:T(8,128)(2,1)S(1)} %slice.372), channel_id=1, source_target_pairs={{0,2},{2,0},{4,6},{6,4},{1,3},{3,1},{5,7},{7,5},{8,10},{10,8},{12,... | collective-permute-start | bytes 737288 | tf_op jit(solution)/shard_map/ppermute | solution.py:27
  87.6 15.6 %collective-permute-start.20 = (bf16[2,48,2560]{2,1,0:T(8,128)(2,1)}, bf16[2,48,2560]{2,1,0:T(8,128)(2,1)S(1)}, u32[]{:S(2)}, u32[]{:S(2)}) collective-permute-start(bf16[2,48,2560]{2,1,0:T(8,128)(2,1)} %pad_maximum_fusion.12), channel_id=1, source_target_pairs={{0,2},{2,0},{4,6},{6,4},{1,3},{3,1},{5,7},{7,5},{8,10},{10,8},{12,... | collective-permute-start | bytes 1474568 | tf_op jit(solution)/shard_map/ppermute | solution.py:27
  89.0 14.2 %collective-permute-start.18 = (bf16[2,48,2560]{2,1,0:T(8,128)(2,1)}, bf16[2,48,2560]{2,1,0:T(8,128)(2,1)S(1)}, u32[]{:S(2)}, u32[]{:S(2)}) collective-permute-start(bf16[2,48,2560]{2,1,0:T(8,128)(2,1)} %pad_maximum_fusion.11), channel_id=1, source_target_pairs={{0,4},{2,6},{4,0},{6,2},{1,5},{3,7},{5,1},{7,3},{8,12},{10,14},{12... | collective-permute-start | bytes 1474568 | tf_op jit(solution)/shard_map/ppermute | solution.py:27
  118.5 12.2 %collective-permute-start.32 = (bf16[48,2560]{1,0:T(8,128)(2,1)S(1)}, bf16[48,2560]{1,0:T(8,128)(2,1)S(1)}, u32[]{:S(2)}, u32[]{:S(2)}) collective-permute-start(bf16[48,2560]{1,0:T(8,128)(2,1)S(1)} %get-tuple-element.59), channel_id=1, source_target_pairs={{0,8},{8,0},{1,9},{9,1},{2,10},{10,2},{3,11},{11,3},{4,12},{12,4},... | collective-permute-start | bytes 737288 | tf_op jit(solution)/shard_map/ppermute | solution.py:21
  123.3 12.7 %collective-permute-start.25 = (bf16[2,48]{1,0:T(2,128)(2,1)S(1)}, bf16[2,48]{1,0:T(2,128)(2,1)S(1)}, u32[]{:S(2)}, u32[]{:S(2)}) collective-permute-start(bf16[2,48]{1,0:T(2,128)(2,1)S(1)} %pad_maximum_fusion.20), channel_id=1, source_target_pairs={{0,4},{2,6},{4,0},{6,2},{1,5},{3,7},{5,1},{7,3},{8,12},{10,14},{12... | collective-permute-start | bytes 584 | tf_op jit(solution)/shard_map/ppermute | solution.py:27
  131.6 20.2 %collective-permute-start.33 = (bf16[2,48,2560]{2,1,0:T(8,128)(2,1)}, bf16[2,48,2560]{2,1,0:T(8,128)(2,1)S(1)}, u32[]{:S(2)}, u32[]{:S(2)}) collective-permute-start(bf16[2,48,2560]{2,1,0:T(8,128)(2,1)} %get-tuple-element.57), channel_id=1, source_target_pairs={{0,2},{2,0},{4,6},{6,4},{1,3},{3,1},{5,7},{7,5},{8,10},{10,8},{12,... | collective-permute-start | bytes 1474568 | tf_op jit(solution)/shard_map/ppermute | solution.py:27
  132.7 19.6 %collective-permute-start.34 = (bf16[2,48,2560]{2,1,0:T(8,128)(2,1)}, bf16[2,48,2560]{2,1,0:T(8,128)(2,1)}, u32[]{:S(2)}, u32[]{:S(2)}) collective-permute-start(bf16[2,48,2560]{2,1,0:T(8,128)(2,1)} %get-tuple-element.57), channel_id=1, source_target_pairs={{0,4},{2,6},{4,0},{6,2},{1,5},{3,7},{5,1},{7,3},{8,12},{10,14},{12... | collective-permute-start | bytes 1474568 | tf_op jit(solution)/shard_map/ppermute | solution.py:27
  133.8 20.6 %collective-permute-start.27 = (bf16[48,2560]{1,0:T(8,128)(2,1)}, bf16[48,2560]{1,0:T(8,128)(2,1)}, u32[]{:S(2)}, u32[]{:S(2)}) collective-permute-start(bf16[48,2560]{1,0:T(8,128)(2,1)} %get-tuple-element.63), channel_id=1, source_target_pairs={{0,8},{8,0},{1,9},{9,1},{2,10},{10,2},{3,11},{11,3},{4,12},{12,4},... | collective-permute-start | bytes 737288 | tf_op jit(solution)/shard_map/ppermute | solution.py:21
  136.1 15.1 %collective-permute-start.26 = (bf16[2,48]{1,0:T(2,128)(2,1)S(1)}, bf16[2,48]{1,0:T(2,128)(2,1)S(1)}, u32[]{:S(2)}, u32[]{:S(2)}) collective-permute-start(bf16[2,48]{1,0:T(2,128)(2,1)S(1)} %pad_maximum_fusion.20), channel_id=1, source_target_pairs={{0,6},{2,4},{4,2},{6,0},{1,7},{3,5},{5,3},{7,1},{8,14},{10,12},{12... | collective-permute-start | bytes 584 | tf_op jit(solution)/shard_map/ppermute | solution.py:27
  155.4 15.0 %collective-permute-start.28 = (bf16[2,48,2560]{2,1,0:T(8,128)(2,1)S(1)}, bf16[2,48,2560]{2,1,0:T(8,128)(2,1)S(1)}, u32[]{:S(2)}, u32[]{:S(2)}) collective-permute-start(bf16[2,48,2560]{2,1,0:T(8,128)(2,1)S(1)} %get-tuple-element.61), channel_id=1, source_target_pairs={{0,2},{2,0},{4,6},{6,4},{1,3},{3,1},{5,7},{7,5},{8,10},{10,8},{12,... | collective-permute-start | bytes 1474568 | tf_op jit(solution)/shard_map/ppermute | solution.py:27
  156.4 15.1 %collective-permute-start.29 = (bf16[2,48,2560]{2,1,0:T(8,128)(2,1)S(1)}, bf16[2,48,2560]{2,1,0:T(8,128)(2,1)S(1)}, u32[]{:S(2)}, u32[]{:S(2)}) collective-permute-start(bf16[2,48,2560]{2,1,0:T(8,128)(2,1)S(1)} %get-tuple-element.61), channel_id=1, source_target_pairs={{0,4},{2,6},{4,0},{6,2},{1,5},{3,7},{5,1},{7,3},{8,12},{10,14},{12... | collective-permute-start | bytes 1474568 | tf_op jit(solution)/shard_map/ppermute | solution.py:27
  183.6 46.9 %reduce-scatter.5.cloned.1.call-start = ((), (), s32[]{:S(2)}) async-start(), calls=%async_computation.3 | async-start | bytes 1474560 | tf_op jit(solution)/shard_map/reduce_scatter | solution.py:263
  196.4 17.4 %collective-permute-start.40 = (bf16[2,48,2560]{2,1,0:T(8,128)(2,1)S(1)}, bf16[2,48,2560]{2,1,0:T(8,128)(2,1)S(1)}, u32[]{:S(2)}, u32[]{:S(2)}) collective-permute-start(bf16[2,48,2560]{2,1,0:T(8,128)(2,1)S(1)} %pad_maximum_fusion.16), channel_id=1, source_target_pairs={{0,2},{2,0},{4,6},{6,4},{1,3},{3,1},{5,7},{7,5},{8,10},{10,8},{12,... | collective-permute-start | bytes 1474568 | tf_op jit(solution)/shard_map/ppermute | solution.py:27
  (70 other events, 588.3 us)
Sparse Core Ops, SparseCore 0:
  183.7 7.6 reduce-scatter.2
  206.1 9.3 reduce-scatter.4

commit v11 on v10

--- a/solution.py
+++ b/solution.py
@@ -177,8 +177,17 @@
 
     prepared = [prepare(moment) for moment in range(micro_count)]
     first_incoming = jnp.where(is_last, output_grads[0], entry_grads[0])
-    first_grads = gather_quad(dispatch_rows(prepared[0][4], first_incoming))
-    rows_gathered = [gather_quad(dispatch_rows(prepared[0][4], prepared[0][2]))]
+    first_both = gather_quad(
+        jnp.concatenate(
+            [
+                dispatch_rows(prepared[0][4], prepared[0][2]),
+                dispatch_rows(prepared[0][4], first_incoming),
+            ],
+            axis=1,
+        )
+    )
+    first_grads = first_both[:, :, capacity:]
+    rows_gathered = [first_both[:, :, :capacity]]
     weights_gathered = [gather_quad(prepared[0][6].reshape(groups, capacity))]
     for current in prepared[1:]:
         later_rows, later_weights, _ = lax.optimization_barrier(

time: 238 us -> 258 us (1.084)
  waiting for transfers between devices: 115 us -> 130 us
  starting transfers between devices: 55 us -> 52.4 us
  matrix products: 16.1 us -> 18.7 us
    ppermute x10 -> x9, waiting for transfers between devices: 38.7 us -> 67.8 us  [rotated(): return lax.ppermute(block, axis, route)]
    ppermute x39 -> x35, waiting for transfers between devices: 76.3 us -> 62.3 us  [flipped(): return lax.ppermute(block, axis, route)]
    ppermute x39 -> x35, starting transfers between devices: 36.3 us -> 31.6 us  [flipped(): return lax.ppermute(block, axis, route)]
    ppermute x10 -> x9, starting transfers between devices: 17.2 us -> 19.3 us  [rotated(): return lax.ppermute(block, axis, route)]
    another operation x12 -> x9, other arithmetic: 5.08 us -> 6.17 us  [gather_quad(): return jnp.stack([staged, first, second, diagonal])]
  transfers between devices with their start and end apart: 52 -> 47, of which waited for: 26 -> 25; matrix products, arithmetic and copies ran while one was open for 16% -> 14% of each run, Pallas kernels for 0% -> 0%
where the time goes in v11:
time: 258 us; the launch traced here: 257 us
  waiting for transfers between devices  130 us (50%)
  starting transfers between devices  52.4 us (20%)
  other arithmetic  24.4 us (9%)
  matrix products  18.7 us (7%)
  local copies, waits for them, and re-layouts  16.6 us (6%)
  between operations  14.9 us (6%)
    ppermute x9, waiting for transfers between devices, rotated(): return lax.ppermute(block, axis, route)  67.8 us
    ppermute x35, waiting for transfers between devices, flipped(): return lax.ppermute(block, axis, route)  62.3 us
    ppermute x35, starting transfers between devices, flipped(): return lax.ppermute(block, axis, route)  31.6 us
    ppermute x9, starting transfers between devices, rotated(): return lax.ppermute(block, axis, route)  19.3 us
    dot_general x6, matrix products, contract_last(): lax.dot_general(first_operand, second_operand, (((1,), (1,)), ((), ())),...  8.84 us
    another operation x9, other arithmetic, gather_quad(): return jnp.stack([staged, first, second, diagonal])  6.17 us
  transfers between devices with their start and end apart: 47, of which 25 were waited for; matrix products, arithmetic and copies ran while one was open for 14% of the time, Pallas kernels for 0%

profile of v11, /device:TPU:0, one launch (start us, length us, event | category | flops | bytes accessed | tf_op | source)
XLA Modules:
  0.0 257.3 jit_solution(4073997983012424055)
XLA Ops:
  14.1 4.1 %collective-permute-start.4 = (bf16[96,2560]{1,0:T(8,128)(2,1)S(1)}, bf16[96,2560]{1,0:T(8,128)(2,1)S(1)}, u32[]{:S(2)}, u32[]{:S(2)}) collective-permute-start(bf16[96,2560]{1,0:T(8,128)(2,1)S(1)} %get-tuple-element.51), channel_id=1, source_target_pairs={{0,8},{8,0},{1,9},{9,1},{2,10},{10,2},{3,11},{11,3},{4,12},{12,4},... | collective-permute-start | bytes 1474568 | tf_op jit(solution)/shard_map/ppermute | solution.py:21
  18.2 21.8 %collective-permute-done.4 = bf16[96,2560]{1,0:T(8,128)(2,1)S(1)} collective-permute-done((bf16[96,2560]{1,0:T(8,128)(2,1)S(1)}, bf16[96,2560]{1,0:T(8,128)(2,1)S(1)}, u32[]{:S(2)}, u32[]{:S(2)}) %collective-permute-start.4) | collective-permute-done | bytes 491552 | tf_op jit(solution)/shard_map/ppermute | solution.py:21
  43.4 3.4 %collective-permute-start = (bf16[48]{0:T(256)(128)(2,1)S(1)}, bf16[48]{0:T(256)(128)(2,1)S(1)}, u32[]{:S(2)}, u32[]{:S(2)}) collective-permute-start(bf16[48]{0:T(256)(128)(2,1)S(1)} %get-tuple-element.97), channel_id=1, source_target_pairs={{0,8},{8,0},{1,9},{9,1},{2,10},{10,2},{3,11},{11,3},{4,12},{12,4},... | collective-permute-start | bytes 296 | tf_op jit(solution)/shard_map/ppermute | solution.py:21
  46.8 17.6 %collective-permute-done = bf16[48]{0:T(256)(128)(2,1)S(1)} collective-permute-done((bf16[48]{0:T(256)(128)(2,1)S(1)}, bf16[48]{0:T(256)(128)(2,1)S(1)}, u32[]{:S(2)}, u32[]{:S(2)}) %collective-permute-start) | collective-permute-done | bytes 128 | tf_op jit(solution)/shard_map/ppermute | solution.py:21
  64.5 4.1 %collective-permute-start.2 = (bf16[2,48]{1,0:T(2,128)(2,1)S(1)}, bf16[2,48]{1,0:T(2,128)(2,1)S(1)}, u32[]{:S(2)}, u32[]{:S(2)}) collective-permute-start(bf16[2,48]{1,0:T(2,128)(2,1)S(1)} %pad_maximum_fusion.18), channel_id=1, source_target_pairs={{0,4},{2,6},{4,0},{6,2},{1,5},{3,7},{5,1},{7,3},{8,12},{10,14},{12... | collective-permute-start | bytes 584 | tf_op jit(solution)/shard_map/ppermute | solution.py:27
  72.2 4.4 %collective-permute-done.3 = bf16[2,48]{1,0:T(2,128)(2,1)S(1)} collective-permute-done((bf16[2,48]{1,0:T(2,128)(2,1)S(1)}, bf16[2,48]{1,0:T(2,128)(2,1)S(1)}, u32[]{:S(2)}, u32[]{:S(2)}) %collective-permute-start.3) | collective-permute-done | bytes 224 | tf_op jit(solution)/shard_map/ppermute | solution.py:27
  81.8 8.6 %collective-permute-done.7 = bf16[2,96,1280]{2,1,0:T(8,128)(2,1)S(1)} collective-permute-done((bf16[2,96,1280]{2,1,0:T(8,128)(2,1)S(1)}, bf16[2,96,1280]{2,1,0:T(8,128)(2,1)S(1)}, u32[]{:S(2)}, u32[]{:S(2)}) %collective-permute-start.7) | collective-permute-done | bytes 491552 | tf_op jit(solution)/shard_map/ppermute | solution.py:27
  96.2 2.7 %multiply_reduce_fusion.1 = (bf16[384]{0:T(512)(128)(2,1)S(1)}, bf16[384,192]{0,1:T(8,128)(2,1)S(1)}, bf16[384,192]{0,1:T(8,128)(2,1)}, bf16[384,192]{0,1:T(8,128)(2,1)S(1)}) fusion(f32[384,192]{0,1:T(8,128)S(1)} %fusion.116, f32[384,192]{0,1:T(8,128)S(1)} %fusion.117, f32[384]{0:T(512)S(1)} %reshape.484, bf16[384,2560]{1,0:T(8,128)(2,1)S(1)} %bitcast.230, ...), kind=kOutput, calls=%fused_computation.116 | convolution fusion | flops 383311488 | bytes 3983617 | tf_op jit(solution)/shard_map/dot_general | solution.py:36
  102.5 5.6 %collective-permute-done.14 = bf16[2,48,1280]{2,1,0:T(8,128)(2,1)S(1)} collective-permute-done((bf16[2,48,1280]{2,1,0:T(8,128)(2,1)S(1)}, bf16[2,48,1280]{2,1,0:T(8,128)(2,1)S(1)}, u32[]{:S(2)}, u32[]{:S(2)}) %collective-permute-start.14) | collective-permute-done | bytes 245792 | tf_op jit(solution)/shard_map/ppermute | solution.py:27
  115.3 7.9 %collective-permute-done.39 = bf16[2,48]{1,0:T(2,128)(2,1)S(1)} collective-permute-done((bf16[2,48]{1,0:T(2,128)(2,1)S(1)}, bf16[2,48]{1,0:T(2,128)(2,1)S(1)}, u32[]{:S(2)}, u32[]{:S(2)}) %collective-permute-start.39) | collective-permute-done | bytes 224 | tf_op jit(solution)/shard_map/ppermute | solution.py:27
  126.3 2.9 %collective-permute-start.16 = (bf16[48,2560]{1,0:T(8,128)(2,1)}, bf16[48,2560]{1,0:T(8,128)(2,1)S(1)}, u32[]{:S(2)}, u32[]{:S(2)}) collective-permute-start(bf16[48,2560]{1,0:T(8,128)(2,1)} %fusion.69), channel_id=1, source_target_pairs={{0,8},{8,0},{1,9},{9,1},{2,10},{10,2},{3,11},{11,3},{4,12},{12,4},... | collective-permute-start | bytes 737288 | tf_op jit(solution)/shard_map/ppermute | solution.py:21
  131.7 6.3 %collective-permute-done.16 = bf16[48,2560]{1,0:T(8,128)(2,1)S(1)} collective-permute-done((bf16[48,2560]{1,0:T(8,128)(2,1)}, bf16[48,2560]{1,0:T(8,128)(2,1)S(1)}, u32[]{:S(2)}, u32[]{:S(2)}) %collective-permute-start.16) | collective-permute-done | bytes 245792 | tf_op jit(solution)/shard_map/ppermute | solution.py:21
  140.3 3.0 %collective-permute-start.27 = (bf16[48,2560]{1,0:T(8,128)(2,1)S(1)}, bf16[48,2560]{1,0:T(8,128)(2,1)S(1)}, u32[]{:S(2)}, u32[]{:S(2)}) collective-permute-start(bf16[48,2560]{1,0:T(8,128)(2,1)S(1)} %get-tuple-element.65), channel_id=1, source_target_pairs={{0,8},{8,0},{1,9},{9,1},{2,10},{10,2},{3,11},{11,3},{4,12},{12,4},... | collective-permute-start | bytes 737288 | tf_op jit(solution)/shard_map/ppermute | solution.py:21
  147.2 6.3 %collective-permute-done.27 = bf16[48,2560]{1,0:T(8,128)(2,1)S(1)} collective-permute-done((bf16[48,2560]{1,0:T(8,128)(2,1)S(1)}, bf16[48,2560]{1,0:T(8,128)(2,1)S(1)}, u32[]{:S(2)}, u32[]{:S(2)}) %collective-permute-start.27) | collective-permute-done | bytes 245792 | tf_op jit(solution)/shard_map/ppermute | solution.py:21
  160.3 5.9 %collective-permute-done.19 = bf16[2,48]{1,0:T(2,128)(2,1)S(1)} collective-permute-done((bf16[2,48]{1,0:T(2,128)(2,1)S(1)}, bf16[2,48]{1,0:T(2,128)(2,1)S(1)}, u32[]{:S(2)}, u32[]{:S(2)}) %collective-permute-start.19) | collective-permute-done | bytes 224 | tf_op jit(solution)/shard_map/ppermute | solution.py:27
  166.2 6.4 %collective-permute-done.21 = bf16[2,48]{1,0:T(2,128)(2,1)S(1)} collective-permute-done((bf16[2,48]{1,0:T(2,128)(2,1)S(1)}, bf16[2,48]{1,0:T(2,128)(2,1)S(1)}, u32[]{:S(2)}, u32[]{:S(2)}) %collective-permute-start.21) | collective-permute-done | bytes 224 | tf_op jit(solution)/shard_map/ppermute | solution.py:27
  185.8 4.8 %collective-permute-done.23 = bf16[2,48,2560]{2,1,0:T(8,128)(2,1)S(1)} collective-permute-done((bf16[2,48,2560]{2,1,0:T(8,128)(2,1)S(1)}, bf16[2,48,2560]{2,1,0:T(8,128)(2,1)S(1)}, u32[]{:S(2)}, u32[]{:S(2)}) %collective-permute-start.23) | collective-permute-done | bytes 491552 | tf_op jit(solution)/shard_map/ppermute | solution.py:27
  200.1 2.9 %multiply_reduce_fusion = (bf16[384]{0:T(512)(128)(2,1)S(1)}, bf16[384,192]{0,1:T(8,128)(2,1)S(1)}, bf16[384,192]{0,1:T(8,128)(2,1)}, bf16[384,192]{0,1:T(8,128)(2,1)S(1)}) fusion(f32[384,192]{0,1:T(8,128)S(1)} %fusion.118, f32[384,192]{0,1:T(8,128)S(1)} %fusion.119, f32[384]{0:T(512)S(1)} %copy-done.35, bf16[384,2560]{1,0:T(8,128)(2,1)S(1)} %bitcast.213, ...), kind=kOutput, calls=%fused_computation.115 | convolution fusion | flops 383311488 | bytes 3983617 | tf_op jit(solution)/shard_map/dot_general | solution.py:36
  203.0 3.0 %convolution_convert_fusion = bf16[384,2560]{1,0:T(8,128)(2,1)} fusion(bf16[384,2560]{1,0:T(8,128)(2,1)S(1)} %bitcast.217, bf16[384,2560]{1,0:T(8,128)(2,1)S(1)} %bitcast.234, bf16[384,192]{0,1:T(8,128)(2,1)S(1)} %get-tuple-element.59, bf16[384,192]{0,1:T(8,128)(2,1)S(1)} %get-tuple-element.53, bf16[384,192]{0,1:T(8,128)(2,1)S(1)} %copy-done.25, ...), kind=kOutput, calls=%fused_computation.4 | convolution fusion | flops 1521156096 | bytes 6488064 | tf_op jit(solution)/shard_map/dot_general | solution.py:42
  211.6 2.5 collective-permute-start.43
  219.0 3.8 %collective-permute-done.32 = bf16[2,48,1280]{2,1,0:T(8,128)(2,1)S(1)} collective-permute-done((bf16[2,48,1280]{2,1,0:T(8,128)(2,1)S(1)}, bf16[2,48,1280]{2,1,0:T(8,128)(2,1)S(1)}, u32[]{:S(2)}, u32[]{:S(2)}) %collective-permute-start.32) | collective-permute-done | bytes 245792 | tf_op jit(solution)/shard_map/ppermute | solution.py:27
  227.4 6.4 %collective-permute-done.44 = f32[48]{0:T(128)S(1)} collective-permute-done((f32[48]{0:T(128)S(1)}, f32[48]{0:T(128)S(1)}, u32[]{:S(2)}, u32[]{:S(2)}) %collective-permute-start.44) | collective-permute-done | bytes 224 | tf_op jit(solution)/shard_map/ppermute | solution.py:21
  235.6 2.7 %collective-permute-start.36 = (bf16[48,2560]{1,0:T(8,128)(2,1)S(1)}, bf16[48,2560]{1,0:T(8,128)(2,1)S(1)}, u32[]{:S(2)}, u32[]{:S(2)}) collective-permute-start(bf16[48,2560]{1,0:T(8,128)(2,1)S(1)} %fusion.70), channel_id=1, source_target_pairs={{0,8},{8,0},{1,9},{9,1},{2,10},{10,2},{3,11},{11,3},{4,12},{12,4},... | collective-permute-start | bytes 737288 | tf_op jit(solution)/shard_map/ppermute | solution.py:21
  238.9 6.4 %collective-permute-done.36 = bf16[48,2560]{1,0:T(8,128)(2,1)S(1)} collective-permute-done((bf16[48,2560]{1,0:T(8,128)(2,1)S(1)}, bf16[48,2560]{1,0:T(8,128)(2,1)S(1)}, u32[]{:S(2)}, u32[]{:S(2)}) %collective-permute-start.36) | collective-permute-done | bytes 245792 | tf_op jit(solution)/shard_map/ppermute | solution.py:21
  (280 shorter events, 99.0 us)
Async XLA Ops:
  7.2 241.1 %reduce-scatter.3.cloned.1.call-start = ((), (), s32[]{:S(2)}) async-start(), calls=%async_computation.2 | async-start | bytes 2949120 | tf_op jit(solution)/shard_map/reduce_scatter | solution.py:269
  14.1 25.9 %collective-permute-start.4 = (bf16[96,2560]{1,0:T(8,128)(2,1)S(1)}, bf16[96,2560]{1,0:T(8,128)(2,1)S(1)}, u32[]{:S(2)}, u32[]{:S(2)}) collective-permute-start(bf16[96,2560]{1,0:T(8,128)(2,1)S(1)} %get-tuple-element.51), channel_id=1, source_target_pairs={{0,8},{8,0},{1,9},{9,1},{2,10},{10,2},{3,11},{11,3},{4,12},{12,4},... | collective-permute-start | bytes 1474568 | tf_op jit(solution)/shard_map/ppermute | solution.py:21
  41.0 35.6 %collective-permute-start.5 = (bf16[2,96,2560]{2,1,0:T(8,128)(2,1)}, bf16[2,96,2560]{2,1,0:T(8,128)(2,1)S(1)}, u32[]{:S(2)}, u32[]{:S(2)}) collective-permute-start(bf16[2,96,2560]{2,1,0:T(8,128)(2,1)} %get-tuple-element.49), channel_id=1, source_target_pairs={{0,2},{2,0},{4,6},{6,4},{1,3},{3,1},{5,7},{7,5},{8,10},{10,8},{12,... | collective-permute-start | bytes 2949128 | tf_op jit(solution)/shard_map/ppermute | solution.py:27
  42.6 34.3 %collective-permute-start.6 = (bf16[2,96,2560]{2,1,0:T(8,128)(2,1)}, bf16[2,96,2560]{2,1,0:T(8,128)(2,1)}, u32[]{:S(2)}, u32[]{:S(2)}) collective-permute-start(bf16[2,96,2560]{2,1,0:T(8,128)(2,1)} %get-tuple-element.49), channel_id=1, source_target_pairs={{0,4},{2,6},{4,0},{6,2},{1,5},{3,7},{5,1},{7,3},{8,12},{10,14},{12... | collective-permute-start | bytes 2949128 | tf_op jit(solution)/shard_map/ppermute | solution.py:27
  43.2 35.6 %collective-permute-start.11 = (bf16[192,1280]{1,0:T(8,128)(2,1)S(1)}, bf16[192,1280]{1,0:T(8,128)(2,1)}, u32[]{:S(2)}, u32[]{:S(2)}) collective-permute-start(bf16[192,1280]{1,0:T(8,128)(2,1)S(1)} %bitcast.238), channel_id=1, source_target_pairs={{0,1},{1,0},{2,3},{3,2},{4,5},{5,4},{6,7},{7,6},{8,9},{9,8},{10,11... | collective-permute-start | bytes 1474568 | tf_op jit(solution)/shard_map/ppermute | solution.py:27
  43.4 21.0 %collective-permute-start = (bf16[48]{0:T(256)(128)(2,1)S(1)}, bf16[48]{0:T(256)(128)(2,1)S(1)}, u32[]{:S(2)}, u32[]{:S(2)}) collective-permute-start(bf16[48]{0:T(256)(128)(2,1)S(1)} %get-tuple-element.97), channel_id=1, source_target_pairs={{0,8},{8,0},{1,9},{9,1},{2,10},{10,2},{3,11},{11,3},{4,12},{12,4},... | collective-permute-start | bytes 296 | tf_op jit(solution)/shard_map/ppermute | solution.py:21
  76.5 19.5 %collective-permute-start.9 = (bf16[192,1280]{1,0:T(8,128)(2,1)}, bf16[192,1280]{1,0:T(8,128)(2,1)}, u32[]{:S(2)}, u32[]{:S(2)}) collective-permute-start(bf16[192,1280]{1,0:T(8,128)(2,1)} %bitcast.255), channel_id=1, source_target_pairs={{0,1},{1,0},{2,3},{3,2},{4,5},{5,4},{6,7},{7,6},{8,9},{9,8},{10,11... | collective-permute-start | bytes 1474568 | tf_op jit(solution)/shard_map/ppermute | solution.py:27
  76.7 13.7 %collective-permute-start.7 = (bf16[2,96,1280]{2,1,0:T(8,128)(2,1)S(1)}, bf16[2,96,1280]{2,1,0:T(8,128)(2,1)S(1)}, u32[]{:S(2)}, u32[]{:S(2)}) collective-permute-start(bf16[2,96,1280]{2,1,0:T(8,128)(2,1)S(1)} %slice.349), channel_id=1, source_target_pairs={{0,4},{2,6},{4,0},{6,2},{1,5},{3,7},{5,1},{7,3},{8,12},{10,14},{12... | collective-permute-start | bytes 1474568 | tf_op jit(solution)/shard_map/ppermute | solution.py:27
  78.2 13.7 %collective-permute-start.8 = (bf16[2,96,1280]{2,1,0:T(8,128)(2,1)S(1)}, bf16[2,96,1280]{2,1,0:T(8,128)(2,1)S(1)}, u32[]{:S(2)}, u32[]{:S(2)}) collective-permute-start(bf16[2,96,1280]{2,1,0:T(8,128)(2,1)S(1)} %slice.350), channel_id=1, source_target_pairs={{0,2},{2,0},{4,6},{6,4},{1,3},{3,1},{5,7},{7,5},{8,10},{10,8},{12,... | collective-permute-start | bytes 1474568 | tf_op jit(solution)/shard_map/ppermute | solution.py:27
  108.9 14.3 %collective-permute-start.15 = (bf16[2,48,2560]{2,1,0:T(8,128)(2,1)}, bf16[2,48,2560]{2,1,0:T(8,128)(2,1)S(1)}, u32[]{:S(2)}, u32[]{:S(2)}) collective-permute-start(bf16[2,48,2560]{2,1,0:T(8,128)(2,1)} %pad_maximum_fusion.11), channel_id=1, source_target_pairs={{0,2},{2,0},{4,6},{6,4},{1,3},{3,1},{5,7},{7,5},{8,10},{10,8},{12,... | collective-permute-start | bytes 1474568 | tf_op jit(solution)/shard_map/ppermute | solution.py:27
  110.4 12.9 %collective-permute-start.13 = (bf16[2,48,2560]{2,1,0:T(8,128)(2,1)}, bf16[2,48,2560]{2,1,0:T(8,128)(2,1)S(1)}, u32[]{:S(2)}, u32[]{:S(2)}) collective-permute-start(bf16[2,48,2560]{2,1,0:T(8,128)(2,1)} %pad_maximum_fusion.10), channel_id=1, source_target_pairs={{0,4},{2,6},{4,0},{6,2},{1,5},{3,7},{5,1},{7,3},{8,12},{10,14},{12... | collective-permute-start | bytes 1474568 | tf_op jit(solution)/shard_map/ppermute | solution.py:27
  126.3 11.6 %collective-permute-start.16 = (bf16[48,2560]{1,0:T(8,128)(2,1)}, bf16[48,2560]{1,0:T(8,128)(2,1)S(1)}, u32[]{:S(2)}, u32[]{:S(2)}) collective-permute-start(bf16[48,2560]{1,0:T(8,128)(2,1)} %fusion.69), channel_id=1, source_target_pairs={{0,8},{8,0},{1,9},{9,1},{2,10},{10,2},{3,11},{11,3},{4,12},{12,4},... | collective-permute-start | bytes 737288 | tf_op jit(solution)/shard_map/ppermute | solution.py:21
  140.3 13.2 %collective-permute-start.27 = (bf16[48,2560]{1,0:T(8,128)(2,1)S(1)}, bf16[48,2560]{1,0:T(8,128)(2,1)S(1)}, u32[]{:S(2)}, u32[]{:S(2)}) collective-permute-start(bf16[48,2560]{1,0:T(8,128)(2,1)S(1)} %get-tuple-element.65), channel_id=1, source_target_pairs={{0,8},{8,0},{1,9},{9,1},{2,10},{10,2},{3,11},{11,3},{4,12},{12,4},... | collective-permute-start | bytes 737288 | tf_op jit(solution)/shard_map/ppermute | solution.py:21
  143.6 11.7 %collective-permute-start.17 = (bf16[64,2560]{1,0:T(8,128)(2,1)S(1)}, bf16[64,2560]{1,0:T(8,128)(2,1)S(1)}, u32[]{:S(2)}, u32[]{:S(2)}) collective-permute-start(bf16[64,2560]{1,0:T(8,128)(2,1)S(1)} %fusion.32), channel_id=1, source_target_pairs={{16,0},{17,1},{18,2},{19,3},{20,4},{21,5},{22,6},{23,7},{24,8},{25... | collective-permute-start | bytes 983048 | tf_op jit(solution)/shard_map/ppermute | solution.py:15
  147.1 12.7 %collective-permute-start.20 = (bf16[2,48]{1,0:T(2,128)(2,1)S(1)}, bf16[2,48]{1,0:T(2,128)(2,1)S(1)}, u32[]{:S(2)}, u32[]{:S(2)}) collective-permute-start(bf16[2,48]{1,0:T(2,128)(2,1)S(1)} %pad_maximum_fusion.19), channel_id=1, source_target_pairs={{0,4},{2,6},{4,0},{6,2},{1,5},{3,7},{5,1},{7,3},{8,12},{10,14},{12... | collective-permute-start | bytes 584 | tf_op jit(solution)/shard_map/ppermute | solution.py:27
  154.3 19.0 %collective-permute-start.28 = (bf16[2,48,2560]{2,1,0:T(8,128)(2,1)}, bf16[2,48,2560]{2,1,0:T(8,128)(2,1)S(1)}, u32[]{:S(2)}, u32[]{:S(2)}) collective-permute-start(bf16[2,48,2560]{2,1,0:T(8,128)(2,1)} %get-tuple-element.63), channel_id=1, source_target_pairs={{0,2},{2,0},{4,6},{6,4},{1,3},{3,1},{5,7},{7,5},{8,10},{10,8},{12,... | collective-permute-start | bytes 1474568 | tf_op jit(solution)/shard_map/ppermute | solution.py:27
  155.4 18.3 %collective-permute-start.29 = (bf16[2,48,2560]{2,1,0:T(8,128)(2,1)}, bf16[2,48,2560]{2,1,0:T(8,128)(2,1)}, u32[]{:S(2)}, u32[]{:S(2)}) collective-permute-start(bf16[2,48,2560]{2,1,0:T(8,128)(2,1)} %get-tuple-element.63), channel_id=1, source_target_pairs={{0,4},{2,6},{4,0},{6,2},{1,5},{3,7},{5,1},{7,3},{8,12},{10,14},{12... | collective-permute-start | bytes 1474568 | tf_op jit(solution)/shard_map/ppermute | solution.py:27
  156.5 19.3 %collective-permute-start.22 = (bf16[48,2560]{1,0:T(8,128)(2,1)}, bf16[48,2560]{1,0:T(8,128)(2,1)}, u32[]{:S(2)}, u32[]{:S(2)}) collective-permute-start(bf16[48,2560]{1,0:T(8,128)(2,1)} %get-tuple-element.69), channel_id=1, source_target_pairs={{0,8},{8,0},{1,9},{9,1},{2,10},{10,2},{3,11},{11,3},{4,12},{12,4},... | collective-permute-start | bytes 737288 | tf_op jit(solution)/shard_map/ppermute | solution.py:21
  159.8 12.8 %collective-permute-start.21 = (bf16[2,48]{1,0:T(2,128)(2,1)S(1)}, bf16[2,48]{1,0:T(2,128)(2,1)S(1)}, u32[]{:S(2)}, u32[]{:S(2)}) collective-permute-start(bf16[2,48]{1,0:T(2,128)(2,1)S(1)} %pad_maximum_fusion.19), channel_id=1, source_target_pairs={{0,6},{2,4},{4,2},{6,0},{1,7},{3,5},{5,3},{7,1},{8,14},{10,12},{12... | collective-permute-start | bytes 584 | tf_op jit(solution)/shard_map/ppermute | solution.py:27
  176.8 13.7 %collective-permute-start.23 = (bf16[2,48,2560]{2,1,0:T(8,128)(2,1)S(1)}, bf16[2,48,2560]{2,1,0:T(8,128)(2,1)S(1)}, u32[]{:S(2)}, u32[]{:S(2)}) collective-permute-start(bf16[2,48,2560]{2,1,0:T(8,128)(2,1)S(1)} %get-tuple-element.67), channel_id=1, source_target_pairs={{0,2},{2,0},{4,6},{6,4},{1,3},{3,1},{5,7},{7,5},{8,10},{10,8},{12,... | collective-permute-start | bytes 1474568 | tf_op jit(solution)/shard_map/ppermute | solution.py:27
  177.8 14.9 %collective-permute-start.24 = (bf16[2,48,2560]{2,1,0:T(8,128)(2,1)S(1)}, bf16[2,48,2560]{2,1,0:T(8,128)(2,1)S(1)}, u32[]{:S(2)}, u32[]{:S(2)}) collective-permute-start(bf16[2,48,2560]{2,1,0:T(8,128)(2,1)S(1)} %get-tuple-element.67), channel_id=1, source_target_pairs={{0,4},{2,6},{4,0},{6,2},{1,5},{3,7},{5,1},{7,3},{8,12},{10,14},{12... | collective-permute-start | bytes 1474568 | tf_op jit(solution)/shard_map/ppermute | solution.py:27
  206.1 44.4 %reduce-scatter.5.cloned.1.call-start = ((), (), s32[]{:S(2)}) async-start(), calls=%async_computation.3 | async-start | bytes 1474560 | tf_op jit(solution)/shard_map/reduce_scatter | solution.py:272
  218.0 16.7 %collective-permute-start.35 = (bf16[2,48,2560]{2,1,0:T(8,128)(2,1)S(1)}, bf16[2,48,2560]{2,1,0:T(8,128)(2,1)S(1)}, u32[]{:S(2)}, u32[]{:S(2)}) collective-permute-start(bf16[2,48,2560]{2,1,0:T(8,128)(2,1)S(1)} %pad_maximum_fusion.15), channel_id=1, source_target_pairs={{0,2},{2,0},{4,6},{6,4},{1,3},{3,1},{5,7},{7,5},{8,10},{10,8},{12,... | collective-permute-start | bytes 1474568 | tf_op jit(solution)/shard_map/ppermute | solution.py:27
  223.7 11.7 %collective-permute-start.33 = (bf16[2,48,2560]{2,1,0:T(8,128)(2,1)}, bf16[2,48,2560]{2,1,0:T(8,128)(2,1)S(1)}, u32[]{:S(2)}, u32[]{:S(2)}) collective-permute-start(bf16[2,48,2560]{2,1,0:T(8,128)(2,1)} %pad_maximum_fusion.14), channel_id=1, source_target_pairs={{0,4},{2,6},{4,0},{6,2},{1,5},{3,7},{5,1},{7,3},{8,12},{10,14},{12... | collective-permute-start | bytes 1474568 | tf_op jit(solution)/shard_map/ppermute | solution.py:27
  (66 other events, 586.7 us)
Sparse Core Ops, SparseCore 0:
  206.2 8.3 reduce-scatter.2
  227.5 8.1 reduce-scatter.4

commit v12 on v10

--- a/solution.py
+++ b/solution.py
@@ -15,16 +15,27 @@
     return lax.ppermute(block, axis, route)
 
 
+def in_streams(block, axis, route):
+    width = block.shape[-1]
+    if width < 2048 or width % 256:
+        return lax.ppermute(block, axis, route)
+    half = width // 2
+    return jnp.concatenate(
+        [lax.ppermute(block[..., :half], axis, route), lax.ppermute(block[..., half:], axis, route)],
+        axis=-1,
+    )
+
+
 def rotated(block, axis, distance):
     size = lax.axis_size(axis)
     route = [(i, (i + distance) % size) for i in range(size)]
-    return lax.ppermute(block, axis, route)
+    return in_streams(block, axis, route)
 
 
 def flipped(block, axis, mask):
     size = lax.axis_size(axis)
     route = [(i, i ^ mask) for i in range(size)]
-    return lax.ppermute(block, axis, route)
+    return in_streams(block, axis, route)
 
 
 def silu_parts(gate_value):

time: 238 us -> 242 us (1.017)
  starting transfers between devices: 55 us -> 75.1 us
  waiting for transfers between devices: 115 us -> 100 us
    ppermute x49 -> x67, starting transfers between devices: 53.5 us -> 73.5 us  [the longest x31 36 us: in_streams(): return lax.ppermute(block, axis, route)]
    ppermute x49 -> x67, waiting for transfers between devices: 115 us -> 100 us  [the longest x31 35.2 us: in_streams(): return lax.ppermute(block, axis, route)]
    another operation x12 -> x20, other arithmetic: 5.08 us -> 1.58 us  [gather_quad(): return jnp.stack([staged, first, second, diagonal])]
    concatenate x4 -> x0, other arithmetic: 2.47 us -> none  [the longest x2 1.62 us: reduce_quad(): jnp.concatenate([(parts[2][..., :half].astype(jnp.float32) + from_first)....]
  transfers between devices with their start and end apart: 52 -> 70, of which waited for: 26 -> 35; matrix products, arithmetic and copies ran while one was open for 16% -> 14% of each run, Pallas kernels for 0% -> 0%
where the time goes in v12:
time: 242 us; the launch traced here: 241 us
  waiting for transfers between devices  100 us (41%)
  starting transfers between devices  75.1 us (31%)
  other arithmetic  19.7 us (8%)
  matrix products  16.2 us (7%)
  between operations  15.1 us (6%)
  local copies, waits for them, and re-layouts  14.9 us (6%)
    ppermute x31, starting transfers between devices, in_streams(): return lax.ppermute(block, axis, route)  36 us
    ppermute x31, waiting for transfers between devices, in_streams(): return lax.ppermute(block, axis, route)  35.2 us
    ppermute x18, waiting for transfers between devices, in_streams(): lax.ppermute(block[..., half:], axis, route)  34.9 us
    ppermute x18, waiting for transfers between devices, in_streams(): lax.ppermute(block[..., :half], axis, route)  30 us
    ppermute x18, starting transfers between devices, in_streams(): lax.ppermute(block[..., :half], axis, route)  20.9 us
    ppermute x18, starting transfers between devices, in_streams(): lax.ppermute(block[..., half:], axis, route)  16.6 us
    dot_general x6, matrix products, contract_last(): lax.dot_general(first_operand, second_operand, (((1,), (1,)), ((), ())),...  6.33 us
    dot_general x2, matrix products, contract_first(): lax.dot_general(first_operand, second_operand, (((0,), (0,)), ((), ())),...  4.88 us
  transfers between devices with their start and end apart: 70, of which 35 were waited for; matrix products, arithmetic and copies ran while one was open for 14% of the time, Pallas kernels for 0%

profile of v12, /device:TPU:0, one launch (start us, length us, event | category | flops | bytes accessed | tf_op | source)
XLA Modules:
  0.0 241.0 jit_solution(17953470863476208772)
XLA Ops:
  10.1 4.0 %collective-permute-start = (bf16[48]{0:T(256)(128)(2,1)S(1)}, bf16[48]{0:T(256)(128)(2,1)S(1)}, u32[]{:S(2)}, u32[]{:S(2)}) collective-permute-start(bf16[48]{0:T(256)(128)(2,1)S(1)} %get-tuple-element.105), channel_id=1, source_target_pairs={{0,8},{8,0},{1,9},{9,1},{2,10},{10,2},{3,11},{11,3},{4,12},{12,4},... | collective-permute-start | bytes 296 | tf_op jit(solution)/shard_map/ppermute | solution.py:21
  17.2 2.9 %collective-permute-start.13 = (bf16[48,1280]{1,0:T(8,128)(2,1)}, bf16[48,1280]{1,0:T(8,128)(2,1)S(1)}, u32[]{:S(2)}, u32[]{:S(2)}) collective-permute-start(bf16[48,1280]{1,0:T(8,128)(2,1)} %get-tuple-element.68), channel_id=1, source_target_pairs={{0,8},{8,0},{1,9},{9,1},{2,10},{10,2},{3,11},{11,3},{4,12},{12,4},... | collective-permute-start | bytes 368648 | tf_op jit(solution)/shard_map/ppermute | solution.py:24
  25.1 3.3 %collective-permute-start.3 = (bf16[2,48]{1,0:T(2,128)(2,1)S(1)}, bf16[2,48]{1,0:T(2,128)(2,1)S(1)}, u32[]{:S(2)}, u32[]{:S(2)}) collective-permute-start(bf16[2,48]{1,0:T(2,128)(2,1)S(1)} %pad_maximum_fusion.15), channel_id=1, source_target_pairs={{0,6},{2,4},{4,2},{6,0},{1,7},{3,5},{5,3},{7,1},{8,14},{10,12},{12... | collective-permute-start | bytes 584 | tf_op jit(solution)/shard_map/ppermute | solution.py:21
  30.1 5.7 %collective-permute-done.13 = bf16[48,1280]{1,0:T(8,128)(2,1)S(1)} collective-permute-done((bf16[48,1280]{1,0:T(8,128)(2,1)}, bf16[48,1280]{1,0:T(8,128)(2,1)S(1)}, u32[]{:S(2)}, u32[]{:S(2)}) %collective-permute-start.13) | collective-permute-done | bytes 122912 | tf_op jit(solution)/shard_map/ppermute | solution.py:24
  35.8 2.7 %collective-permute-done.14 = bf16[48,1280]{1,0:T(8,128)(2,1)} collective-permute-done((bf16[48,1280]{1,0:T(8,128)(2,1)}, bf16[48,1280]{1,0:T(8,128)(2,1)}, u32[]{:S(2)}, u32[]{:S(2)}) %collective-permute-start.14) | collective-permute-done | bytes 122912 | tf_op jit(solution)/shard_map/ppermute | solution.py:24
  41.8 6.6 %collective-permute-done.17 = bf16[2,48,1280]{2,1,0:T(8,128)(2,1)S(1)} collective-permute-done((bf16[2,48,1280]{2,1,0:T(8,128)(2,1)S(1)}, bf16[2,48,1280]{2,1,0:T(8,128)(2,1)S(1)}, u32[]{:S(2)}, u32[]{:S(2)}) %collective-permute-start.17) | collective-permute-done | bytes 245792 | tf_op jit(solution)/shard_map/ppermute | solution.py:24
  49.9 3.4 %collective-permute-done.18 = bf16[2,48,1280]{2,1,0:T(8,128)(2,1)S(1)} collective-permute-done((bf16[2,48,1280]{2,1,0:T(8,128)(2,1)S(1)}, bf16[2,48,1280]{2,1,0:T(8,128)(2,1)S(1)}, u32[]{:S(2)}, u32[]{:S(2)}) %collective-permute-start.18) | collective-permute-done | bytes 245792 | tf_op jit(solution)/shard_map/ppermute | solution.py:24
  56.1 4.8 %collective-permute-done.16 = bf16[2,48,1280]{2,1,0:T(8,128)(2,1)S(1)} collective-permute-done((bf16[2,48,1280]{2,1,0:T(8,128)(2,1)S(1)}, bf16[2,48,1280]{2,1,0:T(8,128)(2,1)S(1)}, u32[]{:S(2)}, u32[]{:S(2)}) %collective-permute-start.16) | collective-permute-done | bytes 245792 | tf_op jit(solution)/shard_map/ppermute | solution.py:24
  63.4 4.2 %collective-permute-done.9 = bf16[2,48,1280]{2,1,0:T(8,128)(2,1)S(1)} collective-permute-done((bf16[2,48,1280]{2,1,0:T(8,128)(2,1)S(1)}, bf16[2,48,1280]{2,1,0:T(8,128)(2,1)S(1)}, u32[]{:S(2)}, u32[]{:S(2)}) %collective-permute-start.9) | collective-permute-done | bytes 245792 | tf_op jit(solution)/shard_map/ppermute | solution.py:24
  69.9 4.1 %collective-permute-done.7 = bf16[2,48,1280]{2,1,0:T(8,128)(2,1)S(1)} collective-permute-done((bf16[2,48,1280]{2,1,0:T(8,128)(2,1)S(1)}, bf16[2,48,1280]{2,1,0:T(8,128)(2,1)S(1)}, u32[]{:S(2)}, u32[]{:S(2)}) %collective-permute-start.7) | collective-permute-done | bytes 245792 | tf_op jit(solution)/shard_map/ppermute | solution.py:24
  77.4 4.3 %collective-permute-done.20 = bf16[2,48,1280]{2,1,0:T(8,128)(2,1)S(1)} collective-permute-done((bf16[2,48,1280]{2,1,0:T(8,128)(2,1)S(1)}, bf16[2,48,1280]{2,1,0:T(8,128)(2,1)S(1)}, u32[]{:S(2)}, u32[]{:S(2)}) %collective-permute-start.20) | collective-permute-done | bytes 245792 | tf_op jit(solution)/shard_map/ppermute | solution.py:21
  103.0 5.2 %collective-permute-done.23 = bf16[2,48,1280]{2,1,0:T(8,128)(2,1)S(1)} collective-permute-done((bf16[2,48,1280]{2,1,0:T(8,128)(2,1)}, bf16[2,48,1280]{2,1,0:T(8,128)(2,1)S(1)}, u32[]{:S(2)}, u32[]{:S(2)}) %collective-permute-start.23) | collective-permute-done | bytes 245792 | tf_op jit(solution)/shard_map/ppermute | solution.py:21
  110.8 6.0 %collective-permute-done.63 = f32[48]{0:T(128)S(1)} collective-permute-done((f32[48]{0:T(128)S(1)}, f32[48]{0:T(128)S(1)}, u32[]{:S(2)}, u32[]{:S(2)}) %collective-permute-start.63) | collective-permute-done | bytes 224 | tf_op jit(solution)/shard_map/ppermute | solution.py:21
  118.8 3.3 %collective-permute-start.29 = (bf16[48,1280]{1,0:T(8,128)(2,1)S(1)}, bf16[48,1280]{1,0:T(8,128)(2,1)S(1)}, u32[]{:S(2)}, u32[]{:S(2)}) collective-permute-start(bf16[48,1280]{1,0:T(8,128)(2,1)S(1)} %get-tuple-element.78), channel_id=1, source_target_pairs={{0,8},{8,0},{1,9},{9,1},{2,10},{10,2},{3,11},{11,3},{4,12},{12,4},... | collective-permute-start | bytes 368648 | tf_op jit(solution)/shard_map/ppermute | solution.py:24
  122.8 8.1 %collective-permute-done.29 = bf16[48,1280]{1,0:T(8,128)(2,1)S(1)} collective-permute-done((bf16[48,1280]{1,0:T(8,128)(2,1)S(1)}, bf16[48,1280]{1,0:T(8,128)(2,1)S(1)}, u32[]{:S(2)}, u32[]{:S(2)}) %collective-permute-start.29) | collective-permute-done | bytes 122912 | tf_op jit(solution)/shard_map/ppermute | solution.py:24
  130.8 2.6 %collective-permute-done.30 = bf16[48,1280]{1,0:T(8,128)(2,1)S(1)} collective-permute-done((bf16[48,1280]{1,0:T(8,128)(2,1)S(1)}, bf16[48,1280]{1,0:T(8,128)(2,1)S(1)}, u32[]{:S(2)}, u32[]{:S(2)}) %collective-permute-start.30) | collective-permute-done | bytes 122912 | tf_op jit(solution)/shard_map/ppermute | solution.py:24
  136.6 2.9 %collective-permute-start.44 = (bf16[48,1280]{1,0:T(8,128)(2,1)}, bf16[48,1280]{1,0:T(8,128)(2,1)}, u32[]{:S(2)}, u32[]{:S(2)}) collective-permute-start(bf16[48,1280]{1,0:T(8,128)(2,1)} %get-tuple-element.76), channel_id=1, source_target_pairs={{0,8},{8,0},{1,9},{9,1},{2,10},{10,2},{3,11},{11,3},{4,12},{12,4},... | collective-permute-start | bytes 368648 | tf_op jit(solution)/shard_map/ppermute | solution.py:24
  158.5 3.0 %collective-permute-done.48 = bf16[2,48,1280]{2,1,0:T(8,128)(2,1)S(1)} collective-permute-done((bf16[2,48,1280]{2,1,0:T(8,128)(2,1)S(1)}, bf16[2,48,1280]{2,1,0:T(8,128)(2,1)S(1)}, u32[]{:S(2)}, u32[]{:S(2)}) %collective-permute-start.48) | collective-permute-done | bytes 245792 | tf_op jit(solution)/shard_map/ppermute | solution.py:24
  163.9 5.5 %collective-permute-done.49 = bf16[2,48,1280]{2,1,0:T(8,128)(2,1)S(1)} collective-permute-done((bf16[2,48,1280]{2,1,0:T(8,128)(2,1)S(1)}, bf16[2,48,1280]{2,1,0:T(8,128)(2,1)S(1)}, u32[]{:S(2)}, u32[]{:S(2)}) %collective-permute-start.49) | collective-permute-done | bytes 245792 | tf_op jit(solution)/shard_map/ppermute | solution.py:24
  180.9 3.5 %collective-permute-done.42 = bf16[2,48,1280]{2,1,0:T(8,128)(2,1)S(1)} collective-permute-done((bf16[2,48,1280]{2,1,0:T(8,128)(2,1)S(1)}, bf16[2,48,1280]{2,1,0:T(8,128)(2,1)S(1)}, u32[]{:S(2)}, u32[]{:S(2)}) %collective-permute-start.42) | collective-permute-done | bytes 245792 | tf_op jit(solution)/shard_map/ppermute | solution.py:21
  188.8 3.0 %convolution_convert_fusion = bf16[384,2560]{1,0:T(8,128)(2,1)} fusion(bf16[384,2560]{1,0:T(8,128)(2,1)S(1)} %bitcast.238, bf16[384,2560]{1,0:T(8,128)(2,1)S(1)} %bitcast.232, bf16[384,192]{0,1:T(8,128)(2,1)S(1)} %get-tuple-element.53, bf16[384,192]{0,1:T(8,128)(2,1)S(1)} %get-tuple-element.47, bf16[384,192]{0,1:T(8,128)(2,1)S(1)} %copy-done.20, ...), kind=kOutput, calls=%fused_computation.4 | convolution fusion | flops 1521156096 | bytes 6488064 | tf_op jit(solution)/shard_map/dot_general | solution.py:53
  205.9 6.4 %collective-permute-done.56 = bf16[2,48,1280]{2,1,0:T(8,128)(2,1)S(1)} collective-permute-done((bf16[2,48,1280]{2,1,0:T(8,128)(2,1)S(1)}, bf16[2,48,1280]{2,1,0:T(8,128)(2,1)S(1)}, u32[]{:S(2)}, u32[]{:S(2)}) %collective-permute-start.56) | collective-permute-done | bytes 245792 | tf_op jit(solution)/shard_map/ppermute | solution.py:21
  215.6 3.0 %collective-permute-done.57 = bf16[2,48,1280]{2,1,0:T(8,128)(2,1)S(1)} collective-permute-done((bf16[2,48,1280]{2,1,0:T(8,128)(2,1)S(1)}, bf16[2,48,1280]{2,1,0:T(8,128)(2,1)S(1)}, u32[]{:S(2)}, u32[]{:S(2)}) %collective-permute-start.57) | collective-permute-done | bytes 245792 | tf_op jit(solution)/shard_map/ppermute | solution.py:24
  222.8 4.3 %collective-permute-done.58 = bf16[48,1280]{1,0:T(8,128)(2,1)S(1)} collective-permute-done((bf16[48,1280]{1,0:T(8,128)(2,1)S(1)}, bf16[48,1280]{1,0:T(8,128)(2,1)S(1)}, u32[]{:S(2)}, u32[]{:S(2)}) %collective-permute-start.58) | collective-permute-done | bytes 122912 | tf_op jit(solution)/shard_map/ppermute | solution.py:24
  (335 shorter events, 123.0 us)
Async XLA Ops:
  7.2 224.8 %reduce-scatter.3.cloned.1.call-start = ((), (), s32[]{:S(2)}) async-start(), calls=%async_computation.2 | async-start | bytes 2949120 | tf_op jit(solution)/shard_map/reduce_scatter | solution.py:271
  15.7 23.9 %collective-permute-start.4 = (bf16[48,1280]{1,0:T(8,128)(2,1)S(1)}, bf16[48,1280]{1,0:T(8,128)(2,1)S(1)}, u32[]{:S(2)}, u32[]{:S(2)}) collective-permute-start(bf16[48,1280]{1,0:T(8,128)(2,1)S(1)} %get-tuple-element.72), channel_id=1, source_target_pairs={{0,8},{8,0},{1,9},{9,1},{2,10},{10,2},{3,11},{11,3},{4,12},{12,4},... | collective-permute-start | bytes 368648 | tf_op jit(solution)/shard_map/ppermute | solution.py:24
  17.2 18.6 %collective-permute-start.13 = (bf16[48,1280]{1,0:T(8,128)(2,1)}, bf16[48,1280]{1,0:T(8,128)(2,1)S(1)}, u32[]{:S(2)}, u32[]{:S(2)}) collective-permute-start(bf16[48,1280]{1,0:T(8,128)(2,1)} %get-tuple-element.68), channel_id=1, source_target_pairs={{0,8},{8,0},{1,9},{9,1},{2,10},{10,2},{3,11},{11,3},{4,12},{12,4},... | collective-permute-start | bytes 368648 | tf_op jit(solution)/shard_map/ppermute | solution.py:24
  20.1 18.5 %collective-permute-start.14 = (bf16[48,1280]{1,0:T(8,128)(2,1)}, bf16[48,1280]{1,0:T(8,128)(2,1)}, u32[]{:S(2)}, u32[]{:S(2)}) collective-permute-start(bf16[48,1280]{1,0:T(8,128)(2,1)} %get-tuple-element.69), channel_id=1, source_target_pairs={{0,8},{8,0},{1,9},{9,1},{2,10},{10,2},{3,11},{11,3},{4,12},{12,4},... | collective-permute-start | bytes 368648 | tf_op jit(solution)/shard_map/ppermute | solution.py:24
  28.4 11.5 %collective-permute-start.5 = (bf16[48,1280]{1,0:T(8,128)(2,1)S(1)}, bf16[48,1280]{1,0:T(8,128)(2,1)S(1)}, u32[]{:S(2)}, u32[]{:S(2)}) collective-permute-start(bf16[48,1280]{1,0:T(8,128)(2,1)S(1)} %get-tuple-element.73), channel_id=1, source_target_pairs={{0,8},{8,0},{1,9},{9,1},{2,10},{10,2},{3,11},{11,3},{4,12},{12,4},... | collective-permute-start | bytes 368648 | tf_op jit(solution)/shard_map/ppermute | solution.py:24
  30.0 45.8 %collective-permute-start.22 = (bf16[192,1280]{1,0:T(8,128)(2,1)S(1)}, bf16[192,1280]{1,0:T(8,128)(2,1)S(1)}, u32[]{:S(2)}, u32[]{:S(2)}) collective-permute-start(bf16[192,1280]{1,0:T(8,128)(2,1)S(1)} %bitcast.249), channel_id=1, source_target_pairs={{0,1},{1,0},{2,3},{3,2},{4,5},{5,4},{6,7},{7,6},{8,9},{9,8},{10,11... | collective-permute-start | bytes 1474568 | tf_op jit(solution)/shard_map/ppermute | solution.py:21
  35.8 40.7 %collective-permute-start.21 = (bf16[192,1280]{1,0:T(8,128)(2,1)}, bf16[192,1280]{1,0:T(8,128)(2,1)S(1)}, u32[]{:S(2)}, u32[]{:S(2)}) collective-permute-start(bf16[192,1280]{1,0:T(8,128)(2,1)} %bitcast.251), channel_id=1, source_target_pairs={{0,1},{1,0},{2,3},{3,2},{4,5},{5,4},{6,7},{7,6},{8,9},{9,8},{10,11... | collective-permute-start | bytes 1474568 | tf_op jit(solution)/shard_map/ppermute | solution.py:21
  38.5 46.9 %collective-permute-start.12 = (bf16[192,1280]{1,0:T(8,128)(2,1)}, bf16[192,1280]{1,0:T(8,128)(2,1)S(1)}, u32[]{:S(2)}, u32[]{:S(2)}) collective-permute-start(bf16[192,1280]{1,0:T(8,128)(2,1)} %bitcast.268), channel_id=1, source_target_pairs={{0,1},{1,0},{2,3},{3,2},{4,5},{5,4},{6,7},{7,6},{8,9},{9,8},{10,11... | collective-permute-start | bytes 1474568 | tf_op jit(solution)/shard_map/ppermute | solution.py:21
  39.9 13.4 %collective-permute-start.18 = (bf16[2,48,1280]{2,1,0:T(8,128)(2,1)S(1)}, bf16[2,48,1280]{2,1,0:T(8,128)(2,1)S(1)}, u32[]{:S(2)}, u32[]{:S(2)}) collective-permute-start(bf16[2,48,1280]{2,1,0:T(8,128)(2,1)S(1)} %get-tuple-element.67), channel_id=1, source_target_pairs={{0,4},{2,6},{4,0},{6,2},{1,5},{3,7},{5,1},{7,3},{8,12},{10,14},{12... | collective-permute-start | bytes 737288 | tf_op jit(solution)/shard_map/ppermute | solution.py:24
  90.0 10.9 %collective-permute-start.27 = (bf16[2,48,1280]{2,1,0:T(8,128)(2,1)}, bf16[2,48,1280]{2,1,0:T(8,128)(2,1)}, u32[]{:S(2)}, u32[]{:S(2)}) collective-permute-start(bf16[2,48,1280]{2,1,0:T(8,128)(2,1)} %get-tuple-element.64), channel_id=1, source_target_pairs={{0,4},{2,6},{4,0},{6,2},{1,5},{3,7},{5,1},{7,3},{8,12},{10,14},{12... | collective-permute-start | bytes 737288 | tf_op jit(solution)/shard_map/ppermute | solution.py:21
  96.5 21.1 %collective-permute-start.25 = (bf16[2,48,1280]{2,1,0:T(8,128)(2,1)}, bf16[2,48,1280]{2,1,0:T(8,128)(2,1)S(1)}, u32[]{:S(2)}, u32[]{:S(2)}) collective-permute-start(bf16[2,48,1280]{2,1,0:T(8,128)(2,1)} %slice.437), channel_id=1, source_target_pairs={{0,4},{2,6},{4,0},{6,2},{1,5},{3,7},{5,1},{7,3},{8,12},{10,14},{12... | collective-permute-start | bytes 737288 | tf_op jit(solution)/shard_map/ppermute | solution.py:24
  98.8 18.8 %collective-permute-start.26 = (bf16[2,48,1280]{2,1,0:T(8,128)(2,1)}, bf16[2,48,1280]{2,1,0:T(8,128)(2,1)}, u32[]{:S(2)}, u32[]{:S(2)}) collective-permute-start(bf16[2,48,1280]{2,1,0:T(8,128)(2,1)} %slice.439), channel_id=1, source_target_pairs={{0,2},{2,0},{4,6},{6,4},{1,3},{3,1},{5,7},{7,5},{8,10},{10,8},{12,... | collective-permute-start | bytes 737288 | tf_op jit(solution)/shard_map/ppermute | solution.py:24
  102.5 15.1 %collective-permute-start.28 = (bf16[2,48,1280]{2,1,0:T(8,128)(2,1)}, bf16[2,48,1280]{2,1,0:T(8,128)(2,1)S(1)}, u32[]{:S(2)}, u32[]{:S(2)}) collective-permute-start(bf16[2,48,1280]{2,1,0:T(8,128)(2,1)} %add_convert_fusion.2), channel_id=1, source_target_pairs={{0,2},{2,0},{4,6},{6,4},{1,3},{3,1},{5,7},{7,5},{8,10},{10,8},{12,... | collective-permute-start | bytes 737288 | tf_op jit(solution)/shard_map/ppermute | solution.py:24
  118.8 12.0 %collective-permute-start.29 = (bf16[48,1280]{1,0:T(8,128)(2,1)S(1)}, bf16[48,1280]{1,0:T(8,128)(2,1)S(1)}, u32[]{:S(2)}, u32[]{:S(2)}) collective-permute-start(bf16[48,1280]{1,0:T(8,128)(2,1)S(1)} %get-tuple-element.78), channel_id=1, source_target_pairs={{0,8},{8,0},{1,9},{9,1},{2,10},{10,2},{3,11},{11,3},{4,12},{12,4},... | collective-permute-start | bytes 368648 | tf_op jit(solution)/shard_map/ppermute | solution.py:24
  122.1 11.3 %collective-permute-start.30 = (bf16[48,1280]{1,0:T(8,128)(2,1)S(1)}, bf16[48,1280]{1,0:T(8,128)(2,1)S(1)}, u32[]{:S(2)}, u32[]{:S(2)}) collective-permute-start(bf16[48,1280]{1,0:T(8,128)(2,1)S(1)} %get-tuple-element.79), channel_id=1, source_target_pairs={{0,8},{8,0},{1,9},{9,1},{2,10},{10,2},{3,11},{11,3},{4,12},{12,4},... | collective-permute-start | bytes 368648 | tf_op jit(solution)/shard_map/ppermute | solution.py:24
  136.6 12.8 %collective-permute-start.44 = (bf16[48,1280]{1,0:T(8,128)(2,1)}, bf16[48,1280]{1,0:T(8,128)(2,1)}, u32[]{:S(2)}, u32[]{:S(2)}) collective-permute-start(bf16[48,1280]{1,0:T(8,128)(2,1)} %get-tuple-element.76), channel_id=1, source_target_pairs={{0,8},{8,0},{1,9},{9,1},{2,10},{10,2},{3,11},{11,3},{4,12},{12,4},... | collective-permute-start | bytes 368648 | tf_op jit(solution)/shard_map/ppermute | solution.py:24
  139.5 12.0 %collective-permute-start.45 = (bf16[48,1280]{1,0:T(8,128)(2,1)}, bf16[48,1280]{1,0:T(8,128)(2,1)}, u32[]{:S(2)}, u32[]{:S(2)}) collective-permute-start(bf16[48,1280]{1,0:T(8,128)(2,1)} %get-tuple-element.77), channel_id=1, source_target_pairs={{0,8},{8,0},{1,9},{9,1},{2,10},{10,2},{3,11},{11,3},{4,12},{12,4},... | collective-permute-start | bytes 368648 | tf_op jit(solution)/shard_map/ppermute | solution.py:24
  154.0 15.4 %collective-permute-start.49 = (bf16[2,48,1280]{2,1,0:T(8,128)(2,1)S(1)}, bf16[2,48,1280]{2,1,0:T(8,128)(2,1)S(1)}, u32[]{:S(2)}, u32[]{:S(2)}) collective-permute-start(bf16[2,48,1280]{2,1,0:T(8,128)(2,1)S(1)} %get-tuple-element.57), channel_id=1, source_target_pairs={{0,4},{2,6},{4,0},{6,2},{1,5},{3,7},{5,1},{7,3},{8,12},{10,14},{12... | collective-permute-start | bytes 737288 | tf_op jit(solution)/shard_map/ppermute | solution.py:24
  156.0 14.8 %collective-permute-start.47 = (bf16[2,48,1280]{2,1,0:T(8,128)(2,1)S(1)}, bf16[2,48,1280]{2,1,0:T(8,128)(2,1)S(1)}, u32[]{:S(2)}, u32[]{:S(2)}) collective-permute-start(bf16[2,48,1280]{2,1,0:T(8,128)(2,1)S(1)} %get-tuple-element.57), channel_id=1, source_target_pairs={{0,2},{2,0},{4,6},{6,4},{1,3},{3,1},{5,7},{7,5},{8,10},{10,8},{12,... | collective-permute-start | bytes 737288 | tf_op jit(solution)/shard_map/ppermute | solution.py:24
  157.2 13.6 %collective-permute-start.36 = (bf16[48,1280]{1,0:T(8,128)(2,1)S(1)}, bf16[48,1280]{1,0:T(8,128)(2,1)S(1)}, u32[]{:S(2)}, u32[]{:S(2)}) collective-permute-start(bf16[48,1280]{1,0:T(8,128)(2,1)S(1)} %get-tuple-element.62), channel_id=1, source_target_pairs={{0,8},{8,0},{1,9},{9,1},{2,10},{10,2},{3,11},{11,3},{4,12},{12,4},... | collective-permute-start | bytes 368648 | tf_op jit(solution)/shard_map/ppermute | solution.py:24
  161.9 11.9 %collective-permute-start.50 = (bf16[2,48,1280]{2,1,0:T(8,128)(2,1)S(1)}, bf16[2,48,1280]{2,1,0:T(8,128)(2,1)S(1)}, u32[]{:S(2)}, u32[]{:S(2)}) collective-permute-start(bf16[2,48,1280]{2,1,0:T(8,128)(2,1)S(1)} %collective-permute-done.46), channel_id=1, source_target_pairs={{0,4},{2,6},{4,0},{6,2},{1,5},{3,7},{5,1},{7,3},{8,12},{10,14},{12... | collective-permute-start | bytes 737288 | tf_op jit(solution)/shard_map/ppermute | solution.py:21
  191.9 42.3 %reduce-scatter.5.cloned.1.call-start = ((), (), s32[]{:S(2)}) async-start(), calls=%async_computation.3 | async-start | bytes 1474560 | tf_op jit(solution)/shard_map/reduce_scatter | solution.py:274
  200.9 14.7 %collective-permute-start.54 = (bf16[2,48,1280]{2,1,0:T(8,128)(2,1)S(1)}, bf16[2,48,1280]{2,1,0:T(8,128)(2,1)S(1)}, u32[]{:S(2)}, u32[]{:S(2)}) collective-permute-start(bf16[2,48,1280]{2,1,0:T(8,128)(2,1)S(1)} %slice.464), channel_id=1, source_target_pairs={{0,4},{2,6},{4,0},{6,2},{1,5},{3,7},{5,1},{7,3},{8,12},{10,14},{12... | collective-permute-start | bytes 737288 | tf_op jit(solution)/shard_map/ppermute | solution.py:24
  201.4 14.2 %collective-permute-start.55 = (bf16[2,48,1280]{2,1,0:T(8,128)(2,1)S(1)}, bf16[2,48,1280]{2,1,0:T(8,128)(2,1)S(1)}, u32[]{:S(2)}, u32[]{:S(2)}) collective-permute-start(bf16[2,48,1280]{2,1,0:T(8,128)(2,1)S(1)} %slice.466), channel_id=1, source_target_pairs={{0,2},{2,0},{4,6},{6,4},{1,3},{3,1},{5,7},{7,5},{8,10},{10,8},{12,... | collective-permute-start | bytes 737288 | tf_op jit(solution)/shard_map/ppermute | solution.py:24
  (86 other events, 716.4 us)
Sparse Core Ops, SparseCore 0:
  192.0 8.0 reduce-scatter.2
  214.8 8.7 reduce-scatter.4

commit v13 on v10

--- a/solution.py
+++ b/solution.py
@@ -71,7 +71,10 @@
 
 
 def gather_quad(blocks):
-    staged = to_experts(blocks)
+    return quad_of(to_experts(blocks))
+
+
+def quad_of(staged):
     quad = lax.axis_size("ej")
     if not relayed(staged):
         return jnp.stack([staged] + [flipped(staged, "ej", t) for t in range(1, quad)])
@@ -151,6 +154,14 @@
     slot_ids = jnp.arange(slot_count, dtype=jnp.int32)
     expert_range = jnp.arange(groups, dtype=jnp.int32)
 
+    def selector_of(chosen):
+        onehot = (chosen[:, None] == expert_range[None, :]).astype(jnp.int32)
+        rank_values = jnp.sum((jnp.cumsum(onehot, axis=0) - 1) * onehot, axis=1)
+        places = ((chosen - me) % groups) * capacity + rank_values
+        placing = places[:, None] == slot_ids[None, :]
+        token_map = jnp.any(placing.reshape(token_rows, pick_count, slot_count), axis=1)
+        return token_map.T.astype(jnp.bfloat16)
+
     def prepare(moment):
         inputs = saved_inputs[0, moment].astype(jnp.float32)
         scales = lax.rsqrt(jnp.mean(inputs * inputs, axis=1, keepdims=True) + EPSILON)
@@ -186,6 +197,34 @@
         )
         rows_gathered.append(gather_quad(later_rows))
         weights_gathered.append(gather_quad(later_weights.reshape(groups, capacity)))
+    below_selectors = [
+        selector_of(shifted(expert_ids[0, moment].reshape(-1), "pipe", 1))
+        for moment in range(micro_count)
+    ]
+    last_staged = []
+    for moment in range(micro_count):
+        own_blocks = dispatch_rows(prepared[moment][4], output_grads[moment])
+        moved = [own_blocks[0]]
+        for s in range(1, groups):
+            pairs = [
+                ((sections - 1) * groups + g, (sections - 1) * groups + (g + s) % groups)
+                for g in range(groups)
+            ]
+            moved.append(lax.ppermute(own_blocks[s], ("pipe", "eg"), pairs))
+        last_staged.append(jnp.stack(moved))
+
+    def relayed_down(leaving_rows, moment):
+        blocks = dispatch_rows(below_selectors[moment], leaving_rows)
+        moved = []
+        for s in range(groups):
+            pairs = [
+                ((p + 1) * groups + g, p * groups + (g + s) % groups)
+                for p in range(sections - 1)
+                for g in range(groups)
+            ]
+            moved.append(lax.ppermute(blocks[s], ("pipe", "eg"), pairs))
+        return jnp.stack(moved)
+
     leaving_list = []
     combine_list = []
     kept_list = []
@@ -198,7 +237,8 @@
         else:
             arriving = shifted(previous, "pipe", -1)
             incoming = jnp.where(is_last, output_grads[moment], arriving)
-            grads_in = gather_quad(dispatch_rows(current[4], incoming))
+            staged = jnp.where(is_last, last_staged[moment], relayed_down(previous, moment))
+            grads_in = quad_of(staged)
         flat_rows = rows_gathered[moment].reshape(-1, feature_count)
         flat_grads = grads_in.reshape(-1, feature_count)
         scale_column = weights_gathered[moment].reshape(-1, 1).astype(jnp.float32)

time: 238 us -> 259 us (1.088)
  starting transfers between devices: 55 us -> 64.6 us
  other arithmetic: 22 us -> 29.7 us
  local copies, waits for them, and re-layouts: 14.2 us -> 20.2 us
  waiting for transfers between devices: 115 us -> 112 us
    ppermute x39, waiting for transfers between devices: 76.3 us -> 61.4 us  [flipped(): return lax.ppermute(block, axis, route)]
    ppermute x0 -> x3, waiting for transfers between devices: none -> 9.78 us  [the longest x2 9.78 us: relayed_down(): moved.append(lax.ppermute(blocks[s], ('pipe', 'eg'), pairs))]
    ppermute x1 -> x2, waiting for transfers between devices: 0.01 us -> 7.08 us  [shifted(): return lax.ppermute(block, axis, route)]
    ppermute x39, starting transfers between devices: 36.3 us -> 41.9 us  [flipped(): return lax.ppermute(block, axis, route)]
    ppermute x10 -> x9, waiting for transfers between devices: 38.7 us -> 33.4 us  [rotated(): return lax.ppermute(block, axis, route)]
    ppermute x10 -> x9, starting transfers between devices: 17.2 us -> 12.2 us  [rotated(): return lax.ppermute(block, axis, route)]
    ppermute x1 -> x2, starting transfers between devices: 1.47 us -> 6.15 us  [shifted(): return lax.ppermute(block, axis, route)]
    ppermute x0 -> x3, starting transfers between devices: none -> 4.25 us  [the longest x2 2.88 us: relayed_down(): moved.append(lax.ppermute(blocks[s], ('pipe', 'eg'), pairs))]
  transfers between devices with their start and end apart: 52 -> 55, of which waited for: 26 -> 24; matrix products, arithmetic and copies ran while one was open for 16% -> 20% of each run, Pallas kernels for 0% -> 0%
where the time goes in v13:
time: 259 us; the launch traced here: 258 us
  waiting for transfers between devices  112 us (43%)
  starting transfers between devices  64.6 us (25%)
  other arithmetic  29.7 us (11%)
  local copies, waits for them, and re-layouts  20.2 us (8%)
  matrix products  16.5 us (6%)
  between operations  15.1 us (6%)
    ppermute x39, waiting for transfers between devices, flipped(): return lax.ppermute(block, axis, route)  61.4 us
    ppermute x39, starting transfers between devices, flipped(): return lax.ppermute(block, axis, route)  41.9 us
    ppermute x9, waiting for transfers between devices, rotated(): return lax.ppermute(block, axis, route)  33.4 us
    ppermute x9, starting transfers between devices, rotated(): return lax.ppermute(block, axis, route)  12.2 us
    ppermute x2, waiting for transfers between devices, relayed_down(): moved.append(lax.ppermute(blocks[s], ('pipe', 'eg'), pairs))  9.78 us
    ppermute x2, waiting for transfers between devices, shifted(): return lax.ppermute(block, axis, route)  7.08 us
    another operation x11, other arithmetic, quad_of(): return jnp.stack([staged, first, second, diagonal])  6.33 us
    dot_general x6, matrix products, contract_last(): lax.dot_general(first_operand, second_operand, (((1,), (1,)), ((), ())),...  6.32 us
  transfers between devices with their start and end apart: 55, of which 24 were waited for; matrix products, arithmetic and copies ran while one was open for 20% of the time, Pallas kernels for 0%

profile of v13, /device:TPU:0, one launch (start us, length us, event | category | flops | bytes accessed | tf_op | source)
XLA Modules:
  0.0 257.9 jit_solution(9988744019504215397)
XLA Ops:
  8.0 4.9 %collective-permute-start.28 = (s32[64]{0:T(128)S(1)}, s32[64]{0:T(128)S(1)}, u32[]{:S(2)}, u32[]{:S(2)}) collective-permute-start(s32[64]{0:T(128)S(1)} %get-tuple-element.94), channel_id=1, source_target_pairs={{0,16},{1,17},{2,18},{3,19},{4,20},{5,21},{6,22},{7,23},{8,24},{9,... | collective-permute-start | bytes 776 | tf_op jit(solution)/shard_map/ppermute | solution.py:15
  16.9 2.6 %collective-permute-start.4 = (bf16[48,2560]{1,0:T(8,128)(2,1)}, bf16[48,2560]{1,0:T(8,128)(2,1)}, u32[]{:S(2)}, u32[]{:S(2)}) collective-permute-start(bf16[48,2560]{1,0:T(8,128)(2,1)} %get-tuple-element.76), channel_id=1, source_target_pairs={{0,8},{8,0},{1,9},{9,1},{2,10},{10,2},{3,11},{11,3},{4,12},{12,4},... | collective-permute-start | bytes 737288 | tf_op jit(solution)/shard_map/ppermute | solution.py:21
  21.9 2.6 %collective-permute-start = (bf16[48]{0:T(256)(128)(2,1)S(1)}, bf16[48]{0:T(256)(128)(2,1)S(1)}, u32[]{:S(2)}, u32[]{:S(2)}) collective-permute-start(bf16[48]{0:T(256)(128)(2,1)S(1)} %get-tuple-element.102), channel_id=1, source_target_pairs={{0,8},{8,0},{1,9},{9,1},{2,10},{10,2},{3,11},{11,3},{4,12},{12,4},... | collective-permute-start | bytes 296 | tf_op jit(solution)/shard_map/ppermute | solution.py:21
  26.4 14.9 %collective-permute-done = bf16[48]{0:T(256)(128)(2,1)S(1)} collective-permute-done((bf16[48]{0:T(256)(128)(2,1)S(1)}, bf16[48]{0:T(256)(128)(2,1)S(1)}, u32[]{:S(2)}, u32[]{:S(2)}) %collective-permute-start) | collective-permute-done | bytes 128 | tf_op jit(solution)/shard_map/ppermute | solution.py:21
  46.6 2.8 %collective-permute-done.3 = bf16[2,48]{1,0:T(2,128)(2,1)S(1)} collective-permute-done((bf16[2,48]{1,0:T(2,128)(2,1)S(1)}, bf16[2,48]{1,0:T(2,128)(2,1)S(1)}, u32[]{:S(2)}, u32[]{:S(2)}) %collective-permute-start.3) | collective-permute-done | bytes 224 | tf_op jit(solution)/shard_map/ppermute | solution.py:27
  57.2 7.6 %collective-permute-done.11 = bf16[2,48,2560]{2,1,0:T(8,128)(2,1)S(1)} collective-permute-done((bf16[2,48,2560]{2,1,0:T(8,128)(2,1)S(1)}, bf16[2,48,2560]{2,1,0:T(8,128)(2,1)S(1)}, u32[]{:S(2)}, u32[]{:S(2)}) %collective-permute-start.11) | collective-permute-done | bytes 491552 | tf_op jit(solution)/shard_map/ppermute | solution.py:27
  67.8 7.5 %collective-permute-done.5 = bf16[2,48,2560]{2,1,0:T(8,128)(2,1)S(1)} collective-permute-done((bf16[2,48,2560]{2,1,0:T(8,128)(2,1)S(1)}, bf16[2,48,2560]{2,1,0:T(8,128)(2,1)S(1)}, u32[]{:S(2)}, u32[]{:S(2)}) %collective-permute-start.5) | collective-permute-done | bytes 491552 | tf_op jit(solution)/shard_map/ppermute | solution.py:27
  77.4 2.7 %collective-permute-done.13 = bf16[2,48,1280]{2,1,0:T(8,128)(2,1)S(1)} collective-permute-done((bf16[2,48,1280]{2,1,0:T(8,128)(2,1)S(1)}, bf16[2,48,1280]{2,1,0:T(8,128)(2,1)S(1)}, u32[]{:S(2)}, u32[]{:S(2)}) %collective-permute-start.13) | collective-permute-done | bytes 245792 | tf_op jit(solution)/shard_map/ppermute | solution.py:27
  90.7 2.5 collective-permute-done.17
  103.0 5.1 %collective-permute-done.45 = bf16[2,48]{1,0:T(2,128)(2,1)S(1)} collective-permute-done((bf16[2,48]{1,0:T(2,128)(2,1)S(1)}, bf16[2,48]{1,0:T(2,128)(2,1)S(1)}, u32[]{:S(2)}, u32[]{:S(2)}) %collective-permute-start.45) | collective-permute-done | bytes 224 | tf_op jit(solution)/shard_map/ppermute | solution.py:27
  109.5 3.4 %collective-permute-start.48 = (f32[48]{0:T(128)S(1)}, f32[48]{0:T(128)S(1)}, u32[]{:S(2)}, u32[]{:S(2)}) collective-permute-start(f32[48]{0:T(128)S(1)} %get-tuple-element.86), channel_id=1, source_target_pairs={{0,8},{8,0},{1,9},{9,1},{2,10},{10,2},{3,11},{11,3},{4,12},{12,4},... | collective-permute-start | bytes 584 | tf_op jit(solution)/shard_map/ppermute | solution.py:21
  117.7 7.3 %collective-permute-done.21 = bf16[48,2560]{1,0:T(8,128)(2,1)S(1)} collective-permute-done((bf16[48,2560]{1,0:T(8,128)(2,1)S(1)}, bf16[48,2560]{1,0:T(8,128)(2,1)S(1)}, u32[]{:S(2)}, u32[]{:S(2)}) %collective-permute-start.21) | collective-permute-done | bytes 245792 | tf_op jit(solution)/shard_map/ppermute | solution.py:21
  131.2 2.9 %collective-permute-start.23 = (bf16[48]{0:T(256)(128)(2,1)S(1)}, bf16[48]{0:T(256)(128)(2,1)S(1)}, u32[]{:S(2)}, u32[]{:S(2)}) collective-permute-start(bf16[48]{0:T(256)(128)(2,1)S(1)} %get-tuple-element.98), channel_id=1, source_target_pairs={{0,8},{8,0},{1,9},{9,1},{2,10},{10,2},{3,11},{11,3},{4,12},{12,4},... | collective-permute-start | bytes 296 | tf_op jit(solution)/shard_map/ppermute | solution.py:21
  135.6 2.9 %collective-permute-done.23 = bf16[48]{0:T(256)(128)(2,1)S(1)} collective-permute-done((bf16[48]{0:T(256)(128)(2,1)S(1)}, bf16[48]{0:T(256)(128)(2,1)S(1)}, u32[]{:S(2)}, u32[]{:S(2)}) %collective-permute-start.23) | collective-permute-done | bytes 128 | tf_op jit(solution)/shard_map/ppermute | solution.py:21
  144.6 9.8 %collective-permute-done.30 = bf16[48,2560]{1,0:T(8,128)(2,1)S(1)} collective-permute-done((bf16[48,2560]{1,0:T(8,128)(2,1)S(1)}, bf16[48,2560]{1,0:T(8,128)(2,1)S(1)}, u32[]{:S(2)}, u32[]{:S(2)}) %collective-permute-start.30) | collective-permute-done | bytes 245792 | tf_op jit(solution)/shard_map/ppermute | solution.py:225
  161.6 7.3 %collective-permute-done.37 = bf16[2,48,2560]{2,1,0:T(8,128)(2,1)} collective-permute-done((bf16[2,48,2560]{2,1,0:T(8,128)(2,1)}, bf16[2,48,2560]{2,1,0:T(8,128)(2,1)}, u32[]{:S(2)}, u32[]{:S(2)}) %collective-permute-start.37) | collective-permute-done | bytes 491552 | tf_op jit(solution)/shard_map/ppermute | solution.py:27
  174.6 4.9 %collective-permute-done.32 = bf16[2,48,2560]{2,1,0:T(8,128)(2,1)} collective-permute-done((bf16[2,48,2560]{2,1,0:T(8,128)(2,1)}, bf16[2,48,2560]{2,1,0:T(8,128)(2,1)}, u32[]{:S(2)}, u32[]{:S(2)}) %collective-permute-start.32) | collective-permute-done | bytes 491552 | tf_op jit(solution)/shard_map/ppermute | solution.py:27
  191.9 3.0 %convolution_convert_fusion = bf16[384,2560]{1,0:T(8,128)(2,1)} fusion(bf16[384,2560]{1,0:T(8,128)(2,1)S(1)} %bitcast.241, bf16[384,2560]{1,0:T(8,128)(2,1)S(1)} %bitcast.235, bf16[384,192]{0,1:T(8,128)(2,1)S(1)} %get-tuple-element.55, bf16[384,192]{0,1:T(8,128)(2,1)S(1)} %get-tuple-element.47, bf16[384,192]{0,1:T(8,128)(2,1)S(1)} %copy-done.26, ...), kind=kOutput, calls=%fused_computation.4 | convolution fusion | flops 1521156096 | bytes 6488064 | tf_op jit(solution)/shard_map/dot_general | solution.py:42
  198.8 2.4 collective-permute-start.40
  203.9 3.2 %collective-permute-start.51 = (bf16[2,48]{1,0:T(2,128)(2,1)}, bf16[2,48]{1,0:T(2,128)(2,1)}, u32[]{:S(2)}, u32[]{:S(2)}) collective-permute-start(bf16[2,48]{1,0:T(2,128)(2,1)} %slice.364), channel_id=1, source_target_pairs={{0,6},{2,4},{4,2},{6,0},{1,7},{3,5},{5,3},{7,1},{8,14},{10,12},{12... | collective-permute-start | bytes 584 | tf_op jit(solution)/shard_map/ppermute | solution.py:27
  209.4 6.9 %collective-permute-done.42 = bf16[2,48,1280]{2,1,0:T(8,128)(2,1)S(1)} collective-permute-done((bf16[2,48,1280]{2,1,0:T(8,128)(2,1)}, bf16[2,48,1280]{2,1,0:T(8,128)(2,1)S(1)}, u32[]{:S(2)}, u32[]{:S(2)}) %collective-permute-start.42) | collective-permute-done | bytes 245792 | tf_op jit(solution)/shard_map/ppermute | solution.py:27
  223.0 3.2 %collective-permute-done.43 = bf16[2,48,2560]{2,1,0:T(8,128)(2,1)S(1)} collective-permute-done((bf16[2,48,2560]{2,1,0:T(8,128)(2,1)}, bf16[2,48,2560]{2,1,0:T(8,128)(2,1)S(1)}, u32[]{:S(2)}, u32[]{:S(2)}) %collective-permute-start.43) | collective-permute-done | bytes 491552 | tf_op jit(solution)/shard_map/ppermute | solution.py:27
  229.7 7.3 %collective-permute-done.44 = bf16[48,2560]{1,0:T(8,128)(2,1)S(1)} collective-permute-done((bf16[48,2560]{1,0:T(8,128)(2,1)S(1)}, bf16[48,2560]{1,0:T(8,128)(2,1)S(1)}, u32[]{:S(2)}, u32[]{:S(2)}) %collective-permute-start.44) | collective-permute-done | bytes 245792 | tf_op jit(solution)/shard_map/ppermute | solution.py:21
  240.5 7.1 %collective-permute-done.22 = bf16[64,2560]{1,0:T(8,128)(2,1)S(1)} collective-permute-done((bf16[64,2560]{1,0:T(8,128)(2,1)S(1)}, bf16[64,2560]{1,0:T(8,128)(2,1)S(1)}, u32[]{:S(2)}, u32[]{:S(2)}) %collective-permute-start.22) | collective-permute-done | bytes 327712 | tf_op jit(solution)/shard_map/ppermute | solution.py:15
  (329 shorter events, 118.2 us)
Async XLA Ops:
  7.2 241.7 %reduce-scatter.3.cloned.1.call-start = ((), (), s32[]{:S(2)}) async-start(), calls=%async_computation.2 | async-start | bytes 2949120 | tf_op jit(solution)/shard_map/reduce_scatter | solution.py:300
  8.0 35.0 %collective-permute-start.28 = (s32[64]{0:T(128)S(1)}, s32[64]{0:T(128)S(1)}, u32[]{:S(2)}, u32[]{:S(2)}) collective-permute-start(s32[64]{0:T(128)S(1)} %get-tuple-element.94), channel_id=1, source_target_pairs={{0,16},{1,17},{2,18},{3,19},{4,20},{5,21},{6,22},{7,23},{8,24},{9,... | collective-permute-start | bytes 776 | tf_op jit(solution)/shard_map/ppermute | solution.py:15
  16.9 35.9 %collective-permute-start.4 = (bf16[48,2560]{1,0:T(8,128)(2,1)}, bf16[48,2560]{1,0:T(8,128)(2,1)}, u32[]{:S(2)}, u32[]{:S(2)}) collective-permute-start(bf16[48,2560]{1,0:T(8,128)(2,1)} %get-tuple-element.76), channel_id=1, source_target_pairs={{0,8},{8,0},{1,9},{9,1},{2,10},{10,2},{3,11},{11,3},{4,12},{12,4},... | collective-permute-start | bytes 737288 | tf_op jit(solution)/shard_map/ppermute | solution.py:21
  21.4 28.2 %collective-permute-start.10 = (bf16[48,2560]{1,0:T(8,128)(2,1)}, bf16[48,2560]{1,0:T(8,128)(2,1)}, u32[]{:S(2)}, u32[]{:S(2)}) collective-permute-start(bf16[48,2560]{1,0:T(8,128)(2,1)} %get-tuple-element.72), channel_id=1, source_target_pairs={{0,8},{8,0},{1,9},{9,1},{2,10},{10,2},{3,11},{11,3},{4,12},{12,4},... | collective-permute-start | bytes 737288 | tf_op jit(solution)/shard_map/ppermute | solution.py:21
  21.7 32.7 %collective-permute-start.16 = (bf16[192,1280]{1,0:T(8,128)(2,1)S(1)}, bf16[192,1280]{1,0:T(8,128)(2,1)}, u32[]{:S(2)}, u32[]{:S(2)}) collective-permute-start(bf16[192,1280]{1,0:T(8,128)(2,1)S(1)} %bitcast.261), channel_id=1, source_target_pairs={{0,1},{1,0},{2,3},{3,2},{4,5},{5,4},{6,7},{7,6},{8,9},{9,8},{10,11... | collective-permute-start | bytes 1474568 | tf_op jit(solution)/shard_map/ppermute | solution.py:27
  21.9 19.4 %collective-permute-start = (bf16[48]{0:T(256)(128)(2,1)S(1)}, bf16[48]{0:T(256)(128)(2,1)S(1)}, u32[]{:S(2)}, u32[]{:S(2)}) collective-permute-start(bf16[48]{0:T(256)(128)(2,1)S(1)} %get-tuple-element.102), channel_id=1, source_target_pairs={{0,8},{8,0},{1,9},{9,1},{2,10},{10,2},{3,11},{11,3},{4,12},{12,4},... | collective-permute-start | bytes 296 | tf_op jit(solution)/shard_map/ppermute | solution.py:21
  46.6 20.4 %collective-permute-start.15 = (bf16[192,1280]{1,0:T(8,128)(2,1)}, bf16[192,1280]{1,0:T(8,128)(2,1)S(1)}, u32[]{:S(2)}, u32[]{:S(2)}) collective-permute-start(bf16[192,1280]{1,0:T(8,128)(2,1)} %bitcast.263), channel_id=1, source_target_pairs={{0,1},{1,0},{2,3},{3,2},{4,5},{5,4},{6,7},{7,6},{8,9},{9,8},{10,11... | collective-permute-start | bytes 1474568 | tf_op jit(solution)/shard_map/ppermute | solution.py:27
  53.9 21.5 %collective-permute-start.5 = (bf16[2,48,2560]{2,1,0:T(8,128)(2,1)S(1)}, bf16[2,48,2560]{2,1,0:T(8,128)(2,1)S(1)}, u32[]{:S(2)}, u32[]{:S(2)}) collective-permute-start(bf16[2,48,2560]{2,1,0:T(8,128)(2,1)S(1)} %get-tuple-element.74), channel_id=1, source_target_pairs={{0,2},{2,0},{4,6},{6,4},{1,3},{3,1},{5,7},{7,5},{8,10},{10,8},{12,... | collective-permute-start | bytes 1474568 | tf_op jit(solution)/shard_map/ppermute | solution.py:27
  54.5 21.9 %collective-permute-start.6 = (bf16[2,48,2560]{2,1,0:T(8,128)(2,1)S(1)}, bf16[2,48,2560]{2,1,0:T(8,128)(2,1)S(1)}, u32[]{:S(2)}, u32[]{:S(2)}) collective-permute-start(bf16[2,48,2560]{2,1,0:T(8,128)(2,1)S(1)} %get-tuple-element.74), channel_id=1, source_target_pairs={{0,4},{2,6},{4,0},{6,2},{1,5},{3,7},{5,1},{7,3},{8,12},{10,14},{12... | collective-permute-start | bytes 1474568 | tf_op jit(solution)/shard_map/ppermute | solution.py:27
  64.8 19.1 %collective-permute-start.9 = (bf16[192,1280]{1,0:T(8,128)(2,1)S(1)}, bf16[192,1280]{1,0:T(8,128)(2,1)S(1)}, u32[]{:S(2)}, u32[]{:S(2)}) collective-permute-start(bf16[192,1280]{1,0:T(8,128)(2,1)S(1)} %bitcast.277), channel_id=1, source_target_pairs={{0,1},{1,0},{2,3},{3,2},{4,5},{5,4},{6,7},{7,6},{8,9},{9,8},{10,11... | collective-permute-start | bytes 1474568 | tf_op jit(solution)/shard_map/ppermute | solution.py:27
  94.1 18.8 %collective-permute-start.18 = (bf16[2,48,2560]{2,1,0:T(8,128)(2,1)}, bf16[2,48,2560]{2,1,0:T(8,128)(2,1)S(1)}, u32[]{:S(2)}, u32[]{:S(2)}) collective-permute-start(bf16[2,48,2560]{2,1,0:T(8,128)(2,1)} %pad_maximum_fusion.11), channel_id=1, source_target_pairs={{0,4},{2,6},{4,0},{6,2},{1,5},{3,7},{5,1},{7,3},{8,12},{10,14},{12... | collective-permute-start | bytes 1474568 | tf_op jit(solution)/shard_map/ppermute | solution.py:27
  108.1 33.1 %collective-permute-start.27 = (bf16[48,2560]{1,0:T(8,128)(2,1)}, bf16[48,2560]{1,0:T(8,128)(2,1)}, u32[]{:S(2)}, u32[]{:S(2)}) collective-permute-start(bf16[48,2560]{1,0:T(8,128)(2,1)} %get-tuple-element.64), channel_id=1, source_target_pairs={{16,24},{24,16},{17,25},{25,17},{18,26},{26,18},{19,27},{27,19},{2... | collective-permute-start | bytes 737288 | tf_op jit(solution)/shard_map/ppermute | solution.py:213
  134.1 20.3 %collective-permute-start.30 = (bf16[48,2560]{1,0:T(8,128)(2,1)S(1)}, bf16[48,2560]{1,0:T(8,128)(2,1)S(1)}, u32[]{:S(2)}, u32[]{:S(2)}) collective-permute-start(bf16[48,2560]{1,0:T(8,128)(2,1)S(1)} %get-tuple-element.66), channel_id=1, source_target_pairs={{16,8},{24,0},{17,9},{25,1},{18,10},{26,2},{19,11},{27,3},{20,12},... | collective-permute-start | bytes 737288 | tf_op jit(solution)/shard_map/ppermute | solution.py:225
  138.6 17.8 %collective-permute-start.24 = (bf16[2,48]{1,0:T(2,128)(2,1)S(1)}, bf16[2,48]{1,0:T(2,128)(2,1)S(1)}, u32[]{:S(2)}, u32[]{:S(2)}) collective-permute-start(bf16[2,48]{1,0:T(2,128)(2,1)S(1)} %pad_maximum_fusion.19), channel_id=1, source_target_pairs={{0,2},{2,0},{4,6},{6,4},{1,3},{3,1},{5,7},{7,5},{8,10},{10,8},{12,... | collective-permute-start | bytes 584 | tf_op jit(solution)/shard_map/ppermute | solution.py:27
  140.3 18.4 %collective-permute-start.25 = (bf16[2,48]{1,0:T(2,128)(2,1)S(1)}, bf16[2,48]{1,0:T(2,128)(2,1)S(1)}, u32[]{:S(2)}, u32[]{:S(2)}) collective-permute-start(bf16[2,48]{1,0:T(2,128)(2,1)S(1)} %pad_maximum_fusion.19), channel_id=1, source_target_pairs={{0,4},{2,6},{4,0},{6,2},{1,5},{3,7},{5,1},{7,3},{8,12},{10,14},{12... | collective-permute-start | bytes 584 | tf_op jit(solution)/shard_map/ppermute | solution.py:27
  141.1 19.5 %collective-permute-start.26 = (bf16[2,48]{1,0:T(2,128)(2,1)S(1)}, bf16[2,48]{1,0:T(2,128)(2,1)S(1)}, u32[]{:S(2)}, u32[]{:S(2)}) collective-permute-start(bf16[2,48]{1,0:T(2,128)(2,1)S(1)} %pad_maximum_fusion.19), channel_id=1, source_target_pairs={{0,6},{2,4},{4,2},{6,0},{1,7},{3,5},{5,3},{7,1},{8,14},{10,12},{12... | collective-permute-start | bytes 584 | tf_op jit(solution)/shard_map/ppermute | solution.py:27
  143.0 18.4 %collective-permute-start.36 = (bf16[2,48,2560]{2,1,0:T(8,128)(2,1)}, bf16[2,48,2560]{2,1,0:T(8,128)(2,1)S(1)}, u32[]{:S(2)}, u32[]{:S(2)}) collective-permute-start(bf16[2,48,2560]{2,1,0:T(8,128)(2,1)} %get-tuple-element.59), channel_id=1, source_target_pairs={{0,2},{2,0},{4,6},{6,4},{1,3},{3,1},{5,7},{7,5},{8,10},{10,8},{12,... | collective-permute-start | bytes 1474568 | tf_op jit(solution)/shard_map/ppermute | solution.py:27
  156.3 17.2 %collective-permute-start.31 = (bf16[2,48,2560]{2,1,0:T(8,128)(2,1)}, bf16[2,48,2560]{2,1,0:T(8,128)(2,1)}, u32[]{:S(2)}, u32[]{:S(2)}) collective-permute-start(bf16[2,48,2560]{2,1,0:T(8,128)(2,1)} %maximum_select_fusion.4), channel_id=1, source_target_pairs={{0,2},{2,0},{4,6},{6,4},{1,3},{3,1},{5,7},{7,5},{8,10},{10,8},{12,... | collective-permute-start | bytes 1474568 | tf_op jit(solution)/shard_map/ppermute | solution.py:27
  158.7 20.7 %collective-permute-start.32 = (bf16[2,48,2560]{2,1,0:T(8,128)(2,1)}, bf16[2,48,2560]{2,1,0:T(8,128)(2,1)}, u32[]{:S(2)}, u32[]{:S(2)}) collective-permute-start(bf16[2,48,2560]{2,1,0:T(8,128)(2,1)} %maximum_select_fusion.4), channel_id=1, source_target_pairs={{0,4},{2,6},{4,0},{6,2},{1,5},{3,7},{5,1},{7,3},{8,12},{10,14},{12... | collective-permute-start | bytes 1474568 | tf_op jit(solution)/shard_map/ppermute | solution.py:27
  161.4 23.2 %collective-permute-start.38 = (bf16[2,48,1280]{2,1,0:T(8,128)(2,1)S(1)}, bf16[2,48,1280]{2,1,0:T(8,128)(2,1)S(1)}, u32[]{:S(2)}, u32[]{:S(2)}) collective-permute-start(bf16[2,48,1280]{2,1,0:T(8,128)(2,1)S(1)} %slice.403), channel_id=1, source_target_pairs={{0,4},{2,6},{4,0},{6,2},{1,5},{3,7},{5,1},{7,3},{8,12},{10,14},{12... | collective-permute-start | bytes 737288 | tf_op jit(solution)/shard_map/ppermute | solution.py:27
  194.9 56.1 %reduce-scatter.5.cloned.1.call-start = ((), (), s32[]{:S(2)}) async-start(), calls=%async_computation.3 | async-start | bytes 1474560 | tf_op jit(solution)/shard_map/reduce_scatter | solution.py:303
  202.4 16.8 %collective-permute-start.49 = (bf16[2,48]{1,0:T(2,128)(2,1)}, bf16[2,48]{1,0:T(2,128)(2,1)S(1)}, u32[]{:S(2)}, u32[]{:S(2)}) collective-permute-start(bf16[2,48]{1,0:T(2,128)(2,1)} %slice.360), channel_id=1, source_target_pairs={{0,2},{2,0},{4,6},{6,4},{1,3},{3,1},{5,7},{7,5},{8,10},{10,8},{12,... | collective-permute-start | bytes 584 | tf_op jit(solution)/shard_map/ppermute | solution.py:27
  202.9 16.3 %collective-permute-start.50 = (bf16[2,48]{1,0:T(2,128)(2,1)}, bf16[2,48]{1,0:T(2,128)(2,1)}, u32[]{:S(2)}, u32[]{:S(2)}) collective-permute-start(bf16[2,48]{1,0:T(2,128)(2,1)} %slice.362), channel_id=1, source_target_pairs={{0,4},{2,6},{4,0},{6,2},{1,5},{3,7},{5,1},{7,3},{8,12},{10,14},{12... | collective-permute-start | bytes 584 | tf_op jit(solution)/shard_map/ppermute | solution.py:27
  203.9 15.8 %collective-permute-start.51 = (bf16[2,48]{1,0:T(2,128)(2,1)}, bf16[2,48]{1,0:T(2,128)(2,1)}, u32[]{:S(2)}, u32[]{:S(2)}) collective-permute-start(bf16[2,48]{1,0:T(2,128)(2,1)} %slice.364), channel_id=1, source_target_pairs={{0,6},{2,4},{4,2},{6,0},{1,7},{3,5},{5,3},{7,1},{8,14},{10,12},{12... | collective-permute-start | bytes 584 | tf_op jit(solution)/shard_map/ppermute | solution.py:27
  (85 other events, 666.7 us)
Sparse Core Ops, SparseCore 0:
  195.0 8.8 reduce-scatter.2
  219.3 6.7 reduce-scatter.4

commit v14 on v10

--- a/solution.py
+++ b/solution.py
@@ -50,19 +50,19 @@
     return jnp.stack(moved)
 
 
-def to_owners(blocks):
-    groups = blocks.shape[0]
-    moved = [blocks[0]] + [
-        rotated(blocks[s].astype(jnp.bfloat16), "eg", -s).astype(jnp.float32)
-        for s in range(1, groups)
-    ]
-    return jnp.stack(moved)
-
-
-def weights_to_owners(blocks):
-    groups = blocks.shape[0]
-    moved = [blocks[0]] + [rotated(blocks[s], "eg", -s) for s in range(1, groups)]
-    return jnp.stack(moved)
+def to_owners(blocks, weights):
+    groups, capacity, width = blocks.shape
+    rows = [blocks[0]]
+    sums = [weights[0]]
+    for s in range(1, groups):
+        high = weights[s].astype(jnp.bfloat16)
+        low = (weights[s] - high.astype(jnp.float32)).astype(jnp.bfloat16)
+        packed = jnp.pad(jnp.stack([high, low]), ((0, 0), (0, width - capacity)))
+        block = jnp.concatenate([blocks[s].astype(jnp.bfloat16), packed], axis=0)
+        got = rotated(block, "eg", -s).astype(jnp.float32)
+        rows.append(got[:capacity])
+        sums.append(got[capacity, :capacity] + got[capacity + 1, :capacity])
+    return jnp.stack(rows), jnp.stack(sums)
 
 
 def relayed(block):
@@ -216,11 +216,9 @@
         )
         hidden_scaled = (hidden * scale_column).astype(jnp.bfloat16)
         kept_list.append((grad_pair, hidden_scaled, flat_rows, flat_grads))
-        rows_back = to_owners(
-            reduce_quad(part_rows.reshape(-1, groups, capacity, feature_count))
-        )
-        weights_back = weights_to_owners(
-            reduce_quad(part_weight.reshape(-1, groups, capacity))
+        rows_back, weights_back = to_owners(
+            reduce_quad(part_rows.reshape(-1, groups, capacity, feature_count)),
+            reduce_quad(part_weight.reshape(-1, groups, capacity)),
         )
         (
             finish_inputs,

time: 238 us -> 235 us (0.987)
  waiting for transfers between devices: 115 us -> 103 us
  local copies, waits for them, and re-layouts: 14.2 us -> 19.3 us
  starting transfers between devices: 55 us -> 60.1 us
    ppermute x10 -> x8, waiting for transfers between devices: 38.7 us -> 25.3 us  [rotated(): return lax.ppermute(block, axis, route)]
    ppermute x39, starting transfers between devices: 36.3 us -> 42.4 us  [flipped(): return lax.ppermute(block, axis, route)]
    slice x2, local copies, waits for them, and re-layouts: 0.07 us -> 2.68 us  [reduce_quad(): from_first = flipped(parts[3][..., :half], 'ej', 1).astype(jnp.float32)]
    ppermute x10 -> x8, starting transfers between devices: 17.2 us -> 16.2 us  [rotated(): return lax.ppermute(block, axis, route)]
  transfers between devices with their start and end apart: 52 -> 50, of which waited for: 26 -> 27; matrix products, arithmetic and copies ran while one was open for 16% -> 13% of each run, Pallas kernels for 0% -> 0%
where the time goes in v14:
time: 235 us; the launch traced here: 234 us
  waiting for transfers between devices  103 us (44%)
  starting transfers between devices  60.1 us (26%)
  other arithmetic  21 us (9%)
  local copies, waits for them, and re-layouts  19.3 us (8%)
  matrix products  15.4 us (7%)
  between operations  15 us (6%)
    ppermute x39, waiting for transfers between devices, flipped(): return lax.ppermute(block, axis, route)  77.8 us
    ppermute x39, starting transfers between devices, flipped(): return lax.ppermute(block, axis, route)  42.4 us
    ppermute x8, waiting for transfers between devices, rotated(): return lax.ppermute(block, axis, route)  25.3 us
    ppermute x8, starting transfers between devices, rotated(): return lax.ppermute(block, axis, route)  16.2 us
    dot_general x6, matrix products, contract_last(): lax.dot_general(first_operand, second_operand, (((1,), (1,)), ((), ())),...  6.48 us
    dot_general x2, matrix products, contract_first(): lax.dot_general(first_operand, second_operand, (((0,), (0,)), ((), ())),...  4.96 us
  transfers between devices with their start and end apart: 50, of which 27 were waited for; matrix products, arithmetic and copies ran while one was open for 13% of the time, Pallas kernels for 0%

profile of v14, /device:TPU:0, one launch (start us, length us, event | category | flops | bytes accessed | tf_op | source)
XLA Modules:
  0.0 234.0 jit_solution(8838778811842099326)
XLA Ops:
  11.3 4.0 %collective-permute-start = (bf16[48]{0:T(256)(128)(2,1)S(1)}, bf16[48]{0:T(256)(128)(2,1)S(1)}, u32[]{:S(2)}, u32[]{:S(2)}) collective-permute-start(bf16[48]{0:T(256)(128)(2,1)S(1)} %get-tuple-element.99), channel_id=1, source_target_pairs={{0,8},{8,0},{1,9},{9,1},{2,10},{10,2},{3,11},{11,3},{4,12},{12,4},... | collective-permute-start | bytes 296 | tf_op jit(solution)/shard_map/ppermute | solution.py:21
  18.9 3.0 %collective-permute-start.10 = (bf16[48,2560]{1,0:T(8,128)(2,1)S(1)}, bf16[48,2560]{1,0:T(8,128)(2,1)S(1)}, u32[]{:S(2)}, u32[]{:S(2)}) collective-permute-start(bf16[48,2560]{1,0:T(8,128)(2,1)S(1)} %get-tuple-element.69), channel_id=1, source_target_pairs={{0,8},{8,0},{1,9},{9,1},{2,10},{10,2},{3,11},{11,3},{4,12},{12,4},... | collective-permute-start | bytes 737288 | tf_op jit(solution)/shard_map/ppermute | solution.py:21
  25.0 3.2 %collective-permute-done.2 = bf16[2,48]{1,0:T(2,128)(2,1)S(1)} collective-permute-done((bf16[2,48]{1,0:T(2,128)(2,1)S(1)}, bf16[2,48]{1,0:T(2,128)(2,1)S(1)}, u32[]{:S(2)}, u32[]{:S(2)}) %collective-permute-start.2) | collective-permute-done | bytes 224 | tf_op jit(solution)/shard_map/ppermute | solution.py:27
  28.2 3.4 %collective-permute-start.3 = (bf16[2,48]{1,0:T(2,128)(2,1)S(1)}, bf16[2,48]{1,0:T(2,128)(2,1)S(1)}, u32[]{:S(2)}, u32[]{:S(2)}) collective-permute-start(bf16[2,48]{1,0:T(2,128)(2,1)S(1)} %pad_maximum_fusion.21), channel_id=1, source_target_pairs={{0,6},{2,4},{4,2},{6,0},{1,7},{3,5},{5,3},{7,1},{8,14},{10,12},{12... | collective-permute-start | bytes 584 | tf_op jit(solution)/shard_map/ppermute | solution.py:27
  33.2 8.5 %collective-permute-done.10 = bf16[48,2560]{1,0:T(8,128)(2,1)S(1)} collective-permute-done((bf16[48,2560]{1,0:T(8,128)(2,1)S(1)}, bf16[48,2560]{1,0:T(8,128)(2,1)S(1)}, u32[]{:S(2)}, u32[]{:S(2)}) %collective-permute-start.10) | collective-permute-done | bytes 245792 | tf_op jit(solution)/shard_map/ppermute | solution.py:21
  48.3 7.8 %collective-permute-done.11 = bf16[2,48,2560]{2,1,0:T(8,128)(2,1)S(1)} collective-permute-done((bf16[2,48,2560]{2,1,0:T(8,128)(2,1)S(1)}, bf16[2,48,2560]{2,1,0:T(8,128)(2,1)S(1)}, u32[]{:S(2)}, u32[]{:S(2)}) %collective-permute-start.11) | collective-permute-done | bytes 491552 | tf_op jit(solution)/shard_map/ppermute | solution.py:27
  59.9 6.7 %collective-permute-done.5 = bf16[2,48,2560]{2,1,0:T(8,128)(2,1)S(1)} collective-permute-done((bf16[2,48,2560]{2,1,0:T(8,128)(2,1)S(1)}, bf16[2,48,2560]{2,1,0:T(8,128)(2,1)S(1)}, u32[]{:S(2)}, u32[]{:S(2)}) %collective-permute-start.5) | collective-permute-done | bytes 491552 | tf_op jit(solution)/shard_map/ppermute | solution.py:27
  68.7 4.6 %collective-permute-done.13 = bf16[2,48,1280]{2,1,0:T(8,128)(2,1)S(1)} collective-permute-done((bf16[2,48,1280]{2,1,0:T(8,128)(2,1)S(1)}, bf16[2,48,1280]{2,1,0:T(8,128)(2,1)S(1)}, u32[]{:S(2)}, u32[]{:S(2)}) %collective-permute-start.13) | collective-permute-done | bytes 245792 | tf_op jit(solution)/shard_map/ppermute | solution.py:27
  91.3 5.3 %collective-permute-done.17 = bf16[2,48,1280]{2,1,0:T(8,128)(2,1)S(1)} collective-permute-done((bf16[2,48,1280]{2,1,0:T(8,128)(2,1)}, bf16[2,48,1280]{2,1,0:T(8,128)(2,1)S(1)}, u32[]{:S(2)}, u32[]{:S(2)}) %collective-permute-start.17) | collective-permute-done | bytes 245792 | tf_op jit(solution)/shard_map/ppermute | solution.py:27
  98.6 4.5 %collective-permute-done.20 = bf16[2,48,2560]{2,1,0:T(8,128)(2,1)S(1)} collective-permute-done((bf16[2,48,2560]{2,1,0:T(8,128)(2,1)S(1)}, bf16[2,48,2560]{2,1,0:T(8,128)(2,1)S(1)}, u32[]{:S(2)}, u32[]{:S(2)}) %collective-permute-start.20) | collective-permute-done | bytes 491552 | tf_op jit(solution)/shard_map/ppermute | solution.py:27
  103.1 4.3 %collective-permute-done.18 = bf16[2,48,2560]{2,1,0:T(8,128)(2,1)S(1)} collective-permute-done((bf16[2,48,2560]{2,1,0:T(8,128)(2,1)S(1)}, bf16[2,48,2560]{2,1,0:T(8,128)(2,1)S(1)}, u32[]{:S(2)}, u32[]{:S(2)}) %collective-permute-start.18) | collective-permute-done | bytes 491552 | tf_op jit(solution)/shard_map/ppermute | solution.py:27
  107.6 3.8 %collective-permute-start.24 = (bf16[50,2560]{1,0:T(8,128)(2,1)S(1)}, bf16[50,2560]{1,0:T(8,128)(2,1)S(1)}, u32[]{:S(2)}, u32[]{:S(2)}) collective-permute-start(bf16[50,2560]{1,0:T(8,128)(2,1)S(1)} %pad_maximum_fusion.17), channel_id=1, source_target_pairs={{0,8},{8,0},{1,9},{9,1},{2,10},{10,2},{3,11},{11,3},{4,12},{12,4},... | collective-permute-start | bytes 768008 | tf_op jit(solution)/shard_map/ppermute | solution.py:21
  112.4 6.6 %collective-permute-done.24 = bf16[50,2560]{1,0:T(8,128)(2,1)S(1)} collective-permute-done((bf16[50,2560]{1,0:T(8,128)(2,1)S(1)}, bf16[50,2560]{1,0:T(8,128)(2,1)S(1)}, u32[]{:S(2)}, u32[]{:S(2)}) %collective-permute-start.24) | collective-permute-done | bytes 256032 | tf_op jit(solution)/shard_map/ppermute | solution.py:21
  129.7 4.3 %collective-permute-done.35 = bf16[48,2560]{1,0:T(8,128)(2,1)S(1)} collective-permute-done((bf16[48,2560]{1,0:T(8,128)(2,1)S(1)}, bf16[48,2560]{1,0:T(8,128)(2,1)S(1)}, u32[]{:S(2)}, u32[]{:S(2)}) %collective-permute-start.35) | collective-permute-done | bytes 245792 | tf_op jit(solution)/shard_map/ppermute | solution.py:21
  135.0 3.0 %collective-permute-start.37 = (bf16[2,48,2560]{2,1,0:T(8,128)(2,1)}, bf16[2,48,2560]{2,1,0:T(8,128)(2,1)}, u32[]{:S(2)}, u32[]{:S(2)}) collective-permute-start(bf16[2,48,2560]{2,1,0:T(8,128)(2,1)} %get-tuple-element.57), channel_id=1, source_target_pairs={{0,4},{2,6},{4,0},{6,2},{1,5},{3,7},{5,1},{7,3},{8,12},{10,14},{12... | collective-permute-start | bytes 1474568 | tf_op jit(solution)/shard_map/ppermute | solution.py:27
  144.0 8.4 %collective-permute-done.29 = bf16[2,48]{1,0:T(2,128)(2,1)S(1)} collective-permute-done((bf16[2,48]{1,0:T(2,128)(2,1)S(1)}, bf16[2,48]{1,0:T(2,128)(2,1)S(1)}, u32[]{:S(2)}, u32[]{:S(2)}) %collective-permute-start.29) | collective-permute-done | bytes 224 | tf_op jit(solution)/shard_map/ppermute | solution.py:27
  153.4 4.3 %collective-permute-start.38 = (bf16[2,48,1280]{2,1,0:T(8,128)(2,1)S(1)}, bf16[2,48,1280]{2,1,0:T(8,128)(2,1)S(1)}, u32[]{:S(2)}, u32[]{:S(2)}) collective-permute-start(bf16[2,48,1280]{2,1,0:T(8,128)(2,1)S(1)} %slice.416), channel_id=1, source_target_pairs={{0,4},{2,6},{4,0},{6,2},{1,5},{3,7},{5,1},{7,3},{8,12},{10,14},{12... | collective-permute-start | bytes 737288 | tf_op jit(solution)/shard_map/ppermute | solution.py:27
  161.9 3.1 %collective-permute-done.39 = bf16[2,48,1280]{2,1,0:T(8,128)(2,1)S(1)} collective-permute-done((bf16[2,48,1280]{2,1,0:T(8,128)(2,1)S(1)}, bf16[2,48,1280]{2,1,0:T(8,128)(2,1)S(1)}, u32[]{:S(2)}, u32[]{:S(2)}) %collective-permute-start.39) | collective-permute-done | bytes 245792 | tf_op jit(solution)/shard_map/ppermute | solution.py:27
  166.5 3.7 %collective-permute-done.31 = bf16[2,48,2560]{2,1,0:T(8,128)(2,1)S(1)} collective-permute-done((bf16[2,48,2560]{2,1,0:T(8,128)(2,1)S(1)}, bf16[2,48,2560]{2,1,0:T(8,128)(2,1)S(1)}, u32[]{:S(2)}, u32[]{:S(2)}) %collective-permute-start.31) | collective-permute-done | bytes 491552 | tf_op jit(solution)/shard_map/ppermute | solution.py:27
  173.6 2.9 %collective-permute-done.33 = bf16[2,48,1280]{2,1,0:T(8,128)(2,1)S(1)} collective-permute-done((bf16[2,48,1280]{2,1,0:T(8,128)(2,1)S(1)}, bf16[2,48,1280]{2,1,0:T(8,128)(2,1)S(1)}, u32[]{:S(2)}, u32[]{:S(2)}) %collective-permute-start.33) | collective-permute-done | bytes 245792 | tf_op jit(solution)/shard_map/ppermute | solution.py:27
  181.0 3.1 %convolution_convert_fusion = bf16[384,2560]{1,0:T(8,128)(2,1)} fusion(bf16[384,2560]{1,0:T(8,128)(2,1)S(1)} %bitcast.220, bf16[384,2560]{1,0:T(8,128)(2,1)S(1)} %bitcast.214, bf16[384,192]{0,1:T(8,128)(2,1)S(1)} %get-tuple-element.53, bf16[384,192]{0,1:T(8,128)(2,1)S(1)} %get-tuple-element.46, bf16[384,192]{0,1:T(8,128)(2,1)S(1)} %copy-done.22, ...), kind=kOutput, calls=%fused_computation.4 | convolution fusion | flops 1521156096 | bytes 6488064 | tf_op jit(solution)/shard_map/dot_general | solution.py:42
  200.8 4.5 %collective-permute-done.43 = bf16[2,48,2560]{2,1,0:T(8,128)(2,1)S(1)} collective-permute-done((bf16[2,48,2560]{2,1,0:T(8,128)(2,1)S(1)}, bf16[2,48,2560]{2,1,0:T(8,128)(2,1)S(1)}, u32[]{:S(2)}, u32[]{:S(2)}) %collective-permute-start.43) | collective-permute-done | bytes 491552 | tf_op jit(solution)/shard_map/ppermute | solution.py:27
  205.2 3.7 %collective-permute-done.41 = bf16[2,48,2560]{2,1,0:T(8,128)(2,1)S(1)} collective-permute-done((bf16[2,48,2560]{2,1,0:T(8,128)(2,1)S(1)}, bf16[2,48,2560]{2,1,0:T(8,128)(2,1)S(1)}, u32[]{:S(2)}, u32[]{:S(2)}) %collective-permute-start.41) | collective-permute-done | bytes 491552 | tf_op jit(solution)/shard_map/ppermute | solution.py:27
  214.1 5.8 %collective-permute-done.47 = bf16[50,2560]{1,0:T(8,128)(2,1)} collective-permute-done((bf16[50,2560]{1,0:T(8,128)(2,1)S(1)}, bf16[50,2560]{1,0:T(8,128)(2,1)}, u32[]{:S(2)}, u32[]{:S(2)}) %collective-permute-start.47) | collective-permute-done | bytes 256032 | tf_op jit(solution)/shard_map/ppermute | solution.py:21
  (294 shorter events, 106.6 us)
Async XLA Ops:
  7.2 217.8 %reduce-scatter.3.cloned.1.call-start = ((), (), s32[]{:S(2)}) async-start(), calls=%async_computation.2 | async-start | bytes 2949120 | tf_op jit(solution)/shard_map/reduce_scatter | solution.py:258
  11.3 10.6 %collective-permute-start = (bf16[48]{0:T(256)(128)(2,1)S(1)}, bf16[48]{0:T(256)(128)(2,1)S(1)}, u32[]{:S(2)}, u32[]{:S(2)}) collective-permute-start(bf16[48]{0:T(256)(128)(2,1)S(1)} %get-tuple-element.99), channel_id=1, source_target_pairs={{0,8},{8,0},{1,9},{9,1},{2,10},{10,2},{3,11},{11,3},{4,12},{12,4},... | collective-permute-start | bytes 296 | tf_op jit(solution)/shard_map/ppermute | solution.py:21
  17.6 25.8 %collective-permute-start.4 = (bf16[48,2560]{1,0:T(8,128)(2,1)S(1)}, bf16[48,2560]{1,0:T(8,128)(2,1)S(1)}, u32[]{:S(2)}, u32[]{:S(2)}) collective-permute-start(bf16[48,2560]{1,0:T(8,128)(2,1)S(1)} %get-tuple-element.73), channel_id=1, source_target_pairs={{0,8},{8,0},{1,9},{9,1},{2,10},{10,2},{3,11},{11,3},{4,12},{12,4},... | collective-permute-start | bytes 737288 | tf_op jit(solution)/shard_map/ppermute | solution.py:21
  18.9 22.9 %collective-permute-start.10 = (bf16[48,2560]{1,0:T(8,128)(2,1)S(1)}, bf16[48,2560]{1,0:T(8,128)(2,1)S(1)}, u32[]{:S(2)}, u32[]{:S(2)}) collective-permute-start(bf16[48,2560]{1,0:T(8,128)(2,1)S(1)} %get-tuple-element.69), channel_id=1, source_target_pairs={{0,8},{8,0},{1,9},{9,1},{2,10},{10,2},{3,11},{11,3},{4,12},{12,4},... | collective-permute-start | bytes 737288 | tf_op jit(solution)/shard_map/ppermute | solution.py:21
  21.8 22.3 %collective-permute-start.16 = (bf16[192,1280]{1,0:T(8,128)(2,1)S(1)}, bf16[192,1280]{1,0:T(8,128)(2,1)S(1)}, u32[]{:S(2)}, u32[]{:S(2)}) collective-permute-start(bf16[192,1280]{1,0:T(8,128)(2,1)S(1)} %bitcast.237), channel_id=1, source_target_pairs={{0,1},{1,0},{2,3},{3,2},{4,5},{5,4},{6,7},{7,6},{8,9},{9,8},{10,11... | collective-permute-start | bytes 1474568 | tf_op jit(solution)/shard_map/ppermute | solution.py:27
  31.6 26.0 %collective-permute-start.15 = (bf16[192,1280]{1,0:T(8,128)(2,1)}, bf16[192,1280]{1,0:T(8,128)(2,1)}, u32[]{:S(2)}, u32[]{:S(2)}) collective-permute-start(bf16[192,1280]{1,0:T(8,128)(2,1)} %bitcast.28), channel_id=1, source_target_pairs={{0,1},{1,0},{2,3},{3,2},{4,5},{5,4},{6,7},{7,6},{8,9},{9,8},{10,11... | collective-permute-start | bytes 1474568 | tf_op jit(solution)/shard_map/ppermute | solution.py:27
  41.9 14.2 %collective-permute-start.11 = (bf16[2,48,2560]{2,1,0:T(8,128)(2,1)S(1)}, bf16[2,48,2560]{2,1,0:T(8,128)(2,1)S(1)}, u32[]{:S(2)}, u32[]{:S(2)}) collective-permute-start(bf16[2,48,2560]{2,1,0:T(8,128)(2,1)S(1)} %get-tuple-element.67), channel_id=1, source_target_pairs={{0,2},{2,0},{4,6},{6,4},{1,3},{3,1},{5,7},{7,5},{8,10},{10,8},{12,... | collective-permute-start | bytes 1474568 | tf_op jit(solution)/shard_map/ppermute | solution.py:27
  43.4 14.2 %collective-permute-start.12 = (bf16[2,48,2560]{2,1,0:T(8,128)(2,1)S(1)}, bf16[2,48,2560]{2,1,0:T(8,128)(2,1)S(1)}, u32[]{:S(2)}, u32[]{:S(2)}) collective-permute-start(bf16[2,48,2560]{2,1,0:T(8,128)(2,1)S(1)} %get-tuple-element.67), channel_id=1, source_target_pairs={{0,4},{2,6},{4,0},{6,2},{1,5},{3,7},{5,1},{7,3},{8,12},{10,14},{12... | collective-permute-start | bytes 1474568 | tf_op jit(solution)/shard_map/ppermute | solution.py:27
  43.5 23.1 %collective-permute-start.5 = (bf16[2,48,2560]{2,1,0:T(8,128)(2,1)S(1)}, bf16[2,48,2560]{2,1,0:T(8,128)(2,1)S(1)}, u32[]{:S(2)}, u32[]{:S(2)}) collective-permute-start(bf16[2,48,2560]{2,1,0:T(8,128)(2,1)S(1)} %get-tuple-element.71), channel_id=1, source_target_pairs={{0,2},{2,0},{4,6},{6,4},{1,3},{3,1},{5,7},{7,5},{8,10},{10,8},{12,... | collective-permute-start | bytes 1474568 | tf_op jit(solution)/shard_map/ppermute | solution.py:27
  44.9 23.2 %collective-permute-start.6 = (bf16[2,48,2560]{2,1,0:T(8,128)(2,1)S(1)}, bf16[2,48,2560]{2,1,0:T(8,128)(2,1)S(1)}, u32[]{:S(2)}, u32[]{:S(2)}) collective-permute-start(bf16[2,48,2560]{2,1,0:T(8,128)(2,1)S(1)} %get-tuple-element.71), channel_id=1, source_target_pairs={{0,4},{2,6},{4,0},{6,2},{1,5},{3,7},{5,1},{7,3},{8,12},{10,14},{12... | collective-permute-start | bytes 1474568 | tf_op jit(solution)/shard_map/ppermute | solution.py:27
  56.1 21.3 %collective-permute-start.9 = (bf16[192,1280]{1,0:T(8,128)(2,1)S(1)}, bf16[192,1280]{1,0:T(8,128)(2,1)S(1)}, u32[]{:S(2)}, u32[]{:S(2)}) collective-permute-start(bf16[192,1280]{1,0:T(8,128)(2,1)S(1)} %bitcast.251), channel_id=1, source_target_pairs={{0,1},{1,0},{2,3},{3,2},{4,5},{5,4},{6,7},{7,6},{8,9},{9,8},{10,11... | collective-permute-start | bytes 1474568 | tf_op jit(solution)/shard_map/ppermute | solution.py:27
  57.6 15.8 %collective-permute-start.13 = (bf16[2,48,1280]{2,1,0:T(8,128)(2,1)S(1)}, bf16[2,48,1280]{2,1,0:T(8,128)(2,1)S(1)}, u32[]{:S(2)}, u32[]{:S(2)}) collective-permute-start(bf16[2,48,1280]{2,1,0:T(8,128)(2,1)S(1)} %slice.397), channel_id=1, source_target_pairs={{0,4},{2,6},{4,0},{6,2},{1,5},{3,7},{5,1},{7,3},{8,12},{10,14},{12... | collective-permute-start | bytes 737288 | tf_op jit(solution)/shard_map/ppermute | solution.py:27
  57.6 15.8 %collective-permute-start.14 = (bf16[2,48,1280]{2,1,0:T(8,128)(2,1)S(1)}, bf16[2,48,1280]{2,1,0:T(8,128)(2,1)S(1)}, u32[]{:S(2)}, u32[]{:S(2)}) collective-permute-start(bf16[2,48,1280]{2,1,0:T(8,128)(2,1)S(1)} %slice.398), channel_id=1, source_target_pairs={{0,2},{2,0},{4,6},{6,4},{1,3},{3,1},{5,7},{7,5},{8,10},{10,8},{12,... | collective-permute-start | bytes 737288 | tf_op jit(solution)/shard_map/ppermute | solution.py:27
  89.9 13.2 %collective-permute-start.20 = (bf16[2,48,2560]{2,1,0:T(8,128)(2,1)S(1)}, bf16[2,48,2560]{2,1,0:T(8,128)(2,1)S(1)}, u32[]{:S(2)}, u32[]{:S(2)}) collective-permute-start(bf16[2,48,2560]{2,1,0:T(8,128)(2,1)S(1)} %pad_maximum_fusion.12), channel_id=1, source_target_pairs={{0,2},{2,0},{4,6},{6,4},{1,3},{3,1},{5,7},{7,5},{8,10},{10,8},{12,... | collective-permute-start | bytes 1474568 | tf_op jit(solution)/shard_map/ppermute | solution.py:27
  96.8 10.6 %collective-permute-start.18 = (bf16[2,48,2560]{2,1,0:T(8,128)(2,1)S(1)}, bf16[2,48,2560]{2,1,0:T(8,128)(2,1)S(1)}, u32[]{:S(2)}, u32[]{:S(2)}) collective-permute-start(bf16[2,48,2560]{2,1,0:T(8,128)(2,1)S(1)} %pad_maximum_fusion.11), channel_id=1, source_target_pairs={{0,4},{2,6},{4,0},{6,2},{1,5},{3,7},{5,1},{7,3},{8,12},{10,14},{12... | collective-permute-start | bytes 1474568 | tf_op jit(solution)/shard_map/ppermute | solution.py:27
  107.6 11.4 %collective-permute-start.24 = (bf16[50,2560]{1,0:T(8,128)(2,1)S(1)}, bf16[50,2560]{1,0:T(8,128)(2,1)S(1)}, u32[]{:S(2)}, u32[]{:S(2)}) collective-permute-start(bf16[50,2560]{1,0:T(8,128)(2,1)S(1)} %pad_maximum_fusion.17), channel_id=1, source_target_pairs={{0,8},{8,0},{1,9},{9,1},{2,10},{10,2},{3,11},{11,3},{4,12},{12,4},... | collective-permute-start | bytes 768008 | tf_op jit(solution)/shard_map/ppermute | solution.py:21
  129.6 11.9 %collective-permute-start.28 = (bf16[2,48]{1,0:T(2,128)(2,1)S(1)}, bf16[2,48]{1,0:T(2,128)(2,1)S(1)}, u32[]{:S(2)}, u32[]{:S(2)}) collective-permute-start(bf16[2,48]{1,0:T(2,128)(2,1)S(1)} %pad_maximum_fusion.22), channel_id=1, source_target_pairs={{0,4},{2,6},{4,0},{6,2},{1,5},{3,7},{5,1},{7,3},{8,12},{10,14},{12... | collective-permute-start | bytes 584 | tf_op jit(solution)/shard_map/ppermute | solution.py:27
  134.8 17.6 %collective-permute-start.36 = (bf16[2,48,2560]{2,1,0:T(8,128)(2,1)}, bf16[2,48,2560]{2,1,0:T(8,128)(2,1)}, u32[]{:S(2)}, u32[]{:S(2)}) collective-permute-start(bf16[2,48,2560]{2,1,0:T(8,128)(2,1)} %get-tuple-element.57), channel_id=1, source_target_pairs={{0,2},{2,0},{4,6},{6,4},{1,3},{3,1},{5,7},{7,5},{8,10},{10,8},{12,... | collective-permute-start | bytes 1474568 | tf_op jit(solution)/shard_map/ppermute | solution.py:27
  135.0 22.8 %collective-permute-start.37 = (bf16[2,48,2560]{2,1,0:T(8,128)(2,1)}, bf16[2,48,2560]{2,1,0:T(8,128)(2,1)}, u32[]{:S(2)}, u32[]{:S(2)}) collective-permute-start(bf16[2,48,2560]{2,1,0:T(8,128)(2,1)} %get-tuple-element.57), channel_id=1, source_target_pairs={{0,4},{2,6},{4,0},{6,2},{1,5},{3,7},{5,1},{7,3},{8,12},{10,14},{12... | collective-permute-start | bytes 1474568 | tf_op jit(solution)/shard_map/ppermute | solution.py:27
  139.2 19.6 %collective-permute-start.30 = (bf16[48,2560]{1,0:T(8,128)(2,1)}, bf16[48,2560]{1,0:T(8,128)(2,1)}, u32[]{:S(2)}, u32[]{:S(2)}) collective-permute-start(bf16[48,2560]{1,0:T(8,128)(2,1)} %get-tuple-element.63), channel_id=1, source_target_pairs={{0,8},{8,0},{1,9},{9,1},{2,10},{10,2},{3,11},{11,3},{4,12},{12,4},... | collective-permute-start | bytes 737288 | tf_op jit(solution)/shard_map/ppermute | solution.py:21
  141.5 10.9 %collective-permute-start.29 = (bf16[2,48]{1,0:T(2,128)(2,1)S(1)}, bf16[2,48]{1,0:T(2,128)(2,1)S(1)}, u32[]{:S(2)}, u32[]{:S(2)}) collective-permute-start(bf16[2,48]{1,0:T(2,128)(2,1)S(1)} %pad_maximum_fusion.22), channel_id=1, source_target_pairs={{0,6},{2,4},{4,2},{6,0},{1,7},{3,5},{5,3},{7,1},{8,14},{10,12},{12... | collective-permute-start | bytes 584 | tf_op jit(solution)/shard_map/ppermute | solution.py:27
  159.8 10.4 %collective-permute-start.31 = (bf16[2,48,2560]{2,1,0:T(8,128)(2,1)S(1)}, bf16[2,48,2560]{2,1,0:T(8,128)(2,1)S(1)}, u32[]{:S(2)}, u32[]{:S(2)}) collective-permute-start(bf16[2,48,2560]{2,1,0:T(8,128)(2,1)S(1)} %get-tuple-element.61), channel_id=1, source_target_pairs={{0,2},{2,0},{4,6},{6,4},{1,3},{3,1},{5,7},{7,5},{8,10},{10,8},{12,... | collective-permute-start | bytes 1474568 | tf_op jit(solution)/shard_map/ppermute | solution.py:27
  186.2 41.0 %reduce-scatter.5.cloned.1.call-start = ((), (), s32[]{:S(2)}) async-start(), calls=%async_computation.3 | async-start | bytes 1474560 | tf_op jit(solution)/shard_map/reduce_scatter | solution.py:261
  209.2 10.8 %collective-permute-start.47 = (bf16[50,2560]{1,0:T(8,128)(2,1)S(1)}, bf16[50,2560]{1,0:T(8,128)(2,1)}, u32[]{:S(2)}, u32[]{:S(2)}) collective-permute-start(bf16[50,2560]{1,0:T(8,128)(2,1)S(1)} %pad_maximum_fusion.18), channel_id=1, source_target_pairs={{0,8},{8,0},{1,9},{9,1},{2,10},{10,2},{3,11},{11,3},{4,12},{12,4},... | collective-permute-start | bytes 768008 | tf_op jit(solution)/shard_map/ppermute | solution.py:21
  (66 other events, 385.6 us)
Sparse Core Ops, SparseCore 0:
  186.3 8.8 reduce-scatter.2
  214.2 7.5 reduce-scatter.4

commit v15 on v14

--- a/solution.py
+++ b/solution.py
@@ -42,6 +42,18 @@
     return lax.dot_general(
         first_operand, second_operand, (((0,), (0,)), ((), ())), preferred_element_type=jnp.float32
     )
+
+
+def rows_and_weights(blocks, weights):
+    groups, capacity, width = blocks.shape
+    rows = [blocks[0]]
+    kept = [weights[0]]
+    for s in range(1, groups):
+        extra = jnp.pad(weights[s][None, :], ((0, 0), (0, width - capacity)))
+        got = rotated(jnp.concatenate([blocks[s], extra], axis=0), "eg", s)
+        rows.append(got[:capacity])
+        kept.append(got[capacity, :capacity])
+    return quad_of(jnp.stack(rows)), quad_of(jnp.stack(kept))
 
 
 def to_experts(blocks):
@@ -71,7 +83,10 @@
 
 
 def gather_quad(blocks):
-    staged = to_experts(blocks)
+    return quad_of(to_experts(blocks))
+
+
+def quad_of(staged):
     quad = lax.axis_size("ej")
     if not relayed(staged):
         return jnp.stack([staged] + [flipped(staged, "ej", t) for t in range(1, quad)])
@@ -178,14 +193,18 @@
     prepared = [prepare(moment) for moment in range(micro_count)]
     first_incoming = jnp.where(is_last, output_grads[0], entry_grads[0])
     first_grads = gather_quad(dispatch_rows(prepared[0][4], first_incoming))
-    rows_gathered = [gather_quad(dispatch_rows(prepared[0][4], prepared[0][2]))]
-    weights_gathered = [gather_quad(prepared[0][6].reshape(groups, capacity))]
+    first_rows, first_weights = rows_and_weights(
+        dispatch_rows(prepared[0][4], prepared[0][2]), prepared[0][6].reshape(groups, capacity)
+    )
+    rows_gathered = [first_rows]
+    weights_gathered = [first_weights]
     for current in prepared[1:]:
         later_rows, later_weights, _ = lax.optimization_barrier(
             (dispatch_rows(current[4], current[2]), current[6], first_grads)
         )
-        rows_gathered.append(gather_quad(later_rows))
-        weights_gathered.append(gather_quad(later_weights.reshape(groups, capacity)))
+        later_gathered = rows_and_weights(later_rows, later_weights.reshape(groups, capacity))
+        rows_gathered.append(later_gathered[0])
+        weights_gathered.append(later_gathered[1])
     leaving_list = []
     combine_list = []
     kept_list = []

time: 235 us -> 256 us (1.089)
  waiting for transfers between devices: 103 us -> 123 us
  starting transfers between devices: 60.1 us -> 52.8 us
  local copies, waits for them, and re-layouts: 19.3 us -> 23.4 us
  other arithmetic: 21 us -> 25 us
    ppermute x8 -> x6, waiting for transfers between devices: 25.3 us -> 48.4 us  [rotated(): return lax.ppermute(block, axis, route)]
    ppermute x8 -> x6, starting transfers between devices: 16.2 us -> 9.69 us  [rotated(): return lax.ppermute(block, axis, route)]
    another operation x16, other arithmetic: 4.41 us -> 8.17 us  [the longest x12 8.13 us: quad_of(): return jnp.stack([staged, first, second, diagonal])]
    ppermute x39, waiting for transfers between devices: 77.8 us -> 75 us  [flipped(): return lax.ppermute(block, axis, route)]
    slice x8 -> x14, local copies, waits for them, and re-layouts: 2.03 us -> 4.81 us  [the longest x4 1.96 us: quad_of(): first[..., :half]]
  transfers between devices with their start and end apart: 50 -> 48, of which waited for: 27 -> 25; matrix products, arithmetic and copies ran while one was open for 13% -> 14% of each run, Pallas kernels for 0% -> 0%
where the time goes in v15:
time: 256 us; the launch traced here: 255 us
  waiting for transfers between devices  123 us (48%)
  starting transfers between devices  52.8 us (21%)
  other arithmetic  25 us (10%)
  local copies, waits for them, and re-layouts  23.4 us (9%)
  matrix products  15.4 us (6%)
  between operations  15 us (6%)
    ppermute x39, waiting for transfers between devices, flipped(): return lax.ppermute(block, axis, route)  75 us
    ppermute x6, waiting for transfers between devices, rotated(): return lax.ppermute(block, axis, route)  48.4 us
    ppermute x39, starting transfers between devices, flipped(): return lax.ppermute(block, axis, route)  41.6 us
    ppermute x6, starting transfers between devices, rotated(): return lax.ppermute(block, axis, route)  9.69 us
    another operation x12, other arithmetic, quad_of(): return jnp.stack([staged, first, second, diagonal])  8.13 us
    dot_general x6, matrix products, contract_last(): lax.dot_general(first_operand, second_operand, (((1,), (1,)), ((), ())),...  6.47 us
  transfers between devices with their start and end apart: 48, of which 25 were waited for; matrix products, arithmetic and copies ran while one was open for 14% of the time, Pallas kernels for 0%

profile of v15, /device:TPU:0, one launch (start us, length us, event | category | flops | bytes accessed | tf_op | source)
XLA Modules:
  0.0 255.2 jit_solution(720586671871946672)
XLA Ops:
  12.1 4.1 %collective-permute-start.4 = (bf16[48,2560]{1,0:T(8,128)(2,1)S(1)}, bf16[48,2560]{1,0:T(8,128)(2,1)S(1)}, u32[]{:S(2)}, u32[]{:S(2)}) collective-permute-start(bf16[48,2560]{1,0:T(8,128)(2,1)S(1)} %get-tuple-element.73), channel_id=1, source_target_pairs={{0,8},{8,0},{1,9},{9,1},{2,10},{10,2},{3,11},{11,3},{4,12},{12,4},... | collective-permute-start | bytes 737288 | tf_op jit(solution)/shard_map/ppermute | solution.py:21
  19.3 15.0 %collective-permute-done.4 = bf16[48,2560]{1,0:T(8,128)(2,1)S(1)} collective-permute-done((bf16[48,2560]{1,0:T(8,128)(2,1)S(1)}, bf16[48,2560]{1,0:T(8,128)(2,1)S(1)}, u32[]{:S(2)}, u32[]{:S(2)}) %collective-permute-start.4) | collective-permute-done | bytes 245792 | tf_op jit(solution)/shard_map/ppermute | solution.py:21
  37.0 2.7 %collective-permute-done = bf16[49,2560]{1,0:T(8,128)(2,1)} collective-permute-done((bf16[49,2560]{1,0:T(8,128)(2,1)}, bf16[49,2560]{1,0:T(8,128)(2,1)}, u32[]{:S(2)}, u32[]{:S(2)}) %collective-permute-start) | collective-permute-done | bytes 250912 | tf_op jit(solution)/shard_map/ppermute | solution.py:21
  47.1 2.4 collective-permute-start.3
  49.5 7.9 %collective-permute-done.3 = bf16[2,48]{1,0:T(2,128)(2,1)S(1)} collective-permute-done((bf16[2,48]{1,0:T(2,128)(2,1)S(1)}, bf16[2,48]{1,0:T(2,128)(2,1)S(1)}, u32[]{:S(2)}, u32[]{:S(2)}) %collective-permute-start.3) | collective-permute-done | bytes 224 | tf_op jit(solution)/shard_map/ppermute | solution.py:27
  67.0 3.3 %collective-permute-done.10 = bf16[2,48,2560]{2,1,0:T(8,128)(2,1)} collective-permute-done((bf16[2,48,2560]{2,1,0:T(8,128)(2,1)}, bf16[2,48,2560]{2,1,0:T(8,128)(2,1)}, u32[]{:S(2)}, u32[]{:S(2)}) %collective-permute-start.10) | collective-permute-done | bytes 491552 | tf_op jit(solution)/shard_map/ppermute | solution.py:27
  74.7 4.2 %collective-permute-done.7 = bf16[2,48,1280]{2,1,0:T(8,128)(2,1)S(1)} collective-permute-done((bf16[2,48,1280]{2,1,0:T(8,128)(2,1)S(1)}, bf16[2,48,1280]{2,1,0:T(8,128)(2,1)S(1)}, u32[]{:S(2)}, u32[]{:S(2)}) %collective-permute-start.7) | collective-permute-done | bytes 245792 | tf_op jit(solution)/shard_map/ppermute | solution.py:27
  96.9 5.2 %collective-permute-done.16 = bf16[2,48,1280]{2,1,0:T(8,128)(2,1)S(1)} collective-permute-done((bf16[2,48,1280]{2,1,0:T(8,128)(2,1)}, bf16[2,48,1280]{2,1,0:T(8,128)(2,1)S(1)}, u32[]{:S(2)}, u32[]{:S(2)}) %collective-permute-start.16) | collective-permute-done | bytes 245792 | tf_op jit(solution)/shard_map/ppermute | solution.py:27
  104.1 3.3 %collective-permute-done.19 = bf16[2,48,2560]{2,1,0:T(8,128)(2,1)S(1)} collective-permute-done((bf16[2,48,2560]{2,1,0:T(8,128)(2,1)S(1)}, bf16[2,48,2560]{2,1,0:T(8,128)(2,1)S(1)}, u32[]{:S(2)}, u32[]{:S(2)}) %collective-permute-start.19) | collective-permute-done | bytes 491552 | tf_op jit(solution)/shard_map/ppermute | solution.py:27
  107.4 6.8 %collective-permute-done.17 = bf16[2,48,2560]{2,1,0:T(8,128)(2,1)S(1)} collective-permute-done((bf16[2,48,2560]{2,1,0:T(8,128)(2,1)S(1)}, bf16[2,48,2560]{2,1,0:T(8,128)(2,1)S(1)}, u32[]{:S(2)}, u32[]{:S(2)}) %collective-permute-start.17) | collective-permute-done | bytes 491552 | tf_op jit(solution)/shard_map/ppermute | solution.py:27
  114.5 2.8 %collective-permute-start.23 = (bf16[50,2560]{1,0:T(8,128)(2,1)S(1)}, bf16[50,2560]{1,0:T(8,128)(2,1)S(1)}, u32[]{:S(2)}, u32[]{:S(2)}) collective-permute-start(bf16[50,2560]{1,0:T(8,128)(2,1)S(1)} %pad_maximum_fusion.17), channel_id=1, source_target_pairs={{0,8},{8,0},{1,9},{9,1},{2,10},{10,2},{3,11},{11,3},{4,12},{12,4},... | collective-permute-start | bytes 768008 | tf_op jit(solution)/shard_map/ppermute | solution.py:21
  118.3 11.2 %collective-permute-done.23 = bf16[50,2560]{1,0:T(8,128)(2,1)S(1)} collective-permute-done((bf16[50,2560]{1,0:T(8,128)(2,1)S(1)}, bf16[50,2560]{1,0:T(8,128)(2,1)S(1)}, u32[]{:S(2)}, u32[]{:S(2)}) %collective-permute-start.23) | collective-permute-done | bytes 256032 | tf_op jit(solution)/shard_map/ppermute | solution.py:21
  137.2 13.3 %collective-permute-done.25 = bf16[49,2560]{1,0:T(8,128)(2,1)S(1)} collective-permute-done((bf16[49,2560]{1,0:T(8,128)(2,1)S(1)}, bf16[49,2560]{1,0:T(8,128)(2,1)S(1)}, u32[]{:S(2)}, u32[]{:S(2)}) %collective-permute-start.25) | collective-permute-done | bytes 250912 | tf_op jit(solution)/shard_map/ppermute | solution.py:21
  157.8 10.9 %collective-permute-done.27 = bf16[2,48]{1,0:T(2,128)(2,1)S(1)} collective-permute-done((bf16[2,48]{1,0:T(2,128)(2,1)S(1)}, bf16[2,48]{1,0:T(2,128)(2,1)S(1)}, u32[]{:S(2)}, u32[]{:S(2)}) %collective-permute-start.27) | collective-permute-done | bytes 224 | tf_op jit(solution)/shard_map/ppermute | solution.py:27
  168.9 4.1 %collective-permute-done.28 = bf16[2,48]{1,0:T(2,128)(2,1)S(1)} collective-permute-done((bf16[2,48]{1,0:T(2,128)(2,1)S(1)}, bf16[2,48]{1,0:T(2,128)(2,1)S(1)}, u32[]{:S(2)}, u32[]{:S(2)}) %collective-permute-start.28) | collective-permute-done | bytes 224 | tf_op jit(solution)/shard_map/ppermute | solution.py:27
  183.0 3.7 %collective-permute-done.30 = bf16[2,48,2560]{2,1,0:T(8,128)(2,1)S(1)} collective-permute-done((bf16[2,48,2560]{2,1,0:T(8,128)(2,1)S(1)}, bf16[2,48,2560]{2,1,0:T(8,128)(2,1)S(1)}, u32[]{:S(2)}, u32[]{:S(2)}) %collective-permute-start.30) | collective-permute-done | bytes 491552 | tf_op jit(solution)/shard_map/ppermute | solution.py:27
  193.0 4.8 %collective-permute-done.33 = bf16[2,48,1280]{2,1,0:T(8,128)(2,1)S(1)} collective-permute-done((bf16[2,48,1280]{2,1,0:T(8,128)(2,1)S(1)}, bf16[2,48,1280]{2,1,0:T(8,128)(2,1)S(1)}, u32[]{:S(2)}, u32[]{:S(2)}) %collective-permute-start.33) | collective-permute-done | bytes 245792 | tf_op jit(solution)/shard_map/ppermute | solution.py:27
  201.5 3.0 %convolution_convert_fusion = bf16[384,2560]{1,0:T(8,128)(2,1)} fusion(bf16[384,2560]{1,0:T(8,128)(2,1)S(1)} %bitcast.224, bf16[384,2560]{1,0:T(8,128)(2,1)S(1)} %bitcast.218, bf16[384,192]{0,1:T(8,128)(2,1)S(1)} %get-tuple-element.53, bf16[384,192]{0,1:T(8,128)(2,1)S(1)} %get-tuple-element.46, bf16[384,192]{0,1:T(8,128)(2,1)S(1)} %copy-done.23, ...), kind=kOutput, calls=%fused_computation.4 | convolution fusion | flops 1521156096 | bytes 6488064 | tf_op jit(solution)/shard_map/dot_general | solution.py:42
  208.6 2.1 collective-permute-start.40
  218.4 2.8 %collective-permute-done.38 = bf16[2,48,1280]{2,1,0:T(8,128)(2,1)S(1)} collective-permute-done((bf16[2,48,1280]{2,1,0:T(8,128)(2,1)}, bf16[2,48,1280]{2,1,0:T(8,128)(2,1)S(1)}, u32[]{:S(2)}, u32[]{:S(2)}) %collective-permute-start.38) | collective-permute-done | bytes 245792 | tf_op jit(solution)/shard_map/ppermute | solution.py:27
  221.4 5.1 %collective-permute-done.41 = bf16[2,48,2560]{2,1,0:T(8,128)(2,1)S(1)} collective-permute-done((bf16[2,48,2560]{2,1,0:T(8,128)(2,1)S(1)}, bf16[2,48,2560]{2,1,0:T(8,128)(2,1)S(1)}, u32[]{:S(2)}, u32[]{:S(2)}) %collective-permute-start.41) | collective-permute-done | bytes 491552 | tf_op jit(solution)/shard_map/ppermute | solution.py:27
  226.4 3.7 %collective-permute-done.39 = bf16[2,48,2560]{2,1,0:T(8,128)(2,1)S(1)} collective-permute-done((bf16[2,48,2560]{2,1,0:T(8,128)(2,1)S(1)}, bf16[2,48,2560]{2,1,0:T(8,128)(2,1)S(1)}, u32[]{:S(2)}, u32[]{:S(2)}) %collective-permute-start.39) | collective-permute-done | bytes 491552 | tf_op jit(solution)/shard_map/ppermute | solution.py:27
  234.9 6.2 %collective-permute-done.45 = bf16[50,2560]{1,0:T(8,128)(2,1)} collective-permute-done((bf16[50,2560]{1,0:T(8,128)(2,1)S(1)}, bf16[50,2560]{1,0:T(8,128)(2,1)}, u32[]{:S(2)}, u32[]{:S(2)}) %collective-permute-start.45) | collective-permute-done | bytes 256032 | tf_op jit(solution)/shard_map/ppermute | solution.py:21
  246.1 2.2 fusion.116
  (300 shorter events, 109.3 us)
Async XLA Ops:
  7.2 238.9 %reduce-scatter.3.cloned.1.call-start = ((), (), s32[]{:S(2)}) async-start(), calls=%async_computation.2 | async-start | bytes 2949120 | tf_op jit(solution)/shard_map/reduce_scatter | solution.py:277
  12.1 22.3 %collective-permute-start.4 = (bf16[48,2560]{1,0:T(8,128)(2,1)S(1)}, bf16[48,2560]{1,0:T(8,128)(2,1)S(1)}, u32[]{:S(2)}, u32[]{:S(2)}) collective-permute-start(bf16[48,2560]{1,0:T(8,128)(2,1)S(1)} %get-tuple-element.73), channel_id=1, source_target_pairs={{0,8},{8,0},{1,9},{9,1},{2,10},{10,2},{3,11},{11,3},{4,12},{12,4},... | collective-permute-start | bytes 737288 | tf_op jit(solution)/shard_map/ppermute | solution.py:21
  18.8 21.0 %collective-permute-start = (bf16[49,2560]{1,0:T(8,128)(2,1)}, bf16[49,2560]{1,0:T(8,128)(2,1)}, u32[]{:S(2)}, u32[]{:S(2)}) collective-permute-start(bf16[49,2560]{1,0:T(8,128)(2,1)} %fusion.69), channel_id=1, source_target_pairs={{0,8},{8,0},{1,9},{9,1},{2,10},{10,2},{3,11},{11,3},{4,12},{12,4},... | collective-permute-start | bytes 752648 | tf_op jit(solution)/shard_map/ppermute | solution.py:21
  18.8 40.1 %collective-permute-start.15 = (bf16[192,1280]{1,0:T(8,128)(2,1)S(1)}, bf16[192,1280]{1,0:T(8,128)(2,1)S(1)}, u32[]{:S(2)}, u32[]{:S(2)}) collective-permute-start(bf16[192,1280]{1,0:T(8,128)(2,1)S(1)} %bitcast.240), channel_id=1, source_target_pairs={{0,1},{1,0},{2,3},{3,2},{4,5},{5,4},{6,7},{7,6},{8,9},{9,8},{10,11... | collective-permute-start | bytes 1474568 | tf_op jit(solution)/shard_map/ppermute | solution.py:27
  18.8 45.8 %collective-permute-start.14 = (bf16[192,1280]{1,0:T(8,128)(2,1)}, bf16[192,1280]{1,0:T(8,128)(2,1)}, u32[]{:S(2)}, u32[]{:S(2)}) collective-permute-start(bf16[192,1280]{1,0:T(8,128)(2,1)} %bitcast.28), channel_id=1, source_target_pairs={{0,1},{1,0},{2,3},{3,2},{4,5},{5,4},{6,7},{7,6},{8,9},{9,8},{10,11... | collective-permute-start | bytes 1474568 | tf_op jit(solution)/shard_map/ppermute | solution.py:27
  35.2 26.6 %collective-permute-start.5 = (bf16[2,48,2560]{2,1,0:T(8,128)(2,1)}, bf16[2,48,2560]{2,1,0:T(8,128)(2,1)S(1)}, u32[]{:S(2)}, u32[]{:S(2)}) collective-permute-start(bf16[2,48,2560]{2,1,0:T(8,128)(2,1)} %get-tuple-element.71), channel_id=1, source_target_pairs={{0,2},{2,0},{4,6},{6,4},{1,3},{3,1},{5,7},{7,5},{8,10},{10,8},{12,... | collective-permute-start | bytes 1474568 | tf_op jit(solution)/shard_map/ppermute | solution.py:27
  44.6 17.3 %collective-permute-start.6 = (bf16[2,48,2560]{2,1,0:T(8,128)(2,1)}, bf16[2,48,2560]{2,1,0:T(8,128)(2,1)}, u32[]{:S(2)}, u32[]{:S(2)}) collective-permute-start(bf16[2,48,2560]{2,1,0:T(8,128)(2,1)} %get-tuple-element.71), channel_id=1, source_target_pairs={{0,4},{2,6},{4,0},{6,2},{1,5},{3,7},{5,1},{7,3},{8,12},{10,14},{12... | collective-permute-start | bytes 1474568 | tf_op jit(solution)/shard_map/ppermute | solution.py:27
  57.3 13.0 %collective-permute-start.10 = (bf16[2,48,2560]{2,1,0:T(8,128)(2,1)}, bf16[2,48,2560]{2,1,0:T(8,128)(2,1)}, u32[]{:S(2)}, u32[]{:S(2)}) collective-permute-start(bf16[2,48,2560]{2,1,0:T(8,128)(2,1)} %get-tuple-element.67), channel_id=1, source_target_pairs={{0,2},{2,0},{4,6},{6,4},{1,3},{3,1},{5,7},{7,5},{8,10},{10,8},{12,... | collective-permute-start | bytes 1474568 | tf_op jit(solution)/shard_map/ppermute | solution.py:27
  59.7 14.4 %collective-permute-start.11 = (bf16[2,48,2560]{2,1,0:T(8,128)(2,1)}, bf16[2,48,2560]{2,1,0:T(8,128)(2,1)S(1)}, u32[]{:S(2)}, u32[]{:S(2)}) collective-permute-start(bf16[2,48,2560]{2,1,0:T(8,128)(2,1)} %get-tuple-element.67), channel_id=1, source_target_pairs={{0,4},{2,6},{4,0},{6,2},{1,5},{3,7},{5,1},{7,3},{8,12},{10,14},{12... | collective-permute-start | bytes 1474568 | tf_op jit(solution)/shard_map/ppermute | solution.py:27
  61.8 18.6 %collective-permute-start.9 = (bf16[192,1280]{1,0:T(8,128)(2,1)S(1)}, bf16[192,1280]{1,0:T(8,128)(2,1)S(1)}, u32[]{:S(2)}, u32[]{:S(2)}) collective-permute-start(bf16[192,1280]{1,0:T(8,128)(2,1)S(1)} %bitcast.251), channel_id=1, source_target_pairs={{0,1},{1,0},{2,3},{3,2},{4,5},{5,4},{6,7},{7,6},{8,9},{9,8},{10,11... | collective-permute-start | bytes 1474568 | tf_op jit(solution)/shard_map/ppermute | solution.py:27
  61.9 17.0 %collective-permute-start.7 = (bf16[2,48,1280]{2,1,0:T(8,128)(2,1)S(1)}, bf16[2,48,1280]{2,1,0:T(8,128)(2,1)S(1)}, u32[]{:S(2)}, u32[]{:S(2)}) collective-permute-start(bf16[2,48,1280]{2,1,0:T(8,128)(2,1)S(1)} %slice.417), channel_id=1, source_target_pairs={{0,4},{2,6},{4,0},{6,2},{1,5},{3,7},{5,1},{7,3},{8,12},{10,14},{12... | collective-permute-start | bytes 737288 | tf_op jit(solution)/shard_map/ppermute | solution.py:27
  64.6 14.3 %collective-permute-start.8 = (bf16[2,48,1280]{2,1,0:T(8,128)(2,1)S(1)}, bf16[2,48,1280]{2,1,0:T(8,128)(2,1)S(1)}, u32[]{:S(2)}, u32[]{:S(2)}) collective-permute-start(bf16[2,48,1280]{2,1,0:T(8,128)(2,1)S(1)} %slice.418), channel_id=1, source_target_pairs={{0,2},{2,0},{4,6},{6,4},{1,3},{3,1},{5,7},{7,5},{8,10},{10,8},{12,... | collective-permute-start | bytes 737288 | tf_op jit(solution)/shard_map/ppermute | solution.py:27
  95.5 11.9 %collective-permute-start.19 = (bf16[2,48,2560]{2,1,0:T(8,128)(2,1)S(1)}, bf16[2,48,2560]{2,1,0:T(8,128)(2,1)S(1)}, u32[]{:S(2)}, u32[]{:S(2)}) collective-permute-start(bf16[2,48,2560]{2,1,0:T(8,128)(2,1)S(1)} %pad_maximum_fusion.12), channel_id=1, source_target_pairs={{0,2},{2,0},{4,6},{6,4},{1,3},{3,1},{5,7},{7,5},{8,10},{10,8},{12,... | collective-permute-start | bytes 1474568 | tf_op jit(solution)/shard_map/ppermute | solution.py:27
  102.3 12.0 %collective-permute-start.17 = (bf16[2,48,2560]{2,1,0:T(8,128)(2,1)S(1)}, bf16[2,48,2560]{2,1,0:T(8,128)(2,1)S(1)}, u32[]{:S(2)}, u32[]{:S(2)}) collective-permute-start(bf16[2,48,2560]{2,1,0:T(8,128)(2,1)S(1)} %pad_maximum_fusion.11), channel_id=1, source_target_pairs={{0,4},{2,6},{4,0},{6,2},{1,5},{3,7},{5,1},{7,3},{8,12},{10,14},{12... | collective-permute-start | bytes 1474568 | tf_op jit(solution)/shard_map/ppermute | solution.py:27
  114.5 15.0 %collective-permute-start.23 = (bf16[50,2560]{1,0:T(8,128)(2,1)S(1)}, bf16[50,2560]{1,0:T(8,128)(2,1)S(1)}, u32[]{:S(2)}, u32[]{:S(2)}) collective-permute-start(bf16[50,2560]{1,0:T(8,128)(2,1)S(1)} %pad_maximum_fusion.17), channel_id=1, source_target_pairs={{0,8},{8,0},{1,9},{9,1},{2,10},{10,2},{3,11},{11,3},{4,12},{12,4},... | collective-permute-start | bytes 768008 | tf_op jit(solution)/shard_map/ppermute | solution.py:21
  135.2 15.2 %collective-permute-start.25 = (bf16[49,2560]{1,0:T(8,128)(2,1)S(1)}, bf16[49,2560]{1,0:T(8,128)(2,1)S(1)}, u32[]{:S(2)}, u32[]{:S(2)}) collective-permute-start(bf16[49,2560]{1,0:T(8,128)(2,1)S(1)} %fusion.70), channel_id=1, source_target_pairs={{0,8},{8,0},{1,9},{9,1},{2,10},{10,2},{3,11},{11,3},{4,12},{12,4},... | collective-permute-start | bytes 752648 | tf_op jit(solution)/shard_map/ppermute | solution.py:21
  135.7 19.0 %collective-permute-start.24 = (bf16[64,2560]{1,0:T(8,128)(2,1)S(1)}, bf16[64,2560]{1,0:T(8,128)(2,1)S(1)}, u32[]{:S(2)}, u32[]{:S(2)}) collective-permute-start(bf16[64,2560]{1,0:T(8,128)(2,1)S(1)} %fusion.32), channel_id=1, source_target_pairs={{16,0},{17,1},{18,2},{19,3},{20,4},{21,5},{22,6},{23,7},{24,8},{25... | collective-permute-start | bytes 983048 | tf_op jit(solution)/shard_map/ppermute | solution.py:15
  151.3 21.9 %collective-permute-start.34 = (bf16[2,48,2560]{2,1,0:T(8,128)(2,1)}, bf16[2,48,2560]{2,1,0:T(8,128)(2,1)}, u32[]{:S(2)}, u32[]{:S(2)}) collective-permute-start(bf16[2,48,2560]{2,1,0:T(8,128)(2,1)} %get-tuple-element.57), channel_id=1, source_target_pairs={{0,2},{2,0},{4,6},{6,4},{1,3},{3,1},{5,7},{7,5},{8,10},{10,8},{12,... | collective-permute-start | bytes 1474568 | tf_op jit(solution)/shard_map/ppermute | solution.py:27
  152.5 21.7 %collective-permute-start.35 = (bf16[2,48,2560]{2,1,0:T(8,128)(2,1)}, bf16[2,48,2560]{2,1,0:T(8,128)(2,1)}, u32[]{:S(2)}, u32[]{:S(2)}) collective-permute-start(bf16[2,48,2560]{2,1,0:T(8,128)(2,1)} %get-tuple-element.57), channel_id=1, source_target_pairs={{0,4},{2,6},{4,0},{6,2},{1,5},{3,7},{5,1},{7,3},{8,12},{10,14},{12... | collective-permute-start | bytes 1474568 | tf_op jit(solution)/shard_map/ppermute | solution.py:27
  152.6 16.1 %collective-permute-start.27 = (bf16[2,48]{1,0:T(2,128)(2,1)S(1)}, bf16[2,48]{1,0:T(2,128)(2,1)S(1)}, u32[]{:S(2)}, u32[]{:S(2)}) collective-permute-start(bf16[2,48]{1,0:T(2,128)(2,1)S(1)} %pad_maximum_fusion.22), channel_id=1, source_target_pairs={{0,4},{2,6},{4,0},{6,2},{1,5},{3,7},{5,1},{7,3},{8,12},{10,14},{12... | collective-permute-start | bytes 584 | tf_op jit(solution)/shard_map/ppermute | solution.py:27
  155.8 20.8 %collective-permute-start.29 = (bf16[48,2560]{1,0:T(8,128)(2,1)}, bf16[48,2560]{1,0:T(8,128)(2,1)}, u32[]{:S(2)}, u32[]{:S(2)}) collective-permute-start(bf16[48,2560]{1,0:T(8,128)(2,1)} %get-tuple-element.63), channel_id=1, source_target_pairs={{0,8},{8,0},{1,9},{9,1},{2,10},{10,2},{3,11},{11,3},{4,12},{12,4},... | collective-permute-start | bytes 737288 | tf_op jit(solution)/shard_map/ppermute | solution.py:21
  157.1 11.9 %collective-permute-start.26 = (bf16[2,48]{1,0:T(2,128)(2,1)S(1)}, bf16[2,48]{1,0:T(2,128)(2,1)S(1)}, u32[]{:S(2)}, u32[]{:S(2)}) collective-permute-start(bf16[2,48]{1,0:T(2,128)(2,1)S(1)} %pad_maximum_fusion.22), channel_id=1, source_target_pairs={{0,2},{2,0},{4,6},{6,4},{1,3},{3,1},{5,7},{7,5},{8,10},{10,8},{12,... | collective-permute-start | bytes 584 | tf_op jit(solution)/shard_map/ppermute | solution.py:27
  206.7 41.6 %reduce-scatter.5.cloned.1.call-start = ((), (), s32[]{:S(2)}) async-start(), calls=%async_computation.3 | async-start | bytes 1474560 | tf_op jit(solution)/shard_map/reduce_scatter | solution.py:280
  230.4 10.7 %collective-permute-start.45 = (bf16[50,2560]{1,0:T(8,128)(2,1)S(1)}, bf16[50,2560]{1,0:T(8,128)(2,1)}, u32[]{:S(2)}, u32[]{:S(2)}) collective-permute-start(bf16[50,2560]{1,0:T(8,128)(2,1)S(1)} %pad_maximum_fusion.18), channel_id=1, source_target_pairs={{0,8},{8,0},{1,9},{9,1},{2,10},{10,2},{3,11},{11,3},{4,12},{12,4},... | collective-permute-start | bytes 768008 | tf_op jit(solution)/shard_map/ppermute | solution.py:21
  (66 other events, 384.3 us)
Sparse Core Ops, SparseCore 0:
  206.8 9.6 reduce-scatter.2
  235.0 7.7 reduce-scatter.4

commit v16 on v14

--- a/solution.py
+++ b/solution.py
@@ -216,9 +216,17 @@
         )
         hidden_scaled = (hidden * scale_column).astype(jnp.bfloat16)
         kept_list.append((grad_pair, hidden_scaled, flat_rows, flat_grads))
+        weight_rows = jnp.pad(
+            part_weight.reshape(-1, groups, 1, capacity),
+            ((0, 0), (0, 0), (0, 0), (0, feature_count - capacity)),
+        )
+        quad_total = reduce_quad(
+            jnp.concatenate(
+                [part_rows.reshape(-1, groups, capacity, feature_count), weight_rows], axis=2
+            )
+        )
         rows_back, weights_back = to_owners(
-            reduce_quad(part_rows.reshape(-1, groups, capacity, feature_count)),
-            reduce_quad(part_weight.reshape(-1, groups, capacity)),
+            quad_total[:, :capacity], quad_total[:, capacity, :capacity]
         )
         (
             finish_inputs,

time: 235 us -> 238 us (1.013)
  waiting for transfers between devices: 103 us -> 110 us
  local copies, waits for them, and re-layouts: 19.3 us -> 16.4 us
  starting transfers between devices: 60.1 us -> 57.2 us
    ppermute x39 -> x33, starting transfers between devices: 42.4 us -> 32.3 us  [flipped(): return lax.ppermute(block, axis, route)]
    ppermute x8, starting transfers between devices: 16.2 us -> 23.3 us  [rotated(): return lax.ppermute(block, axis, route)]
    ppermute x8, waiting for transfers between devices: 25.3 us -> 29 us  [rotated(): return lax.ppermute(block, axis, route)]
    ppermute x39 -> x33, waiting for transfers between devices: 77.8 us -> 80.6 us  [flipped(): return lax.ppermute(block, axis, route)]
    slice x2, local copies, waits for them, and re-layouts: 2.68 us -> 0.08 us  [reduce_quad(): from_first = flipped(parts[3][..., :half], 'ej', 1).astype(jnp.float32)]
  transfers between devices with their start and end apart: 50 -> 44, of which waited for: 27 -> 27; matrix products, arithmetic and copies ran while one was open for 13% -> 13% of each run, Pallas kernels for 0% -> 0%
where the time goes in v16:
time: 238 us
  waiting for transfers between devices  110 us (46%)
  starting transfers between devices  57.2 us (24%)
  other arithmetic  22.7 us (10%)
  local copies, waits for them, and re-layouts  16.4 us (7%)
  matrix products  16.4 us (7%)
  between operations  15.1 us (6%)
    ppermute x33, waiting for transfers between devices, flipped(): return lax.ppermute(block, axis, route)  80.6 us
    ppermute x33, starting transfers between devices, flipped(): return lax.ppermute(block, axis, route)  32.3 us
    ppermute x8, waiting for transfers between devices, rotated(): return lax.ppermute(block, axis, route)  29 us
    ppermute x8, starting transfers between devices, rotated(): return lax.ppermute(block, axis, route)  23.3 us
    dot_general x6, matrix products, contract_last(): lax.dot_general(first_operand, second_operand, (((1,), (1,)), ((), ())),...  6.51 us
    dot_general x2, matrix products, contract_first(): lax.dot_general(first_operand, second_operand, (((0,), (0,)), ((), ())),...  4.93 us
  transfers between devices with their start and end apart: 44, of which 27 were waited for; matrix products, arithmetic and copies ran while one was open for 13% of the time, Pallas kernels for 0%

profile of v16, /device:TPU:0, one launch (start us, length us, event | category | flops | bytes accessed | tf_op | source)
XLA Modules:
  0.0 237.6 jit_solution(7648390813304991141)
XLA Ops:
  11.2 4.0 %collective-permute-start = (bf16[48]{0:T(256)(128)(2,1)S(1)}, bf16[48]{0:T(256)(128)(2,1)S(1)}, u32[]{:S(2)}, u32[]{:S(2)}) collective-permute-start(bf16[48]{0:T(256)(128)(2,1)S(1)} %get-tuple-element.90), channel_id=1, source_target_pairs={{0,8},{8,0},{1,9},{9,1},{2,10},{10,2},{3,11},{11,3},{4,12},{12,4},... | collective-permute-start | bytes 296 | tf_op jit(solution)/shard_map/ppermute | solution.py:21
  24.9 3.2 %collective-permute-done.2 = bf16[2,48]{1,0:T(2,128)(2,1)S(1)} collective-permute-done((bf16[2,48]{1,0:T(2,128)(2,1)S(1)}, bf16[2,48]{1,0:T(2,128)(2,1)S(1)}, u32[]{:S(2)}, u32[]{:S(2)}) %collective-permute-start.2) | collective-permute-done | bytes 224 | tf_op jit(solution)/shard_map/ppermute | solution.py:27
  28.1 3.4 %collective-permute-start.3 = (bf16[2,48]{1,0:T(2,128)(2,1)S(1)}, bf16[2,48]{1,0:T(2,128)(2,1)S(1)}, u32[]{:S(2)}, u32[]{:S(2)}) collective-permute-start(bf16[2,48]{1,0:T(2,128)(2,1)S(1)} %pad_maximum_fusion.21), channel_id=1, source_target_pairs={{0,6},{2,4},{4,2},{6,0},{1,7},{3,5},{5,3},{7,1},{8,14},{10,12},{12... | collective-permute-start | bytes 584 | tf_op jit(solution)/shard_map/ppermute | solution.py:27
  33.1 8.5 %collective-permute-done.10 = bf16[48,2560]{1,0:T(8,128)(2,1)S(1)} collective-permute-done((bf16[48,2560]{1,0:T(8,128)(2,1)S(1)}, bf16[48,2560]{1,0:T(8,128)(2,1)S(1)}, u32[]{:S(2)}, u32[]{:S(2)}) %collective-permute-start.10) | collective-permute-done | bytes 245792 | tf_op jit(solution)/shard_map/ppermute | solution.py:21
  48.2 7.8 %collective-permute-done.11 = bf16[2,48,2560]{2,1,0:T(8,128)(2,1)S(1)} collective-permute-done((bf16[2,48,2560]{2,1,0:T(8,128)(2,1)S(1)}, bf16[2,48,2560]{2,1,0:T(8,128)(2,1)S(1)}, u32[]{:S(2)}, u32[]{:S(2)}) %collective-permute-start.11) | collective-permute-done | bytes 491552 | tf_op jit(solution)/shard_map/ppermute | solution.py:27
  59.9 6.6 %collective-permute-done.5 = bf16[2,48,2560]{2,1,0:T(8,128)(2,1)S(1)} collective-permute-done((bf16[2,48,2560]{2,1,0:T(8,128)(2,1)S(1)}, bf16[2,48,2560]{2,1,0:T(8,128)(2,1)S(1)}, u32[]{:S(2)}, u32[]{:S(2)}) %collective-permute-start.5) | collective-permute-done | bytes 491552 | tf_op jit(solution)/shard_map/ppermute | solution.py:27
  68.6 4.6 %collective-permute-done.13 = bf16[2,48,1280]{2,1,0:T(8,128)(2,1)S(1)} collective-permute-done((bf16[2,48,1280]{2,1,0:T(8,128)(2,1)S(1)}, bf16[2,48,1280]{2,1,0:T(8,128)(2,1)S(1)}, u32[]{:S(2)}, u32[]{:S(2)}) %collective-permute-start.13) | collective-permute-done | bytes 245792 | tf_op jit(solution)/shard_map/ppermute | solution.py:27
  83.0 5.7 %collective-permute-done.17 = bf16[2,49,1280]{2,1,0:T(8,128)(2,1)S(1)} collective-permute-done((bf16[2,49,1280]{2,1,0:T(8,128)(2,1)S(1)}, bf16[2,49,1280]{2,1,0:T(8,128)(2,1)S(1)}, u32[]{:S(2)}, u32[]{:S(2)}) %collective-permute-start.17) | collective-permute-done | bytes 250912 | tf_op jit(solution)/shard_map/ppermute | solution.py:27
  91.8 8.1 %collective-permute-done.20 = bf16[2,49,2560]{2,0,1:T(2,128)(2,1)S(1)} collective-permute-done((bf16[2,49,2560]{2,0,1:T(2,128)(2,1)S(1)}, bf16[2,49,2560]{2,0,1:T(2,128)(2,1)S(1)}, u32[]{:S(2)}, u32[]{:S(2)}) %collective-permute-start.20) | collective-permute-done | bytes 501792 | tf_op jit(solution)/shard_map/ppermute | solution.py:27
  101.4 4.7 %collective-permute-start.21 = (bf16[50,2560]{1,0:T(8,128)(2,1)S(1)}, bf16[50,2560]{1,0:T(8,128)(2,1)S(1)}, u32[]{:S(2)}, u32[]{:S(2)}) collective-permute-start(bf16[50,2560]{1,0:T(8,128)(2,1)S(1)} %pad_maximum_fusion.17), channel_id=1, source_target_pairs={{0,8},{8,0},{1,9},{9,1},{2,10},{10,2},{3,11},{11,3},{4,12},{12,4},... | collective-permute-start | bytes 768008 | tf_op jit(solution)/shard_map/ppermute | solution.py:21
  106.9 7.8 %collective-permute-done.21 = bf16[50,2560]{1,0:T(8,128)(2,1)S(1)} collective-permute-done((bf16[50,2560]{1,0:T(8,128)(2,1)S(1)}, bf16[50,2560]{1,0:T(8,128)(2,1)S(1)}, u32[]{:S(2)}, u32[]{:S(2)}) %collective-permute-start.21) | collective-permute-done | bytes 256032 | tf_op jit(solution)/shard_map/ppermute | solution.py:21
  120.6 3.0 %collective-permute-start.32 = (bf16[48,2560]{1,0:T(8,128)(2,1)S(1)}, bf16[48,2560]{1,0:T(8,128)(2,1)S(1)}, u32[]{:S(2)}, u32[]{:S(2)}) collective-permute-start(bf16[48,2560]{1,0:T(8,128)(2,1)S(1)} %get-tuple-element.64), channel_id=1, source_target_pairs={{0,8},{8,0},{1,9},{9,1},{2,10},{10,2},{3,11},{11,3},{4,12},{12,4},... | collective-permute-start | bytes 737288 | tf_op jit(solution)/shard_map/ppermute | solution.py:21
  126.0 7.0 %collective-permute-done.32 = bf16[48,2560]{1,0:T(8,128)(2,1)S(1)} collective-permute-done((bf16[48,2560]{1,0:T(8,128)(2,1)S(1)}, bf16[48,2560]{1,0:T(8,128)(2,1)S(1)}, u32[]{:S(2)}, u32[]{:S(2)}) %collective-permute-start.32) | collective-permute-done | bytes 245792 | tf_op jit(solution)/shard_map/ppermute | solution.py:21
  137.0 3.4 %collective-permute-start.27 = (bf16[48,2560]{1,0:T(8,128)(2,1)}, bf16[48,2560]{1,0:T(8,128)(2,1)}, u32[]{:S(2)}, u32[]{:S(2)}) collective-permute-start(bf16[48,2560]{1,0:T(8,128)(2,1)} %get-tuple-element.68), channel_id=1, source_target_pairs={{0,8},{8,0},{1,9},{9,1},{2,10},{10,2},{3,11},{11,3},{4,12},{12,4},... | collective-permute-start | bytes 737288 | tf_op jit(solution)/shard_map/ppermute | solution.py:21
  142.0 3.1 %collective-permute-done.24 = bf16[2,48]{1,0:T(2,128)(2,1)S(1)} collective-permute-done((bf16[2,48]{1,0:T(2,128)(2,1)S(1)}, bf16[2,48]{1,0:T(2,128)(2,1)S(1)}, u32[]{:S(2)}, u32[]{:S(2)}) %collective-permute-start.24) | collective-permute-done | bytes 224 | tf_op jit(solution)/shard_map/ppermute | solution.py:27
  145.1 6.7 %collective-permute-done.26 = bf16[2,48]{1,0:T(2,128)(2,1)S(1)} collective-permute-done((bf16[2,48]{1,0:T(2,128)(2,1)S(1)}, bf16[2,48]{1,0:T(2,128)(2,1)S(1)}, u32[]{:S(2)}, u32[]{:S(2)}) %collective-permute-start.26) | collective-permute-done | bytes 224 | tf_op jit(solution)/shard_map/ppermute | solution.py:27
  165.0 5.8 %collective-permute-done.28 = bf16[2,48,2560]{2,1,0:T(8,128)(2,1)S(1)} collective-permute-done((bf16[2,48,2560]{2,1,0:T(8,128)(2,1)S(1)}, bf16[2,48,2560]{2,1,0:T(8,128)(2,1)S(1)}, u32[]{:S(2)}, u32[]{:S(2)}) %collective-permute-start.28) | collective-permute-done | bytes 491552 | tf_op jit(solution)/shard_map/ppermute | solution.py:27
  173.7 3.4 %collective-permute-done.30 = bf16[2,48,1280]{2,1,0:T(8,128)(2,1)S(1)} collective-permute-done((bf16[2,48,1280]{2,1,0:T(8,128)(2,1)S(1)}, bf16[2,48,1280]{2,1,0:T(8,128)(2,1)S(1)}, u32[]{:S(2)}, u32[]{:S(2)}) %collective-permute-start.30) | collective-permute-done | bytes 245792 | tf_op jit(solution)/shard_map/ppermute | solution.py:27
  186.8 3.0 %convolution_convert_fusion = bf16[384,2560]{1,0:T(8,128)(2,1)} fusion(bf16[384,2560]{1,0:T(8,128)(2,1)S(1)} %bitcast.254, bf16[384,2560]{1,0:T(8,128)(2,1)S(1)} %bitcast.248, bf16[384,192]{0,1:T(8,128)(2,1)S(1)} %copy-done.30, bf16[384,192]{0,1:T(8,128)(2,1)S(1)} %copy-done.29, bf16[384,192]{0,1:T(8,128)(2,1)S(1)} %copy-done.27, ...), kind=kOutput, calls=%fused_computation.7 | convolution fusion | flops 1521156096 | bytes 6488064 | tf_op jit(solution)/shard_map/dot_general | solution.py:42
  192.8 3.7 %collective-permute-done.39 = bf16[2,49,1280]{2,1,0:T(8,128)(2,1)S(1)} collective-permute-done((bf16[2,49,1280]{2,1,0:T(8,128)(2,1)S(1)}, bf16[2,49,1280]{2,1,0:T(8,128)(2,1)S(1)}, u32[]{:S(2)}, u32[]{:S(2)}) %collective-permute-start.39) | collective-permute-done | bytes 250912 | tf_op jit(solution)/shard_map/ppermute | solution.py:27
  202.8 4.1 %collective-permute-done.40 = bf16[2,49,2560]{2,0,1:T(2,128)(2,1)S(1)} collective-permute-done((bf16[2,49,2560]{2,0,1:T(2,128)(2,1)S(1)}, bf16[2,49,2560]{2,0,1:T(2,128)(2,1)S(1)}, u32[]{:S(2)}, u32[]{:S(2)}) %collective-permute-start.40) | collective-permute-done | bytes 501792 | tf_op jit(solution)/shard_map/ppermute | solution.py:27
  206.9 3.4 %collective-permute-done.38 = bf16[2,49,2560]{2,0,1:T(2,128)(2,1)S(1)} collective-permute-done((bf16[2,49,2560]{2,0,1:T(2,128)(2,1)S(1)}, bf16[2,49,2560]{2,0,1:T(2,128)(2,1)S(1)}, u32[]{:S(2)}, u32[]{:S(2)}) %collective-permute-start.38) | collective-permute-done | bytes 501792 | tf_op jit(solution)/shard_map/ppermute | solution.py:27
  211.6 5.1 %collective-permute-start.41 = (bf16[50,2560]{1,0:T(8,128)(2,1)S(1)}, bf16[50,2560]{1,0:T(8,128)(2,1)S(1)}, u32[]{:S(2)}, u32[]{:S(2)}) collective-permute-start(bf16[50,2560]{1,0:T(8,128)(2,1)S(1)} %pad_maximum_fusion.18), channel_id=1, source_target_pairs={{0,8},{8,0},{1,9},{9,1},{2,10},{10,2},{3,11},{11,3},{4,12},{12,4},... | collective-permute-start | bytes 768008 | tf_op jit(solution)/shard_map/ppermute | solution.py:21
  218.8 5.7 %collective-permute-done.41 = bf16[50,2560]{1,0:T(8,128)(2,1)S(1)} collective-permute-done((bf16[50,2560]{1,0:T(8,128)(2,1)S(1)}, bf16[50,2560]{1,0:T(8,128)(2,1)S(1)}, u32[]{:S(2)}, u32[]{:S(2)}) %collective-permute-start.41) | collective-permute-done | bytes 256032 | tf_op jit(solution)/shard_map/ppermute | solution.py:21
  (305 shorter events, 100.5 us)
Async XLA Ops:
  7.2 221.4 %reduce-scatter.3.cloned.1.call-start = ((), (), s32[]{:S(2)}) async-start(), calls=%async_computation.2 | async-start | bytes 2949120 | tf_op jit(solution)/shard_map/reduce_scatter | solution.py:266
  17.5 25.8 %collective-permute-start.4 = (bf16[48,2560]{1,0:T(8,128)(2,1)S(1)}, bf16[48,2560]{1,0:T(8,128)(2,1)S(1)}, u32[]{:S(2)}, u32[]{:S(2)}) collective-permute-start(bf16[48,2560]{1,0:T(8,128)(2,1)S(1)} %get-tuple-element.76), channel_id=1, source_target_pairs={{0,8},{8,0},{1,9},{9,1},{2,10},{10,2},{3,11},{11,3},{4,12},{12,4},... | collective-permute-start | bytes 737288 | tf_op jit(solution)/shard_map/ppermute | solution.py:21
  18.8 22.9 %collective-permute-start.10 = (bf16[48,2560]{1,0:T(8,128)(2,1)S(1)}, bf16[48,2560]{1,0:T(8,128)(2,1)S(1)}, u32[]{:S(2)}, u32[]{:S(2)}) collective-permute-start(bf16[48,2560]{1,0:T(8,128)(2,1)S(1)} %get-tuple-element.72), channel_id=1, source_target_pairs={{0,8},{8,0},{1,9},{9,1},{2,10},{10,2},{3,11},{11,3},{4,12},{12,4},... | collective-permute-start | bytes 737288 | tf_op jit(solution)/shard_map/ppermute | solution.py:21
  21.7 22.3 %collective-permute-start.16 = (bf16[192,1280]{1,0:T(8,128)(2,1)S(1)}, bf16[192,1280]{1,0:T(8,128)(2,1)S(1)}, u32[]{:S(2)}, u32[]{:S(2)}) collective-permute-start(bf16[192,1280]{1,0:T(8,128)(2,1)S(1)} %bitcast.263), channel_id=1, source_target_pairs={{0,1},{1,0},{2,3},{3,2},{4,5},{5,4},{6,7},{7,6},{8,9},{9,8},{10,11... | collective-permute-start | bytes 1474568 | tf_op jit(solution)/shard_map/ppermute | solution.py:27
  31.5 26.0 %collective-permute-start.15 = (bf16[192,1280]{1,0:T(8,128)(2,1)}, bf16[192,1280]{1,0:T(8,128)(2,1)}, u32[]{:S(2)}, u32[]{:S(2)}) collective-permute-start(bf16[192,1280]{1,0:T(8,128)(2,1)} %bitcast.28), channel_id=1, source_target_pairs={{0,1},{1,0},{2,3},{3,2},{4,5},{5,4},{6,7},{7,6},{8,9},{9,8},{10,11... | collective-permute-start | bytes 1474568 | tf_op jit(solution)/shard_map/ppermute | solution.py:27
  41.8 14.2 %collective-permute-start.11 = (bf16[2,48,2560]{2,1,0:T(8,128)(2,1)S(1)}, bf16[2,48,2560]{2,1,0:T(8,128)(2,1)S(1)}, u32[]{:S(2)}, u32[]{:S(2)}) collective-permute-start(bf16[2,48,2560]{2,1,0:T(8,128)(2,1)S(1)} %get-tuple-element.70), channel_id=1, source_target_pairs={{0,2},{2,0},{4,6},{6,4},{1,3},{3,1},{5,7},{7,5},{8,10},{10,8},{12,... | collective-permute-start | bytes 1474568 | tf_op jit(solution)/shard_map/ppermute | solution.py:27
  43.3 14.2 %collective-permute-start.12 = (bf16[2,48,2560]{2,1,0:T(8,128)(2,1)S(1)}, bf16[2,48,2560]{2,1,0:T(8,128)(2,1)S(1)}, u32[]{:S(2)}, u32[]{:S(2)}) collective-permute-start(bf16[2,48,2560]{2,1,0:T(8,128)(2,1)S(1)} %get-tuple-element.70), channel_id=1, source_target_pairs={{0,4},{2,6},{4,0},{6,2},{1,5},{3,7},{5,1},{7,3},{8,12},{10,14},{12... | collective-permute-start | bytes 1474568 | tf_op jit(solution)/shard_map/ppermute | solution.py:27
  43.4 23.1 %collective-permute-start.5 = (bf16[2,48,2560]{2,1,0:T(8,128)(2,1)S(1)}, bf16[2,48,2560]{2,1,0:T(8,128)(2,1)S(1)}, u32[]{:S(2)}, u32[]{:S(2)}) collective-permute-start(bf16[2,48,2560]{2,1,0:T(8,128)(2,1)S(1)} %get-tuple-element.74), channel_id=1, source_target_pairs={{0,2},{2,0},{4,6},{6,4},{1,3},{3,1},{5,7},{7,5},{8,10},{10,8},{12,... | collective-permute-start | bytes 1474568 | tf_op jit(solution)/shard_map/ppermute | solution.py:27
  44.8 23.2 %collective-permute-start.6 = (bf16[2,48,2560]{2,1,0:T(8,128)(2,1)S(1)}, bf16[2,48,2560]{2,1,0:T(8,128)(2,1)S(1)}, u32[]{:S(2)}, u32[]{:S(2)}) collective-permute-start(bf16[2,48,2560]{2,1,0:T(8,128)(2,1)S(1)} %get-tuple-element.74), channel_id=1, source_target_pairs={{0,4},{2,6},{4,0},{6,2},{1,5},{3,7},{5,1},{7,3},{8,12},{10,14},{12... | collective-permute-start | bytes 1474568 | tf_op jit(solution)/shard_map/ppermute | solution.py:27
  56.0 21.3 %collective-permute-start.9 = (bf16[192,1280]{1,0:T(8,128)(2,1)S(1)}, bf16[192,1280]{1,0:T(8,128)(2,1)S(1)}, u32[]{:S(2)}, u32[]{:S(2)}) collective-permute-start(bf16[192,1280]{1,0:T(8,128)(2,1)S(1)} %bitcast.277), channel_id=1, source_target_pairs={{0,1},{1,0},{2,3},{3,2},{4,5},{5,4},{6,7},{7,6},{8,9},{9,8},{10,11... | collective-permute-start | bytes 1474568 | tf_op jit(solution)/shard_map/ppermute | solution.py:27
  57.5 15.8 %collective-permute-start.13 = (bf16[2,48,1280]{2,1,0:T(8,128)(2,1)S(1)}, bf16[2,48,1280]{2,1,0:T(8,128)(2,1)S(1)}, u32[]{:S(2)}, u32[]{:S(2)}) collective-permute-start(bf16[2,48,1280]{2,1,0:T(8,128)(2,1)S(1)} %slice.337), channel_id=1, source_target_pairs={{0,4},{2,6},{4,0},{6,2},{1,5},{3,7},{5,1},{7,3},{8,12},{10,14},{12... | collective-permute-start | bytes 737288 | tf_op jit(solution)/shard_map/ppermute | solution.py:27
  57.5 15.8 %collective-permute-start.14 = (bf16[2,48,1280]{2,1,0:T(8,128)(2,1)S(1)}, bf16[2,48,1280]{2,1,0:T(8,128)(2,1)S(1)}, u32[]{:S(2)}, u32[]{:S(2)}) collective-permute-start(bf16[2,48,1280]{2,1,0:T(8,128)(2,1)S(1)} %slice.338), channel_id=1, source_target_pairs={{0,2},{2,0},{4,6},{6,4},{1,3},{3,1},{5,7},{7,5},{8,10},{10,8},{12,... | collective-permute-start | bytes 737288 | tf_op jit(solution)/shard_map/ppermute | solution.py:27
  101.4 13.3 %collective-permute-start.21 = (bf16[50,2560]{1,0:T(8,128)(2,1)S(1)}, bf16[50,2560]{1,0:T(8,128)(2,1)S(1)}, u32[]{:S(2)}, u32[]{:S(2)}) collective-permute-start(bf16[50,2560]{1,0:T(8,128)(2,1)S(1)} %pad_maximum_fusion.17), channel_id=1, source_target_pairs={{0,8},{8,0},{1,9},{9,1},{2,10},{10,2},{3,11},{11,3},{4,12},{12,4},... | collective-permute-start | bytes 768008 | tf_op jit(solution)/shard_map/ppermute | solution.py:21
  120.6 12.5 %collective-permute-start.32 = (bf16[48,2560]{1,0:T(8,128)(2,1)S(1)}, bf16[48,2560]{1,0:T(8,128)(2,1)S(1)}, u32[]{:S(2)}, u32[]{:S(2)}) collective-permute-start(bf16[48,2560]{1,0:T(8,128)(2,1)S(1)} %get-tuple-element.64), channel_id=1, source_target_pairs={{0,8},{8,0},{1,9},{9,1},{2,10},{10,2},{3,11},{11,3},{4,12},{12,4},... | collective-permute-start | bytes 737288 | tf_op jit(solution)/shard_map/ppermute | solution.py:21
  123.9 11.9 %collective-permute-start.22 = (bf16[64,2560]{1,0:T(8,128)(2,1)S(1)}, bf16[64,2560]{1,0:T(8,128)(2,1)S(1)}, u32[]{:S(2)}, u32[]{:S(2)}) collective-permute-start(bf16[64,2560]{1,0:T(8,128)(2,1)S(1)} %fusion.36), channel_id=1, source_target_pairs={{16,0},{17,1},{18,2},{19,3},{20,4},{21,5},{22,6},{23,7},{24,8},{25... | collective-permute-start | bytes 983048 | tf_op jit(solution)/shard_map/ppermute | solution.py:15
  125.4 15.5 %collective-permute-start.25 = (bf16[2,48]{1,0:T(2,128)(2,1)S(1)}, bf16[2,48]{1,0:T(2,128)(2,1)S(1)}, u32[]{:S(2)}, u32[]{:S(2)}) collective-permute-start(bf16[2,48]{1,0:T(2,128)(2,1)S(1)} %pad_maximum_fusion.22), channel_id=1, source_target_pairs={{0,4},{2,6},{4,0},{6,2},{1,5},{3,7},{5,1},{7,3},{8,12},{10,14},{12... | collective-permute-start | bytes 584 | tf_op jit(solution)/shard_map/ppermute | solution.py:27
  134.1 18.4 %collective-permute-start.33 = (bf16[2,48,2560]{2,1,0:T(8,128)(2,1)}, bf16[2,48,2560]{2,1,0:T(8,128)(2,1)S(1)}, u32[]{:S(2)}, u32[]{:S(2)}) collective-permute-start(bf16[2,48,2560]{2,1,0:T(8,128)(2,1)} %get-tuple-element.62), channel_id=1, source_target_pairs={{0,2},{2,0},{4,6},{6,4},{1,3},{3,1},{5,7},{7,5},{8,10},{10,8},{12,... | collective-permute-start | bytes 1474568 | tf_op jit(solution)/shard_map/ppermute | solution.py:27
  135.7 18.6 %collective-permute-start.34 = (bf16[2,48,2560]{2,1,0:T(8,128)(2,1)}, bf16[2,48,2560]{2,1,0:T(8,128)(2,1)S(1)}, u32[]{:S(2)}, u32[]{:S(2)}) collective-permute-start(bf16[2,48,2560]{2,1,0:T(8,128)(2,1)} %get-tuple-element.62), channel_id=1, source_target_pairs={{0,4},{2,6},{4,0},{6,2},{1,5},{3,7},{5,1},{7,3},{8,12},{10,14},{12... | collective-permute-start | bytes 1474568 | tf_op jit(solution)/shard_map/ppermute | solution.py:27
  137.0 18.9 %collective-permute-start.27 = (bf16[48,2560]{1,0:T(8,128)(2,1)}, bf16[48,2560]{1,0:T(8,128)(2,1)}, u32[]{:S(2)}, u32[]{:S(2)}) collective-permute-start(bf16[48,2560]{1,0:T(8,128)(2,1)} %get-tuple-element.68), channel_id=1, source_target_pairs={{0,8},{8,0},{1,9},{9,1},{2,10},{10,2},{3,11},{11,3},{4,12},{12,4},... | collective-permute-start | bytes 737288 | tf_op jit(solution)/shard_map/ppermute | solution.py:21
  141.0 10.8 %collective-permute-start.26 = (bf16[2,48]{1,0:T(2,128)(2,1)S(1)}, bf16[2,48]{1,0:T(2,128)(2,1)S(1)}, u32[]{:S(2)}, u32[]{:S(2)}) collective-permute-start(bf16[2,48]{1,0:T(2,128)(2,1)S(1)} %pad_maximum_fusion.22), channel_id=1, source_target_pairs={{0,6},{2,4},{4,2},{6,0},{1,7},{3,5},{5,3},{7,1},{8,14},{10,12},{12... | collective-permute-start | bytes 584 | tf_op jit(solution)/shard_map/ppermute | solution.py:27
  157.0 13.9 %collective-permute-start.28 = (bf16[2,48,2560]{2,1,0:T(8,128)(2,1)S(1)}, bf16[2,48,2560]{2,1,0:T(8,128)(2,1)S(1)}, u32[]{:S(2)}, u32[]{:S(2)}) collective-permute-start(bf16[2,48,2560]{2,1,0:T(8,128)(2,1)S(1)} %get-tuple-element.66), channel_id=1, source_target_pairs={{0,2},{2,0},{4,6},{6,4},{1,3},{3,1},{5,7},{7,5},{8,10},{10,8},{12,... | collective-permute-start | bytes 1474568 | tf_op jit(solution)/shard_map/ppermute | solution.py:27
  157.5 13.8 %collective-permute-start.29 = (bf16[2,48,2560]{2,1,0:T(8,128)(2,1)S(1)}, bf16[2,48,2560]{2,1,0:T(8,128)(2,1)S(1)}, u32[]{:S(2)}, u32[]{:S(2)}) collective-permute-start(bf16[2,48,2560]{2,1,0:T(8,128)(2,1)S(1)} %get-tuple-element.66), channel_id=1, source_target_pairs={{0,4},{2,6},{4,0},{6,2},{1,5},{3,7},{5,1},{7,3},{8,12},{10,14},{12... | collective-permute-start | bytes 1474568 | tf_op jit(solution)/shard_map/ppermute | solution.py:27
  189.8 41.0 %reduce-scatter.5.cloned.1.call-start = ((), (), s32[]{:S(2)}) async-start(), calls=%async_computation.3 | async-start | bytes 1474560 | tf_op jit(solution)/shard_map/reduce_scatter | solution.py:269
  211.6 12.8 %collective-permute-start.41 = (bf16[50,2560]{1,0:T(8,128)(2,1)S(1)}, bf16[50,2560]{1,0:T(8,128)(2,1)S(1)}, u32[]{:S(2)}, u32[]{:S(2)}) collective-permute-start(bf16[50,2560]{1,0:T(8,128)(2,1)S(1)} %pad_maximum_fusion.18), channel_id=1, source_target_pairs={{0,8},{8,0},{1,9},{9,1},{2,10},{10,2},{3,11},{11,3},{4,12},{12,4},... | collective-permute-start | bytes 768008 | tf_op jit(solution)/shard_map/ppermute | solution.py:21
  (72 other events, 477.1 us)
Sparse Core Ops, SparseCore 0:
  189.9 11.3 reduce-scatter.2
  218.9 5.7 reduce-scatter.4

commit v17 on v14

--- a/solution.py
+++ b/solution.py
@@ -130,21 +130,17 @@
     slot_count = groups * capacity
     low_half = lax.axis_index("dp") == 0
 
-    def whole_rows(stored):
-        if lax.axis_size("dp") != 2:
-            return lax.all_gather(stored, "dp", axis=1, tiled=True)
+    stored = jnp.stack([gate_weight[0], up_weight[0], down_weight[0]])
+    if lax.axis_size("dp") == 2:
         partner = flipped(stored, "dp", 1)
-        return jnp.where(
+        whole = jnp.where(
             low_half,
-            jnp.concatenate([stored, partner], axis=1),
-            jnp.concatenate([partner, stored], axis=1),
-        )
-
-    gate_full, up_full, down_full = (
-        whole_rows(gate_weight[0]),
-        whole_rows(up_weight[0]),
-        whole_rows(down_weight[0]),
-    )
+            jnp.concatenate([stored, partner], axis=2),
+            jnp.concatenate([partner, stored], axis=2),
+        )
+    else:
+        whole = lax.all_gather(stored, "dp", axis=2, tiled=True)
+    gate_full, up_full, down_full = whole[0], whole[1], whole[2]
     hidden_count = gate_full.shape[0]
     paired_weights = jnp.concatenate([gate_full, up_full], axis=0)
     gain_row = norm_gain[0][None, :]

time: 235 us -> 258 us (1.098)
  waiting for transfers between devices: 103 us -> 135 us
  starting transfers between devices: 60.1 us -> 45.6 us
  other arithmetic: 21 us -> 24.6 us
    ppermute x8, waiting for transfers between devices: 25.3 us -> 42.7 us  [rotated(): return lax.ppermute(block, axis, route)]
    ppermute x39 -> x37, waiting for transfers between devices: 77.8 us -> 92.6 us  [flipped(): return lax.ppermute(block, axis, route)]
    ppermute x39 -> x37, starting transfers between devices: 42.4 us -> 32.8 us  [flipped(): return lax.ppermute(block, axis, route)]
    ppermute x8, starting transfers between devices: 16.2 us -> 11.3 us  [rotated(): return lax.ppermute(block, axis, route)]
    another operation x12, other arithmetic: 4.37 us -> 8.16 us  [gather_quad(): return jnp.stack([staged, first, second, diagonal])]
  transfers between devices with their start and end apart: 50 -> 48, of which waited for: 27 -> 30; matrix products, arithmetic and copies ran while one was open for 13% -> 13% of each run, Pallas kernels for 0% -> 0%
where the time goes in v17:
time: 258 us
  waiting for transfers between devices  135 us (52%)
  starting transfers between devices  45.6 us (18%)
  other arithmetic  24.6 us (10%)
  local copies, waits for them, and re-layouts  21.8 us (8%)
  matrix products  15.4 us (6%)
  between operations  15 us (6%)
    ppermute x37, waiting for transfers between devices, flipped(): return lax.ppermute(block, axis, route)  92.6 us
    ppermute x8, waiting for transfers between devices, rotated(): return lax.ppermute(block, axis, route)  42.7 us
    ppermute x37, starting transfers between devices, flipped(): return lax.ppermute(block, axis, route)  32.8 us
    ppermute x8, starting transfers between devices, rotated(): return lax.ppermute(block, axis, route)  11.3 us
    another operation x12, other arithmetic, gather_quad(): return jnp.stack([staged, first, second, diagonal])  8.16 us
    dot_general x6, matrix products, contract_last(): lax.dot_general(first_operand, second_operand, (((1,), (1,)), ((), ())),...  6.41 us
  transfers between devices with their start and end apart: 48, of which 30 were waited for; matrix products, arithmetic and copies ran while one was open for 13% of the time, Pallas kernels for 0%

profile of v17, /device:TPU:0, one launch (start us, length us, event | category | flops | bytes accessed | tf_op | source)
XLA Modules:
  0.0 257.7 jit_solution(2122547367439874159)
XLA Ops:
  11.3 4.0 %collective-permute-start = (bf16[48]{0:T(256)(128)(2,1)S(1)}, bf16[48]{0:T(256)(128)(2,1)S(1)}, u32[]{:S(2)}, u32[]{:S(2)}) collective-permute-start(bf16[48]{0:T(256)(128)(2,1)S(1)} %get-tuple-element.101), channel_id=1, source_target_pairs={{0,8},{8,0},{1,9},{9,1},{2,10},{10,2},{3,11},{11,3},{4,12},{12,4},... | collective-permute-start | bytes 296 | tf_op jit(solution)/shard_map/ppermute | solution.py:21
  19.5 3.0 %collective-permute-start.10 = (bf16[48,2560]{1,0:T(8,128)(2,1)S(1)}, bf16[48,2560]{1,0:T(8,128)(2,1)S(1)}, u32[]{:S(2)}, u32[]{:S(2)}) collective-permute-start(bf16[48,2560]{1,0:T(8,128)(2,1)S(1)} %get-tuple-element.71), channel_id=1, source_target_pairs={{0,8},{8,0},{1,9},{9,1},{2,10},{10,2},{3,11},{11,3},{4,12},{12,4},... | collective-permute-start | bytes 737288 | tf_op jit(solution)/shard_map/ppermute | solution.py:21
  22.5 16.0 %collective-permute-done.4 = bf16[48,2560]{1,0:T(8,128)(2,1)S(1)} collective-permute-done((bf16[48,2560]{1,0:T(8,128)(2,1)}, bf16[48,2560]{1,0:T(8,128)(2,1)S(1)}, u32[]{:S(2)}, u32[]{:S(2)}) %collective-permute-start.4) | collective-permute-done | bytes 245792 | tf_op jit(solution)/shard_map/ppermute | solution.py:21
  47.2 5.7 %collective-permute-done.5 = bf16[2,48,2560]{2,1,0:T(8,128)(2,1)S(1)} collective-permute-done((bf16[2,48,2560]{2,1,0:T(8,128)(2,1)S(1)}, bf16[2,48,2560]{2,1,0:T(8,128)(2,1)S(1)}, u32[]{:S(2)}, u32[]{:S(2)}) %collective-permute-start.5) | collective-permute-done | bytes 491552 | tf_op jit(solution)/shard_map/ppermute | solution.py:27
  55.6 9.4 %collective-permute-done.2 = bf16[2,48]{1,0:T(2,128)(2,1)S(1)} collective-permute-done((bf16[2,48]{1,0:T(2,128)(2,1)S(1)}, bf16[2,48]{1,0:T(2,128)(2,1)S(1)}, u32[]{:S(2)}, u32[]{:S(2)}) %collective-permute-start.2) | collective-permute-done | bytes 224 | tf_op jit(solution)/shard_map/ppermute | solution.py:27
  65.4 3.1 %collective-permute-done.1 = bf16[2,48]{1,0:T(2,128)(2,1)S(1)} collective-permute-done((bf16[2,48]{1,0:T(2,128)(2,1)S(1)}, bf16[2,48]{1,0:T(2,128)(2,1)S(1)}, u32[]{:S(2)}, u32[]{:S(2)}) %collective-permute-start.1) | collective-permute-done | bytes 224 | tf_op jit(solution)/shard_map/ppermute | solution.py:27
  68.5 4.4 %collective-permute-done.3 = bf16[2,48]{1,0:T(2,128)(2,1)S(1)} collective-permute-done((bf16[2,48]{1,0:T(2,128)(2,1)S(1)}, bf16[2,48]{1,0:T(2,128)(2,1)S(1)}, u32[]{:S(2)}, u32[]{:S(2)}) %collective-permute-start.3) | collective-permute-done | bytes 224 | tf_op jit(solution)/shard_map/ppermute | solution.py:27
  76.9 5.7 %collective-permute-done.13 = bf16[2,48,1280]{2,1,0:T(8,128)(2,1)S(1)} collective-permute-done((bf16[2,48,1280]{2,1,0:T(8,128)(2,1)S(1)}, bf16[2,48,1280]{2,1,0:T(8,128)(2,1)S(1)}, u32[]{:S(2)}, u32[]{:S(2)}) %collective-permute-start.13) | collective-permute-done | bytes 245792 | tf_op jit(solution)/shard_map/ppermute | solution.py:27
  86.1 2.9 %maximum_select_fusion = bf16[3,192,2560]{2,1,0:T(8,128)(2,1)S(1)} fusion(bf16[3,192,1280]{2,1,0:T(8,128)(2,1)} %collective-permute-done.9, bf16[3,192,1280]{2,1,0:T(8,128)(2,1)S(1)} %constant_dynamic-update-slice_fusion, pred[]{:T(512)S(6)} %eq.120), kind=kLoop, calls=%fused_computation.20 | loop fusion | flops 13271040 | bytes 5898241 | tf_op jit(solution)/shard_map/jit(_where)/select_n | solution.py:136
  104.0 5.4 %collective-permute-done.15 = bf16[2,48,1280]{2,1,0:T(8,128)(2,1)S(1)} collective-permute-done((bf16[2,48,1280]{2,1,0:T(8,128)(2,1)}, bf16[2,48,1280]{2,1,0:T(8,128)(2,1)S(1)}, u32[]{:S(2)}, u32[]{:S(2)}) %collective-permute-start.15) | collective-permute-done | bytes 245792 | tf_op jit(solution)/shard_map/ppermute | solution.py:27
  109.7 7.4 %collective-permute-done.18 = bf16[2,48,2560]{2,1,0:T(8,128)(2,1)S(1)} collective-permute-done((bf16[2,48,2560]{2,1,0:T(8,128)(2,1)S(1)}, bf16[2,48,2560]{2,1,0:T(8,128)(2,1)S(1)}, u32[]{:S(2)}, u32[]{:S(2)}) %collective-permute-start.18) | collective-permute-done | bytes 491552 | tf_op jit(solution)/shard_map/ppermute | solution.py:27
  119.7 11.0 %collective-permute-done.22 = bf16[50,2560]{1,0:T(8,128)(2,1)S(1)} collective-permute-done((bf16[50,2560]{1,0:T(8,128)(2,1)S(1)}, bf16[50,2560]{1,0:T(8,128)(2,1)S(1)}, u32[]{:S(2)}, u32[]{:S(2)}) %collective-permute-start.22) | collective-permute-done | bytes 256032 | tf_op jit(solution)/shard_map/ppermute | solution.py:21
  136.4 3.0 %collective-permute-start.33 = (bf16[48,2560]{1,0:T(8,128)(2,1)S(1)}, bf16[48,2560]{1,0:T(8,128)(2,1)S(1)}, u32[]{:S(2)}, u32[]{:S(2)}) collective-permute-start(bf16[48,2560]{1,0:T(8,128)(2,1)S(1)} %get-tuple-element.61), channel_id=1, source_target_pairs={{0,8},{8,0},{1,9},{9,1},{2,10},{10,2},{3,11},{11,3},{4,12},{12,4},... | collective-permute-start | bytes 737288 | tf_op jit(solution)/shard_map/ppermute | solution.py:21
  141.2 3.4 %collective-permute-done.24 = bf16[48]{0:T(256)(128)(2,1)S(1)} collective-permute-done((bf16[48]{0:T(256)(128)(2,1)S(1)}, bf16[48]{0:T(256)(128)(2,1)S(1)}, u32[]{:S(2)}, u32[]{:S(2)}) %collective-permute-start.24) | collective-permute-done | bytes 128 | tf_op jit(solution)/shard_map/ppermute | solution.py:21
  144.7 4.1 %collective-permute-done.33 = bf16[48,2560]{1,0:T(8,128)(2,1)S(1)} collective-permute-done((bf16[48,2560]{1,0:T(8,128)(2,1)S(1)}, bf16[48,2560]{1,0:T(8,128)(2,1)S(1)}, u32[]{:S(2)}, u32[]{:S(2)}) %collective-permute-start.33) | collective-permute-done | bytes 245792 | tf_op jit(solution)/shard_map/ppermute | solution.py:21
  156.6 6.6 %collective-permute-done.25 = bf16[2,48]{1,0:T(2,128)(2,1)S(1)} collective-permute-done((bf16[2,48]{1,0:T(2,128)(2,1)S(1)}, bf16[2,48]{1,0:T(2,128)(2,1)S(1)}, u32[]{:S(2)}, u32[]{:S(2)}) %collective-permute-start.25) | collective-permute-done | bytes 224 | tf_op jit(solution)/shard_map/ppermute | solution.py:27
  163.3 6.3 %collective-permute-done.27 = bf16[2,48]{1,0:T(2,128)(2,1)S(1)} collective-permute-done((bf16[2,48]{1,0:T(2,128)(2,1)S(1)}, bf16[2,48]{1,0:T(2,128)(2,1)S(1)}, u32[]{:S(2)}, u32[]{:S(2)}) %collective-permute-start.27) | collective-permute-done | bytes 224 | tf_op jit(solution)/shard_map/ppermute | solution.py:27
  177.9 3.0 %collective-permute-done.37 = bf16[2,48,1280]{2,1,0:T(8,128)(2,1)S(1)} collective-permute-done((bf16[2,48,1280]{2,1,0:T(8,128)(2,1)S(1)}, bf16[2,48,1280]{2,1,0:T(8,128)(2,1)S(1)}, u32[]{:S(2)}, u32[]{:S(2)}) %collective-permute-start.37) | collective-permute-done | bytes 245792 | tf_op jit(solution)/shard_map/ppermute | solution.py:27
  182.6 6.8 %collective-permute-done.29 = bf16[2,48,2560]{2,1,0:T(8,128)(2,1)S(1)} collective-permute-done((bf16[2,48,2560]{2,1,0:T(8,128)(2,1)S(1)}, bf16[2,48,2560]{2,1,0:T(8,128)(2,1)S(1)}, u32[]{:S(2)}, u32[]{:S(2)}) %collective-permute-start.29) | collective-permute-done | bytes 491552 | tf_op jit(solution)/shard_map/ppermute | solution.py:27
  200.0 3.0 %convolution_convert_fusion = bf16[384,2560]{1,0:T(8,128)(2,1)} fusion(bf16[384,2560]{1,0:T(8,128)(2,1)S(1)} %bitcast.229, bf16[384,2560]{1,0:T(8,128)(2,1)S(1)} %bitcast.223, bf16[384,192]{0,1:T(8,128)(2,1)S(1)} %get-tuple-element.55, bf16[384,192]{0,1:T(8,128)(2,1)S(1)} %get-tuple-element.48, bf16[384,192]{0,1:T(8,128)(2,1)S(1)} %copy-done.29, ...), kind=kOutput, calls=%fused_computation.4 | convolution fusion | flops 1521156096 | bytes 6488064 | tf_op jit(solution)/shard_map/dot_general | solution.py:42
  215.9 5.4 %collective-permute-done.38 = bf16[2,48,1280]{2,1,0:T(8,128)(2,1)S(1)} collective-permute-done((bf16[2,48,1280]{2,1,0:T(8,128)(2,1)}, bf16[2,48,1280]{2,1,0:T(8,128)(2,1)S(1)}, u32[]{:S(2)}, u32[]{:S(2)}) %collective-permute-start.38) | collective-permute-done | bytes 245792 | tf_op jit(solution)/shard_map/ppermute | solution.py:27
  221.7 4.8 %collective-permute-done.41 = bf16[2,48,2560]{2,1,0:T(8,128)(2,1)S(1)} collective-permute-done((bf16[2,48,2560]{2,1,0:T(8,128)(2,1)S(1)}, bf16[2,48,2560]{2,1,0:T(8,128)(2,1)S(1)}, u32[]{:S(2)}, u32[]{:S(2)}) %collective-permute-start.41) | collective-permute-done | bytes 491552 | tf_op jit(solution)/shard_map/ppermute | solution.py:27
  226.5 6.8 %collective-permute-done.39 = bf16[2,48,2560]{2,1,0:T(8,128)(2,1)S(1)} collective-permute-done((bf16[2,48,2560]{2,1,0:T(8,128)(2,1)S(1)}, bf16[2,48,2560]{2,1,0:T(8,128)(2,1)S(1)}, u32[]{:S(2)}, u32[]{:S(2)}) %collective-permute-start.39) | collective-permute-done | bytes 491552 | tf_op jit(solution)/shard_map/ppermute | solution.py:27
  237.9 5.7 %collective-permute-done.45 = bf16[50,2560]{1,0:T(8,128)(2,1)} collective-permute-done((bf16[50,2560]{1,0:T(8,128)(2,1)S(1)}, bf16[50,2560]{1,0:T(8,128)(2,1)}, u32[]{:S(2)}, u32[]{:S(2)}) %collective-permute-start.45) | collective-permute-done | bytes 256032 | tf_op jit(solution)/shard_map/ppermute | solution.py:21
  (297 shorter events, 105.9 us)
Async XLA Ops:
  7.2 241.5 %reduce-scatter.3.cloned.1.call-start = ((), (), s32[]{:S(2)}) async-start(), calls=%async_computation.2 | async-start | bytes 2949120 | tf_op jit(solution)/shard_map/reduce_scatter | solution.py:254
  11.3 33.8 %collective-permute-start = (bf16[48]{0:T(256)(128)(2,1)S(1)}, bf16[48]{0:T(256)(128)(2,1)S(1)}, u32[]{:S(2)}, u32[]{:S(2)}) collective-permute-start(bf16[48]{0:T(256)(128)(2,1)S(1)} %get-tuple-element.101), channel_id=1, source_target_pairs={{0,8},{8,0},{1,9},{9,1},{2,10},{10,2},{3,11},{11,3},{4,12},{12,4},... | collective-permute-start | bytes 296 | tf_op jit(solution)/shard_map/ppermute | solution.py:21
  18.3 20.2 %collective-permute-start.4 = (bf16[48,2560]{1,0:T(8,128)(2,1)}, bf16[48,2560]{1,0:T(8,128)(2,1)S(1)}, u32[]{:S(2)}, u32[]{:S(2)}) collective-permute-start(bf16[48,2560]{1,0:T(8,128)(2,1)} %get-tuple-element.75), channel_id=1, source_target_pairs={{0,8},{8,0},{1,9},{9,1},{2,10},{10,2},{3,11},{11,3},{4,12},{12,4},... | collective-permute-start | bytes 737288 | tf_op jit(solution)/shard_map/ppermute | solution.py:21
  19.5 23.2 %collective-permute-start.10 = (bf16[48,2560]{1,0:T(8,128)(2,1)S(1)}, bf16[48,2560]{1,0:T(8,128)(2,1)S(1)}, u32[]{:S(2)}, u32[]{:S(2)}) collective-permute-start(bf16[48,2560]{1,0:T(8,128)(2,1)S(1)} %get-tuple-element.71), channel_id=1, source_target_pairs={{0,8},{8,0},{1,9},{9,1},{2,10},{10,2},{3,11},{11,3},{4,12},{12,4},... | collective-permute-start | bytes 737288 | tf_op jit(solution)/shard_map/ppermute | solution.py:21
  38.6 14.2 %collective-permute-start.5 = (bf16[2,48,2560]{2,1,0:T(8,128)(2,1)S(1)}, bf16[2,48,2560]{2,1,0:T(8,128)(2,1)S(1)}, u32[]{:S(2)}, u32[]{:S(2)}) collective-permute-start(bf16[2,48,2560]{2,1,0:T(8,128)(2,1)S(1)} %get-tuple-element.73), channel_id=1, source_target_pairs={{0,2},{2,0},{4,6},{6,4},{1,3},{3,1},{5,7},{7,5},{8,10},{10,8},{12,... | collective-permute-start | bytes 1474568 | tf_op jit(solution)/shard_map/ppermute | solution.py:27
  40.1 14.2 %collective-permute-start.6 = (bf16[2,48,2560]{2,1,0:T(8,128)(2,1)S(1)}, bf16[2,48,2560]{2,1,0:T(8,128)(2,1)S(1)}, u32[]{:S(2)}, u32[]{:S(2)}) collective-permute-start(bf16[2,48,2560]{2,1,0:T(8,128)(2,1)S(1)} %get-tuple-element.73), channel_id=1, source_target_pairs={{0,4},{2,6},{4,0},{6,2},{1,5},{3,7},{5,1},{7,3},{8,12},{10,14},{12... | collective-permute-start | bytes 1474568 | tf_op jit(solution)/shard_map/ppermute | solution.py:27
  43.6 29.5 %collective-permute-start.11 = (bf16[2,48,2560]{2,1,0:T(8,128)(2,1)}, bf16[2,48,2560]{2,1,0:T(8,128)(2,1)}, u32[]{:S(2)}, u32[]{:S(2)}) collective-permute-start(bf16[2,48,2560]{2,1,0:T(8,128)(2,1)} %get-tuple-element.69), channel_id=1, source_target_pairs={{0,2},{2,0},{4,6},{6,4},{1,3},{3,1},{5,7},{7,5},{8,10},{10,8},{12,... | collective-permute-start | bytes 1474568 | tf_op jit(solution)/shard_map/ppermute | solution.py:27
  45.1 29.1 %collective-permute-start.12 = (bf16[2,48,2560]{2,1,0:T(8,128)(2,1)}, bf16[2,48,2560]{2,1,0:T(8,128)(2,1)}, u32[]{:S(2)}, u32[]{:S(2)}) collective-permute-start(bf16[2,48,2560]{2,1,0:T(8,128)(2,1)} %get-tuple-element.69), channel_id=1, source_target_pairs={{0,4},{2,6},{4,0},{6,2},{1,5},{3,7},{5,1},{7,3},{8,12},{10,14},{12... | collective-permute-start | bytes 1474568 | tf_op jit(solution)/shard_map/ppermute | solution.py:27
  45.1 19.9 %collective-permute-start.2 = (bf16[2,48]{1,0:T(2,128)(2,1)S(1)}, bf16[2,48]{1,0:T(2,128)(2,1)S(1)}, u32[]{:S(2)}, u32[]{:S(2)}) collective-permute-start(bf16[2,48]{1,0:T(2,128)(2,1)S(1)} %pad_maximum_fusion.21), channel_id=1, source_target_pairs={{0,4},{2,6},{4,0},{6,2},{1,5},{3,7},{5,1},{7,3},{8,12},{10,14},{12... | collective-permute-start | bytes 584 | tf_op jit(solution)/shard_map/ppermute | solution.py:27
  52.8 22.9 %collective-permute-start.7 = (bf16[2,48,1280]{2,1,0:T(8,128)(2,1)S(1)}, bf16[2,48,1280]{2,1,0:T(8,128)(2,1)}, u32[]{:S(2)}, u32[]{:S(2)}) collective-permute-start(bf16[2,48,1280]{2,1,0:T(8,128)(2,1)S(1)} %slice.405), channel_id=1, source_target_pairs={{0,4},{2,6},{4,0},{6,2},{1,5},{3,7},{5,1},{7,3},{8,12},{10,14},{12... | collective-permute-start | bytes 737288 | tf_op jit(solution)/shard_map/ppermute | solution.py:27
  55.1 20.7 %collective-permute-start.8 = (bf16[2,48,1280]{2,1,0:T(8,128)(2,1)}, bf16[2,48,1280]{2,1,0:T(8,128)(2,1)}, u32[]{:S(2)}, u32[]{:S(2)}) collective-permute-start(bf16[2,48,1280]{2,1,0:T(8,128)(2,1)} %slice.406), channel_id=1, source_target_pairs={{0,2},{2,0},{4,6},{6,4},{1,3},{3,1},{5,7},{7,5},{8,10},{10,8},{12,... | collective-permute-start | bytes 737288 | tf_op jit(solution)/shard_map/ppermute | solution.py:27
  72.9 13.1 %collective-permute-start.9 = (bf16[3,192,1280]{2,1,0:T(8,128)(2,1)S(1)}, bf16[3,192,1280]{2,1,0:T(8,128)(2,1)}, u32[]{:S(2)}, u32[]{:S(2)}) collective-permute-start(bf16[3,192,1280]{2,1,0:T(8,128)(2,1)S(1)} %constant_dynamic-update-slice_fusion), channel_id=1, source_target_pairs={{0,1},{1,0},{2,3},{3,2},{4,5},{5,4},{6,7},{7,6},{8,9},{9,8},{10,11... | collective-permute-start | bytes 4423688 | tf_op jit(solution)/shard_map/ppermute | solution.py:27
  102.6 14.6 %collective-permute-start.18 = (bf16[2,48,2560]{2,1,0:T(8,128)(2,1)S(1)}, bf16[2,48,2560]{2,1,0:T(8,128)(2,1)S(1)}, u32[]{:S(2)}, u32[]{:S(2)}) collective-permute-start(bf16[2,48,2560]{2,1,0:T(8,128)(2,1)S(1)} %pad_maximum_fusion.12), channel_id=1, source_target_pairs={{0,2},{2,0},{4,6},{6,4},{1,3},{3,1},{5,7},{7,5},{8,10},{10,8},{12,... | collective-permute-start | bytes 1474568 | tf_op jit(solution)/shard_map/ppermute | solution.py:27
  118.6 12.0 %collective-permute-start.22 = (bf16[50,2560]{1,0:T(8,128)(2,1)S(1)}, bf16[50,2560]{1,0:T(8,128)(2,1)S(1)}, u32[]{:S(2)}, u32[]{:S(2)}) collective-permute-start(bf16[50,2560]{1,0:T(8,128)(2,1)S(1)} %pad_maximum_fusion.17), channel_id=1, source_target_pairs={{0,8},{8,0},{1,9},{9,1},{2,10},{10,2},{3,11},{11,3},{4,12},{12,4},... | collective-permute-start | bytes 768008 | tf_op jit(solution)/shard_map/ppermute | solution.py:21
  136.4 12.4 %collective-permute-start.33 = (bf16[48,2560]{1,0:T(8,128)(2,1)S(1)}, bf16[48,2560]{1,0:T(8,128)(2,1)S(1)}, u32[]{:S(2)}, u32[]{:S(2)}) collective-permute-start(bf16[48,2560]{1,0:T(8,128)(2,1)S(1)} %get-tuple-element.61), channel_id=1, source_target_pairs={{0,8},{8,0},{1,9},{9,1},{2,10},{10,2},{3,11},{11,3},{4,12},{12,4},... | collective-permute-start | bytes 737288 | tf_op jit(solution)/shard_map/ppermute | solution.py:21
  139.8 12.1 %collective-permute-start.23 = (bf16[64,2560]{1,0:T(8,128)(2,1)S(1)}, bf16[64,2560]{1,0:T(8,128)(2,1)S(1)}, u32[]{:S(2)}, u32[]{:S(2)}) collective-permute-start(bf16[64,2560]{1,0:T(8,128)(2,1)S(1)} %fusion.34), channel_id=1, source_target_pairs={{16,0},{17,1},{18,2},{19,3},{20,4},{21,5},{22,6},{23,7},{24,8},{25... | collective-permute-start | bytes 983048 | tf_op jit(solution)/shard_map/ppermute | solution.py:15
  149.7 20.0 %collective-permute-start.34 = (bf16[2,48,2560]{2,1,0:T(8,128)(2,1)}, bf16[2,48,2560]{2,1,0:T(8,128)(2,1)}, u32[]{:S(2)}, u32[]{:S(2)}) collective-permute-start(bf16[2,48,2560]{2,1,0:T(8,128)(2,1)} %get-tuple-element.59), channel_id=1, source_target_pairs={{0,2},{2,0},{4,6},{6,4},{1,3},{3,1},{5,7},{7,5},{8,10},{10,8},{12,... | collective-permute-start | bytes 1474568 | tf_op jit(solution)/shard_map/ppermute | solution.py:27
  151.9 19.2 %collective-permute-start.35 = (bf16[2,48,2560]{2,1,0:T(8,128)(2,1)}, bf16[2,48,2560]{2,1,0:T(8,128)(2,1)}, u32[]{:S(2)}, u32[]{:S(2)}) collective-permute-start(bf16[2,48,2560]{2,1,0:T(8,128)(2,1)} %get-tuple-element.59), channel_id=1, source_target_pairs={{0,4},{2,6},{4,0},{6,2},{1,5},{3,7},{5,1},{7,3},{8,12},{10,14},{12... | collective-permute-start | bytes 1474568 | tf_op jit(solution)/shard_map/ppermute | solution.py:27
  153.0 20.8 %collective-permute-start.28 = (bf16[48,2560]{1,0:T(8,128)(2,1)}, bf16[48,2560]{1,0:T(8,128)(2,1)}, u32[]{:S(2)}, u32[]{:S(2)}) collective-permute-start(bf16[48,2560]{1,0:T(8,128)(2,1)} %get-tuple-element.65), channel_id=1, source_target_pairs={{0,8},{8,0},{1,9},{9,1},{2,10},{10,2},{3,11},{11,3},{4,12},{12,4},... | collective-permute-start | bytes 737288 | tf_op jit(solution)/shard_map/ppermute | solution.py:21
  154.7 14.9 %collective-permute-start.27 = (bf16[2,48]{1,0:T(2,128)(2,1)S(1)}, bf16[2,48]{1,0:T(2,128)(2,1)S(1)}, u32[]{:S(2)}, u32[]{:S(2)}) collective-permute-start(bf16[2,48]{1,0:T(2,128)(2,1)S(1)} %pad_maximum_fusion.22), channel_id=1, source_target_pairs={{0,6},{2,4},{4,2},{6,0},{1,7},{3,5},{5,3},{7,1},{8,14},{10,12},{12... | collective-permute-start | bytes 584 | tf_op jit(solution)/shard_map/ppermute | solution.py:27
  174.8 14.6 %collective-permute-start.29 = (bf16[2,48,2560]{2,1,0:T(8,128)(2,1)S(1)}, bf16[2,48,2560]{2,1,0:T(8,128)(2,1)S(1)}, u32[]{:S(2)}, u32[]{:S(2)}) collective-permute-start(bf16[2,48,2560]{2,1,0:T(8,128)(2,1)S(1)} %get-tuple-element.63), channel_id=1, source_target_pairs={{0,2},{2,0},{4,6},{6,4},{1,3},{3,1},{5,7},{7,5},{8,10},{10,8},{12,... | collective-permute-start | bytes 1474568 | tf_op jit(solution)/shard_map/ppermute | solution.py:27
  175.2 15.3 %collective-permute-start.30 = (bf16[2,48,2560]{2,1,0:T(8,128)(2,1)S(1)}, bf16[2,48,2560]{2,1,0:T(8,128)(2,1)S(1)}, u32[]{:S(2)}, u32[]{:S(2)}) collective-permute-start(bf16[2,48,2560]{2,1,0:T(8,128)(2,1)S(1)} %get-tuple-element.63), channel_id=1, source_target_pairs={{0,4},{2,6},{4,0},{6,2},{1,5},{3,7},{5,1},{7,3},{8,12},{10,14},{12... | collective-permute-start | bytes 1474568 | tf_op jit(solution)/shard_map/ppermute | solution.py:27
  205.2 45.7 %reduce-scatter.5.cloned.1.call-start = ((), (), s32[]{:S(2)}) async-start(), calls=%async_computation.3 | async-start | bytes 1474560 | tf_op jit(solution)/shard_map/reduce_scatter | solution.py:257
  221.4 12.0 %collective-permute-start.39 = (bf16[2,48,2560]{2,1,0:T(8,128)(2,1)S(1)}, bf16[2,48,2560]{2,1,0:T(8,128)(2,1)S(1)}, u32[]{:S(2)}, u32[]{:S(2)}) collective-permute-start(bf16[2,48,2560]{2,1,0:T(8,128)(2,1)S(1)} %pad_maximum_fusion.15), channel_id=1, source_target_pairs={{0,4},{2,6},{4,0},{6,2},{1,5},{3,7},{5,1},{7,3},{8,12},{10,14},{12... | collective-permute-start | bytes 1474568 | tf_op jit(solution)/shard_map/ppermute | solution.py:27
  (66 other events, 416.0 us)
Sparse Core Ops, SparseCore 0:
  205.3 7.9 reduce-scatter.2
  238.0 7.2 reduce-scatter.4

commit v18 on v14

--- a/solution.py
+++ b/solution.py
@@ -181,9 +181,7 @@
     rows_gathered = [gather_quad(dispatch_rows(prepared[0][4], prepared[0][2]))]
     weights_gathered = [gather_quad(prepared[0][6].reshape(groups, capacity))]
     for current in prepared[1:]:
-        later_rows, later_weights, _ = lax.optimization_barrier(
-            (dispatch_rows(current[4], current[2]), current[6], first_grads)
-        )
+        later_rows, later_weights = dispatch_rows(current[4], current[2]), current[6]
         rows_gathered.append(gather_quad(later_rows))
         weights_gathered.append(gather_quad(later_weights.reshape(groups, capacity)))
     leaving_list = []

time: 235 us -> 234 us (level)
  transfers between devices with their start and end apart: 50 -> 50, of which waited for: 27 -> 28; matrix products, arithmetic and copies ran while one was open for 13% -> 16% of each run, Pallas kernels for 0% -> 0%
where the time goes in v18:
time: 234 us
  waiting for transfers between devices  103 us (44%)
  starting transfers between devices  58.5 us (25%)
  other arithmetic  21.7 us (9%)
  local copies, waits for them, and re-layouts  19.9 us (9%)
  matrix products  15.4 us (7%)
  between operations  15 us (6%)
    ppermute x39, waiting for transfers between devices, flipped(): return lax.ppermute(block, axis, route)  76.9 us
    ppermute x39, starting transfers between devices, flipped(): return lax.ppermute(block, axis, route)  40.4 us
    ppermute x8, waiting for transfers between devices, rotated(): return lax.ppermute(block, axis, route)  26.3 us
    ppermute x8, starting transfers between devices, rotated(): return lax.ppermute(block, axis, route)  16.5 us
    dot_general x6, matrix products, contract_last(): lax.dot_general(first_operand, second_operand, (((1,), (1,)), ((), ())),...  6.48 us
    dot_general x2, matrix products, contract_first(): lax.dot_general(first_operand, second_operand, (((0,), (0,)), ((), ())),...  4.94 us
  transfers between devices with their start and end apart: 50, of which 28 were waited for; matrix products, arithmetic and copies ran while one was open for 16% of the time, Pallas kernels for 0%

profile of v18, /device:TPU:0, one launch (start us, length us, event | category | flops | bytes accessed | tf_op | source)
XLA Modules:
  0.0 233.7 jit_solution(17398138074344217983)
XLA Ops:
  10.9 4.0 %collective-permute-start = (bf16[48]{0:T(256)(128)(2,1)S(1)}, bf16[48]{0:T(256)(128)(2,1)S(1)}, u32[]{:S(2)}, u32[]{:S(2)}) collective-permute-start(bf16[48]{0:T(256)(128)(2,1)S(1)} %get-tuple-element.95), channel_id=1, source_target_pairs={{0,8},{8,0},{1,9},{9,1},{2,10},{10,2},{3,11},{11,3},{4,12},{12,4},... | collective-permute-start | bytes 296 | tf_op jit(solution)/shard_map/ppermute | solution.py:21
  18.5 3.0 %collective-permute-start.10 = (bf16[48,2560]{1,0:T(8,128)(2,1)S(1)}, bf16[48,2560]{1,0:T(8,128)(2,1)S(1)}, u32[]{:S(2)}, u32[]{:S(2)}) collective-permute-start(bf16[48,2560]{1,0:T(8,128)(2,1)S(1)} %get-tuple-element.65), channel_id=1, source_target_pairs={{0,8},{8,0},{1,9},{9,1},{2,10},{10,2},{3,11},{11,3},{4,12},{12,4},... | collective-permute-start | bytes 737288 | tf_op jit(solution)/shard_map/ppermute | solution.py:21
  24.6 3.2 %collective-permute-done.2 = bf16[2,48]{1,0:T(2,128)(2,1)S(1)} collective-permute-done((bf16[2,48]{1,0:T(2,128)(2,1)S(1)}, bf16[2,48]{1,0:T(2,128)(2,1)S(1)}, u32[]{:S(2)}, u32[]{:S(2)}) %collective-permute-start.2) | collective-permute-done | bytes 224 | tf_op jit(solution)/shard_map/ppermute | solution.py:27
  27.9 3.4 %collective-permute-start.3 = (bf16[2,48]{1,0:T(2,128)(2,1)S(1)}, bf16[2,48]{1,0:T(2,128)(2,1)S(1)}, u32[]{:S(2)}, u32[]{:S(2)}) collective-permute-start(bf16[2,48]{1,0:T(2,128)(2,1)S(1)} %pad_maximum_fusion.21), channel_id=1, source_target_pairs={{0,6},{2,4},{4,2},{6,0},{1,7},{3,5},{5,3},{7,1},{8,14},{10,12},{12... | collective-permute-start | bytes 584 | tf_op jit(solution)/shard_map/ppermute | solution.py:27
  33.5 8.0 %collective-permute-done.10 = bf16[48,2560]{1,0:T(8,128)(2,1)S(1)} collective-permute-done((bf16[48,2560]{1,0:T(8,128)(2,1)S(1)}, bf16[48,2560]{1,0:T(8,128)(2,1)S(1)}, u32[]{:S(2)}, u32[]{:S(2)}) %collective-permute-start.10) | collective-permute-done | bytes 245792 | tf_op jit(solution)/shard_map/ppermute | solution.py:21
  47.9 7.8 %collective-permute-done.11 = bf16[2,48,2560]{2,1,0:T(8,128)(2,1)S(1)} collective-permute-done((bf16[2,48,2560]{2,1,0:T(8,128)(2,1)S(1)}, bf16[2,48,2560]{2,1,0:T(8,128)(2,1)S(1)}, u32[]{:S(2)}, u32[]{:S(2)}) %collective-permute-start.11) | collective-permute-done | bytes 491552 | tf_op jit(solution)/shard_map/ppermute | solution.py:27
  59.6 6.6 %collective-permute-done.5 = bf16[2,48,2560]{2,1,0:T(8,128)(2,1)S(1)} collective-permute-done((bf16[2,48,2560]{2,1,0:T(8,128)(2,1)S(1)}, bf16[2,48,2560]{2,1,0:T(8,128)(2,1)S(1)}, u32[]{:S(2)}, u32[]{:S(2)}) %collective-permute-start.5) | collective-permute-done | bytes 491552 | tf_op jit(solution)/shard_map/ppermute | solution.py:27
  68.4 4.6 %collective-permute-done.13 = bf16[2,48,1280]{2,1,0:T(8,128)(2,1)S(1)} collective-permute-done((bf16[2,48,1280]{2,1,0:T(8,128)(2,1)S(1)}, bf16[2,48,1280]{2,1,0:T(8,128)(2,1)S(1)}, u32[]{:S(2)}, u32[]{:S(2)}) %collective-permute-start.13) | collective-permute-done | bytes 245792 | tf_op jit(solution)/shard_map/ppermute | solution.py:27
  73.3 2.6 %collective-permute-done.7 = bf16[2,48,1280]{2,1,0:T(8,128)(2,1)S(1)} collective-permute-done((bf16[2,48,1280]{2,1,0:T(8,128)(2,1)S(1)}, bf16[2,48,1280]{2,1,0:T(8,128)(2,1)S(1)}, u32[]{:S(2)}, u32[]{:S(2)}) %collective-permute-start.7) | collective-permute-done | bytes 245792 | tf_op jit(solution)/shard_map/ppermute | solution.py:27
  91.0 5.3 %collective-permute-done.17 = bf16[2,48,1280]{2,1,0:T(8,128)(2,1)S(1)} collective-permute-done((bf16[2,48,1280]{2,1,0:T(8,128)(2,1)}, bf16[2,48,1280]{2,1,0:T(8,128)(2,1)S(1)}, u32[]{:S(2)}, u32[]{:S(2)}) %collective-permute-start.17) | collective-permute-done | bytes 245792 | tf_op jit(solution)/shard_map/ppermute | solution.py:27
  98.2 4.5 %collective-permute-done.20 = bf16[2,48,2560]{2,1,0:T(8,128)(2,1)S(1)} collective-permute-done((bf16[2,48,2560]{2,1,0:T(8,128)(2,1)S(1)}, bf16[2,48,2560]{2,1,0:T(8,128)(2,1)S(1)}, u32[]{:S(2)}, u32[]{:S(2)}) %collective-permute-start.20) | collective-permute-done | bytes 491552 | tf_op jit(solution)/shard_map/ppermute | solution.py:27
  102.7 4.3 %collective-permute-done.18 = bf16[2,48,2560]{2,1,0:T(8,128)(2,1)S(1)} collective-permute-done((bf16[2,48,2560]{2,1,0:T(8,128)(2,1)S(1)}, bf16[2,48,2560]{2,1,0:T(8,128)(2,1)S(1)}, u32[]{:S(2)}, u32[]{:S(2)}) %collective-permute-start.18) | collective-permute-done | bytes 491552 | tf_op jit(solution)/shard_map/ppermute | solution.py:27
  107.2 3.9 %collective-permute-start.24 = (bf16[50,2560]{1,0:T(8,128)(2,1)S(1)}, bf16[50,2560]{1,0:T(8,128)(2,1)S(1)}, u32[]{:S(2)}, u32[]{:S(2)}) collective-permute-start(bf16[50,2560]{1,0:T(8,128)(2,1)S(1)} %pad_maximum_fusion.17), channel_id=1, source_target_pairs={{0,8},{8,0},{1,9},{9,1},{2,10},{10,2},{3,11},{11,3},{4,12},{12,4},... | collective-permute-start | bytes 768008 | tf_op jit(solution)/shard_map/ppermute | solution.py:21
  111.2 7.5 %collective-permute-done.26 = bf16[48]{0:T(256)(128)(2,1)S(1)} collective-permute-done((bf16[48]{0:T(256)(128)(2,1)S(1)}, bf16[48]{0:T(256)(128)(2,1)S(1)}, u32[]{:S(2)}, u32[]{:S(2)}) %collective-permute-start.26) | collective-permute-done | bytes 128 | tf_op jit(solution)/shard_map/ppermute | solution.py:21
  125.6 2.7 %collective-permute-start.35 = (bf16[48,2560]{1,0:T(8,128)(2,1)S(1)}, bf16[48,2560]{1,0:T(8,128)(2,1)S(1)}, u32[]{:S(2)}, u32[]{:S(2)}) collective-permute-start(bf16[48,2560]{1,0:T(8,128)(2,1)S(1)} %get-tuple-element.55), channel_id=1, source_target_pairs={{0,8},{8,0},{1,9},{9,1},{2,10},{10,2},{3,11},{11,3},{4,12},{12,4},... | collective-permute-start | bytes 737288 | tf_op jit(solution)/shard_map/ppermute | solution.py:21
  130.2 5.0 %collective-permute-done.35 = bf16[48,2560]{1,0:T(8,128)(2,1)S(1)} collective-permute-done((bf16[48,2560]{1,0:T(8,128)(2,1)S(1)}, bf16[48,2560]{1,0:T(8,128)(2,1)S(1)}, u32[]{:S(2)}, u32[]{:S(2)}) %collective-permute-start.35) | collective-permute-done | bytes 245792 | tf_op jit(solution)/shard_map/ppermute | solution.py:21
  145.3 6.4 %collective-permute-done.29 = bf16[2,48]{1,0:T(2,128)(2,1)S(1)} collective-permute-done((bf16[2,48]{1,0:T(2,128)(2,1)}, bf16[2,48]{1,0:T(2,128)(2,1)S(1)}, u32[]{:S(2)}, u32[]{:S(2)}) %collective-permute-start.29) | collective-permute-done | bytes 224 | tf_op jit(solution)/shard_map/ppermute | solution.py:27
  153.3 2.6 %collective-permute-start.38 = (bf16[2,48,1280]{2,1,0:T(8,128)(2,1)S(1)}, bf16[2,48,1280]{2,1,0:T(8,128)(2,1)S(1)}, u32[]{:S(2)}, u32[]{:S(2)}) collective-permute-start(bf16[2,48,1280]{2,1,0:T(8,128)(2,1)S(1)} %slice.423), channel_id=1, source_target_pairs={{0,4},{2,6},{4,0},{6,2},{1,5},{3,7},{5,1},{7,3},{8,12},{10,14},{12... | collective-permute-start | bytes 737288 | tf_op jit(solution)/shard_map/ppermute | solution.py:27
  160.1 2.6 %collective-permute-done.38 = bf16[2,48,1280]{2,1,0:T(8,128)(2,1)S(1)} collective-permute-done((bf16[2,48,1280]{2,1,0:T(8,128)(2,1)S(1)}, bf16[2,48,1280]{2,1,0:T(8,128)(2,1)S(1)}, u32[]{:S(2)}, u32[]{:S(2)}) %collective-permute-start.38) | collective-permute-done | bytes 245792 | tf_op jit(solution)/shard_map/ppermute | solution.py:27
  165.8 3.7 %collective-permute-done.31 = bf16[2,48,2560]{2,1,0:T(8,128)(2,1)S(1)} collective-permute-done((bf16[2,48,2560]{2,1,0:T(8,128)(2,1)S(1)}, bf16[2,48,2560]{2,1,0:T(8,128)(2,1)S(1)}, u32[]{:S(2)}, u32[]{:S(2)}) %collective-permute-start.31) | collective-permute-done | bytes 491552 | tf_op jit(solution)/shard_map/ppermute | solution.py:27
  181.1 3.0 %convolution_convert_fusion = bf16[384,2560]{1,0:T(8,128)(2,1)} fusion(bf16[384,2560]{1,0:T(8,128)(2,1)S(1)} %bitcast.218, bf16[384,2560]{1,0:T(8,128)(2,1)S(1)} %bitcast.212, bf16[384,192]{0,1:T(8,128)(2,1)S(1)} %get-tuple-element.49, bf16[384,192]{0,1:T(8,128)(2,1)S(1)} %get-tuple-element.42, bf16[384,192]{0,1:T(8,128)(2,1)S(1)} %copy-done.22, ...), kind=kOutput, calls=%fused_computation.4 | convolution fusion | flops 1521156096 | bytes 6488064 | tf_op jit(solution)/shard_map/dot_general | solution.py:42
  200.8 4.5 %collective-permute-done.43 = bf16[2,48,2560]{2,1,0:T(8,128)(2,1)S(1)} collective-permute-done((bf16[2,48,2560]{2,1,0:T(8,128)(2,1)S(1)}, bf16[2,48,2560]{2,1,0:T(8,128)(2,1)S(1)}, u32[]{:S(2)}, u32[]{:S(2)}) %collective-permute-start.43) | collective-permute-done | bytes 491552 | tf_op jit(solution)/shard_map/ppermute | solution.py:27
  205.3 3.3 %collective-permute-done.41 = bf16[2,48,2560]{2,1,0:T(8,128)(2,1)S(1)} collective-permute-done((bf16[2,48,2560]{2,1,0:T(8,128)(2,1)S(1)}, bf16[2,48,2560]{2,1,0:T(8,128)(2,1)S(1)}, u32[]{:S(2)}, u32[]{:S(2)}) %collective-permute-start.41) | collective-permute-done | bytes 491552 | tf_op jit(solution)/shard_map/ppermute | solution.py:27
  213.9 5.8 %collective-permute-done.47 = bf16[50,2560]{1,0:T(8,128)(2,1)} collective-permute-done((bf16[50,2560]{1,0:T(8,128)(2,1)S(1)}, bf16[50,2560]{1,0:T(8,128)(2,1)}, u32[]{:S(2)}, u32[]{:S(2)}) %collective-permute-start.47) | collective-permute-done | bytes 256032 | tf_op jit(solution)/shard_map/ppermute | solution.py:21
  (302 shorter events, 110.4 us)
Async XLA Ops:
  7.2 217.5 %reduce-scatter.3.cloned.1.call-start = ((), (), s32[]{:S(2)}) async-start(), calls=%async_computation.2 | async-start | bytes 2949120 | tf_op jit(solution)/shard_map/reduce_scatter | solution.py:256
  10.9 10.6 %collective-permute-start = (bf16[48]{0:T(256)(128)(2,1)S(1)}, bf16[48]{0:T(256)(128)(2,1)S(1)}, u32[]{:S(2)}, u32[]{:S(2)}) collective-permute-start(bf16[48]{0:T(256)(128)(2,1)S(1)} %get-tuple-element.95), channel_id=1, source_target_pairs={{0,8},{8,0},{1,9},{9,1},{2,10},{10,2},{3,11},{11,3},{4,12},{12,4},... | collective-permute-start | bytes 296 | tf_op jit(solution)/shard_map/ppermute | solution.py:21
  17.2 25.8 %collective-permute-start.4 = (bf16[48,2560]{1,0:T(8,128)(2,1)S(1)}, bf16[48,2560]{1,0:T(8,128)(2,1)S(1)}, u32[]{:S(2)}, u32[]{:S(2)}) collective-permute-start(bf16[48,2560]{1,0:T(8,128)(2,1)S(1)} %get-tuple-element.69), channel_id=1, source_target_pairs={{0,8},{8,0},{1,9},{9,1},{2,10},{10,2},{3,11},{11,3},{4,12},{12,4},... | collective-permute-start | bytes 737288 | tf_op jit(solution)/shard_map/ppermute | solution.py:21
  18.5 22.9 %collective-permute-start.10 = (bf16[48,2560]{1,0:T(8,128)(2,1)S(1)}, bf16[48,2560]{1,0:T(8,128)(2,1)S(1)}, u32[]{:S(2)}, u32[]{:S(2)}) collective-permute-start(bf16[48,2560]{1,0:T(8,128)(2,1)S(1)} %get-tuple-element.65), channel_id=1, source_target_pairs={{0,8},{8,0},{1,9},{9,1},{2,10},{10,2},{3,11},{11,3},{4,12},{12,4},... | collective-permute-start | bytes 737288 | tf_op jit(solution)/shard_map/ppermute | solution.py:21
  21.5 22.3 %collective-permute-start.16 = (bf16[192,1280]{1,0:T(8,128)(2,1)S(1)}, bf16[192,1280]{1,0:T(8,128)(2,1)S(1)}, u32[]{:S(2)}, u32[]{:S(2)}) collective-permute-start(bf16[192,1280]{1,0:T(8,128)(2,1)S(1)} %bitcast.235), channel_id=1, source_target_pairs={{0,1},{1,0},{2,3},{3,2},{4,5},{5,4},{6,7},{7,6},{8,9},{9,8},{10,11... | collective-permute-start | bytes 1474568 | tf_op jit(solution)/shard_map/ppermute | solution.py:27
  31.3 26.0 %collective-permute-start.15 = (bf16[192,1280]{1,0:T(8,128)(2,1)}, bf16[192,1280]{1,0:T(8,128)(2,1)}, u32[]{:S(2)}, u32[]{:S(2)}) collective-permute-start(bf16[192,1280]{1,0:T(8,128)(2,1)} %bitcast.28), channel_id=1, source_target_pairs={{0,1},{1,0},{2,3},{3,2},{4,5},{5,4},{6,7},{7,6},{8,9},{9,8},{10,11... | collective-permute-start | bytes 1474568 | tf_op jit(solution)/shard_map/ppermute | solution.py:27
  41.5 14.2 %collective-permute-start.11 = (bf16[2,48,2560]{2,1,0:T(8,128)(2,1)S(1)}, bf16[2,48,2560]{2,1,0:T(8,128)(2,1)S(1)}, u32[]{:S(2)}, u32[]{:S(2)}) collective-permute-start(bf16[2,48,2560]{2,1,0:T(8,128)(2,1)S(1)} %get-tuple-element.63), channel_id=1, source_target_pairs={{0,2},{2,0},{4,6},{6,4},{1,3},{3,1},{5,7},{7,5},{8,10},{10,8},{12,... | collective-permute-start | bytes 1474568 | tf_op jit(solution)/shard_map/ppermute | solution.py:27
  43.1 14.2 %collective-permute-start.12 = (bf16[2,48,2560]{2,1,0:T(8,128)(2,1)S(1)}, bf16[2,48,2560]{2,1,0:T(8,128)(2,1)S(1)}, u32[]{:S(2)}, u32[]{:S(2)}) collective-permute-start(bf16[2,48,2560]{2,1,0:T(8,128)(2,1)S(1)} %get-tuple-element.63), channel_id=1, source_target_pairs={{0,4},{2,6},{4,0},{6,2},{1,5},{3,7},{5,1},{7,3},{8,12},{10,14},{12... | collective-permute-start | bytes 1474568 | tf_op jit(solution)/shard_map/ppermute | solution.py:27
  43.1 23.1 %collective-permute-start.5 = (bf16[2,48,2560]{2,1,0:T(8,128)(2,1)S(1)}, bf16[2,48,2560]{2,1,0:T(8,128)(2,1)S(1)}, u32[]{:S(2)}, u32[]{:S(2)}) collective-permute-start(bf16[2,48,2560]{2,1,0:T(8,128)(2,1)S(1)} %get-tuple-element.67), channel_id=1, source_target_pairs={{0,2},{2,0},{4,6},{6,4},{1,3},{3,1},{5,7},{7,5},{8,10},{10,8},{12,... | collective-permute-start | bytes 1474568 | tf_op jit(solution)/shard_map/ppermute | solution.py:27
  44.5 23.2 %collective-permute-start.6 = (bf16[2,48,2560]{2,1,0:T(8,128)(2,1)S(1)}, bf16[2,48,2560]{2,1,0:T(8,128)(2,1)S(1)}, u32[]{:S(2)}, u32[]{:S(2)}) collective-permute-start(bf16[2,48,2560]{2,1,0:T(8,128)(2,1)S(1)} %get-tuple-element.67), channel_id=1, source_target_pairs={{0,4},{2,6},{4,0},{6,2},{1,5},{3,7},{5,1},{7,3},{8,12},{10,14},{12... | collective-permute-start | bytes 1474568 | tf_op jit(solution)/shard_map/ppermute | solution.py:27
  55.7 21.3 %collective-permute-start.9 = (bf16[192,1280]{1,0:T(8,128)(2,1)S(1)}, bf16[192,1280]{1,0:T(8,128)(2,1)S(1)}, u32[]{:S(2)}, u32[]{:S(2)}) collective-permute-start(bf16[192,1280]{1,0:T(8,128)(2,1)S(1)} %bitcast.248), channel_id=1, source_target_pairs={{0,1},{1,0},{2,3},{3,2},{4,5},{5,4},{6,7},{7,6},{8,9},{9,8},{10,11... | collective-permute-start | bytes 1474568 | tf_op jit(solution)/shard_map/ppermute | solution.py:27
  57.2 15.8 %collective-permute-start.13 = (bf16[2,48,1280]{2,1,0:T(8,128)(2,1)S(1)}, bf16[2,48,1280]{2,1,0:T(8,128)(2,1)S(1)}, u32[]{:S(2)}, u32[]{:S(2)}) collective-permute-start(bf16[2,48,1280]{2,1,0:T(8,128)(2,1)S(1)} %slice.402), channel_id=1, source_target_pairs={{0,4},{2,6},{4,0},{6,2},{1,5},{3,7},{5,1},{7,3},{8,12},{10,14},{12... | collective-permute-start | bytes 737288 | tf_op jit(solution)/shard_map/ppermute | solution.py:27
  57.2 15.8 %collective-permute-start.14 = (bf16[2,48,1280]{2,1,0:T(8,128)(2,1)S(1)}, bf16[2,48,1280]{2,1,0:T(8,128)(2,1)S(1)}, u32[]{:S(2)}, u32[]{:S(2)}) collective-permute-start(bf16[2,48,1280]{2,1,0:T(8,128)(2,1)S(1)} %slice.403), channel_id=1, source_target_pairs={{0,2},{2,0},{4,6},{6,4},{1,3},{3,1},{5,7},{7,5},{8,10},{10,8},{12,... | collective-permute-start | bytes 737288 | tf_op jit(solution)/shard_map/ppermute | solution.py:27
  89.5 13.2 %collective-permute-start.20 = (bf16[2,48,2560]{2,1,0:T(8,128)(2,1)S(1)}, bf16[2,48,2560]{2,1,0:T(8,128)(2,1)S(1)}, u32[]{:S(2)}, u32[]{:S(2)}) collective-permute-start(bf16[2,48,2560]{2,1,0:T(8,128)(2,1)S(1)} %pad_maximum_fusion.12), channel_id=1, source_target_pairs={{0,2},{2,0},{4,6},{6,4},{1,3},{3,1},{5,7},{7,5},{8,10},{10,8},{12,... | collective-permute-start | bytes 1474568 | tf_op jit(solution)/shard_map/ppermute | solution.py:27
  96.4 10.6 %collective-permute-start.18 = (bf16[2,48,2560]{2,1,0:T(8,128)(2,1)S(1)}, bf16[2,48,2560]{2,1,0:T(8,128)(2,1)S(1)}, u32[]{:S(2)}, u32[]{:S(2)}) collective-permute-start(bf16[2,48,2560]{2,1,0:T(8,128)(2,1)S(1)} %pad_maximum_fusion.11), channel_id=1, source_target_pairs={{0,4},{2,6},{4,0},{6,2},{1,5},{3,7},{5,1},{7,3},{8,12},{10,14},{12... | collective-permute-start | bytes 1474568 | tf_op jit(solution)/shard_map/ppermute | solution.py:27
  107.2 12.8 %collective-permute-start.24 = (bf16[50,2560]{1,0:T(8,128)(2,1)S(1)}, bf16[50,2560]{1,0:T(8,128)(2,1)S(1)}, u32[]{:S(2)}, u32[]{:S(2)}) collective-permute-start(bf16[50,2560]{1,0:T(8,128)(2,1)S(1)} %pad_maximum_fusion.17), channel_id=1, source_target_pairs={{0,8},{8,0},{1,9},{9,1},{2,10},{10,2},{3,11},{11,3},{4,12},{12,4},... | collective-permute-start | bytes 768008 | tf_op jit(solution)/shard_map/ppermute | solution.py:21
  119.1 23.0 %collective-permute-start.28 = (bf16[2,48]{1,0:T(2,128)(2,1)}, bf16[2,48]{1,0:T(2,128)(2,1)}, u32[]{:S(2)}, u32[]{:S(2)}) collective-permute-start(bf16[2,48]{1,0:T(2,128)(2,1)} %pad_maximum_fusion.22), channel_id=1, source_target_pairs={{0,4},{2,6},{4,0},{6,2},{1,5},{3,7},{5,1},{7,3},{8,12},{10,14},{12... | collective-permute-start | bytes 584 | tf_op jit(solution)/shard_map/ppermute | solution.py:27
  136.1 16.2 %collective-permute-start.36 = (bf16[2,48,2560]{2,1,0:T(8,128)(2,1)}, bf16[2,48,2560]{2,1,0:T(8,128)(2,1)}, u32[]{:S(2)}, u32[]{:S(2)}) collective-permute-start(bf16[2,48,2560]{2,1,0:T(8,128)(2,1)} %get-tuple-element.53), channel_id=1, source_target_pairs={{0,2},{2,0},{4,6},{6,4},{1,3},{3,1},{5,7},{7,5},{8,10},{10,8},{12,... | collective-permute-start | bytes 1474568 | tf_op jit(solution)/shard_map/ppermute | solution.py:27
  136.1 19.9 %collective-permute-start.37 = (bf16[2,48,2560]{2,1,0:T(8,128)(2,1)}, bf16[2,48,2560]{2,1,0:T(8,128)(2,1)}, u32[]{:S(2)}, u32[]{:S(2)}) collective-permute-start(bf16[2,48,2560]{2,1,0:T(8,128)(2,1)} %get-tuple-element.53), channel_id=1, source_target_pairs={{0,4},{2,6},{4,0},{6,2},{1,5},{3,7},{5,1},{7,3},{8,12},{10,14},{12... | collective-permute-start | bytes 1474568 | tf_op jit(solution)/shard_map/ppermute | solution.py:27
  139.1 19.1 %collective-permute-start.30 = (bf16[48,2560]{1,0:T(8,128)(2,1)}, bf16[48,2560]{1,0:T(8,128)(2,1)}, u32[]{:S(2)}, u32[]{:S(2)}) collective-permute-start(bf16[48,2560]{1,0:T(8,128)(2,1)} %get-tuple-element.59), channel_id=1, source_target_pairs={{0,8},{8,0},{1,9},{9,1},{2,10},{10,2},{3,11},{11,3},{4,12},{12,4},... | collective-permute-start | bytes 737288 | tf_op jit(solution)/shard_map/ppermute | solution.py:21
  159.3 10.3 %collective-permute-start.31 = (bf16[2,48,2560]{2,1,0:T(8,128)(2,1)S(1)}, bf16[2,48,2560]{2,1,0:T(8,128)(2,1)S(1)}, u32[]{:S(2)}, u32[]{:S(2)}) collective-permute-start(bf16[2,48,2560]{2,1,0:T(8,128)(2,1)S(1)} %get-tuple-element.57), channel_id=1, source_target_pairs={{0,2},{2,0},{4,6},{6,4},{1,3},{3,1},{5,7},{7,5},{8,10},{10,8},{12,... | collective-permute-start | bytes 1474568 | tf_op jit(solution)/shard_map/ppermute | solution.py:27
  160.1 11.0 %collective-permute-start.32 = (bf16[2,48,2560]{2,1,0:T(8,128)(2,1)S(1)}, bf16[2,48,2560]{2,1,0:T(8,128)(2,1)S(1)}, u32[]{:S(2)}, u32[]{:S(2)}) collective-permute-start(bf16[2,48,2560]{2,1,0:T(8,128)(2,1)S(1)} %get-tuple-element.57), channel_id=1, source_target_pairs={{0,4},{2,6},{4,0},{6,2},{1,5},{3,7},{5,1},{7,3},{8,12},{10,14},{12... | collective-permute-start | bytes 1474568 | tf_op jit(solution)/shard_map/ppermute | solution.py:27
  186.3 40.6 %reduce-scatter.5.cloned.1.call-start = ((), (), s32[]{:S(2)}) async-start(), calls=%async_computation.3 | async-start | bytes 1474560 | tf_op jit(solution)/shard_map/reduce_scatter | solution.py:259
  208.9 10.8 %collective-permute-start.47 = (bf16[50,2560]{1,0:T(8,128)(2,1)S(1)}, bf16[50,2560]{1,0:T(8,128)(2,1)}, u32[]{:S(2)}, u32[]{:S(2)}) collective-permute-start(bf16[50,2560]{1,0:T(8,128)(2,1)S(1)} %pad_maximum_fusion.18), channel_id=1, source_target_pairs={{0,8},{8,0},{1,9},{9,1},{2,10},{10,2},{3,11},{11,3},{4,12},{12,4},... | collective-permute-start | bytes 768008 | tf_op jit(solution)/shard_map/ppermute | solution.py:21
  (70 other events, 418.1 us)
Sparse Core Ops, SparseCore 0:
  186.4 9.2 reduce-scatter.2
  214.0 8.1 reduce-scatter.4

commit v19 on v14

--- a/solution.py
+++ b/solution.py
@@ -177,8 +177,8 @@
 
     prepared = [prepare(moment) for moment in range(micro_count)]
     first_incoming = jnp.where(is_last, output_grads[0], entry_grads[0])
+    rows_gathered = [gather_quad(dispatch_rows(prepared[0][4], prepared[0][2]))]
     first_grads = gather_quad(dispatch_rows(prepared[0][4], first_incoming))
-    rows_gathered = [gather_quad(dispatch_rows(prepared[0][4], prepared[0][2]))]
     weights_gathered = [gather_quad(prepared[0][6].reshape(groups, capacity))]
     for current in prepared[1:]:
         later_rows, later_weights, _ = lax.optimization_barrier(

time: 235 us -> 235 us (level)
  no operation moved by 1% of the time
where the time goes in v19:
time: 235 us; the launch traced here: 234 us
  waiting for transfers between devices  103 us (44%)
  starting transfers between devices  60.1 us (26%)
  other arithmetic  21 us (9%)
  local copies, waits for them, and re-layouts  19.3 us (8%)
  matrix products  15.4 us (7%)
  between operations  15 us (6%)
    ppermute x39, waiting for transfers between devices, flipped(): return lax.ppermute(block, axis, route)  77.8 us
    ppermute x39, starting transfers between devices, flipped(): return lax.ppermute(block, axis, route)  42.4 us
    ppermute x8, waiting for transfers between devices, rotated(): return lax.ppermute(block, axis, route)  25.3 us
    ppermute x8, starting transfers between devices, rotated(): return lax.ppermute(block, axis, route)  16.2 us
    dot_general x6, matrix products, contract_last(): lax.dot_general(first_operand, second_operand, (((1,), (1,)), ((), ())),...  6.48 us
    dot_general x2, matrix products, contract_first(): lax.dot_general(first_operand, second_operand, (((0,), (0,)), ((), ())),...  4.96 us
  transfers between devices with their start and end apart: 50, of which 27 were waited for; matrix products, arithmetic and copies ran while one was open for 13% of the time, Pallas kernels for 0%

profile of v19, /device:TPU:0, one launch (start us, length us, event | category | flops | bytes accessed | tf_op | source)
XLA Modules:
  0.0 234.0 jit_solution(8838778811842099326)
XLA Ops:
  11.3 4.0 %collective-permute-start = (bf16[48]{0:T(256)(128)(2,1)S(1)}, bf16[48]{0:T(256)(128)(2,1)S(1)}, u32[]{:S(2)}, u32[]{:S(2)}) collective-permute-start(bf16[48]{0:T(256)(128)(2,1)S(1)} %get-tuple-element.99), channel_id=1, source_target_pairs={{0,8},{8,0},{1,9},{9,1},{2,10},{10,2},{3,11},{11,3},{4,12},{12,4},... | collective-permute-start | bytes 296 | tf_op jit(solution)/shard_map/ppermute | solution.py:21
  18.9 3.0 %collective-permute-start.10 = (bf16[48,2560]{1,0:T(8,128)(2,1)S(1)}, bf16[48,2560]{1,0:T(8,128)(2,1)S(1)}, u32[]{:S(2)}, u32[]{:S(2)}) collective-permute-start(bf16[48,2560]{1,0:T(8,128)(2,1)S(1)} %get-tuple-element.69), channel_id=1, source_target_pairs={{0,8},{8,0},{1,9},{9,1},{2,10},{10,2},{3,11},{11,3},{4,12},{12,4},... | collective-permute-start | bytes 737288 | tf_op jit(solution)/shard_map/ppermute | solution.py:21
  25.0 3.2 %collective-permute-done.2 = bf16[2,48]{1,0:T(2,128)(2,1)S(1)} collective-permute-done((bf16[2,48]{1,0:T(2,128)(2,1)S(1)}, bf16[2,48]{1,0:T(2,128)(2,1)S(1)}, u32[]{:S(2)}, u32[]{:S(2)}) %collective-permute-start.2) | collective-permute-done | bytes 224 | tf_op jit(solution)/shard_map/ppermute | solution.py:27
  28.2 3.4 %collective-permute-start.3 = (bf16[2,48]{1,0:T(2,128)(2,1)S(1)}, bf16[2,48]{1,0:T(2,128)(2,1)S(1)}, u32[]{:S(2)}, u32[]{:S(2)}) collective-permute-start(bf16[2,48]{1,0:T(2,128)(2,1)S(1)} %pad_maximum_fusion.21), channel_id=1, source_target_pairs={{0,6},{2,4},{4,2},{6,0},{1,7},{3,5},{5,3},{7,1},{8,14},{10,12},{12... | collective-permute-start | bytes 584 | tf_op jit(solution)/shard_map/ppermute | solution.py:27
  33.2 8.5 %collective-permute-done.10 = bf16[48,2560]{1,0:T(8,128)(2,1)S(1)} collective-permute-done((bf16[48,2560]{1,0:T(8,128)(2,1)S(1)}, bf16[48,2560]{1,0:T(8,128)(2,1)S(1)}, u32[]{:S(2)}, u32[]{:S(2)}) %collective-permute-start.10) | collective-permute-done | bytes 245792 | tf_op jit(solution)/shard_map/ppermute | solution.py:21
  48.3 7.8 %collective-permute-done.11 = bf16[2,48,2560]{2,1,0:T(8,128)(2,1)S(1)} collective-permute-done((bf16[2,48,2560]{2,1,0:T(8,128)(2,1)S(1)}, bf16[2,48,2560]{2,1,0:T(8,128)(2,1)S(1)}, u32[]{:S(2)}, u32[]{:S(2)}) %collective-permute-start.11) | collective-permute-done | bytes 491552 | tf_op jit(solution)/shard_map/ppermute | solution.py:27
  59.9 6.7 %collective-permute-done.5 = bf16[2,48,2560]{2,1,0:T(8,128)(2,1)S(1)} collective-permute-done((bf16[2,48,2560]{2,1,0:T(8,128)(2,1)S(1)}, bf16[2,48,2560]{2,1,0:T(8,128)(2,1)S(1)}, u32[]{:S(2)}, u32[]{:S(2)}) %collective-permute-start.5) | collective-permute-done | bytes 491552 | tf_op jit(solution)/shard_map/ppermute | solution.py:27
  68.7 4.6 %collective-permute-done.13 = bf16[2,48,1280]{2,1,0:T(8,128)(2,1)S(1)} collective-permute-done((bf16[2,48,1280]{2,1,0:T(8,128)(2,1)S(1)}, bf16[2,48,1280]{2,1,0:T(8,128)(2,1)S(1)}, u32[]{:S(2)}, u32[]{:S(2)}) %collective-permute-start.13) | collective-permute-done | bytes 245792 | tf_op jit(solution)/shard_map/ppermute | solution.py:27
  91.3 5.3 %collective-permute-done.17 = bf16[2,48,1280]{2,1,0:T(8,128)(2,1)S(1)} collective-permute-done((bf16[2,48,1280]{2,1,0:T(8,128)(2,1)}, bf16[2,48,1280]{2,1,0:T(8,128)(2,1)S(1)}, u32[]{:S(2)}, u32[]{:S(2)}) %collective-permute-start.17) | collective-permute-done | bytes 245792 | tf_op jit(solution)/shard_map/ppermute | solution.py:27
  98.6 4.5 %collective-permute-done.20 = bf16[2,48,2560]{2,1,0:T(8,128)(2,1)S(1)} collective-permute-done((bf16[2,48,2560]{2,1,0:T(8,128)(2,1)S(1)}, bf16[2,48,2560]{2,1,0:T(8,128)(2,1)S(1)}, u32[]{:S(2)}, u32[]{:S(2)}) %collective-permute-start.20) | collective-permute-done | bytes 491552 | tf_op jit(solution)/shard_map/ppermute | solution.py:27
  103.1 4.3 %collective-permute-done.18 = bf16[2,48,2560]{2,1,0:T(8,128)(2,1)S(1)} collective-permute-done((bf16[2,48,2560]{2,1,0:T(8,128)(2,1)S(1)}, bf16[2,48,2560]{2,1,0:T(8,128)(2,1)S(1)}, u32[]{:S(2)}, u32[]{:S(2)}) %collective-permute-start.18) | collective-permute-done | bytes 491552 | tf_op jit(solution)/shard_map/ppermute | solution.py:27
  107.6 3.8 %collective-permute-start.24 = (bf16[50,2560]{1,0:T(8,128)(2,1)S(1)}, bf16[50,2560]{1,0:T(8,128)(2,1)S(1)}, u32[]{:S(2)}, u32[]{:S(2)}) collective-permute-start(bf16[50,2560]{1,0:T(8,128)(2,1)S(1)} %pad_maximum_fusion.17), channel_id=1, source_target_pairs={{0,8},{8,0},{1,9},{9,1},{2,10},{10,2},{3,11},{11,3},{4,12},{12,4},... | collective-permute-start | bytes 768008 | tf_op jit(solution)/shard_map/ppermute | solution.py:21
  112.4 6.6 %collective-permute-done.24 = bf16[50,2560]{1,0:T(8,128)(2,1)S(1)} collective-permute-done((bf16[50,2560]{1,0:T(8,128)(2,1)S(1)}, bf16[50,2560]{1,0:T(8,128)(2,1)S(1)}, u32[]{:S(2)}, u32[]{:S(2)}) %collective-permute-start.24) | collective-permute-done | bytes 256032 | tf_op jit(solution)/shard_map/ppermute | solution.py:21
  129.7 4.3 %collective-permute-done.35 = bf16[48,2560]{1,0:T(8,128)(2,1)S(1)} collective-permute-done((bf16[48,2560]{1,0:T(8,128)(2,1)S(1)}, bf16[48,2560]{1,0:T(8,128)(2,1)S(1)}, u32[]{:S(2)}, u32[]{:S(2)}) %collective-permute-start.35) | collective-permute-done | bytes 245792 | tf_op jit(solution)/shard_map/ppermute | solution.py:21
  135.0 3.0 %collective-permute-start.37 = (bf16[2,48,2560]{2,1,0:T(8,128)(2,1)}, bf16[2,48,2560]{2,1,0:T(8,128)(2,1)}, u32[]{:S(2)}, u32[]{:S(2)}) collective-permute-start(bf16[2,48,2560]{2,1,0:T(8,128)(2,1)} %get-tuple-element.57), channel_id=1, source_target_pairs={{0,4},{2,6},{4,0},{6,2},{1,5},{3,7},{5,1},{7,3},{8,12},{10,14},{12... | collective-permute-start | bytes 1474568 | tf_op jit(solution)/shard_map/ppermute | solution.py:27
  144.0 8.4 %collective-permute-done.29 = bf16[2,48]{1,0:T(2,128)(2,1)S(1)} collective-permute-done((bf16[2,48]{1,0:T(2,128)(2,1)S(1)}, bf16[2,48]{1,0:T(2,128)(2,1)S(1)}, u32[]{:S(2)}, u32[]{:S(2)}) %collective-permute-start.29) | collective-permute-done | bytes 224 | tf_op jit(solution)/shard_map/ppermute | solution.py:27
  153.4 4.3 %collective-permute-start.38 = (bf16[2,48,1280]{2,1,0:T(8,128)(2,1)S(1)}, bf16[2,48,1280]{2,1,0:T(8,128)(2,1)S(1)}, u32[]{:S(2)}, u32[]{:S(2)}) collective-permute-start(bf16[2,48,1280]{2,1,0:T(8,128)(2,1)S(1)} %slice.416), channel_id=1, source_target_pairs={{0,4},{2,6},{4,0},{6,2},{1,5},{3,7},{5,1},{7,3},{8,12},{10,14},{12... | collective-permute-start | bytes 737288 | tf_op jit(solution)/shard_map/ppermute | solution.py:27
  161.9 3.1 %collective-permute-done.39 = bf16[2,48,1280]{2,1,0:T(8,128)(2,1)S(1)} collective-permute-done((bf16[2,48,1280]{2,1,0:T(8,128)(2,1)S(1)}, bf16[2,48,1280]{2,1,0:T(8,128)(2,1)S(1)}, u32[]{:S(2)}, u32[]{:S(2)}) %collective-permute-start.39) | collective-permute-done | bytes 245792 | tf_op jit(solution)/shard_map/ppermute | solution.py:27
  166.5 3.7 %collective-permute-done.31 = bf16[2,48,2560]{2,1,0:T(8,128)(2,1)S(1)} collective-permute-done((bf16[2,48,2560]{2,1,0:T(8,128)(2,1)S(1)}, bf16[2,48,2560]{2,1,0:T(8,128)(2,1)S(1)}, u32[]{:S(2)}, u32[]{:S(2)}) %collective-permute-start.31) | collective-permute-done | bytes 491552 | tf_op jit(solution)/shard_map/ppermute | solution.py:27
  173.6 2.9 %collective-permute-done.33 = bf16[2,48,1280]{2,1,0:T(8,128)(2,1)S(1)} collective-permute-done((bf16[2,48,1280]{2,1,0:T(8,128)(2,1)S(1)}, bf16[2,48,1280]{2,1,0:T(8,128)(2,1)S(1)}, u32[]{:S(2)}, u32[]{:S(2)}) %collective-permute-start.33) | collective-permute-done | bytes 245792 | tf_op jit(solution)/shard_map/ppermute | solution.py:27
  181.0 3.1 %convolution_convert_fusion = bf16[384,2560]{1,0:T(8,128)(2,1)} fusion(bf16[384,2560]{1,0:T(8,128)(2,1)S(1)} %bitcast.220, bf16[384,2560]{1,0:T(8,128)(2,1)S(1)} %bitcast.214, bf16[384,192]{0,1:T(8,128)(2,1)S(1)} %get-tuple-element.53, bf16[384,192]{0,1:T(8,128)(2,1)S(1)} %get-tuple-element.46, bf16[384,192]{0,1:T(8,128)(2,1)S(1)} %copy-done.22, ...), kind=kOutput, calls=%fused_computation.4 | convolution fusion | flops 1521156096 | bytes 6488064 | tf_op jit(solution)/shard_map/dot_general | solution.py:42
  200.8 4.5 %collective-permute-done.43 = bf16[2,48,2560]{2,1,0:T(8,128)(2,1)S(1)} collective-permute-done((bf16[2,48,2560]{2,1,0:T(8,128)(2,1)S(1)}, bf16[2,48,2560]{2,1,0:T(8,128)(2,1)S(1)}, u32[]{:S(2)}, u32[]{:S(2)}) %collective-permute-start.43) | collective-permute-done | bytes 491552 | tf_op jit(solution)/shard_map/ppermute | solution.py:27
  205.2 3.7 %collective-permute-done.41 = bf16[2,48,2560]{2,1,0:T(8,128)(2,1)S(1)} collective-permute-done((bf16[2,48,2560]{2,1,0:T(8,128)(2,1)S(1)}, bf16[2,48,2560]{2,1,0:T(8,128)(2,1)S(1)}, u32[]{:S(2)}, u32[]{:S(2)}) %collective-permute-start.41) | collective-permute-done | bytes 491552 | tf_op jit(solution)/shard_map/ppermute | solution.py:27
  214.1 5.8 %collective-permute-done.47 = bf16[50,2560]{1,0:T(8,128)(2,1)} collective-permute-done((bf16[50,2560]{1,0:T(8,128)(2,1)S(1)}, bf16[50,2560]{1,0:T(8,128)(2,1)}, u32[]{:S(2)}, u32[]{:S(2)}) %collective-permute-start.47) | collective-permute-done | bytes 256032 | tf_op jit(solution)/shard_map/ppermute | solution.py:21
  (294 shorter events, 106.6 us)
Async XLA Ops:
  7.2 217.8 %reduce-scatter.3.cloned.1.call-start = ((), (), s32[]{:S(2)}) async-start(), calls=%async_computation.2 | async-start | bytes 2949120 | tf_op jit(solution)/shard_map/reduce_scatter | solution.py:258
  11.3 10.6 %collective-permute-start = (bf16[48]{0:T(256)(128)(2,1)S(1)}, bf16[48]{0:T(256)(128)(2,1)S(1)}, u32[]{:S(2)}, u32[]{:S(2)}) collective-permute-start(bf16[48]{0:T(256)(128)(2,1)S(1)} %get-tuple-element.99), channel_id=1, source_target_pairs={{0,8},{8,0},{1,9},{9,1},{2,10},{10,2},{3,11},{11,3},{4,12},{12,4},... | collective-permute-start | bytes 296 | tf_op jit(solution)/shard_map/ppermute | solution.py:21
  17.6 25.8 %collective-permute-start.4 = (bf16[48,2560]{1,0:T(8,128)(2,1)S(1)}, bf16[48,2560]{1,0:T(8,128)(2,1)S(1)}, u32[]{:S(2)}, u32[]{:S(2)}) collective-permute-start(bf16[48,2560]{1,0:T(8,128)(2,1)S(1)} %get-tuple-element.73), channel_id=1, source_target_pairs={{0,8},{8,0},{1,9},{9,1},{2,10},{10,2},{3,11},{11,3},{4,12},{12,4},... | collective-permute-start | bytes 737288 | tf_op jit(solution)/shard_map/ppermute | solution.py:21
  18.9 22.9 %collective-permute-start.10 = (bf16[48,2560]{1,0:T(8,128)(2,1)S(1)}, bf16[48,2560]{1,0:T(8,128)(2,1)S(1)}, u32[]{:S(2)}, u32[]{:S(2)}) collective-permute-start(bf16[48,2560]{1,0:T(8,128)(2,1)S(1)} %get-tuple-element.69), channel_id=1, source_target_pairs={{0,8},{8,0},{1,9},{9,1},{2,10},{10,2},{3,11},{11,3},{4,12},{12,4},... | collective-permute-start | bytes 737288 | tf_op jit(solution)/shard_map/ppermute | solution.py:21
  21.8 22.3 %collective-permute-start.16 = (bf16[192,1280]{1,0:T(8,128)(2,1)S(1)}, bf16[192,1280]{1,0:T(8,128)(2,1)S(1)}, u32[]{:S(2)}, u32[]{:S(2)}) collective-permute-start(bf16[192,1280]{1,0:T(8,128)(2,1)S(1)} %bitcast.237), channel_id=1, source_target_pairs={{0,1},{1,0},{2,3},{3,2},{4,5},{5,4},{6,7},{7,6},{8,9},{9,8},{10,11... | collective-permute-start | bytes 1474568 | tf_op jit(solution)/shard_map/ppermute | solution.py:27
  31.6 26.0 %collective-permute-start.15 = (bf16[192,1280]{1,0:T(8,128)(2,1)}, bf16[192,1280]{1,0:T(8,128)(2,1)}, u32[]{:S(2)}, u32[]{:S(2)}) collective-permute-start(bf16[192,1280]{1,0:T(8,128)(2,1)} %bitcast.28), channel_id=1, source_target_pairs={{0,1},{1,0},{2,3},{3,2},{4,5},{5,4},{6,7},{7,6},{8,9},{9,8},{10,11... | collective-permute-start | bytes 1474568 | tf_op jit(solution)/shard_map/ppermute | solution.py:27
  41.9 14.2 %collective-permute-start.11 = (bf16[2,48,2560]{2,1,0:T(8,128)(2,1)S(1)}, bf16[2,48,2560]{2,1,0:T(8,128)(2,1)S(1)}, u32[]{:S(2)}, u32[]{:S(2)}) collective-permute-start(bf16[2,48,2560]{2,1,0:T(8,128)(2,1)S(1)} %get-tuple-element.67), channel_id=1, source_target_pairs={{0,2},{2,0},{4,6},{6,4},{1,3},{3,1},{5,7},{7,5},{8,10},{10,8},{12,... | collective-permute-start | bytes 1474568 | tf_op jit(solution)/shard_map/ppermute | solution.py:27
  43.4 14.2 %collective-permute-start.12 = (bf16[2,48,2560]{2,1,0:T(8,128)(2,1)S(1)}, bf16[2,48,2560]{2,1,0:T(8,128)(2,1)S(1)}, u32[]{:S(2)}, u32[]{:S(2)}) collective-permute-start(bf16[2,48,2560]{2,1,0:T(8,128)(2,1)S(1)} %get-tuple-element.67), channel_id=1, source_target_pairs={{0,4},{2,6},{4,0},{6,2},{1,5},{3,7},{5,1},{7,3},{8,12},{10,14},{12... | collective-permute-start | bytes 1474568 | tf_op jit(solution)/shard_map/ppermute | solution.py:27
  43.5 23.1 %collective-permute-start.5 = (bf16[2,48,2560]{2,1,0:T(8,128)(2,1)S(1)}, bf16[2,48,2560]{2,1,0:T(8,128)(2,1)S(1)}, u32[]{:S(2)}, u32[]{:S(2)}) collective-permute-start(bf16[2,48,2560]{2,1,0:T(8,128)(2,1)S(1)} %get-tuple-element.71), channel_id=1, source_target_pairs={{0,2},{2,0},{4,6},{6,4},{1,3},{3,1},{5,7},{7,5},{8,10},{10,8},{12,... | collective-permute-start | bytes 1474568 | tf_op jit(solution)/shard_map/ppermute | solution.py:27
  44.9 23.2 %collective-permute-start.6 = (bf16[2,48,2560]{2,1,0:T(8,128)(2,1)S(1)}, bf16[2,48,2560]{2,1,0:T(8,128)(2,1)S(1)}, u32[]{:S(2)}, u32[]{:S(2)}) collective-permute-start(bf16[2,48,2560]{2,1,0:T(8,128)(2,1)S(1)} %get-tuple-element.71), channel_id=1, source_target_pairs={{0,4},{2,6},{4,0},{6,2},{1,5},{3,7},{5,1},{7,3},{8,12},{10,14},{12... | collective-permute-start | bytes 1474568 | tf_op jit(solution)/shard_map/ppermute | solution.py:27
  56.1 21.3 %collective-permute-start.9 = (bf16[192,1280]{1,0:T(8,128)(2,1)S(1)}, bf16[192,1280]{1,0:T(8,128)(2,1)S(1)}, u32[]{:S(2)}, u32[]{:S(2)}) collective-permute-start(bf16[192,1280]{1,0:T(8,128)(2,1)S(1)} %bitcast.251), channel_id=1, source_target_pairs={{0,1},{1,0},{2,3},{3,2},{4,5},{5,4},{6,7},{7,6},{8,9},{9,8},{10,11... | collective-permute-start | bytes 1474568 | tf_op jit(solution)/shard_map/ppermute | solution.py:27
  57.6 15.8 %collective-permute-start.13 = (bf16[2,48,1280]{2,1,0:T(8,128)(2,1)S(1)}, bf16[2,48,1280]{2,1,0:T(8,128)(2,1)S(1)}, u32[]{:S(2)}, u32[]{:S(2)}) collective-permute-start(bf16[2,48,1280]{2,1,0:T(8,128)(2,1)S(1)} %slice.397), channel_id=1, source_target_pairs={{0,4},{2,6},{4,0},{6,2},{1,5},{3,7},{5,1},{7,3},{8,12},{10,14},{12... | collective-permute-start | bytes 737288 | tf_op jit(solution)/shard_map/ppermute | solution.py:27
  57.6 15.8 %collective-permute-start.14 = (bf16[2,48,1280]{2,1,0:T(8,128)(2,1)S(1)}, bf16[2,48,1280]{2,1,0:T(8,128)(2,1)S(1)}, u32[]{:S(2)}, u32[]{:S(2)}) collective-permute-start(bf16[2,48,1280]{2,1,0:T(8,128)(2,1)S(1)} %slice.398), channel_id=1, source_target_pairs={{0,2},{2,0},{4,6},{6,4},{1,3},{3,1},{5,7},{7,5},{8,10},{10,8},{12,... | collective-permute-start | bytes 737288 | tf_op jit(solution)/shard_map/ppermute | solution.py:27
  89.9 13.2 %collective-permute-start.20 = (bf16[2,48,2560]{2,1,0:T(8,128)(2,1)S(1)}, bf16[2,48,2560]{2,1,0:T(8,128)(2,1)S(1)}, u32[]{:S(2)}, u32[]{:S(2)}) collective-permute-start(bf16[2,48,2560]{2,1,0:T(8,128)(2,1)S(1)} %pad_maximum_fusion.12), channel_id=1, source_target_pairs={{0,2},{2,0},{4,6},{6,4},{1,3},{3,1},{5,7},{7,5},{8,10},{10,8},{12,... | collective-permute-start | bytes 1474568 | tf_op jit(solution)/shard_map/ppermute | solution.py:27
  96.8 10.6 %collective-permute-start.18 = (bf16[2,48,2560]{2,1,0:T(8,128)(2,1)S(1)}, bf16[2,48,2560]{2,1,0:T(8,128)(2,1)S(1)}, u32[]{:S(2)}, u32[]{:S(2)}) collective-permute-start(bf16[2,48,2560]{2,1,0:T(8,128)(2,1)S(1)} %pad_maximum_fusion.11), channel_id=1, source_target_pairs={{0,4},{2,6},{4,0},{6,2},{1,5},{3,7},{5,1},{7,3},{8,12},{10,14},{12... | collective-permute-start | bytes 1474568 | tf_op jit(solution)/shard_map/ppermute | solution.py:27
  107.6 11.4 %collective-permute-start.24 = (bf16[50,2560]{1,0:T(8,128)(2,1)S(1)}, bf16[50,2560]{1,0:T(8,128)(2,1)S(1)}, u32[]{:S(2)}, u32[]{:S(2)}) collective-permute-start(bf16[50,2560]{1,0:T(8,128)(2,1)S(1)} %pad_maximum_fusion.17), channel_id=1, source_target_pairs={{0,8},{8,0},{1,9},{9,1},{2,10},{10,2},{3,11},{11,3},{4,12},{12,4},... | collective-permute-start | bytes 768008 | tf_op jit(solution)/shard_map/ppermute | solution.py:21
  129.6 11.9 %collective-permute-start.28 = (bf16[2,48]{1,0:T(2,128)(2,1)S(1)}, bf16[2,48]{1,0:T(2,128)(2,1)S(1)}, u32[]{:S(2)}, u32[]{:S(2)}) collective-permute-start(bf16[2,48]{1,0:T(2,128)(2,1)S(1)} %pad_maximum_fusion.22), channel_id=1, source_target_pairs={{0,4},{2,6},{4,0},{6,2},{1,5},{3,7},{5,1},{7,3},{8,12},{10,14},{12... | collective-permute-start | bytes 584 | tf_op jit(solution)/shard_map/ppermute | solution.py:27
  134.8 17.6 %collective-permute-start.36 = (bf16[2,48,2560]{2,1,0:T(8,128)(2,1)}, bf16[2,48,2560]{2,1,0:T(8,128)(2,1)}, u32[]{:S(2)}, u32[]{:S(2)}) collective-permute-start(bf16[2,48,2560]{2,1,0:T(8,128)(2,1)} %get-tuple-element.57), channel_id=1, source_target_pairs={{0,2},{2,0},{4,6},{6,4},{1,3},{3,1},{5,7},{7,5},{8,10},{10,8},{12,... | collective-permute-start | bytes 1474568 | tf_op jit(solution)/shard_map/ppermute | solution.py:27
  135.0 22.8 %collective-permute-start.37 = (bf16[2,48,2560]{2,1,0:T(8,128)(2,1)}, bf16[2,48,2560]{2,1,0:T(8,128)(2,1)}, u32[]{:S(2)}, u32[]{:S(2)}) collective-permute-start(bf16[2,48,2560]{2,1,0:T(8,128)(2,1)} %get-tuple-element.57), channel_id=1, source_target_pairs={{0,4},{2,6},{4,0},{6,2},{1,5},{3,7},{5,1},{7,3},{8,12},{10,14},{12... | collective-permute-start | bytes 1474568 | tf_op jit(solution)/shard_map/ppermute | solution.py:27
  139.2 19.6 %collective-permute-start.30 = (bf16[48,2560]{1,0:T(8,128)(2,1)}, bf16[48,2560]{1,0:T(8,128)(2,1)}, u32[]{:S(2)}, u32[]{:S(2)}) collective-permute-start(bf16[48,2560]{1,0:T(8,128)(2,1)} %get-tuple-element.63), channel_id=1, source_target_pairs={{0,8},{8,0},{1,9},{9,1},{2,10},{10,2},{3,11},{11,3},{4,12},{12,4},... | collective-permute-start | bytes 737288 | tf_op jit(solution)/shard_map/ppermute | solution.py:21
  141.5 10.9 %collective-permute-start.29 = (bf16[2,48]{1,0:T(2,128)(2,1)S(1)}, bf16[2,48]{1,0:T(2,128)(2,1)S(1)}, u32[]{:S(2)}, u32[]{:S(2)}) collective-permute-start(bf16[2,48]{1,0:T(2,128)(2,1)S(1)} %pad_maximum_fusion.22), channel_id=1, source_target_pairs={{0,6},{2,4},{4,2},{6,0},{1,7},{3,5},{5,3},{7,1},{8,14},{10,12},{12... | collective-permute-start | bytes 584 | tf_op jit(solution)/shard_map/ppermute | solution.py:27
  159.8 10.4 %collective-permute-start.31 = (bf16[2,48,2560]{2,1,0:T(8,128)(2,1)S(1)}, bf16[2,48,2560]{2,1,0:T(8,128)(2,1)S(1)}, u32[]{:S(2)}, u32[]{:S(2)}) collective-permute-start(bf16[2,48,2560]{2,1,0:T(8,128)(2,1)S(1)} %get-tuple-element.61), channel_id=1, source_target_pairs={{0,2},{2,0},{4,6},{6,4},{1,3},{3,1},{5,7},{7,5},{8,10},{10,8},{12,... | collective-permute-start | bytes 1474568 | tf_op jit(solution)/shard_map/ppermute | solution.py:27
  186.2 41.0 %reduce-scatter.5.cloned.1.call-start = ((), (), s32[]{:S(2)}) async-start(), calls=%async_computation.3 | async-start | bytes 1474560 | tf_op jit(solution)/shard_map/reduce_scatter | solution.py:261
  209.2 10.8 %collective-permute-start.47 = (bf16[50,2560]{1,0:T(8,128)(2,1)S(1)}, bf16[50,2560]{1,0:T(8,128)(2,1)}, u32[]{:S(2)}, u32[]{:S(2)}) collective-permute-start(bf16[50,2560]{1,0:T(8,128)(2,1)S(1)} %pad_maximum_fusion.18), channel_id=1, source_target_pairs={{0,8},{8,0},{1,9},{9,1},{2,10},{10,2},{3,11},{11,3},{4,12},{12,4},... | collective-permute-start | bytes 768008 | tf_op jit(solution)/shard_map/ppermute | solution.py:21
  (66 other events, 385.6 us)
Sparse Core Ops, SparseCore 0:
  186.3 8.8 reduce-scatter.2
  214.2 7.5 reduce-scatter.4
